TPU v7x, 128 devices: a whole 4x4x4 slice. The times are simulated.
128 devices in a mesh: region: 8 (over x, core), shard: 16 (over y, z).
Axes of the slice: x: 4, y: 4, z: 4, core: 2. Of those that a mesh axis runs over, the one named last changes fastest.
Arguments:
- features: bfloat16 [262144, 256], P(('region', 'shard')), may hold values from -6 to 6
- kernel_map: int32 [27, 2048], replicated, may hold values from -1 to 2047, as said below
- weights: bfloat16 [27, 256, 256], replicated, may hold values from -0.078125 to 0.078125
- out_grad: bfloat16 [262144, 256], P(('region', 'shard')), may hold values from -6 to 6
Outputs:
- conv_out: bfloat16 [262144, 256], P(('region', 'shard'))
- in_grad: bfloat16 [262144, 256], P(('region', 'shard'))
- weight_grad: float32 [27, 256, 256], P(None, 'shard')
Inputs may be any that keep to these rules, and one draw needn't show every extreme that they name: `kernel_map`: -1 marks a missing pair. The centre offset 27 // 2 maps every block to itself. Every other source block lies on the output block's own device, on another device of the same index of region, or on the device of the same index of shard in the next lower or next higher region. For each device, the output blocks it owns name at most 4 distinct blocks of any one other device; in every region some device names exactly 4 blocks of every other device of its region, and in every draw some device names exactly 4 blocks of a device of a neighbouring region.
All inputs are finite; a program needn't handle non-finite values.
Results may differ from a plain program's by a relative error of at most 0.0028.
Values may be sent and summed in bfloat16 or wider, within the bound.
No kernel may reach another device: no remote copies, remote signals or barrier semaphores. Data moves between devices by JAX's collectives and lax.ppermute only.
A program may use at most 320 MiB of HBM per device.

v0:
```python
import math

import jax
import jax.numpy as jnp
from jax import lax
from jax.sharding import PartitionSpec as P

VOX = 128


def padded(cells, sides, width):
    for axis, dim in sides:
        count = lax.axis_size(axis)
        ends = count - 1
        head = lax.slice_in_dim(cells, 0, width, axis=dim)
        tail = lax.slice_in_dim(cells, cells.shape[dim] - width, cells.shape[dim], axis=dim)
        cells = jnp.concatenate(
            [
                lax.ppermute(tail, axis, [(i, (i + 1) % count) for i in range(ends)]),
                cells,
                lax.ppermute(head, axis, [((i + 1) % count, i) for i in range(ends)]),
            ],
            axis=dim,
        )
    return cells


def choose_slots(wanted, capacity):
    ranks = jnp.cumsum(wanted.astype(jnp.int32), axis=-1) - 1
    places = jnp.arange(capacity, dtype=jnp.int32)
    chosen = wanted[..., None, :] & (ranks[..., None, :] == places[:, None])
    return (chosen, ranks)


def body(features, kernel_map, weights, out_grad):
    n_shard = lax.axis_size("shard")
    n_region = lax.axis_size("region")
    my_shard = lax.axis_index("shard")
    my_region = lax.axis_index("region")
    channels = features.shape[1]
    voxels = VOX
    blocks_dev = features.shape[0] // voxels
    capacity = blocks_dev // 4
    total_blocks = kernel_map.shape[1]
    offsets = kernel_map.shape[0]
    region_blocks = n_shard * blocks_dev
    my_device = my_region * n_shard + my_shard
    first = my_device * blocks_dev
    region_base = my_region * region_blocks
    own_blocks = features.reshape(blocks_dev, voxels, channels)
    grad_blocks = out_grad.reshape(blocks_dev, voxels, channels)
    block_range = jnp.arange(blocks_dev, dtype=jnp.int32)
    own_ids = first + block_range
    shard_ids = jnp.arange(n_shard, dtype=jnp.int32)
    peer_maps = lax.dynamic_slice_in_dim(kernel_map, region_base, region_blocks, 1).reshape(
        offsets, n_shard, blocks_dev
    )
    asked = jnp.any(peer_maps[..., None] == own_ids, axis=(0, 2)) & (shard_ids[:, None] != my_shard)
    lower_maps = lax.dynamic_slice_in_dim(
        kernel_map, jnp.maximum(first - region_blocks, 0), blocks_dev, 1
    )
    upper_maps = lax.dynamic_slice_in_dim(
        kernel_map, jnp.minimum(first + region_blocks, total_blocks - blocks_dev), blocks_dev, 1
    )
    asked_lower = jnp.any(lower_maps[..., None] == own_ids, axis=(0, 1)) & (my_region > 0)
    asked_upper = jnp.any(upper_maps[..., None] == own_ids, axis=(0, 1)) & (
        my_region < n_region - 1
    )
    chosen, _ = choose_slots(asked, capacity)
    chosen_lower, _ = choose_slots(asked_lower, capacity)
    chosen_upper, _ = choose_slots(asked_upper, capacity)
    chosen_rims = jnp.concatenate([chosen_lower, chosen_upper], axis=0)
    outgoing = jnp.einsum(
        "pcj,jvd->pcvd", chosen.astype(jnp.bfloat16), own_blocks, preferred_element_type=jnp.float32
    ).astype(jnp.bfloat16)
    rim_blocks = jnp.einsum(
        "cj,jvd->cvd",
        chosen_rims.astype(jnp.bfloat16),
        own_blocks,
        preferred_element_type=jnp.float32,
    ).astype(jnp.bfloat16)
    incoming = lax.all_to_all(outgoing, "shard", split_axis=0, concat_axis=0, tiled=True)
    rims = padded(rim_blocks, (("region", 0),), capacity)
    sources = lax.dynamic_slice_in_dim(kernel_map, first, blocks_dev, 1)
    present = sources >= 0
    region_ids = region_base + jnp.arange(region_blocks, dtype=jnp.int32)
    matches = present[..., None] & (sources[..., None] == region_ids)
    needed = jnp.any(matches, axis=(0, 1)).reshape(n_shard, blocks_dev) & (
        shard_ids[:, None] != my_shard
    )
    _, ranks = choose_slots(needed, capacity)
    local_pos = jnp.broadcast_to(block_range, (n_shard, blocks_dev))
    remote_pos = blocks_dev + shard_ids[:, None] * capacity + ranks
    positions = jnp.where(shard_ids[:, None] == my_shard, local_pos, remote_pos).reshape(
        region_blocks
    )
    table_index = jnp.sum(jnp.where(matches, positions, 0), axis=-1)
    rim_start = blocks_dev + n_shard * capacity
    lower_matches = present[..., None] & (sources[..., None] == first - region_blocks + block_range)
    _, lower_ranks = choose_slots(jnp.any(lower_matches, axis=(0, 1)), capacity)
    table_index = table_index + jnp.sum(
        jnp.where(lower_matches, rim_start + lower_ranks, 0), axis=-1
    )
    upper_matches = present[..., None] & (sources[..., None] == first + region_blocks + block_range)
    _, upper_ranks = choose_slots(jnp.any(upper_matches, axis=(0, 1)), capacity)
    table_index = table_index + jnp.sum(
        jnp.where(upper_matches, rim_start + capacity + upper_ranks, 0), axis=-1
    )
    table_rows = rim_start + 2 * capacity
    table_index = jnp.where(present, table_index, table_rows)
    table = jnp.concatenate(
        [
            own_blocks,
            incoming.reshape(n_shard * capacity, voxels, channels),
            rims[:capacity],
            rims[rims.shape[0] - capacity :],
            jnp.zeros((1, voxels, channels), jnp.bfloat16),
        ],
        axis=0,
    )
    gathered = jnp.take(table, table_index, axis=0)
    conv_out = jnp.einsum(
        "kbvc,kcd->bvd", gathered, weights, preferred_element_type=jnp.float32
    ).astype(jnp.bfloat16)
    scale = 1.0 / math.sqrt(total_blocks * voxels)
    kernel_term = (
        jnp.einsum("kbvc,bvd->kcd", gathered, grad_blocks, preferred_element_type=jnp.float32)
        * scale
    )
    backward = jnp.einsum("bvd,kcd->kbvc", grad_blocks, weights, preferred_element_type=jnp.float32)
    table_grad = jax.ops.segment_sum(
        backward.reshape(offsets * blocks_dev, voxels, channels),
        table_index.reshape(-1),
        num_segments=table_rows + 1,
    )
    input_acc = table_grad[:blocks_dev]
    remote_sums = table_grad[blocks_dev:table_rows].astype(jnp.bfloat16)
    returned = lax.all_to_all(
        remote_sums[: n_shard * capacity].reshape(n_shard, capacity, voxels, channels),
        "shard",
        split_axis=0,
        concat_axis=0,
        tiled=True,
    )
    input_acc = input_acc + jnp.einsum(
        "pcj,pcvd->jvd",
        chosen.astype(jnp.float32),
        returned.astype(jnp.float32),
        precision=lax.Precision.HIGHEST,
    )
    rim_back = padded(remote_sums[n_shard * capacity :], (("region", 0),), capacity)
    rim_wide = rim_back.astype(jnp.float32)
    input_acc = input_acc + jnp.einsum(
        "cj,cvd->jvd",
        chosen_lower.astype(jnp.float32),
        rim_wide[:capacity],
        precision=lax.Precision.HIGHEST,
    )
    input_acc = input_acc + jnp.einsum(
        "cj,cvd->jvd",
        chosen_upper.astype(jnp.float32),
        rim_wide[rim_wide.shape[0] - capacity :],
        precision=lax.Precision.HIGHEST,
    )
    in_grad = input_acc.reshape(blocks_dev * voxels, channels).astype(jnp.bfloat16)
    share_width = channels // n_shard
    summed = lax.psum(kernel_term, ("region", "shard"))
    weight_grad = lax.dynamic_slice_in_dim(summed, my_shard * share_width, share_width, 1)
    return (conv_out.reshape(blocks_dev * voxels, channels), in_grad, weight_grad)


def solution(mesh):
    return jax.shard_map(
        body,
        mesh=mesh,
        in_specs=(P(("region", "shard"), None), P(), P(), P(("region", "shard"), None)),
        out_specs=(
            P(("region", "shard"), None),
            P(("region", "shard"), None),
            P(None, "shard", None),
        ),
        check_vma=False,
    )
```

profile of v0, /device:TPU:1, one launch (start us, length us, event | category | flops | bytes accessed | tf_op | source)
XLA Modules:
  0.0 612.5 jit_solution(3704366862129396821)
XLA Ops:
  23.8 2.9 convolution_convert_fusion
  26.7 3.4 copy.72
  30.2 8.6 %all-to-all-start = ((bf16[16,4,128,256]{3,2,1,0:T(8,128)(2,1)}), bf16[16,4,128,256]{3,2,1,0:T(8,128)(2,1)}, u32[]{:S(2)}, u32[]{:S(2)}) async-start(bf16[16,4,128,256]{3,2,1,0:T(8,128)(2,1)} %copy.72), calls=%async_computation | async-start | bytes 8388608 | tf_op jit(solution)/shard_map/all_to_all | solution.py:82
  63.1 20.9 %fusion.6 = f32[27,256,16,128]{3,1,2,0:T(8,128)} fusion(bf16[16,128,256,1]{2,1,0,3:T(8,128)(2,1)} %bitcast.70, bf16[27,256,256]{2,1,0:T(8,128)(2,1)S(1)} %copy-done), kind=kOutput, calls=%fused_computation.10 | convolution fusion | flops 7247757312 | bytes 61210624 | tf_op jit(solution)/shard_map/bvd,kcd->kbvc/dot_general | solution.py:130
  83.9 54.8 %copy.82 = f32[432,128,256]{2,1,0:T(8,128)} copy(f32[432,128,256]{1,2,0:T(8,128)} %bitcast.64) | data formatting | bytes 113246208 | tf_op jit(solution)/shard_map/reshape | solution.py:132
  138.8 5.8 broadcast_in_dim.91
  144.6 127.9 %scatter_fusion = f32[89,128,256]{2,1,0:T(8,128)} fusion(f32[89,128,256]{2,1,0:T(8,128)} %broadcast_in_dim.91, s32[432]{0:T(512)} %reshape.277, f32[432,128,256]{2,1,0:T(8,128)} %copy.82), kind=kCustom, calls=%fused_computation.1 | custom fusion | flops 14155776 | bytes 169871040 | tf_op jit(solution)/shard_map/scatter-add | solution.py:131
  272.5 13.2 %copy.108 = bf16[89,128,256]{2,0,1:T(8,128)(2,1)} copy(f32[89,128,256]{2,1,0:T(8,128)} %scatter_fusion) | data formatting | bytes 17498112 | tf_op jit(solution)/shard_map/scatter-add | solution.py:131
  289.9 3.1 collective-permute-start.3
  309.7 2.5 collective-permute-start
  312.2 2.7 collective-permute-start.1
  318.7 4.7 slice.39
  323.4 15.6 %copy.83 = f32[89,128,256]{2,0,1:T(8,128)} copy(f32[89,128,256]{2,1,0:T(8,128)} %scatter_fusion) | data formatting | bytes 23330816 | tf_op jit(solution)/shard_map/scatter-add | solution.py:131
  339.0 4.6 copy.85
  343.6 5.7 copy.86
  349.3 12.8 %all-to-all-start.1 = ((bf16[16,4,128,256]{3,1,2,0:T(4,128)(2,1)}), bf16[16,4,128,256]{3,1,2,0:T(4,128)(2,1)}, u32[]{:S(2)}, u32[]{:S(2)}) async-start(bf16[16,4,128,256]{3,1,2,0:T(4,128)(2,1)} %copy.86), calls=%async_computation.1 | async-start | bytes 8388608 | tf_op jit(solution)/shard_map/all_to_all | solution.py:138
  362.1 4.8 constant_dynamic-update-slice_fusion
  370.9 16.6 %gather_fusion = bf16[432,128,256]{2,1,0:T(8,128)(2,1)} fusion(bf16[89,128,256]{2,1,0:T(8,128)(2,1)} %broadcast_dynamic-update-slice_fusion, s32[1024]{0:T(1024)S(1)} %pad_clamp_fusion), kind=kCustom, calls=%fused_computation | custom fusion | bytes 56624832 | tf_op jit(solution)/shard_map/jit(_take)/gather | solution.py:121
  387.4 36.7 %copy.80 = bf16[27,16,128,256]{2,3,1,0:T(8,128)(2,1)} copy(bf16[27,16,128,256]{3,2,1,0:T(8,128)(2,1)} %bitcast.65) | data formatting | bytes 56623104 | tf_op jit(solution)/shard_map/jit(_take)/gather | solution.py:121
  424.2 16.1 %bitcast_multiply_fusion = f32[27,256,256]{2,1,0:T(8,128)} fusion(bf16[16,128,256,1]{2,1,0,3:T(8,128)(2,1)} %bitcast.71, bf16[27,16,128,256]{2,3,1,0:T(8,128)(2,1)} %copy.80, pred[27,16]{1,0:T(8,128)(4,1)S(1)} %copy-done.5), kind=kOutput, calls=%fused_computation.7 | convolution fusion | flops 7263682560 | bytes 36438448 | tf_op jit(solution)/shard_map/kbvc,bvd->kcd/dot_general | solution.py:127
  440.3 2.8 fusion.37
  443.2 4.7 fusion.4
  451.6 20.1 %bitcast_convert_fusion = bf16[16,128,256]{2,1,0:T(8,128)(2,1)} fusion(bf16[27,256,256]{2,1,0:T(8,128)(2,1)S(1)} %copy-done, bf16[27,16,128,256]{2,3,1,0:T(8,128)(2,1)} %copy.80, pred[27,16]{1,0:T(8,128)(4,1)S(1)} %copy-done.5), kind=kOutput, calls=%fused_computation.18 | convolution fusion | flops 7262437376 | bytes 32899504 | tf_op jit(solution)/shard_map/kbvc,kcd->bvd/dot_general | solution.py:122
  471.8 131.7 %all-reduce.2.cloned.1.call-done = f32[27,256,256]{2,1,0:T(8,128)} async-done(((f32[27,256,256]{2,1,0:T(8,128)}), f32[27,256,256]{2,1,0:T(8,128)}) %all-reduce.2.cloned.1.call-update) | async-done | bytes 7077904 | tf_op jit(solution)/shard_map/psum | solution.py:167
  (89 shorter events, 75.0 us)
Async XLA Ops:
  7.2 55.9 %copy-start = (bf16[27,256,256]{2,1,0:T(8,128)(2,1)S(1)}, bf16[27,256,256]{2,1,0:T(8,128)(2,1)}, u32[]{:S(2)}) copy-start(bf16[27,256,256]{2,1,0:T(8,128)(2,1)} %param.6) | copy-start | bytes 10616836
  9.6 0.6 copy-start.2
  30.2 319.1 %all-to-all-start = ((bf16[16,4,128,256]{3,2,1,0:T(8,128)(2,1)}), bf16[16,4,128,256]{3,2,1,0:T(8,128)(2,1)}, u32[]{:S(2)}, u32[]{:S(2)}) async-start(bf16[16,4,128,256]{3,2,1,0:T(8,128)(2,1)} %copy.72), calls=%async_computation | async-start | bytes 8388608 | tf_op jit(solution)/shard_map/all_to_all | solution.py:82
  41.8 0.6 copy-start.8
  288.0 152.3 %collective-permute-start.2 = (bf16[4,128,256]{2,0,1:T(4,128)(2,1)}, bf16[4,128,256]{2,0,1:T(4,128)(2,1)}, u32[]{:S(2)}, u32[]{:S(2)}) collective-permute-start(bf16[4,128,256]{2,0,1:T(4,128)(2,1)} %get-tuple-element.20), channel_id=1, source_target_pairs={{0,16},{16,32},{32,48},{48,64},{64,80},{80,96},{96,112},{1,17},{17... | collective-permute-start | bytes 786440 | tf_op jit(solution)/shard_map/ppermute | solution.py:19
  289.9 158.0 %collective-permute-start.3 = (bf16[4,128,256]{2,0,1:T(4,128)(2,1)}, bf16[4,128,256]{2,0,1:T(4,128)(2,1)}, u32[]{:S(2)}, u32[]{:S(2)}) collective-permute-start(bf16[4,128,256]{2,0,1:T(4,128)(2,1)} %get-tuple-element.19), channel_id=1, source_target_pairs={{16,0},{32,16},{48,32},{64,48},{80,64},{96,80},{112,96},{17,1},{33... | collective-permute-start | bytes 786440 | tf_op jit(solution)/shard_map/ppermute | solution.py:21
  306.3 8.7 %copy-start.7 = (pred[4,16]{1,0:T(4,128)(4,1)}, pred[4,16]{1,0:T(4,128)(4,1)S(1)}, u32[]{:S(2)}) copy-start(pred[4,16]{1,0:T(4,128)(4,1)S(1)} %fusion.31) | copy-start | bytes 196
  306.9 8.1 %copy-start.6 = (pred[4,16]{1,0:T(4,128)(4,1)}, pred[4,16]{1,0:T(4,128)(4,1)S(1)}, u32[]{:S(2)}) copy-start(pred[4,16]{1,0:T(4,128)(4,1)S(1)} %fusion.32) | copy-start | bytes 196
  309.7 57.2 %collective-permute-start = (bf16[4,128,256]{2,0,1:T(4,128)(2,1)}, bf16[4,128,256]{2,0,1:T(4,128)(2,1)}, u32[]{:S(2)}, u32[]{:S(2)}) collective-permute-start(bf16[4,128,256]{2,0,1:T(4,128)(2,1)} %get-tuple-element.22), channel_id=1, source_target_pairs={{0,16},{16,32},{32,48},{48,64},{64,80},{80,96},{96,112},{1,17},{17... | collective-permute-start | bytes 786440 | tf_op jit(solution)/shard_map/ppermute | solution.py:19
  312.2 56.4 %collective-permute-start.1 = (bf16[4,128,256]{2,0,1:T(4,128)(2,1)}, bf16[4,128,256]{2,0,1:T(4,128)(2,1)}, u32[]{:S(2)}, u32[]{:S(2)}) collective-permute-start(bf16[4,128,256]{2,0,1:T(4,128)(2,1)} %get-tuple-element.21), channel_id=1, source_target_pairs={{16,0},{32,16},{48,32},{64,48},{80,64},{96,80},{112,96},{17,1},{33... | collective-permute-start | bytes 786440 | tf_op jit(solution)/shard_map/ppermute | solution.py:21
  349.3 93.9 %all-to-all-start.1 = ((bf16[16,4,128,256]{3,1,2,0:T(4,128)(2,1)}), bf16[16,4,128,256]{3,1,2,0:T(4,128)(2,1)}, u32[]{:S(2)}, u32[]{:S(2)}) async-start(bf16[16,4,128,256]{3,1,2,0:T(4,128)(2,1)} %copy.86), calls=%async_computation.1 | async-start | bytes 8388608 | tf_op jit(solution)/shard_map/all_to_all | solution.py:138
  362.1 241.3 %all-reduce.2.cloned.1.call-start = ((), (), s32[]{:S(2)}) async-start(), calls=%async_computation.2 | async-start | bytes 14155776 | tf_op jit(solution)/shard_map/psum | solution.py:167
  387.4 36.7 %copy-start.5 = (pred[27,16]{1,0:T(8,128)(4,1)S(1)}, pred[27,16]{1,0:T(8,128)(4,1)}, u32[]{:S(2)}) copy-start(pred[27,16]{1,0:T(8,128)(4,1)} %get-tuple-element.9) | copy-start | bytes 1300
  440.3 2.9 copy-start.3
  440.3 2.9 copy-start.4
  443.2 4.7 copy-start.1
Sparse Core Ops, SparseCore 0:
  440.4 162.9 all-reduce.1
where the time goes:
time: 623 us; the launch traced here: 613 us
  local copies, waits for them, and re-layouts  204 us (33%)
  other arithmetic  159 us (26%)
  waiting for transfers between devices  132 us (21%)
  matrix products  71.9 us (12%)
  starting transfers between devices  31.7 us (5%)
  between operations  14.7 us (2%)
    psum x1, waiting for transfers between devices, body(): summed = lax.psum(kernel_term, ('region', 'shard'))  132 us
    scatter-add x1, other arithmetic, body(): jax.ops.segment_sum(backward.reshape(offsets * blocks_dev, voxels, channe...  128 us
    reshape x1, local copies, waits for them, and re-layouts, body(): backward.reshape(offsets * blocks_dev, voxels, channels)  54.8 us
    gather x2, local copies, waits for them, and re-layouts, body(): gathered = jnp.take(table, table_index, axis=0)  53.3 us
    scatter-add x2, local copies, waits for them, and re-layouts, body(): jax.ops.segment_sum(backward.reshape(offsets * blocks_dev, voxels, channe...  28.8 us
    dot_general x1, matrix products, body(): jnp.einsum('bvd,kcd->kbvc', grad_blocks, weights, preferred_element_type=...  20.9 us
    dot_general x1, matrix products, body(): jnp.einsum('kbvc,kcd->bvd', gathered, weights, preferred_element_type=jnp...  20.1 us
    dot_general x1, matrix products, body(): jnp.einsum('kbvc,bvd->kcd', gathered, grad_blocks, preferred_element_type...  16.1 us
  transfers between devices with their start and end apart: 7, of which 1 were waited for; matrix products, arithmetic and copies ran while one was open for 67% of the time, Pallas kernels for 0%

commit v1 on v0

--- a/solution.py
+++ b/solution.py
@@ -3,6 +3,8 @@
 import jax
 import jax.numpy as jnp
 from jax import lax
+from jax.experimental import pallas as pl
+from jax.experimental.pallas import tpu as pltpu
 from jax.sharding import PartitionSpec as P
 
 VOX = 128
@@ -30,6 +32,45 @@
     places = jnp.arange(capacity, dtype=jnp.int32)
     chosen = wanted[..., None, :] & (ranks[..., None, :] == places[:, None])
     return (chosen, ranks)
+
+
+def _table_grad_kernel(idx_ref, grad_ref, w_ref, out_ref):
+    k = pl.program_id(0)
+    blocks, voxels, channels = grad_ref.shape
+    rows = out_ref.shape[0]
+
+    @pl.when(k == 0)
+    def _():
+        out_ref[...] = jnp.zeros_like(out_ref)
+
+    rows_in = grad_ref[...].reshape(blocks * voxels, channels)
+    back = lax.dot_general(
+        rows_in, w_ref[0], (((1,), (1,)), ((), ())), preferred_element_type=jnp.float32
+    )
+    for b in range(blocks):
+        t = jnp.clip(idx_ref[k * blocks + b], 0, rows - 1)
+        out_ref[t] += back[b * voxels : (b + 1) * voxels]
+
+
+def table_grad_sums(table_index, grad_blocks, weights, rows):
+    blocks, voxels, channels = grad_blocks.shape
+    offsets = weights.shape[0]
+    return pl.pallas_call(
+        _table_grad_kernel,
+        out_shape=jax.ShapeDtypeStruct((rows, voxels, channels), jnp.float32),
+        grid_spec=pltpu.PrefetchScalarGridSpec(
+            num_scalar_prefetch=1,
+            grid=(offsets,),
+            in_specs=[
+                pl.BlockSpec((blocks, voxels, channels), lambda k, idx: (0, 0, 0)),
+                pl.BlockSpec((1, channels, channels), lambda k, idx: (k, 0, 0)),
+            ],
+            out_specs=pl.BlockSpec((rows, voxels, channels), lambda k, idx: (0, 0, 0)),
+        ),
+        compiler_params=pltpu.CompilerParams(
+            dimension_semantics=("arbitrary",), vmem_limit_bytes=56 * 1024 * 1024
+        ),
+    )(table_index.reshape(-1), grad_blocks, weights)
 
 
 def body(features, kernel_map, weights, out_grad):
@@ -127,12 +168,7 @@
         jnp.einsum("kbvc,bvd->kcd", gathered, grad_blocks, preferred_element_type=jnp.float32)
         * scale
     )
-    backward = jnp.einsum("bvd,kcd->kbvc", grad_blocks, weights, preferred_element_type=jnp.float32)
-    table_grad = jax.ops.segment_sum(
-        backward.reshape(offsets * blocks_dev, voxels, channels),
-        table_index.reshape(-1),
-        num_segments=table_rows + 1,
-    )
+    table_grad = table_grad_sums(table_index, grad_blocks, weights, table_rows + 1)
     input_acc = table_grad[:blocks_dev]
     remote_sums = table_grad[blocks_dev:table_rows].astype(jnp.bfloat16)
     returned = lax.all_to_all(
@@ -163,9 +199,8 @@
         precision=lax.Precision.HIGHEST,
     )
     in_grad = input_acc.reshape(blocks_dev * voxels, channels).astype(jnp.bfloat16)
-    share_width = channels // n_shard
-    summed = lax.psum(kernel_term, ("region", "shard"))
-    weight_grad = lax.dynamic_slice_in_dim(summed, my_shard * share_width, share_width, 1)
+    scattered = lax.psum_scatter(kernel_term, "shard", scatter_dimension=1, tiled=True)
+    weight_grad = lax.psum(scattered, "region")
     return (conv_out.reshape(blocks_dev * voxels, channels), in_grad, weight_grad)
 
 

time: 623 us -> 379 us (0.61); the launches traced: 613 us -> 377 us
  other arithmetic: 159 us -> 16.7 us
  local copies, waits for them, and re-layouts: 204 us -> 79.5 us
  Pallas kernels: 0 us -> 27.1 us
  waiting for transfers between devices: 132 us -> 158 us
  matrix products: 71.9 us -> 47.9 us
    scatter-add x1 -> x0, other arithmetic: 128 us -> none  [body(): jax.ops.segment_sum(backward.reshape(offsets * blocks_dev, voxels, channe...]
    psum x1, waiting for transfers between devices: 132 us -> 62 us  [body(): weight_grad = lax.psum(scattered, 'region')]
    reshape x1, local copies, waits for them, and re-layouts: 54.8 us -> 0.66 us  [table_grad_sums(): table_index.reshape(-1)]
    all_to_all x1, waiting for transfers between devices: 0.01 us -> 49.3 us  [body(): lax.all_to_all(outgoing, 'shard', split_axis=0, concat_axis=0, tiled=True)]
    all_to_all x1, waiting for transfers between devices: 0.01 us -> 43.1 us  [body(): lax.all_to_all(remote_sums[:n_shard * capacity].reshape(n_shard, capacity...]
    scatter-add x2 -> x0, local copies, waits for them, and re-layouts: 28.8 us -> none  [body(): jax.ops.segment_sum(backward.reshape(offsets * blocks_dev, voxels, channe...]
    pallas_call x0 -> x1, Pallas kernels: none -> 27.1 us  [table_grad_sums(): pl.pallas_call(_table_grad_kernel, out_shape=jax.ShapeDtypeStruct((rows,...]
    dot_general x1 -> x0, matrix products: 20.9 us -> none  [body(): jnp.einsum('bvd,kcd->kbvc', grad_blocks, weights, preferred_element_type=...]
  transfers between devices with their start and end apart: 7 -> 8, of which waited for: 1 -> 6; matrix products, arithmetic and copies ran while one was open for 67% -> 16% of each run, Pallas kernels for 0% -> 7%
where the time goes in v1:
time: 379 us; the launch traced here: 377 us
  waiting for transfers between devices  158 us (42%)
  local copies, waits for them, and re-layouts  79.5 us (21%)
  matrix products  47.9 us (13%)
  starting transfers between devices  32.7 us (9%)
  Pallas kernels  27.1 us (7%)
  other arithmetic  16.7 us (4%)
  between operations  14.3 us (4%)
    psum x1, waiting for transfers between devices, body(): weight_grad = lax.psum(scattered, 'region')  62 us
    gather x2, local copies, waits for them, and re-layouts, body(): gathered = jnp.take(table, table_index, axis=0)  53.2 us
    all_to_all x1, waiting for transfers between devices, body(): lax.all_to_all(outgoing, 'shard', split_axis=0, concat_axis=0, tiled=True)  49.3 us
    all_to_all x1, waiting for transfers between devices, body(): lax.all_to_all(remote_sums[:n_shard * capacity].reshape(n_shard, capacity...  43.1 us
    pallas_call x1, Pallas kernels, table_grad_sums(): pl.pallas_call(_table_grad_kernel, out_shape=jax.ShapeDtypeStruct((rows,...  27.1 us
    dot_general x1, matrix products, body(): jnp.einsum('kbvc,kcd->bvd', gathered, weights, preferred_element_type=jnp...  20.2 us
    dot_general x1, matrix products, body(): jnp.einsum('kbvc,bvd->kcd', gathered, grad_blocks, preferred_element_type...  15.9 us
    unnamed x11, local copies, waits for them, and re-layouts  11.4 us
  transfers between devices with their start and end apart: 8, of which 6 were waited for; matrix products, arithmetic and copies ran while one was open for 16% of the time, Pallas kernels for 7%

profile of v1, /device:TPU:1, one launch (start us, length us, event | category | flops | bytes accessed | tf_op | source)
XLA Modules:
  0.0 376.6 jit_solution(81050119374872153)
XLA Ops:
  10.1 2.9 convolution_convert_fusion
  13.0 3.6 copy.77
  16.6 8.8 %all-to-all-start = ((bf16[16,4,128,256]{3,2,1,0:T(8,128)(2,1)}), bf16[16,4,128,256]{3,2,1,0:T(8,128)(2,1)}, u32[]{:S(2)}, u32[]{:S(2)}) async-start(bf16[16,4,128,256]{3,2,1,0:T(8,128)(2,1)} %copy.77), calls=%async_computation | async-start | bytes 8388608 | tf_op jit(solution)/shard_map/all_to_all | solution.py:123
  28.1 4.0 %collective-permute-start = (bf16[4,128,256]{2,0,1:T(4,128)(2,1)S(1)}, bf16[4,128,256]{2,0,1:T(4,128)(2,1)S(1)}, u32[]{:S(2)}, u32[]{:S(2)}) collective-permute-start(bf16[4,128,256]{2,0,1:T(4,128)(2,1)S(1)} %get-tuple-element.22), channel_id=1, source_target_pairs={{0,16},{16,32},{32,48},{48,64},{64,80},{80,96},{96,112},{1,17},{17... | collective-permute-start | bytes 786440 | tf_op jit(solution)/shard_map/ppermute | solution.py:21
  32.0 2.1 collective-permute-start.1
  37.6 49.3 %all-to-all-done = bf16[16,4,128,256]{3,2,1,0:T(8,128)(2,1)} async-done(((bf16[16,4,128,256]{3,2,1,0:T(8,128)(2,1)}), bf16[16,4,128,256]{3,2,1,0:T(8,128)(2,1)}, u32[]{:S(2)}, u32[]{:S(2)}) %all-to-all-start) | async-done | bytes 4194336 | tf_op jit(solution)/shard_map/all_to_all | solution.py:123
  86.9 4.7 %constant_dynamic-update-slice_fusion = bf16[89,128,256]{2,1,0:T(8,128)(2,1)} fusion(bf16[89,128,256]{2,1,0:T(8,128)(2,1)} %constant_dynamic-update-slice_fusion.1, bf16[64,128,256]{2,1,0:T(8,128)(2,1)} %bitcast.6), kind=kLoop, calls=%fused_computation.51 | loop fusion | bytes 8388608
  93.7 16.4 %gather_fusion = bf16[432,128,256]{2,1,0:T(8,128)(2,1)} fusion(bf16[89,128,256]{2,1,0:T(8,128)(2,1)} %broadcast_dynamic-update-slice_fusion, s32[1024]{0:T(1024)S(1)} %pad_clamp_fusion), kind=kCustom, calls=%fused_computation | custom fusion | bytes 56624832 | tf_op jit(solution)/shard_map/jit(_take)/gather | solution.py:162
  110.1 36.8 %copy.85 = bf16[27,16,128,256]{2,3,1,0:T(8,128)(2,1)} copy(bf16[27,16,128,256]{3,2,1,0:T(8,128)(2,1)} %bitcast.54) | data formatting | bytes 56623104 | tf_op jit(solution)/shard_map/jit(_take)/gather | solution.py:162
  146.9 15.9 %bitcast_multiply_fusion = f32[27,256,256]{2,1,0:T(8,128)} fusion(bf16[16,128,256,1]{2,1,0,3:T(8,128)(2,1)S(1)} %bitcast.60, bf16[27,16,128,256]{2,3,1,0:T(8,128)(2,1)} %copy.85, pred[27,16]{1,0:T(8,128)(4,1)S(1)} %get-tuple-element.9), kind=kOutput, calls=%fused_computation.6 | convolution fusion | flops 7263682560 | bytes 36438448 | tf_op jit(solution)/shard_map/kbvc,bvd->kcd/dot_general | solution.py:168
  163.4 27.1 %shard_map.67 = f32[89,128,256]{2,1,0:T(8,128)} custom-call(s32[432]{0:T(512)} %reshape.260.idx_ref, bf16[16,128,256]{2,1,0:T(8,128)(2,1)} %bitcast.59, bf16[27,256,256]{2,1,0:T(8,128)(2,1)} %w_ref.1), custom_call_target="tpu_custom_call" | custom-call | tf_op jit(solution)/shard_map/pallas_call | solution.py:58
  190.5 5.6 %convert.7 = bf16[89,128,256]{2,1,0:T(8,128)(2,1)S(1)} convert(f32[89,128,256]{2,1,0:T(8,128)} %shard_map.67) | non-fusion elementwise | flops 2916352 | bytes 17498112 | tf_op jit(solution)/shard_map/convert.4
  196.1 2.4 copy-done
  198.8 5.5 %copy.87 = bf16[16,4,128,256]{3,1,2,0:T(4,128)(2,1)} copy(bf16[16,4,128,256]{3,2,1,0:T(8,128)(2,1)S(1)} %bitcast.55) | data formatting | bytes 8388608 | tf_op jit(solution)/shard_map/reshape | solution.py:175
  204.3 9.1 %all-to-all-start.1 = ((bf16[16,4,128,256]{3,1,2,0:T(4,128)(2,1)}), bf16[16,4,128,256]{3,1,2,0:T(4,128)(2,1)}, u32[]{:S(2)}, u32[]{:S(2)}) async-start(bf16[16,4,128,256]{3,1,2,0:T(4,128)(2,1)} %copy.87), calls=%async_computation.1 | async-start | bytes 8388608 | tf_op jit(solution)/shard_map/all_to_all | solution.py:174
  214.5 5.5 %collective-permute-start.3 = (bf16[4,128,256]{2,1,0:T(8,128)(2,1)S(1)}, bf16[4,128,256]{2,1,0:T(8,128)(2,1)S(1)}, u32[]{:S(2)}, u32[]{:S(2)}) collective-permute-start(bf16[4,128,256]{2,1,0:T(8,128)(2,1)S(1)} %get-tuple-element.20), channel_id=1, source_target_pairs={{16,0},{32,16},{48,32},{64,48},{80,64},{96,80},{112,96},{17,1},{33... | collective-permute-start | bytes 786440 | tf_op jit(solution)/shard_map/ppermute | solution.py:23
  220.1 3.1 collective-permute-start.2
  223.2 2.3 collective-permute-done.3
  226.5 1.8 fusion.21
  228.3 43.1 %all-to-all-done.1 = bf16[16,4,128,256]{3,1,2,0:T(4,128)(2,1)} async-done(((bf16[16,4,128,256]{3,1,2,0:T(4,128)(2,1)}), bf16[16,4,128,256]{3,1,2,0:T(4,128)(2,1)}, u32[]{:S(2)}, u32[]{:S(2)}) %all-to-all-start.1) | async-done | bytes 4194336 | tf_op jit(solution)/shard_map/all_to_all | solution.py:174
  271.4 5.9 %fusion.10 = f32[16,128,256]{2,0,1:T(8,128)} fusion(bf16[16,4,128,256]{3,1,2,0:T(4,128)(2,1)} %all-to-all-done.1, s32[16,16]{0,1:T(8,128)S(1)} %copy.74, pred[16,16]{0,1:T(8,128)(4,1)S(1)} %copy.73), kind=kOutput, calls=%fused_computation.17 | convolution fusion | flops 67110912 | bytes 6292736 | tf_op jit(solution)/shard_map/pcj,pcvd->jvd/dot_general | solution.py:181
  277.3 20.2 %bitcast_convert_fusion = bf16[16,128,256]{2,1,0:T(8,128)(2,1)} fusion(bf16[27,256,256]{2,1,0:T(8,128)(2,1)} %w_ref.1, bf16[27,16,128,256]{2,3,1,0:T(8,128)(2,1)} %copy.85, pred[27,16]{1,0:T(8,128)(4,1)S(1)} %get-tuple-element.9), kind=kOutput, calls=%fused_computation.15 | convolution fusion | flops 7262437376 | bytes 32899504 | tf_op jit(solution)/shard_map/kbvc,kcd->bvd/dot_general | solution.py:163
  298.8 7.2 %fusion.9 = bf16[16,128,256]{2,1,0:T(8,128)(2,1)} fusion(f32[89,128,256]{2,1,0:T(8,128)} %shard_map.67, f32[16,128,256]{2,0,1:T(8,128)S(1)} %fusion.19, f32[16,128,256]{2,0,1:T(8,128)} %fusion.21, f32[16,128,256]{2,0,1:T(8,128)} %fusion.10), kind=kLoop, calls=%fused_computation.14 | loop fusion | flops 2097152 | bytes 9437184 | tf_op jit(solution)/shard_map/convert_element_type | solution.py:201
  306.0 62.0 %all-reduce.2.cloned.1.call-done = f32[27,16,256]{2,1,0:T(8,128)} async-done(((f32[27,16,256]{2,1,0:T(8,128)}), f32[27,16,256]{2,1,0:T(8,128)}) %all-reduce.2.cloned.1.call-update) | async-done | bytes 442384 | tf_op jit(solution)/shard_map/psum | solution.py:203
  (75 shorter events, 17.2 us)
Async XLA Ops:
  16.6 10.6 %copy-start.1 = (bf16[2048,256]{1,0:T(8,128)(2,1)S(1)}, bf16[2048,256]{1,0:T(8,128)(2,1)}, u32[]{:S(2)}) copy-start(bf16[2048,256]{1,0:T(8,128)(2,1)} %param.4) | copy-start | bytes 3145732
  16.6 70.3 %all-to-all-start = ((bf16[16,4,128,256]{3,2,1,0:T(8,128)(2,1)}), bf16[16,4,128,256]{3,2,1,0:T(8,128)(2,1)}, u32[]{:S(2)}, u32[]{:S(2)}) async-start(bf16[16,4,128,256]{3,2,1,0:T(8,128)(2,1)} %copy.77), calls=%async_computation | async-start | bytes 8388608 | tf_op jit(solution)/shard_map/all_to_all | solution.py:123
  25.4 273.4 %reduce-scatter.2.cloned.1.call-start = ((), (), s32[]{:S(2)}) async-start(), calls=%async_computation.3 | async-start | bytes 7520256 | tf_op jit(solution)/shard_map/reduce_scatter | solution.py:202
  28.1 63.5 %collective-permute-start = (bf16[4,128,256]{2,0,1:T(4,128)(2,1)S(1)}, bf16[4,128,256]{2,0,1:T(4,128)(2,1)S(1)}, u32[]{:S(2)}, u32[]{:S(2)}) collective-permute-start(bf16[4,128,256]{2,0,1:T(4,128)(2,1)S(1)} %get-tuple-element.22), channel_id=1, source_target_pairs={{0,16},{16,32},{32,48},{48,64},{64,80},{80,96},{96,112},{1,17},{17... | collective-permute-start | bytes 786440 | tf_op jit(solution)/shard_map/ppermute | solution.py:21
  32.0 60.3 %collective-permute-start.1 = (bf16[4,128,256]{2,0,1:T(4,128)(2,1)S(1)}, bf16[4,128,256]{2,0,1:T(4,128)(2,1)S(1)}, u32[]{:S(2)}, u32[]{:S(2)}) collective-permute-start(bf16[4,128,256]{2,0,1:T(4,128)(2,1)S(1)} %get-tuple-element.21), channel_id=1, source_target_pairs={{16,0},{32,16},{48,32},{64,48},{80,64},{96,80},{112,96},{17,1},{33... | collective-permute-start | bytes 786440 | tf_op jit(solution)/shard_map/ppermute | solution.py:23
  110.1 36.8 %copy-start.2 = (bf16[2048,256]{1,0:T(8,128)(2,1)S(1)}, bf16[2048,256]{1,0:T(8,128)(2,1)}, u32[]{:S(2)}) copy-start(bf16[2048,256]{1,0:T(8,128)(2,1)} %param.7) | copy-start | bytes 3145732
  196.1 2.4 copy-start
  204.3 67.1 %all-to-all-start.1 = ((bf16[16,4,128,256]{3,1,2,0:T(4,128)(2,1)}), bf16[16,4,128,256]{3,1,2,0:T(4,128)(2,1)}, u32[]{:S(2)}, u32[]{:S(2)}) async-start(bf16[16,4,128,256]{3,1,2,0:T(4,128)(2,1)} %copy.87), calls=%async_computation.1 | async-start | bytes 8388608 | tf_op jit(solution)/shard_map/all_to_all | solution.py:174
  213.4 154.6 %all-reduce.2.cloned.1.call-start = ((), (), s32[]{:S(2)}) async-start(), calls=%async_computation.4 | async-start | bytes 884736 | tf_op jit(solution)/shard_map/psum | solution.py:203
  214.5 10.9 %collective-permute-start.3 = (bf16[4,128,256]{2,1,0:T(8,128)(2,1)S(1)}, bf16[4,128,256]{2,1,0:T(8,128)(2,1)S(1)}, u32[]{:S(2)}, u32[]{:S(2)}) collective-permute-start(bf16[4,128,256]{2,1,0:T(8,128)(2,1)S(1)} %get-tuple-element.20), channel_id=1, source_target_pairs={{16,0},{32,16},{48,32},{64,48},{80,64},{96,80},{112,96},{17,1},{33... | collective-permute-start | bytes 786440 | tf_op jit(solution)/shard_map/ppermute | solution.py:23
  220.1 6.4 %collective-permute-start.2 = (bf16[4,128,256]{2,1,0:T(8,128)(2,1)S(1)}, bf16[4,128,256]{2,1,0:T(8,128)(2,1)S(1)}, u32[]{:S(2)}, u32[]{:S(2)}) collective-permute-start(bf16[4,128,256]{2,1,0:T(8,128)(2,1)S(1)} %get-tuple-element.19), channel_id=1, source_target_pairs={{0,16},{16,32},{32,48},{48,64},{64,80},{80,96},{96,112},{1,17},{17... | collective-permute-start | bytes 786440 | tf_op jit(solution)/shard_map/ppermute | solution.py:21
Sparse Core Ops, SparseCore 0:
  162.9 135.8 reduce-scatter.1
  301.3 66.6 all-reduce.1

commit v2 on v1

--- a/solution.py
+++ b/solution.py
@@ -1,3 +1,4 @@
+import functools
 import math
 
 import jax
@@ -71,6 +72,68 @@
             dimension_semantics=("arbitrary",), vmem_limit_bytes=56 * 1024 * 1024
         ),
     )(table_index.reshape(-1), grad_blocks, weights)
+
+
+def _forward_kernel(idx_ref, table_ref, tablet_ref, w_ref, grad_ref, out_ref, wg_ref, g_ref, gt_ref, acc_ref, *, scale):
+    k = pl.program_id(0)
+    voxels = table_ref.shape[1]
+    blocks = grad_ref.shape[0] // voxels
+    rows = table_ref.shape[0]
+    for b in range(blocks):
+        t = jnp.clip(idx_ref[k * blocks + b], 0, rows - 1)
+        g_ref[pl.ds(b * voxels, voxels), :] = table_ref[t]
+        gt_ref[:, pl.ds(b * voxels, voxels)] = tablet_ref[t]
+    part = jnp.dot(g_ref[...], w_ref[0], preferred_element_type=jnp.float32)
+
+    @pl.when(k == 0)
+    def _():
+        acc_ref[...] = part
+
+    @pl.when(k > 0)
+    def _():
+        acc_ref[...] += part
+
+    wg_ref[0] = jnp.dot(gt_ref[...], grad_ref[...], preferred_element_type=jnp.float32) * scale
+
+    @pl.when(k == pl.num_programs(0) - 1)
+    def _():
+        out_ref[...] = acc_ref[...].astype(out_ref.dtype)
+
+
+def forward_terms(table_index, table, weights, grad_rows, scale):
+    rows, voxels, channels = table.shape
+    offsets = weights.shape[0]
+    count = grad_rows.shape[0]
+    tablet = jnp.swapaxes(table, 1, 2)
+    return pl.pallas_call(
+        functools.partial(_forward_kernel, scale=scale),
+        out_shape=(
+            jax.ShapeDtypeStruct((count, channels), jnp.bfloat16),
+            jax.ShapeDtypeStruct((offsets, channels, channels), jnp.float32),
+        ),
+        grid_spec=pltpu.PrefetchScalarGridSpec(
+            num_scalar_prefetch=1,
+            grid=(offsets,),
+            in_specs=[
+                pl.BlockSpec((rows, voxels, channels), lambda k, idx: (0, 0, 0)),
+                pl.BlockSpec((rows, channels, voxels), lambda k, idx: (0, 0, 0)),
+                pl.BlockSpec((1, channels, channels), lambda k, idx: (k, 0, 0)),
+                pl.BlockSpec((count, channels), lambda k, idx: (0, 0)),
+            ],
+            out_specs=[
+                pl.BlockSpec((count, channels), lambda k, idx: (0, 0)),
+                pl.BlockSpec((1, channels, channels), lambda k, idx: (k, 0, 0)),
+            ],
+            scratch_shapes=[
+                pltpu.VMEM((count, channels), jnp.bfloat16),
+                pltpu.VMEM((channels, count), jnp.bfloat16),
+                pltpu.VMEM((count, channels), jnp.float32),
+            ],
+        ),
+        compiler_params=pltpu.CompilerParams(
+            dimension_semantics=("arbitrary",), vmem_limit_bytes=56 * 1024 * 1024
+        ),
+    )(table_index.reshape(-1), table, tablet, weights, grad_rows)
 
 
 def body(features, kernel_map, weights, out_grad):
@@ -149,6 +212,8 @@
     )
     table_rows = rim_start + 2 * capacity
     table_index = jnp.where(present, table_index, table_rows)
+    table_grad = table_grad_sums(table_index, grad_blocks, weights, table_rows + 1)
+    incoming, rims, table_grad = lax.optimization_barrier((incoming, rims, table_grad))
     table = jnp.concatenate(
         [
             own_blocks,
@@ -159,16 +224,10 @@
         ],
         axis=0,
     )
-    gathered = jnp.take(table, table_index, axis=0)
-    conv_out = jnp.einsum(
-        "kbvc,kcd->bvd", gathered, weights, preferred_element_type=jnp.float32
-    ).astype(jnp.bfloat16)
     scale = 1.0 / math.sqrt(total_blocks * voxels)
-    kernel_term = (
-        jnp.einsum("kbvc,bvd->kcd", gathered, grad_blocks, preferred_element_type=jnp.float32)
-        * scale
-    )
-    table_grad = table_grad_sums(table_index, grad_blocks, weights, table_rows + 1)
+    conv_out, kernel_term = forward_terms(
+        table_index, table, weights, grad_blocks.reshape(blocks_dev * voxels, channels), scale
+    )
     input_acc = table_grad[:blocks_dev]
     remote_sums = table_grad[blocks_dev:table_rows].astype(jnp.bfloat16)
     returned = lax.all_to_all(
@@ -201,7 +260,7 @@
     in_grad = input_acc.reshape(blocks_dev * voxels, channels).astype(jnp.bfloat16)
     scattered = lax.psum_scatter(kernel_term, "shard", scatter_dimension=1, tiled=True)
     weight_grad = lax.psum(scattered, "region")
-    return (conv_out.reshape(blocks_dev * voxels, channels), in_grad, weight_grad)
+    return (conv_out, in_grad, weight_grad)
 
 
 def solution(mesh):

time: 379 us -> 373 us (0.984)
  Pallas kernels: 27.1 us -> 78.6 us
  local copies, waits for them, and re-layouts: 79.5 us -> 41.6 us
  matrix products: 47.9 us -> 11.9 us
  waiting for transfers between devices: 158 us -> 173 us
    gather x2 -> x0, local copies, waits for them, and re-layouts: 53.2 us -> none  [body(): gathered = jnp.take(table, table_index, axis=0)]
    pallas_call x0 -> x1, Pallas kernels: none -> 51.4 us  [forward_terms(): pl.pallas_call(functools.partial(_forward_kernel, scale=scale), out_shape...]
    reduce_scatter x1, waiting for transfers between devices: 1.3 us -> 52.4 us  [body(): lax.psum_scatter(kernel_term, 'shard', scatter_dimension=1, tiled=True)]
    dot_general x2 -> x0, matrix products: 36.1 us -> none  [the longest x1 20.2 us: body(): jnp.einsum('kbvc,kcd->bvd', gathered, weights, preferred_element_type=jnp...]
    all_to_all x1, waiting for transfers between devices: 49.3 us -> 19.5 us  [body(): lax.all_to_all(outgoing, 'shard', split_axis=0, concat_axis=0, tiled=True)]
    concatenate x1 -> x2, local copies, waits for them, and re-layouts: 0.62 us -> 9.04 us  [body(): jnp.concatenate([own_blocks, incoming.reshape(n_shard * capacity, voxels,...]
    psum x1, waiting for transfers between devices: 62 us -> 53.6 us  [body(): weight_grad = lax.psum(scattered, 'region')]
    optimization_barrier x0 -> x1, local copies, waits for them, and re-layouts: none -> 6.38 us  [body(): lax.optimization_barrier((incoming, rims, table_grad))]
  transfers between devices with their start and end apart: 8 -> 8, of which waited for: 6 -> 6; matrix products, arithmetic and copies ran while one was open for 16% -> 10% of each run, Pallas kernels for 7% -> 7%
where the time goes in v2:
time: 373 us; the launch traced here: 369 us
  waiting for transfers between devices  173 us (46%)
  Pallas kernels  78.6 us (21%)
  local copies, waits for them, and re-layouts  41.6 us (11%)
  starting transfers between devices  32.7 us (9%)
  other arithmetic  17.4 us (5%)
  between operations  14.3 us (4%)
  matrix products  11.9 us (3%)
    psum x1, waiting for transfers between devices, body(): weight_grad = lax.psum(scattered, 'region')  53.6 us
    reduce_scatter x1, waiting for transfers between devices, body(): lax.psum_scatter(kernel_term, 'shard', scatter_dimension=1, tiled=True)  52.4 us
    pallas_call x1, Pallas kernels, forward_terms(): pl.pallas_call(functools.partial(_forward_kernel, scale=scale), out_shape...  51.4 us
    all_to_all x1, waiting for transfers between devices, body(): lax.all_to_all(remote_sums[:n_shard * capacity].reshape(n_shard, capacity...  45 us
    pallas_call x1, Pallas kernels, table_grad_sums(): pl.pallas_call(_table_grad_kernel, out_shape=jax.ShapeDtypeStruct((rows,...  27.3 us
    all_to_all x1, waiting for transfers between devices, body(): lax.all_to_all(outgoing, 'shard', split_axis=0, concat_axis=0, tiled=True)  19.5 us
    unnamed x9, local copies, waits for them, and re-layouts  11.2 us
    all_to_all x1, starting transfers between devices, body(): lax.all_to_all(remote_sums[:n_shard * capacity].reshape(n_shard, capacity...  9.63 us
  transfers between devices with their start and end apart: 8, of which 6 were waited for; matrix products, arithmetic and copies ran while one was open for 10% of the time, Pallas kernels for 7%

profile of v2, /device:TPU:1, one launch (start us, length us, event | category | flops | bytes accessed | tf_op | source)
XLA Modules:
  0.0 369.4 jit_solution(8469090739208400905)
XLA Ops:
  10.1 2.9 convolution_convert_fusion
  13.0 3.5 copy.76
  16.6 8.8 %all-to-all-start = ((bf16[16,4,128,256]{3,2,1,0:T(8,128)(2,1)}), bf16[16,4,128,256]{3,2,1,0:T(8,128)(2,1)}, u32[]{:S(2)}, u32[]{:S(2)}) async-start(bf16[16,4,128,256]{3,2,1,0:T(8,128)(2,1)} %copy.76), calls=%async_computation | async-start | bytes 8388608 | tf_op jit(solution)/shard_map/all_to_all | solution.py:186
  28.3 4.0 %collective-permute-start = (bf16[4,128,256]{1,2,0:T(8,128)(2,1)S(1)}, bf16[4,128,256]{1,2,0:T(8,128)(2,1)S(1)}, u32[]{:S(2)}, u32[]{:S(2)}) collective-permute-start(bf16[4,128,256]{1,2,0:T(8,128)(2,1)S(1)} %get-tuple-element.29), channel_id=1, source_target_pairs={{0,16},{16,32},{32,48},{48,64},{64,80},{80,96},{96,112},{1,17},{17... | collective-permute-start | bytes 786440 | tf_op jit(solution)/shard_map/ppermute | solution.py:22
  32.3 2.1 collective-permute-start.1
  38.0 27.3 %shard_map.67 = f32[89,128,256]{2,1,0:T(8,128)} custom-call(s32[432]{0:T(512)} %reshape.250.idx_ref, bf16[16,128,256]{2,1,0:T(8,128)(2,1)} %bitcast.44, bf16[27,256,256]{2,1,0:T(8,128)(2,1)} %w_ref.3), custom_call_target="tpu_custom_call" | custom-call | tf_op jit(solution)/shard_map/pallas_call | solution.py:59
  67.4 19.5 %all-to-all-done = bf16[16,4,128,256]{3,2,1,0:T(8,128)(2,1)} async-done(((bf16[16,4,128,256]{3,2,1,0:T(8,128)(2,1)}), bf16[16,4,128,256]{3,2,1,0:T(8,128)(2,1)}, u32[]{:S(2)}, u32[]{:S(2)}) %all-to-all-start) | async-done | bytes 4194336 | tf_op jit(solution)/shard_map/all_to_all | solution.py:186
  86.8 6.4 %copy.83 = bf16[16,4,128,256]{2,3,1,0:T(8,128)(2,1)} copy(bf16[16,4,128,256]{3,2,1,0:T(8,128)(2,1)} %all-to-all-done) | data formatting | bytes 8388608 | tf_op jit(solution)/shard_map/optimization_barrier | solution.py:216
  93.2 4.7 %constant_dynamic-update-slice_fusion = bf16[89,128,256]{1,2,0:T(8,128)(2,1)} fusion(bf16[89,128,256]{1,2,0:T(8,128)(2,1)} %constant_dynamic-update-slice_fusion.1, bf16[64,128,256]{1,2,0:T(8,128)(2,1)} %bitcast.39), kind=kLoop, calls=%fused_computation.41 | loop fusion | bytes 8388608
  100.0 8.4 %copy.85.table_ref = bf16[89,128,256]{2,1,0:T(8,128)(2,1)} copy(bf16[89,128,256]{1,2,0:T(8,128)(2,1)} %broadcast_dynamic-update-slice_fusion) | data formatting | bytes 11665408 | tf_op jit(solution)/shard_map/concatenate | solution.py:217
  108.4 51.4 %shard_map.68 = (bf16[2048,256]{1,0:T(8,128)(2,1)}, f32[27,256,256]{2,1,0:T(8,128)}) custom-call(s32[432]{0:T(512)} %reshape.250.idx_ref, bf16[89,128,256]{2,1,0:T(8,128)(2,1)} %copy.85.table_ref, bf16[89,256,128]{2,1,0:T(8,128)(2,1)} %bitcast.38, bf16[27,256,256]{2,1,0:T(8,128)(2,1)} %w_ref.3, bf16[2048,256]{1,0:T(8,128)(2,1)} %grad_ref.1), custom_call_target="tpu_custom_call" | custom-call | tf_op jit(solution)/shard_map/pallas_call | solution.py:108
  159.8 5.2 %convert.7 = bf16[89,128,256]{2,1,0:T(8,128)(2,1)S(1)} convert(f32[89,128,256]{2,1,0:T(8,128)} %shard_map.67) | non-fusion elementwise | flops 2916352 | bytes 17498112 | tf_op jit(solution)/shard_map/convert.4
  165.3 2.2 copy-done
  167.5 5.5 %copy.86 = bf16[16,4,128,256]{3,1,2,0:T(4,128)(2,1)} copy(bf16[16,4,128,256]{3,2,1,0:T(8,128)(2,1)S(1)} %bitcast.40) | data formatting | bytes 8388608 | tf_op jit(solution)/shard_map/reshape | solution.py:234
  172.9 9.6 %all-to-all-start.1 = ((bf16[16,4,128,256]{3,1,2,0:T(4,128)(2,1)}), bf16[16,4,128,256]{3,1,2,0:T(4,128)(2,1)}, u32[]{:S(2)}, u32[]{:S(2)}) async-start(bf16[16,4,128,256]{3,1,2,0:T(4,128)(2,1)} %copy.86), calls=%async_computation.1 | async-start | bytes 8388608 | tf_op jit(solution)/shard_map/all_to_all | solution.py:233
  183.7 4.8 %collective-permute-start.3 = (bf16[4,128,256]{2,1,0:T(8,128)(2,1)S(1)}, bf16[4,128,256]{2,1,0:T(8,128)(2,1)S(1)}, u32[]{:S(2)}, u32[]{:S(2)}) collective-permute-start(bf16[4,128,256]{2,1,0:T(8,128)(2,1)S(1)} %get-tuple-element.28), channel_id=1, source_target_pairs={{16,0},{32,16},{48,32},{64,48},{80,64},{96,80},{112,96},{17,1},{33... | collective-permute-start | bytes 786440 | tf_op jit(solution)/shard_map/ppermute | solution.py:24
  188.6 3.3 collective-permute-start.2
  191.8 2.3 collective-permute-done.3
  194.9 1.8 fusion.13
  196.7 45.0 %all-to-all-done.1 = bf16[16,4,128,256]{3,1,2,0:T(4,128)(2,1)} async-done(((bf16[16,4,128,256]{3,1,2,0:T(4,128)(2,1)}), bf16[16,4,128,256]{3,1,2,0:T(4,128)(2,1)}, u32[]{:S(2)}, u32[]{:S(2)}) %all-to-all-start.1) | async-done | bytes 4194336 | tf_op jit(solution)/shard_map/all_to_all | solution.py:233
  241.7 5.9 %fusion.3 = f32[16,128,256]{2,0,1:T(8,128)} fusion(bf16[16,4,128,256]{3,1,2,0:T(4,128)(2,1)} %all-to-all-done.1, s32[16,16]{0,1:T(8,128)S(1)} %copy.73, pred[16,16]{0,1:T(8,128)(4,1)S(1)} %copy.72), kind=kOutput, calls=%fused_computation.8 | convolution fusion | flops 67110912 | bytes 6292736 | tf_op jit(solution)/shard_map/pcj,pcvd->jvd/dot_general | solution.py:240
  247.6 52.4 %reduce-scatter.2.cloned.1.call-done = f32[27,16,256]{2,1,0:T(8,128)} async-done(((f32[27,256,256]{2,1,0:T(8,128)}), f32[27,16,256]{2,1,0:T(8,128)}) %reduce-scatter.2.cloned.1.call-update) | async-done | bytes 442384 | tf_op jit(solution)/shard_map/reduce_scatter | solution.py:261
  300.0 7.2 %fusion.2 = bf16[16,128,256]{2,1,0:T(8,128)(2,1)} fusion(f32[16,128,256]{2,0,1:T(8,128)S(1)} %fusion.11, f32[16,128,256]{2,0,1:T(8,128)} %fusion.13, f32[16,128,256]{2,0,1:T(8,128)} %fusion.3, f32[89,128,256]{2,1,0:T(8,128)} %shard_map.67), kind=kLoop, calls=%fused_computation.4 | loop fusion | flops 2097152 | bytes 9437184 | tf_op jit(solution)/shard_map/convert_element_type | solution.py:260
  307.2 53.6 %all-reduce.2.cloned.1.call-done = f32[27,16,256]{2,1,0:T(8,128)} async-done(((f32[27,16,256]{2,1,0:T(8,128)}), f32[27,16,256]{2,1,0:T(8,128)}) %all-reduce.2.cloned.1.call-update) | async-done | bytes 442384 | tf_op jit(solution)/shard_map/psum | solution.py:262
  (72 shorter events, 17.5 us)
Async XLA Ops:
  16.5 10.6 %copy-start.1 = (bf16[2048,256]{1,0:T(8,128)(2,1)S(1)}, bf16[2048,256]{1,0:T(8,128)(2,1)}, u32[]{:S(2)}) copy-start(bf16[2048,256]{1,0:T(8,128)(2,1)} %param.4) | copy-start | bytes 3145732
  16.6 70.3 %all-to-all-start = ((bf16[16,4,128,256]{3,2,1,0:T(8,128)(2,1)}), bf16[16,4,128,256]{3,2,1,0:T(8,128)(2,1)}, u32[]{:S(2)}, u32[]{:S(2)}) async-start(bf16[16,4,128,256]{3,2,1,0:T(8,128)(2,1)} %copy.76), calls=%async_computation | async-start | bytes 8388608 | tf_op jit(solution)/shard_map/all_to_all | solution.py:186
  25.3 274.7 %reduce-scatter.2.cloned.1.call-start = ((), (), s32[]{:S(2)}) async-start(), calls=%async_computation.3 | async-start | bytes 7520256 | tf_op jit(solution)/shard_map/reduce_scatter | solution.py:261
  28.3 38.0 %collective-permute-start = (bf16[4,128,256]{1,2,0:T(8,128)(2,1)S(1)}, bf16[4,128,256]{1,2,0:T(8,128)(2,1)S(1)}, u32[]{:S(2)}, u32[]{:S(2)}) collective-permute-start(bf16[4,128,256]{1,2,0:T(8,128)(2,1)S(1)} %get-tuple-element.29), channel_id=1, source_target_pairs={{0,16},{16,32},{32,48},{48,64},{64,80},{80,96},{96,112},{1,17},{17... | collective-permute-start | bytes 786440 | tf_op jit(solution)/shard_map/ppermute | solution.py:22
  32.3 34.0 %collective-permute-start.1 = (bf16[4,128,256]{1,2,0:T(8,128)(2,1)S(1)}, bf16[4,128,256]{1,2,0:T(8,128)(2,1)}, u32[]{:S(2)}, u32[]{:S(2)}) collective-permute-start(bf16[4,128,256]{1,2,0:T(8,128)(2,1)S(1)} %get-tuple-element.30), channel_id=1, source_target_pairs={{16,0},{32,16},{48,32},{64,48},{80,64},{96,80},{112,96},{17,1},{33... | collective-permute-start | bytes 786440 | tf_op jit(solution)/shard_map/ppermute | solution.py:24
  165.0 2.5 copy-start
  172.9 68.8 %all-to-all-start.1 = ((bf16[16,4,128,256]{3,1,2,0:T(4,128)(2,1)}), bf16[16,4,128,256]{3,1,2,0:T(4,128)(2,1)}, u32[]{:S(2)}, u32[]{:S(2)}) async-start(bf16[16,4,128,256]{3,1,2,0:T(4,128)(2,1)} %copy.86), calls=%async_computation.1 | async-start | bytes 8388608 | tf_op jit(solution)/shard_map/all_to_all | solution.py:233
  182.6 178.2 %all-reduce.2.cloned.1.call-start = ((), (), s32[]{:S(2)}) async-start(), calls=%async_computation.4 | async-start | bytes 884736 | tf_op jit(solution)/shard_map/psum | solution.py:262
  183.7 10.4 %collective-permute-start.3 = (bf16[4,128,256]{2,1,0:T(8,128)(2,1)S(1)}, bf16[4,128,256]{2,1,0:T(8,128)(2,1)S(1)}, u32[]{:S(2)}, u32[]{:S(2)}) collective-permute-start(bf16[4,128,256]{2,1,0:T(8,128)(2,1)S(1)} %get-tuple-element.28), channel_id=1, source_target_pairs={{16,0},{32,16},{48,32},{64,48},{80,64},{96,80},{112,96},{17,1},{33... | collective-permute-start | bytes 786440 | tf_op jit(solution)/shard_map/ppermute | solution.py:24
  188.6 6.4 %collective-permute-start.2 = (bf16[4,128,256]{2,1,0:T(8,128)(2,1)S(1)}, bf16[4,128,256]{2,1,0:T(8,128)(2,1)S(1)}, u32[]{:S(2)}, u32[]{:S(2)}) collective-permute-start(bf16[4,128,256]{2,1,0:T(8,128)(2,1)S(1)} %get-tuple-element.27), channel_id=1, source_target_pairs={{0,16},{16,32},{32,48},{48,64},{64,80},{80,96},{96,112},{1,17},{17... | collective-permute-start | bytes 786440 | tf_op jit(solution)/shard_map/ppermute | solution.py:22
Sparse Core Ops, SparseCore 0:
  159.9 140.0 reduce-scatter.1
  302.5 58.2 all-reduce.1

commit v3 on v2

--- a/solution.py
+++ b/solution.py
@@ -68,61 +68,68 @@
             ],
             out_specs=pl.BlockSpec((rows, voxels, channels), lambda k, idx: (0, 0, 0)),
         ),
+        cost_estimate=pl.CostEstimate(
+            flops=2 * offsets * blocks * voxels * channels * channels,
+            transcendentals=0,
+            bytes_accessed=weights.size * 2 + grad_blocks.size * 2 + rows * voxels * channels * 4,
+        ),
         compiler_params=pltpu.CompilerParams(
             dimension_semantics=("arbitrary",), vmem_limit_bytes=56 * 1024 * 1024
         ),
     )(table_index.reshape(-1), grad_blocks, weights)
 
 
-def _forward_kernel(idx_ref, table_ref, tablet_ref, w_ref, grad_ref, out_ref, wg_ref, g_ref, gt_ref, acc_ref, *, scale):
+def _forward_kernel(
+    idx_ref, table_ref, tablet_ref, w_ref, grad_ref, acc_in_ref, out_ref, wg_ref, g_ref, gt_ref, acc_ref,
+    *, scale, first,
+):
     k = pl.program_id(0)
     voxels = table_ref.shape[1]
     blocks = grad_ref.shape[0] // voxels
     rows = table_ref.shape[0]
     for b in range(blocks):
-        t = jnp.clip(idx_ref[k * blocks + b], 0, rows - 1)
+        t = jnp.clip(idx_ref[(k + first) * blocks + b], 0, rows - 1)
         g_ref[pl.ds(b * voxels, voxels), :] = table_ref[t]
         gt_ref[:, pl.ds(b * voxels, voxels)] = tablet_ref[t]
     part = jnp.dot(g_ref[...], w_ref[0], preferred_element_type=jnp.float32)
 
     @pl.when(k == 0)
     def _():
-        acc_ref[...] = part
+        acc_ref[...] = acc_in_ref[...] + part
 
     @pl.when(k > 0)
     def _():
         acc_ref[...] += part
 
-    wg_ref[0] = jnp.dot(gt_ref[...], grad_ref[...], preferred_element_type=jnp.float32) * scale
+    wg_ref[...] = jnp.dot(gt_ref[...], grad_ref[...], preferred_element_type=jnp.float32) * scale
 
     @pl.when(k == pl.num_programs(0) - 1)
     def _():
         out_ref[...] = acc_ref[...].astype(out_ref.dtype)
 
 
-def forward_terms(table_index, table, weights, grad_rows, scale):
+def forward_terms(table_index, table, tablet, weights, grad_rows, acc_in, first, last, out_dtype, scale):
     rows, voxels, channels = table.shape
-    offsets = weights.shape[0]
     count = grad_rows.shape[0]
-    tablet = jnp.swapaxes(table, 1, 2)
     return pl.pallas_call(
-        functools.partial(_forward_kernel, scale=scale),
+        functools.partial(_forward_kernel, scale=scale, first=first),
         out_shape=(
-            jax.ShapeDtypeStruct((count, channels), jnp.bfloat16),
-            jax.ShapeDtypeStruct((offsets, channels, channels), jnp.float32),
+            jax.ShapeDtypeStruct((count, channels), out_dtype),
+            jax.ShapeDtypeStruct((channels, (last - first) * channels), jnp.float32),
         ),
         grid_spec=pltpu.PrefetchScalarGridSpec(
             num_scalar_prefetch=1,
-            grid=(offsets,),
+            grid=(last - first,),
             in_specs=[
                 pl.BlockSpec((rows, voxels, channels), lambda k, idx: (0, 0, 0)),
                 pl.BlockSpec((rows, channels, voxels), lambda k, idx: (0, 0, 0)),
-                pl.BlockSpec((1, channels, channels), lambda k, idx: (k, 0, 0)),
+                pl.BlockSpec((1, channels, channels), lambda k, idx: (k + first, 0, 0)),
+                pl.BlockSpec((count, channels), lambda k, idx: (0, 0)),
                 pl.BlockSpec((count, channels), lambda k, idx: (0, 0)),
             ],
             out_specs=[
                 pl.BlockSpec((count, channels), lambda k, idx: (0, 0)),
-                pl.BlockSpec((1, channels, channels), lambda k, idx: (k, 0, 0)),
+                pl.BlockSpec((channels, channels), lambda k, idx: (0, k)),
             ],
             scratch_shapes=[
                 pltpu.VMEM((count, channels), jnp.bfloat16),
@@ -130,10 +137,15 @@
                 pltpu.VMEM((count, channels), jnp.float32),
             ],
         ),
+        cost_estimate=pl.CostEstimate(
+            flops=4 * (last - first) * count * channels * channels,
+            transcendentals=0,
+            bytes_accessed=2 * table.size * 2 + (last - first) * channels * channels * 6 + count * channels * 10,
+        ),
         compiler_params=pltpu.CompilerParams(
             dimension_semantics=("arbitrary",), vmem_limit_bytes=56 * 1024 * 1024
         ),
-    )(table_index.reshape(-1), table, tablet, weights, grad_rows)
+    )(table_index.reshape(-1), table, tablet, weights, grad_rows, acc_in)
 
 
 def body(features, kernel_map, weights, out_grad):
@@ -213,6 +225,15 @@
     table_rows = rim_start + 2 * capacity
     table_index = jnp.where(present, table_index, table_rows)
     table_grad = table_grad_sums(table_index, grad_blocks, weights, table_rows + 1)
+    remote_sums = table_grad[blocks_dev:table_rows].astype(jnp.bfloat16)
+    returned = lax.all_to_all(
+        remote_sums[: n_shard * capacity].reshape(n_shard, capacity, voxels, channels),
+        "shard",
+        split_axis=0,
+        concat_axis=0,
+        tiled=True,
+    )
+    rim_back = padded(remote_sums[n_shard * capacity :], (("region", 0),), capacity)
     incoming, rims, table_grad = lax.optimization_barrier((incoming, rims, table_grad))
     table = jnp.concatenate(
         [
@@ -224,26 +245,24 @@
         ],
         axis=0,
     )
+    share = channels // (n_shard * n_region)
+    tablet = table.reshape(table_rows + 1, voxels, n_shard, n_region, share)
+    tablet = jnp.transpose(tablet, (0, 3, 2, 4, 1)).reshape(table_rows + 1, channels, voxels)
     scale = 1.0 / math.sqrt(total_blocks * voxels)
+    grad_rows = grad_blocks.reshape(blocks_dev * voxels, channels)
     conv_out, kernel_term = forward_terms(
-        table_index, table, weights, grad_blocks.reshape(blocks_dev * voxels, channels), scale
-    )
+        table_index, table, tablet, weights, grad_rows,
+        jnp.zeros((blocks_dev * voxels, channels), jnp.float32), 0, offsets, jnp.bfloat16, scale,
+    )
+    kernel_term = kernel_term.reshape(channels, offsets, channels)
+    scattered = lax.psum_scatter(kernel_term, ("region", "shard"), scatter_dimension=0, tiled=True)
     input_acc = table_grad[:blocks_dev]
-    remote_sums = table_grad[blocks_dev:table_rows].astype(jnp.bfloat16)
-    returned = lax.all_to_all(
-        remote_sums[: n_shard * capacity].reshape(n_shard, capacity, voxels, channels),
-        "shard",
-        split_axis=0,
-        concat_axis=0,
-        tiled=True,
-    )
     input_acc = input_acc + jnp.einsum(
         "pcj,pcvd->jvd",
         chosen.astype(jnp.float32),
         returned.astype(jnp.float32),
         precision=lax.Precision.HIGHEST,
     )
-    rim_back = padded(remote_sums[n_shard * capacity :], (("region", 0),), capacity)
     rim_wide = rim_back.astype(jnp.float32)
     input_acc = input_acc + jnp.einsum(
         "cj,cvd->jvd",
@@ -258,8 +277,7 @@
         precision=lax.Precision.HIGHEST,
     )
     in_grad = input_acc.reshape(blocks_dev * voxels, channels).astype(jnp.bfloat16)
-    scattered = lax.psum_scatter(kernel_term, "shard", scatter_dimension=1, tiled=True)
-    weight_grad = lax.psum(scattered, "region")
+    weight_grad = jnp.swapaxes(lax.all_gather(scattered, "region", axis=0, tiled=True), 0, 1)
     return (conv_out, in_grad, weight_grad)
 
 

time: 373 us -> 900 us (2.41)
  waiting for transfers between devices: 173 us -> 625 us
  blocking collectives: 0 us -> 45.3 us
  local copies, waits for them, and re-layouts: 41.6 us -> 74.7 us
    reduce_scatter x1, waiting for transfers between devices: 52.4 us -> 568 us  [body(): lax.psum_scatter(kernel_term, ('region', 'shard'), scatter_dimension=0, t...]
    psum x1 -> x0, waiting for transfers between devices: 53.6 us -> none  [body(): weight_grad = lax.psum(scattered, 'region')]
    all_gather x0 -> x1, blocking collectives: none -> 45.3 us  [body(): lax.all_gather(scattered, 'region', axis=0, tiled=True)]
    unnamed x9 -> x16, local copies, waits for them, and re-layouts: 11.2 us -> 24.9 us
    reshape x1, local copies, waits for them, and re-layouts: 0.65 us -> 10.3 us  [body(): kernel_term = kernel_term.reshape(channels, offsets, channels)]
  transfers between devices with their start and end apart: 8 -> 7, of which waited for: 6 -> 4; matrix products, arithmetic and copies ran while one was open for 10% -> 4% of each run, Pallas kernels for 7% -> 3%
where the time goes in v3:
time: 900 us; the launch traced here: 898 us
  waiting for transfers between devices  625 us (69%)
  Pallas kernels  79.6 us (9%)
  local copies, waits for them, and re-layouts  74.7 us (8%)
  blocking collectives  45.3 us (5%)
  starting transfers between devices  32.4 us (4%)
  other arithmetic  16.3 us (2%)
  between operations  14.3 us (2%)
  matrix products  10.7 us (1%)
    reduce_scatter x1, waiting for transfers between devices, body(): lax.psum_scatter(kernel_term, ('region', 'shard'), scatter_dimension=0, t...  568 us
    pallas_call x1, Pallas kernels, forward_terms(): pl.pallas_call(functools.partial(_forward_kernel, scale=scale, first=firs...  52.3 us
    all_gather x1, blocking collectives, body(): lax.all_gather(scattered, 'region', axis=0, tiled=True)  45.3 us
    all_to_all x1, waiting for transfers between devices, body(): lax.all_to_all(remote_sums[:n_shard * capacity].reshape(n_shard, capacity...  36.6 us
    pallas_call x1, Pallas kernels, table_grad_sums(): pl.pallas_call(_table_grad_kernel, out_shape=jax.ShapeDtypeStruct((rows,...  27.3 us
    unnamed x16, local copies, waits for them, and re-layouts  24.9 us
  transfers between devices with their start and end apart: 7, of which 4 were waited for; matrix products, arithmetic and copies ran while one was open for 4% of the time, Pallas kernels for 3%

profile of v3, /device:TPU:1, one launch (start us, length us, event | category | flops | bytes accessed | tf_op | source)
XLA Modules:
  0.0 898.1 jit_solution(1886217832670106588)
XLA Ops:
  10.1 2.9 convolution_convert_fusion
  13.0 3.5 copy.91
  16.6 8.8 all-to-all-start
  30.9 3.2 collective-permute-start
  38.9 27.3 %shard_map.67 = f32[89,128,256]{2,1,0:T(8,128)} custom-call(s32[432]{0:T(512)} %reshape.264.idx_ref, bf16[16,128,256]{2,1,0:T(8,128)(2,1)} %bitcast.64, bf16[27,256,256]{2,1,0:T(8,128)(2,1)} %w_ref.3), custom_call_target="tpu_custom_call" | custom-call | flops 7247757312 | bytes 16252928 | tf_op jit(solution)/shard_map/pallas_call | solution.py:59
  69.2 17.6 %all-to-all-done = bf16[16,4,128,256]{3,2,1,0:T(8,128)(2,1)} async-done(((bf16[16,4,128,256]{3,2,1,0:T(8,128)(2,1)}), bf16[16,4,128,256]{3,2,1,0:T(8,128)(2,1)}, u32[]{:S(2)}, u32[]{:S(2)}) %all-to-all-start) | async-done | bytes 4194336 | tf_op jit(solution)/shard_map/all_to_all | solution.py:198
  86.8 6.4 copy.99
  93.2 4.7 constant_dynamic-update-slice_fusion.2
  100.4 10.3 %constant_dynamic-update-slice_fusion.6 = bf16[89,128,16,8,2]{1,4,3,2,0:T(2,128)(2,1)} fusion(bf16[89,128,16,8,2]{1,4,3,2,0:T(2,128)(2,1)} %copy_dynamic-update-slice_fusion, bf16[64,128,16,8,2]{1,4,3,2,0:T(2,128)(2,1)} %bitcast.53), kind=kLoop, calls=%fused_computation.43 | loop fusion | bytes 8388608
  113.2 6.8 copy.103
  121.4 52.3 %shard_map.68 = (bf16[2048,256]{1,0:T(8,128)(2,1)}, f32[256,6912]{1,0:T(8,128)}) custom-call(s32[432]{0:T(512)} %reshape.264.idx_ref, bf16[89,128,256]{2,1,0:T(8,128)(2,1)} %broadcast_dynamic-update-slice_fusion.1.table_ref, bf16[89,256,128]{2,1,0:T(8,128)(2,1)} %bitcast.56, bf16[27,256,256]{2,1,0:T(8,128)(2,1)} %w_ref.3, bf16[2048,256]{1,0:T(8,128)(2,1)} %grad_ref.1, ...), custom_call_target="tpu_custom_call" | custom-call | flops 14495514624 | bytes 27525120 | tf_op jit(solution)/shard_map/pallas_call | solution.py:114
  173.7 8.5 copy.111
  182.2 10.3 %copy.112 = f32[256,27,256]{2,1,0:T(8,128)} copy(f32[256,27,256]{0,2,1:T(8,128)} %bitcast.49) | data formatting | bytes 14155776 | tf_op jit(solution)/shard_map/reshape | solution.py:257
  192.5 5.2 convert.7
  200.5 5.4 copy.104
  205.9 9.7 %all-to-all-start.1 = ((bf16[16,4,128,256]{3,1,2,0:T(4,128)(2,1)}), bf16[16,4,128,256]{3,1,2,0:T(4,128)(2,1)}, u32[]{:S(2)}, u32[]{:S(2)}) async-start(bf16[16,4,128,256]{3,1,2,0:T(4,128)(2,1)} %copy.104), calls=%async_computation.1 | async-start | bytes 8388608 | tf_op jit(solution)/shard_map/all_to_all | solution.py:229
  216.7 4.8 collective-permute-start.3
  221.5 3.0 collective-permute-start.2
  224.5 2.9 collective-permute-done.3
  229.8 36.6 %all-to-all-done.1 = bf16[16,4,128,256]{3,1,2,0:T(4,128)(2,1)} async-done(((bf16[16,4,128,256]{3,1,2,0:T(4,128)(2,1)}), bf16[16,4,128,256]{3,1,2,0:T(4,128)(2,1)}, u32[]{:S(2)}, u32[]{:S(2)}) %all-to-all-start.1) | async-done | bytes 4194336 | tf_op jit(solution)/shard_map/all_to_all | solution.py:229
  266.4 4.7 fusion.3
  271.1 6.1 fusion.2
  277.3 567.7 %reduce-scatter.2.cloned.1.call-done = f32[2,27,256]{2,1,0:T(8,128)} async-done(((f32[256,27,256]{2,1,0:T(8,128)}), f32[2,27,256]{2,1,0:T(8,128)}) %reduce-scatter.2.cloned.1.call-update) | async-done | bytes 55312 | tf_op jit(solution)/shard_map/reduce_scatter | solution.py:258
  844.9 45.3 %all_gather.3 = f32[16,27,256]{2,1,0:T(8,128)S(1)} all-gather(f32[2,27,256]{2,1,0:T(8,128)} %reduce-scatter.2.cloned.1.call-done), channel_id=1, replica_groups=mesh['region'=8,'shard'=16] {'region'}, dimensions={0}, use_global_device_ids=true | all-gather | bytes 497664 | tf_op jit(solution)/shard_map/all_gather | solution.py:280
  (83 shorter events, 29.7 us)
Async XLA Ops:
  16.5 10.6 %copy-start.1 = (bf16[2048,256]{1,0:T(8,128)(2,1)S(1)}, bf16[2048,256]{1,0:T(8,128)(2,1)}, u32[]{:S(2)}) copy-start(bf16[2048,256]{1,0:T(8,128)(2,1)} %param.4) | copy-start | bytes 3145732
  16.6 70.3 %all-to-all-start = ((bf16[16,4,128,256]{3,2,1,0:T(8,128)(2,1)}), bf16[16,4,128,256]{3,2,1,0:T(8,128)(2,1)}, u32[]{:S(2)}, u32[]{:S(2)}) async-start(bf16[16,4,128,256]{3,2,1,0:T(8,128)(2,1)} %copy.91), calls=%async_computation | async-start | bytes 8388608 | tf_op jit(solution)/shard_map/all_to_all | solution.py:198
  25.3 819.6 %reduce-scatter.2.cloned.1.call-start = ((), (), s32[]{:S(2)}) async-start(), calls=%async_computation.3 | async-start | bytes 8454144 | tf_op jit(solution)/shard_map/reduce_scatter | solution.py:258
  28.0 40.1 %collective-permute-start.1 = (bf16[4,128,256]{2,1,0:T(8,128)(2,1)S(1)}, bf16[4,128,256]{2,1,0:T(8,128)(2,1)S(1)}, u32[]{:S(2)}, u32[]{:S(2)}) collective-permute-start(bf16[4,128,256]{2,1,0:T(8,128)(2,1)S(1)} %get-tuple-element.42), channel_id=1, source_target_pairs={{16,0},{32,16},{48,32},{64,48},{80,64},{96,80},{112,96},{17,1},{33... | collective-permute-start | bytes 786440 | tf_op jit(solution)/shard_map/ppermute | solution.py:24
  30.9 37.3 %collective-permute-start = (bf16[4,128,256]{2,1,0:T(8,128)(2,1)S(1)}, bf16[4,128,256]{2,1,0:T(8,128)(2,1)}, u32[]{:S(2)}, u32[]{:S(2)}) collective-permute-start(bf16[4,128,256]{2,1,0:T(8,128)(2,1)S(1)} %get-tuple-element.41), channel_id=1, source_target_pairs={{0,16},{16,32},{32,48},{48,64},{64,80},{80,96},{96,112},{1,17},{17... | collective-permute-start | bytes 786440 | tf_op jit(solution)/shard_map/ppermute | solution.py:22
  197.7 2.5 copy-start
  205.9 60.5 %all-to-all-start.1 = ((bf16[16,4,128,256]{3,1,2,0:T(4,128)(2,1)}), bf16[16,4,128,256]{3,1,2,0:T(4,128)(2,1)}, u32[]{:S(2)}, u32[]{:S(2)}) async-start(bf16[16,4,128,256]{3,1,2,0:T(4,128)(2,1)} %copy.104), calls=%async_computation.1 | async-start | bytes 8388608 | tf_op jit(solution)/shard_map/all_to_all | solution.py:229
  216.7 10.7 %collective-permute-start.3 = (bf16[4,128,256]{2,1,0:T(8,128)(2,1)S(1)}, bf16[4,128,256]{2,1,0:T(8,128)(2,1)S(1)}, u32[]{:S(2)}, u32[]{:S(2)}) collective-permute-start(bf16[4,128,256]{2,1,0:T(8,128)(2,1)S(1)} %get-tuple-element.37), channel_id=1, source_target_pairs={{16,0},{32,16},{48,32},{64,48},{80,64},{96,80},{112,96},{17,1},{33... | collective-permute-start | bytes 786440 | tf_op jit(solution)/shard_map/ppermute | solution.py:24
  221.5 6.4 collective-permute-start.2
  266.4 4.7 copy-start.2
Sparse Core Ops, SparseCore 0:
  192.6 652.2 reduce-scatter.1

commit v4 on v3

--- a/solution.py
+++ b/solution.py
@@ -101,7 +101,7 @@
     def _():
         acc_ref[...] += part
 
-    wg_ref[...] = jnp.dot(gt_ref[...], grad_ref[...], preferred_element_type=jnp.float32) * scale
+    wg_ref[0] = jnp.dot(gt_ref[...], grad_ref[...], preferred_element_type=jnp.float32) * scale
 
     @pl.when(k == pl.num_programs(0) - 1)
     def _():
@@ -115,7 +115,7 @@
         functools.partial(_forward_kernel, scale=scale, first=first),
         out_shape=(
             jax.ShapeDtypeStruct((count, channels), out_dtype),
-            jax.ShapeDtypeStruct((channels, (last - first) * channels), jnp.float32),
+            jax.ShapeDtypeStruct((last - first, channels, channels), jnp.float32),
         ),
         grid_spec=pltpu.PrefetchScalarGridSpec(
             num_scalar_prefetch=1,
@@ -129,7 +129,7 @@
             ],
             out_specs=[
                 pl.BlockSpec((count, channels), lambda k, idx: (0, 0)),
-                pl.BlockSpec((channels, channels), lambda k, idx: (0, k)),
+                pl.BlockSpec((1, channels, channels), lambda k, idx: (k, 0, 0)),
             ],
             scratch_shapes=[
                 pltpu.VMEM((count, channels), jnp.bfloat16),
@@ -146,6 +146,15 @@
             dimension_semantics=("arbitrary",), vmem_limit_bytes=56 * 1024 * 1024
         ),
     )(table_index.reshape(-1), table, tablet, weights, grad_rows, acc_in)
+
+
+def region_sum(value, count):
+    step = 1
+    while step < count:
+        pairs = [(i, i ^ step) for i in range(count)]
+        value = value + lax.ppermute(value, "region", pairs)
+        step *= 2
+    return value
 
 
 def body(features, kernel_map, weights, out_grad):
@@ -226,13 +235,14 @@
     table_index = jnp.where(present, table_index, table_rows)
     table_grad = table_grad_sums(table_index, grad_blocks, weights, table_rows + 1)
     remote_sums = table_grad[blocks_dev:table_rows].astype(jnp.bfloat16)
-    returned = lax.all_to_all(
-        remote_sums[: n_shard * capacity].reshape(n_shard, capacity, voxels, channels),
-        "shard",
-        split_axis=0,
-        concat_axis=0,
-        tiled=True,
-    )
+    sums_by_peer = remote_sums[: n_shard * capacity].reshape(n_shard, capacity, voxels, channels)
+    received = [jnp.zeros((capacity, voxels, channels), jnp.bfloat16)]
+    for shift in range(1, n_shard):
+        piece = lax.dynamic_index_in_dim(sums_by_peer, (my_shard + shift) % n_shard, 0, keepdims=False)
+        received.append(
+            lax.ppermute(piece, "shard", [(i, (i + shift) % n_shard) for i in range(n_shard)])
+        )
+    chosen_by_shift = jnp.take(chosen, (my_shard - shard_ids) % n_shard, axis=0)
     rim_back = padded(remote_sums[n_shard * capacity :], (("region", 0),), capacity)
     incoming, rims, table_grad = lax.optimization_barrier((incoming, rims, table_grad))
     table = jnp.concatenate(
@@ -245,21 +255,25 @@
         ],
         axis=0,
     )
-    share = channels // (n_shard * n_region)
-    tablet = table.reshape(table_rows + 1, voxels, n_shard, n_region, share)
-    tablet = jnp.transpose(tablet, (0, 3, 2, 4, 1)).reshape(table_rows + 1, channels, voxels)
+    tablet = jnp.swapaxes(table, 1, 2)
     scale = 1.0 / math.sqrt(total_blocks * voxels)
     grad_rows = grad_blocks.reshape(blocks_dev * voxels, channels)
-    conv_out, kernel_term = forward_terms(
+    half = offsets // 2
+    conv_part, term_a = forward_terms(
         table_index, table, tablet, weights, grad_rows,
-        jnp.zeros((blocks_dev * voxels, channels), jnp.float32), 0, offsets, jnp.bfloat16, scale,
-    )
-    kernel_term = kernel_term.reshape(channels, offsets, channels)
-    scattered = lax.psum_scatter(kernel_term, ("region", "shard"), scatter_dimension=0, tiled=True)
+        jnp.zeros((blocks_dev * voxels, channels), jnp.float32), 0, half, jnp.float32, scale,
+    )
+    received, conv_part = lax.optimization_barrier((received, conv_part))
+    conv_out, term_b = forward_terms(
+        table_index, table, tablet, weights, grad_rows, conv_part, half, offsets, jnp.bfloat16, scale,
+    )
+    kernel_term = jnp.concatenate([term_a, term_b], axis=0)
+    returned = jnp.stack(received)
+    scattered = lax.psum_scatter(kernel_term, "shard", scatter_dimension=1, tiled=True)
     input_acc = table_grad[:blocks_dev]
     input_acc = input_acc + jnp.einsum(
         "pcj,pcvd->jvd",
-        chosen.astype(jnp.float32),
+        chosen_by_shift.astype(jnp.float32),
         returned.astype(jnp.float32),
         precision=lax.Precision.HIGHEST,
     )
@@ -277,7 +291,7 @@
         precision=lax.Precision.HIGHEST,
     )
     in_grad = input_acc.reshape(blocks_dev * voxels, channels).astype(jnp.bfloat16)
-    weight_grad = jnp.swapaxes(lax.all_gather(scattered, "region", axis=0, tiled=True), 0, 1)
+    weight_grad = region_sum(scattered, n_region)
     return (conv_out, in_grad, weight_grad)
 
 

time: 900 us -> 398 us (0.44)
  waiting for transfers between devices: 625 us -> 83.6 us
  starting transfers between devices: 32.4 us -> 83.2 us
  blocking collectives: 45.3 us -> 0 us
  local copies, waits for them, and re-layouts: 74.7 us -> 89.5 us
  other arithmetic: 16.3 us -> 26.1 us
    reduce_scatter x1, waiting for transfers between devices: 568 us -> 75.5 us  [body(): lax.psum_scatter(kernel_term, 'shard', scatter_dimension=1, tiled=True)]
    ppermute x0 -> x18, starting transfers between devices: none -> 61.2 us  [the longest x15 55.4 us: body(): lax.ppermute(piece, 'shard', [(i, (i + shift) % n_shard) for i in range(n...]
    all_gather x1 -> x0, blocking collectives: 45.3 us -> none  [body(): lax.all_gather(scattered, 'region', axis=0, tiled=True)]
    another operation x0 -> x17, local copies, waits for them, and re-layouts: none -> 43.9 us  [body(): returned = jnp.stack(received)]
    all_to_all x1 -> x0, waiting for transfers between devices: 36.6 us -> none  [body(): lax.all_to_all(remote_sums[:n_shard * capacity].reshape(n_shard, capacity...]
    all_to_all x1, waiting for transfers between devices: 17.6 us -> 0.01 us  [body(): lax.all_to_all(outgoing, 'shard', split_axis=0, concat_axis=0, tiled=True)]
    reshape x2 -> x1, local copies, waits for them, and re-layouts: 15.7 us -> 0.65 us  [body(): own_blocks = features.reshape(blocks_dev, voxels, channels)]
    unnamed x16 -> x68, local copies, waits for them, and re-layouts: 24.9 us -> 10.6 us
  transfers between devices with their start and end apart: 7 -> 24, of which waited for: 4 -> 4; matrix products, arithmetic and copies ran while one was open for 4% -> 27% of each run, Pallas kernels for 3% -> 14%
where the time goes in v4:
time: 398 us; the launch traced here: 394 us
  local copies, waits for them, and re-layouts  89.5 us (22%)
  Pallas kernels  87.3 us (22%)
  waiting for transfers between devices  83.6 us (21%)
  starting transfers between devices  83.2 us (21%)
  other arithmetic  26.1 us (7%)
  between operations  14.8 us (4%)
  matrix products  9.35 us (2%)
    reduce_scatter x1, waiting for transfers between devices, body(): lax.psum_scatter(kernel_term, 'shard', scatter_dimension=1, tiled=True)  75.5 us
    pallas_call x2, Pallas kernels, forward_terms(): pl.pallas_call(functools.partial(_forward_kernel, scale=scale, first=firs...  60.1 us
    ppermute x15, starting transfers between devices, body(): lax.ppermute(piece, 'shard', [(i, (i + shift) % n_shard) for i in range(n...  55.4 us
    another operation x17, local copies, waits for them, and re-layouts, body(): returned = jnp.stack(received)  43.9 us
    pallas_call x1, Pallas kernels, table_grad_sums(): pl.pallas_call(_table_grad_kernel, out_shape=jax.ShapeDtypeStruct((rows,...  27.2 us
    unnamed x68, local copies, waits for them, and re-layouts  10.6 us
    ppermute x2, starting transfers between devices, padded(): lax.ppermute(tail, axis, [(i, (i + 1) % count) for i in range(ends)])  9.41 us
    concatenate x2, local copies, waits for them, and re-layouts, body(): jnp.concatenate([own_blocks, incoming.reshape(n_shard * capacity, voxels,...  9.33 us
  transfers between devices with their start and end apart: 24, of which 4 were waited for; matrix products, arithmetic and copies ran while one was open for 27% of the time, Pallas kernels for 14%

profile of v4, /device:TPU:1, one launch (start us, length us, event | category | flops | bytes accessed | tf_op | source)
XLA Modules:
  0.0 393.9 jit_solution(3069416791222013115)
XLA Ops:
  15.9 8.8 %all-to-all-start = ((bf16[16,4,128,256]{3,2,1,0:T(8,128)(2,1)}), bf16[16,4,128,256]{3,2,1,0:T(8,128)(2,1)}, u32[]{:S(2)}, u32[]{:S(2)}) async-start(bf16[16,4,128,256]{3,2,1,0:T(8,128)(2,1)} %copy.115), calls=%async_computation | async-start | bytes 8388608 | tf_op jit(solution)/shard_map/all_to_all | solution.py:207
  28.4 3.9 %collective-permute-start = (bf16[4,128,256]{1,2,0:T(8,128)(2,1)}, bf16[4,128,256]{1,2,0:T(8,128)(2,1)}, u32[]{:S(2)}, u32[]{:S(2)}) collective-permute-start(bf16[4,128,256]{1,2,0:T(8,128)(2,1)} %get-tuple-element.82), channel_id=1, source_target_pairs={{0,16},{16,32},{32,48},{48,64},{64,80},{80,96},{96,112},{1,17},{17... | collective-permute-start | bytes 786440 | tf_op jit(solution)/shard_map/ppermute | solution.py:22
  37.4 27.2 %shard_map.67 = f32[89,128,256]{2,1,0:T(8,128)} custom-call(s32[432]{0:T(512)} %reshape.305.idx_ref, bf16[16,128,256]{2,1,0:T(8,128)(2,1)} %bitcast.108, bf16[27,256,256]{2,1,0:T(8,128)(2,1)} %w_ref.5), custom_call_target="tpu_custom_call" | custom-call | flops 7247757312 | bytes 16252928 | tf_op jit(solution)/shard_map/pallas_call | solution.py:59
  64.6 5.2 %convert.7 = bf16[89,128,256]{2,1,0:T(8,128)(2,1)S(1)} convert(f32[89,128,256]{2,1,0:T(8,128)} %shard_map.67) | non-fusion elementwise | flops 2916352 | bytes 17498112 | tf_op jit(solution)/shard_map/convert.4
  74.8 4.0 %dynamic-slice_bitcast_fusion = (bf16[4,128,256]{2,1,0:T(8,128)(2,1)}, bf16[4,128,256]{2,1,0:T(8,128)(2,1)}, bf16[4,128,256]{2,1,0:T(8,128)(2,1)}, bf16[4,128,25...) fusion(bf16[16,4,128,256]{3,2,1,0:T(8,128)(2,1)} %bitcast.85, ...), kind=kLoop, calls=%fused_computation.21 | loop fusion | bytes 7864380 | tf_op jit(solution)/shard_map/jit(dynamic_index_in_dim)/squeeze | solution.py:241
  78.8 5.0 %collective-permute-start.16 = (bf16[4,128,256]{2,1,0:T(8,128)(2,1)}, bf16[4,128,256]{2,1,0:T(8,128)(2,1)S(1)}, u32[]{:S(2)}, u32[]{:S(2)}) collective-permute-start(bf16[4,128,256]{2,1,0:T(8,128)(2,1)} %get-tuple-element.67), channel_id=1, source_target_pairs={{0,15},{1,0},{2,1},{3,2},{4,3},{5,4},{6,5},{7,6},{8,7},{9,8},{10,9... | collective-permute-start | bytes 786440 | tf_op jit(solution)/shard_map/ppermute | solution.py:243
  90.6 6.4 %copy.122 = bf16[16,4,128,256]{2,3,1,0:T(8,128)(2,1)} copy(bf16[16,4,128,256]{3,2,1,0:T(8,128)(2,1)} %all-to-all-done) | data formatting | bytes 8388608 | tf_op jit(solution)/shard_map/optimization_barrier | solution.py:247
  97.0 4.7 %constant_dynamic-update-slice_fusion = bf16[89,128,256]{1,2,0:T(8,128)(2,1)} fusion(bf16[89,128,256]{1,2,0:T(8,128)(2,1)} %constant_dynamic-update-slice_fusion.1, bf16[64,128,256]{1,2,0:T(8,128)(2,1)} %bitcast.84), kind=kLoop, calls=%fused_computation.53 | loop fusion | bytes 8388608
  102.4 3.6 collective-permute-start.11
  106.0 9.1 %collective-permute-start.9 = (bf16[4,128,256]{2,1,0:T(8,128)(2,1)}, bf16[4,128,256]{2,1,0:T(8,128)(2,1)S(1)}, u32[]{:S(2)}, u32[]{:S(2)}) collective-permute-start(bf16[4,128,256]{2,1,0:T(8,128)(2,1)} %get-tuple-element.74), channel_id=1, source_target_pairs={{0,8},{1,9},{2,10},{3,11},{4,12},{5,13},{6,14},{7,15},{8,0},{9,1},... | collective-permute-start | bytes 786440 | tf_op jit(solution)/shard_map/ppermute | solution.py:243
  119.6 8.7 %copy.125.table_ref = bf16[89,128,256]{2,1,0:T(8,128)(2,1)} copy(bf16[89,128,256]{1,2,0:T(8,128)(2,1)} %broadcast_dynamic-update-slice_fusion) | data formatting | bytes 11665408 | tf_op jit(solution)/shard_map/concatenate | solution.py:248
  128.4 17.5 %collective-permute-start.6 = (bf16[4,128,256]{2,1,0:T(8,128)(2,1)}, bf16[4,128,256]{2,1,0:T(8,128)(2,1)S(1)}, u32[]{:S(2)}, u32[]{:S(2)}) collective-permute-start(bf16[4,128,256]{2,1,0:T(8,128)(2,1)} %get-tuple-element.77), channel_id=1, source_target_pairs={{0,5},{1,6},{2,7},{3,8},{4,9},{5,10},{6,11},{7,12},{8,13},{9,14},{... | collective-permute-start | bytes 786440 | tf_op jit(solution)/shard_map/ppermute | solution.py:243
  146.1 8.0 %collective-permute-start.4 = (bf16[4,128,256]{2,1,0:T(8,128)(2,1)S(1)}, bf16[4,128,256]{2,1,0:T(8,128)(2,1)S(1)}, u32[]{:S(2)}, u32[]{:S(2)}) collective-permute-start(bf16[4,128,256]{2,1,0:T(8,128)(2,1)S(1)} %copy-done.22), channel_id=1, source_target_pairs={{0,3},{1,4},{2,5},{3,6},{4,7},{5,8},{6,9},{7,10},{8,11},{9,12},{10... | collective-permute-start | bytes 786440 | tf_op jit(solution)/shard_map/ppermute | solution.py:243
  154.2 4.6 %collective-permute-start.3 = (bf16[4,128,256]{2,1,0:T(8,128)(2,1)S(1)}, bf16[4,128,256]{2,1,0:T(8,128)(2,1)S(1)}, u32[]{:S(2)}, u32[]{:S(2)}) collective-permute-start(bf16[4,128,256]{2,1,0:T(8,128)(2,1)S(1)} %copy-done.21), channel_id=1, source_target_pairs={{0,2},{1,3},{2,4},{3,5},{4,6},{5,7},{6,8},{7,9},{8,10},{9,11},{10,... | collective-permute-start | bytes 786440 | tf_op jit(solution)/shard_map/ppermute | solution.py:243
  158.8 3.5 collective-permute-start.2
  163.8 29.3 %shard_map.68 = (f32[2048,256]{1,0:T(8,128)}, f32[13,256,256]{2,1,0:T(8,128)}) custom-call(s32[432]{0:T(512)} %reshape.305.idx_ref, bf16[89,128,256]{2,1,0:T(8,128)(2,1)} %copy.125.table_ref, bf16[89,256,128]{2,1,0:T(8,128)(2,1)} %bitcast.89, bf16[27,256,256]{2,1,0:T(8,128)(2,1)} %w_ref.5, bf16[2048,256]{1,0:T(8,128)(2,1)} %grad_ref.3, ...), custom_call_target="tpu_custom_call" | custom-call | flops 6979321856 | bytes 22020096 | tf_op jit(solution)/shard_map/pallas_call | solution.py:114
  193.9 30.9 %shard_map.69 = (bf16[2048,256]{1,0:T(8,128)(2,1)}, f32[14,256,256]{2,1,0:T(8,128)}) custom-call(s32[432]{0:T(512)} %reshape.305.idx_ref, bf16[89,128,256]{2,1,0:T(8,128)(2,1)} %copy.125.table_ref, bf16[89,256,128]{2,1,0:T(8,128)(2,1)} %bitcast.90, bf16[27,256,256]{2,1,0:T(8,128)(2,1)} %w_ref.5, bf16[2048,256]{1,0:T(8,128)(2,1)} %grad_ref.3, ...), custom_call_target="tpu_custom_call" | custom-call | flops 7516192768 | bytes 22413312 | tf_op jit(solution)/shard_map/pallas_call | solution.py:114
  224.9 5.6 %pad_maximum_fusion = f32[27,256,256]{2,1,0:T(8,128)} fusion(f32[14,256,256]{2,1,0:T(8,128)} %get-tuple-element.50, f32[13,256,256]{2,1,0:T(8,128)S(1)} %copy-done.3), kind=kLoop, calls=%fused_computation.1 | loop fusion | flops 1769472 | bytes 14155776 | tf_op jit(solution)/shard_map/concatenate | solution.py:270
  232.3 5.5 %collective-permute-start.17 = (bf16[4,128,256]{2,1,0:T(8,128)(2,1)}, bf16[4,128,256]{2,1,0:T(8,128)(2,1)S(1)}, u32[]{:S(2)}, u32[]{:S(2)}) collective-permute-start(bf16[4,128,256]{2,1,0:T(8,128)(2,1)} %get-tuple-element.65), channel_id=1, source_target_pairs={{0,16},{16,32},{32,48},{48,64},{64,80},{80,96},{96,112},{1,17},{17... | collective-permute-start | bytes 786440 | tf_op jit(solution)/shard_map/ppermute | solution.py:22
  240.4 75.5 %reduce-scatter.2.cloned.1.call-done = f32[27,16,256]{2,1,0:T(8,128)} async-done(((f32[27,256,256]{2,1,0:T(8,128)}), f32[27,16,256]{2,1,0:T(8,128)}) %reduce-scatter.2.cloned.1.call-update) | async-done | bytes 442384 | tf_op jit(solution)/shard_map/reduce_scatter | solution.py:272
  345.1 23.2 %stack.67 = bf16[16,4,128,256]{3,0,1,2:T(8,128)(2,1)} concatenate(bf16[1,4,128,256]{3,0,1,2:T(2,128)(2,1)S(1)} %copy.126, bf16[1,4,128,256]{3,0,1,2:T(2,128)(2,1)S(1)} %copy.127, bf16[1,4,128,256]{3,0,1,2:T(2,128)(2,1)} %copy.128, bf16[1,4,128,256]{3,0,1,2:T(2,128)(2,1)} %copy.129, bf16[1,4,128,256]{3,0,1,2:T(2,128)(2,1)} %copy.130, bf16[1,4,128,256]{3,0,1,2:T(2,128)(2,1)} %copy.131, ...), dimensions={0} | concatenate | bytes 8388608 | tf_op jit(solution)/shard_map/stack | solution.py:271
  368.4 3.7 convolution_bitcast_fusion
  376.1 6.1 %fusion = bf16[16,128,256]{2,1,0:T(8,128)(2,1)} fusion(f32[16,128,256]{2,0,1:T(8,128)S(1)} %fusion.6, f32[16,128,256]{2,0,1:T(8,128)S(1)} %copy-done.2, f32[16,128,256]{2,0,1:T(8,128)S(1)} %convolution_bitcast_fusion, f32[89,128,256]{2,1,0:T(8,128)} %shard_map.67), kind=kLoop, calls=%fused_computation.4 | loop fusion | flops 2097152 | bytes 9437184 | tf_op jit(solution)/shard_map/convert_element_type | solution.py:293
  382.2 4.0 %collective-permute-done.21 = f32[27,16,256]{2,1,0:T(8,128)S(1)} collective-permute-done((f32[27,16,256]{2,1,0:T(8,128)S(1)}, f32[27,16,256]{2,1,0:T(8,128)S(1)}, u32[]{:S(2)}, u32[]{:S(2)}) %collective-permute-start.21) | collective-permute-done | bytes 442400 | tf_op jit(solution)/shard_map/ppermute | solution.py:155
  (192 shorter events, 75.1 us)
Async XLA Ops:
  15.9 74.7 %all-to-all-start = ((bf16[16,4,128,256]{3,2,1,0:T(8,128)(2,1)}), bf16[16,4,128,256]{3,2,1,0:T(8,128)(2,1)}, u32[]{:S(2)}, u32[]{:S(2)}) async-start(bf16[16,4,128,256]{3,2,1,0:T(8,128)(2,1)} %copy.115), calls=%async_computation | async-start | bytes 8388608 | tf_op jit(solution)/shard_map/all_to_all | solution.py:207
  24.7 291.2 %reduce-scatter.2.cloned.1.call-start = ((), (), s32[]{:S(2)}) async-start(), calls=%async_computation.2 | async-start | bytes 7520256 | tf_op jit(solution)/shard_map/reduce_scatter | solution.py:272
  28.4 58.6 %collective-permute-start = (bf16[4,128,256]{1,2,0:T(8,128)(2,1)}, bf16[4,128,256]{1,2,0:T(8,128)(2,1)}, u32[]{:S(2)}, u32[]{:S(2)}) collective-permute-start(bf16[4,128,256]{1,2,0:T(8,128)(2,1)} %get-tuple-element.82), channel_id=1, source_target_pairs={{0,16},{16,32},{32,48},{48,64},{64,80},{80,96},{96,112},{1,17},{17... | collective-permute-start | bytes 786440 | tf_op jit(solution)/shard_map/ppermute | solution.py:22
  32.4 54.9 %collective-permute-start.1 = (bf16[4,128,256]{1,2,0:T(8,128)(2,1)}, bf16[4,128,256]{1,2,0:T(8,128)(2,1)}, u32[]{:S(2)}, u32[]{:S(2)}) collective-permute-start(bf16[4,128,256]{1,2,0:T(8,128)(2,1)} %get-tuple-element.83), channel_id=1, source_target_pairs={{16,0},{32,16},{48,32},{64,48},{80,64},{96,80},{112,96},{17,1},{33... | collective-permute-start | bytes 786440 | tf_op jit(solution)/shard_map/ppermute | solution.py:24
  78.8 23.5 %collective-permute-start.16 = (bf16[4,128,256]{2,1,0:T(8,128)(2,1)}, bf16[4,128,256]{2,1,0:T(8,128)(2,1)S(1)}, u32[]{:S(2)}, u32[]{:S(2)}) collective-permute-start(bf16[4,128,256]{2,1,0:T(8,128)(2,1)} %get-tuple-element.67), channel_id=1, source_target_pairs={{0,15},{1,0},{2,1},{3,2},{4,3},{5,4},{6,5},{7,6},{8,7},{9,8},{10,9... | collective-permute-start | bytes 786440 | tf_op jit(solution)/shard_map/ppermute | solution.py:243
  83.8 22.1 %collective-permute-start.15 = (bf16[4,128,256]{2,1,0:T(8,128)(2,1)}, bf16[4,128,256]{2,1,0:T(8,128)(2,1)S(1)}, u32[]{:S(2)}, u32[]{:S(2)}) collective-permute-start(bf16[4,128,256]{2,1,0:T(8,128)(2,1)} %get-tuple-element.68), channel_id=1, source_target_pairs={{0,14},{1,15},{2,0},{3,1},{4,2},{5,3},{6,4},{7,5},{8,6},{9,7},{10,... | collective-permute-start | bytes 786440 | tf_op jit(solution)/shard_map/ppermute | solution.py:243
  84.4 21.5 %collective-permute-start.14 = (bf16[4,128,256]{2,1,0:T(8,128)(2,1)}, bf16[4,128,256]{2,1,0:T(8,128)(2,1)S(1)}, u32[]{:S(2)}, u32[]{:S(2)}) collective-permute-start(bf16[4,128,256]{2,1,0:T(8,128)(2,1)} %get-tuple-element.69), channel_id=1, source_target_pairs={{0,13},{1,14},{2,15},{3,0},{4,1},{5,2},{6,3},{7,4},{8,5},{9,6},{10... | collective-permute-start | bytes 786440 | tf_op jit(solution)/shard_map/ppermute | solution.py:243
  87.0 28.1 %collective-permute-start.13 = (bf16[4,128,256]{2,1,0:T(8,128)(2,1)}, bf16[4,128,256]{2,1,0:T(8,128)(2,1)S(1)}, u32[]{:S(2)}, u32[]{:S(2)}) collective-permute-start(bf16[4,128,256]{2,1,0:T(8,128)(2,1)} %get-tuple-element.70), channel_id=1, source_target_pairs={{0,12},{1,13},{2,14},{3,15},{4,0},{5,1},{6,2},{7,3},{8,4},{9,5},{1... | collective-permute-start | bytes 786440 | tf_op jit(solution)/shard_map/ppermute | solution.py:243
  87.3 30.9 %collective-permute-start.12 = (bf16[4,128,256]{2,1,0:T(8,128)(2,1)}, bf16[4,128,256]{2,1,0:T(8,128)(2,1)S(1)}, u32[]{:S(2)}, u32[]{:S(2)}) collective-permute-start(bf16[4,128,256]{2,1,0:T(8,128)(2,1)} %get-tuple-element.71), channel_id=1, source_target_pairs={{0,11},{1,12},{2,13},{3,14},{4,15},{5,0},{6,1},{7,2},{8,3},{9,4},{... | collective-permute-start | bytes 786440 | tf_op jit(solution)/shard_map/ppermute | solution.py:243
  102.4 26.0 %collective-permute-start.11 = (bf16[4,128,256]{2,1,0:T(8,128)(2,1)}, bf16[4,128,256]{2,1,0:T(8,128)(2,1)S(1)}, u32[]{:S(2)}, u32[]{:S(2)}) collective-permute-start(bf16[4,128,256]{2,1,0:T(8,128)(2,1)} %get-tuple-element.72), channel_id=1, source_target_pairs={{0,10},{1,11},{2,12},{3,13},{4,14},{5,15},{6,0},{7,1},{8,2},{9,3},... | collective-permute-start | bytes 786440 | tf_op jit(solution)/shard_map/ppermute | solution.py:243
  105.9 39.9 %collective-permute-start.10 = (bf16[4,128,256]{2,1,0:T(8,128)(2,1)}, bf16[4,128,256]{2,1,0:T(8,128)(2,1)S(1)}, u32[]{:S(2)}, u32[]{:S(2)}) collective-permute-start(bf16[4,128,256]{2,1,0:T(8,128)(2,1)} %get-tuple-element.73), channel_id=1, source_target_pairs={{0,9},{1,10},{2,11},{3,12},{4,13},{5,14},{6,15},{7,0},{8,1},{9,2},... | collective-permute-start | bytes 786440 | tf_op jit(solution)/shard_map/ppermute | solution.py:243
  106.0 40.2 %collective-permute-start.9 = (bf16[4,128,256]{2,1,0:T(8,128)(2,1)}, bf16[4,128,256]{2,1,0:T(8,128)(2,1)S(1)}, u32[]{:S(2)}, u32[]{:S(2)}) collective-permute-start(bf16[4,128,256]{2,1,0:T(8,128)(2,1)} %get-tuple-element.74), channel_id=1, source_target_pairs={{0,8},{1,9},{2,10},{3,11},{4,12},{5,13},{6,14},{7,15},{8,0},{9,1},... | collective-permute-start | bytes 786440 | tf_op jit(solution)/shard_map/ppermute | solution.py:243
  115.1 39.1 %collective-permute-start.8 = (bf16[4,128,256]{2,1,0:T(8,128)(2,1)}, bf16[4,128,256]{2,1,0:T(8,128)(2,1)S(1)}, u32[]{:S(2)}, u32[]{:S(2)}) collective-permute-start(bf16[4,128,256]{2,1,0:T(8,128)(2,1)} %get-tuple-element.75), channel_id=1, source_target_pairs={{0,7},{1,8},{2,9},{3,10},{4,11},{5,12},{6,13},{7,14},{8,15},{9,0},... | collective-permute-start | bytes 786440 | tf_op jit(solution)/shard_map/ppermute | solution.py:243
  118.2 40.6 %collective-permute-start.7 = (bf16[4,128,256]{2,1,0:T(8,128)(2,1)}, bf16[4,128,256]{2,1,0:T(8,128)(2,1)}, u32[]{:S(2)}, u32[]{:S(2)}) collective-permute-start(bf16[4,128,256]{2,1,0:T(8,128)(2,1)} %get-tuple-element.76), channel_id=1, source_target_pairs={{0,6},{1,7},{2,8},{3,9},{4,10},{5,11},{6,12},{7,13},{8,14},{9,15},... | collective-permute-start | bytes 786440 | tf_op jit(solution)/shard_map/ppermute | solution.py:243
  128.4 64.7 %collective-permute-start.6 = (bf16[4,128,256]{2,1,0:T(8,128)(2,1)}, bf16[4,128,256]{2,1,0:T(8,128)(2,1)S(1)}, u32[]{:S(2)}, u32[]{:S(2)}) collective-permute-start(bf16[4,128,256]{2,1,0:T(8,128)(2,1)} %get-tuple-element.77), channel_id=1, source_target_pairs={{0,5},{1,6},{2,7},{3,8},{4,9},{5,10},{6,11},{7,12},{8,13},{9,14},{... | collective-permute-start | bytes 786440 | tf_op jit(solution)/shard_map/ppermute | solution.py:243
  145.9 47.2 %collective-permute-start.5 = (bf16[4,128,256]{2,1,0:T(8,128)(2,1)S(1)}, bf16[4,128,256]{2,1,0:T(8,128)(2,1)S(1)}, u32[]{:S(2)}, u32[]{:S(2)}) collective-permute-start(bf16[4,128,256]{2,1,0:T(8,128)(2,1)S(1)} %copy-done.23), channel_id=1, source_target_pairs={{0,4},{1,5},{2,6},{3,7},{4,8},{5,9},{6,10},{7,11},{8,12},{9,13},{1... | collective-permute-start | bytes 786440 | tf_op jit(solution)/shard_map/ppermute | solution.py:243
  146.1 47.0 %collective-permute-start.4 = (bf16[4,128,256]{2,1,0:T(8,128)(2,1)S(1)}, bf16[4,128,256]{2,1,0:T(8,128)(2,1)S(1)}, u32[]{:S(2)}, u32[]{:S(2)}) collective-permute-start(bf16[4,128,256]{2,1,0:T(8,128)(2,1)S(1)} %copy-done.22), channel_id=1, source_target_pairs={{0,3},{1,4},{2,5},{3,6},{4,7},{5,8},{6,9},{7,10},{8,11},{9,12},{10... | collective-permute-start | bytes 786440 | tf_op jit(solution)/shard_map/ppermute | solution.py:243
  154.2 38.9 %collective-permute-start.3 = (bf16[4,128,256]{2,1,0:T(8,128)(2,1)S(1)}, bf16[4,128,256]{2,1,0:T(8,128)(2,1)S(1)}, u32[]{:S(2)}, u32[]{:S(2)}) collective-permute-start(bf16[4,128,256]{2,1,0:T(8,128)(2,1)S(1)} %copy-done.21), channel_id=1, source_target_pairs={{0,2},{1,3},{2,4},{3,5},{4,6},{5,7},{6,8},{7,9},{8,10},{9,11},{10,... | collective-permute-start | bytes 786440 | tf_op jit(solution)/shard_map/ppermute | solution.py:243
  158.8 34.3 %collective-permute-start.2 = (bf16[4,128,256]{2,1,0:T(8,128)(2,1)S(1)}, bf16[4,128,256]{2,1,0:T(8,128)(2,1)S(1)}, u32[]{:S(2)}, u32[]{:S(2)}) collective-permute-start(bf16[4,128,256]{2,1,0:T(8,128)(2,1)S(1)} %copy-done.20), channel_id=1, source_target_pairs={{0,1},{1,2},{2,3},{3,4},{4,5},{5,6},{6,7},{7,8},{8,9},{9,10},{10,1... | collective-permute-start | bytes 786440 | tf_op jit(solution)/shard_map/ppermute | solution.py:243
  232.3 90.0 %collective-permute-start.17 = (bf16[4,128,256]{2,1,0:T(8,128)(2,1)}, bf16[4,128,256]{2,1,0:T(8,128)(2,1)S(1)}, u32[]{:S(2)}, u32[]{:S(2)}) collective-permute-start(bf16[4,128,256]{2,1,0:T(8,128)(2,1)} %get-tuple-element.65), channel_id=1, source_target_pairs={{0,16},{16,32},{32,48},{48,64},{64,80},{80,96},{96,112},{1,17},{17... | collective-permute-start | bytes 786440 | tf_op jit(solution)/shard_map/ppermute | solution.py:22
  237.8 80.1 %collective-permute-start.18 = (bf16[4,128,256]{2,1,0:T(8,128)(2,1)S(1)}, bf16[4,128,256]{2,1,0:T(8,128)(2,1)S(1)}, u32[]{:S(2)}, u32[]{:S(2)}) collective-permute-start(bf16[4,128,256]{2,1,0:T(8,128)(2,1)S(1)} %get-tuple-element.66), channel_id=1, source_target_pairs={{16,0},{32,16},{48,32},{64,48},{80,64},{96,80},{112,96},{17,1},{33... | collective-permute-start | bytes 786440 | tf_op jit(solution)/shard_map/ppermute | solution.py:24
  315.9 3.4 collective-permute-start.19
  321.1 51.0 %collective-permute-start.20 = (f32[27,16,256]{2,1,0:T(8,128)}, f32[27,16,256]{2,1,0:T(8,128)}, u32[]{:S(2)}, u32[]{:S(2)}) collective-permute-start(f32[27,16,256]{2,1,0:T(8,128)} %add.393), channel_id=1, source_target_pairs={{0,32},{16,48},{32,0},{48,16},{64,96},{80,112},{96,64},{112,80},{1... | collective-permute-start | bytes 1327112 | tf_op jit(solution)/shard_map/ppermute | solution.py:155
  373.3 12.9 %collective-permute-start.21 = (f32[27,16,256]{2,1,0:T(8,128)S(1)}, f32[27,16,256]{2,1,0:T(8,128)S(1)}, u32[]{:S(2)}, u32[]{:S(2)}) collective-permute-start(f32[27,16,256]{2,1,0:T(8,128)S(1)} %add.394), channel_id=1, source_target_pairs={{0,64},{16,80},{32,96},{48,112},{64,0},{80,16},{96,32},{112,48},{1... | collective-permute-start | bytes 1327112 | tf_op jit(solution)/shard_map/ppermute | solution.py:155
  (32 other events, 719.7 us)
Sparse Core Ops, SparseCore 0:
  230.7 85.1 reduce-scatter.1

commit v5 on v4

--- a/solution.py
+++ b/solution.py
@@ -235,14 +235,13 @@
     table_index = jnp.where(present, table_index, table_rows)
     table_grad = table_grad_sums(table_index, grad_blocks, weights, table_rows + 1)
     remote_sums = table_grad[blocks_dev:table_rows].astype(jnp.bfloat16)
-    sums_by_peer = remote_sums[: n_shard * capacity].reshape(n_shard, capacity, voxels, channels)
-    received = [jnp.zeros((capacity, voxels, channels), jnp.bfloat16)]
-    for shift in range(1, n_shard):
-        piece = lax.dynamic_index_in_dim(sums_by_peer, (my_shard + shift) % n_shard, 0, keepdims=False)
-        received.append(
-            lax.ppermute(piece, "shard", [(i, (i + shift) % n_shard) for i in range(n_shard)])
-        )
-    chosen_by_shift = jnp.take(chosen, (my_shard - shard_ids) % n_shard, axis=0)
+    returned = lax.all_to_all(
+        remote_sums[: n_shard * capacity].reshape(n_shard, capacity, voxels, channels),
+        "shard",
+        split_axis=0,
+        concat_axis=0,
+        tiled=True,
+    )
     rim_back = padded(remote_sums[n_shard * capacity :], (("region", 0),), capacity)
     incoming, rims, table_grad = lax.optimization_barrier((incoming, rims, table_grad))
     table = jnp.concatenate(
@@ -263,17 +262,16 @@
         table_index, table, tablet, weights, grad_rows,
         jnp.zeros((blocks_dev * voxels, channels), jnp.float32), 0, half, jnp.float32, scale,
     )
-    received, conv_part = lax.optimization_barrier((received, conv_part))
+    returned, conv_part = lax.optimization_barrier((returned, conv_part))
     conv_out, term_b = forward_terms(
         table_index, table, tablet, weights, grad_rows, conv_part, half, offsets, jnp.bfloat16, scale,
     )
     kernel_term = jnp.concatenate([term_a, term_b], axis=0)
-    returned = jnp.stack(received)
     scattered = lax.psum_scatter(kernel_term, "shard", scatter_dimension=1, tiled=True)
     input_acc = table_grad[:blocks_dev]
     input_acc = input_acc + jnp.einsum(
         "pcj,pcvd->jvd",
-        chosen_by_shift.astype(jnp.float32),
+        chosen.astype(jnp.float32),
         returned.astype(jnp.float32),
         precision=lax.Precision.HIGHEST,
     )

time: 398 us -> 327 us (0.82)
  local copies, waits for them, and re-layouts: 89.5 us -> 41.4 us
  starting transfers between devices: 83.2 us -> 37.1 us
  waiting for transfers between devices: 83.6 us -> 112 us
    ppermute x15 -> x0, starting transfers between devices: 55.4 us -> none  [body(): lax.ppermute(piece, 'shard', [(i, (i + shift) % n_shard) for i in range(n...]
    another operation x17 -> x0, local copies, waits for them, and re-layouts: 43.9 us -> none  [body(): returned = jnp.stack(received)]
    all_to_all x1, waiting for transfers between devices: 0.01 us -> 18.2 us  [body(): lax.all_to_all(outgoing, 'shard', split_axis=0, concat_axis=0, tiled=True)]
    all_to_all x0 -> x1, starting transfers between devices: none -> 9.63 us  [body(): lax.all_to_all(remote_sums[:n_shard * capacity].reshape(n_shard, capacity...]
    reshape x0 -> x1, local copies, waits for them, and re-layouts: none -> 5.5 us  [body(): remote_sums[:n_shard * capacity]]
    ppermute x3, waiting for transfers between devices: 4.9 us -> 9.77 us  [region_sum(): value = value + lax.ppermute(value, 'region', pairs)]
    ppermute x2, waiting for transfers between devices: 0.01 us -> 4.44 us  [padded(): lax.ppermute(head, axis, [((i + 1) % count, i) for i in range(ends)])]
    reduce_scatter x1, waiting for transfers between devices: 75.5 us -> 79.6 us  [body(): lax.psum_scatter(kernel_term, 'shard', scatter_dimension=1, tiled=True)]
  transfers between devices with their start and end apart: 24 -> 10, of which waited for: 4 -> 6; matrix products, arithmetic and copies ran while one was open for 27% -> 17% of each run, Pallas kernels for 14% -> 17%
where the time goes in v5:
time: 327 us; the launch traced here: 326 us
  waiting for transfers between devices  112 us (34%)
  Pallas kernels  87.4 us (27%)
  local copies, waits for them, and re-layouts  41.4 us (13%)
  starting transfers between devices  37.1 us (11%)
  other arithmetic  23.9 us (7%)
  between operations  14.3 us (4%)
  matrix products  9.2 us (3%)
    reduce_scatter x1, waiting for transfers between devices, body(): lax.psum_scatter(kernel_term, 'shard', scatter_dimension=1, tiled=True)  79.6 us
    pallas_call x2, Pallas kernels, forward_terms(): pl.pallas_call(functools.partial(_forward_kernel, scale=scale, first=firs...  60.1 us
    pallas_call x1, Pallas kernels, table_grad_sums(): pl.pallas_call(_table_grad_kernel, out_shape=jax.ShapeDtypeStruct((rows,...  27.2 us
    all_to_all x1, waiting for transfers between devices, body(): lax.all_to_all(outgoing, 'shard', split_axis=0, concat_axis=0, tiled=True)  18.2 us
    ppermute x3, waiting for transfers between devices, region_sum(): value = value + lax.ppermute(value, 'region', pairs)  9.77 us
    all_to_all x1, starting transfers between devices, body(): lax.all_to_all(remote_sums[:n_shard * capacity].reshape(n_shard, capacity...  9.63 us
    unnamed x10, local copies, waits for them, and re-layouts  9.41 us
    concatenate x2, local copies, waits for them, and re-layouts, body(): jnp.concatenate([own_blocks, incoming.reshape(n_shard * capacity, voxels,...  9.12 us
  transfers between devices with their start and end apart: 10, of which 6 were waited for; matrix products, arithmetic and copies ran while one was open for 17% of the time, Pallas kernels for 17%

profile of v5, /device:TPU:1, one launch (start us, length us, event | category | flops | bytes accessed | tf_op | source)
XLA Modules:
  0.0 325.6 jit_solution(4955800406404930864)
XLA Ops:
  10.1 2.9 convolution_convert_fusion
  13.0 3.5 %copy.79 = bf16[16,4,128,256]{3,2,1,0:T(8,128)(2,1)} copy(bf16[16,4,128,256]{3,0,2,1:T(8,128)(2,1)S(1)} %convolution_convert_fusion) | data formatting | bytes 8388608 | tf_op jit(solution)/shard_map/convert_element_type | solution.py:200
  16.5 8.6 %all-to-all-start = ((bf16[16,4,128,256]{3,2,1,0:T(8,128)(2,1)}), bf16[16,4,128,256]{3,2,1,0:T(8,128)(2,1)}, u32[]{:S(2)}, u32[]{:S(2)}) async-start(bf16[16,4,128,256]{3,2,1,0:T(8,128)(2,1)} %copy.79), calls=%async_computation | async-start | bytes 8388608 | tf_op jit(solution)/shard_map/all_to_all | solution.py:207
  28.1 27.2 %shard_map.67 = f32[89,128,256]{2,1,0:T(8,128)} custom-call(s32[432]{0:T(512)} %reshape.251.idx_ref, bf16[16,128,256]{2,1,0:T(8,128)(2,1)} %bitcast.47, bf16[27,256,256]{2,1,0:T(8,128)(2,1)} %w_ref.5), custom_call_target="tpu_custom_call" | custom-call | flops 7247757312 | bytes 16252928 | tf_op jit(solution)/shard_map/pallas_call | solution.py:59
  55.3 5.2 %convert.7 = bf16[89,128,256]{2,1,0:T(8,128)(2,1)S(1)} convert(f32[89,128,256]{2,1,0:T(8,128)} %shard_map.67) | non-fusion elementwise | flops 2916352 | bytes 17498112 | tf_op jit(solution)/shard_map/convert.4
  60.8 2.2 copy-done
  63.0 5.5 %copy.88 = bf16[16,4,128,256]{3,1,2,0:T(4,128)(2,1)} copy(bf16[16,4,128,256]{3,2,1,0:T(8,128)(2,1)S(1)} %bitcast.39) | data formatting | bytes 8388608 | tf_op jit(solution)/shard_map/reshape | solution.py:239
  68.5 18.2 %all-to-all-done = bf16[16,4,128,256]{3,2,1,0:T(8,128)(2,1)} async-done(((bf16[16,4,128,256]{3,2,1,0:T(8,128)(2,1)}), bf16[16,4,128,256]{3,2,1,0:T(8,128)(2,1)}, u32[]{:S(2)}, u32[]{:S(2)}) %all-to-all-start) | async-done | bytes 4194336 | tf_op jit(solution)/shard_map/all_to_all | solution.py:207
  86.6 9.6 %all-to-all-start.1 = ((bf16[16,4,128,256]{3,1,2,0:T(4,128)(2,1)}), bf16[16,4,128,256]{3,1,2,0:T(4,128)(2,1)}, u32[]{:S(2)}, u32[]{:S(2)}) async-start(bf16[16,4,128,256]{3,1,2,0:T(4,128)(2,1)} %copy.88), calls=%async_computation.1 | async-start | bytes 8388608 | tf_op jit(solution)/shard_map/all_to_all | solution.py:238
  99.4 6.0 %collective-permute-start = (bf16[4,128,256]{1,2,0:T(8,128)(2,1)S(1)}, bf16[4,128,256]{1,2,0:T(8,128)(2,1)S(1)}, u32[]{:S(2)}, u32[]{:S(2)}) collective-permute-start(bf16[4,128,256]{1,2,0:T(8,128)(2,1)S(1)} %get-tuple-element.37), channel_id=1, source_target_pairs={{0,16},{16,32},{32,48},{48,64},{64,80},{80,96},{96,112},{1,17},{17... | collective-permute-start | bytes 786440 | tf_op jit(solution)/shard_map/ppermute | solution.py:22
  109.1 4.4 %collective-permute-done.1 = bf16[4,128,256]{1,2,0:T(8,128)(2,1)} collective-permute-done((bf16[4,128,256]{1,2,0:T(8,128)(2,1)S(1)}, bf16[4,128,256]{1,2,0:T(8,128)(2,1)}, u32[]{:S(2)}, u32[]{:S(2)}) %collective-permute-start.1) | collective-permute-done | bytes 262176 | tf_op jit(solution)/shard_map/ppermute | solution.py:24
  114.6 6.4 %copy.86 = bf16[16,4,128,256]{2,3,1,0:T(8,128)(2,1)} copy(bf16[16,4,128,256]{3,2,1,0:T(8,128)(2,1)} %all-to-all-done) | data formatting | bytes 8388608 | tf_op jit(solution)/shard_map/optimization_barrier | solution.py:246
  121.0 4.7 %constant_dynamic-update-slice_fusion = bf16[89,128,256]{1,2,0:T(8,128)(2,1)} fusion(bf16[89,128,256]{1,2,0:T(8,128)(2,1)} %constant_dynamic-update-slice_fusion.1, bf16[64,128,256]{1,2,0:T(8,128)(2,1)} %bitcast.38), kind=kLoop, calls=%fused_computation.42 | loop fusion | bytes 8388608
  127.8 8.5 %copy.90.table_ref = bf16[89,128,256]{2,1,0:T(8,128)(2,1)} copy(bf16[89,128,256]{1,2,0:T(8,128)(2,1)} %broadcast_dynamic-update-slice_fusion) | data formatting | bytes 11665408 | tf_op jit(solution)/shard_map/concatenate | solution.py:247
  137.8 29.2 %shard_map.68 = (f32[2048,256]{1,0:T(8,128)}, f32[13,256,256]{2,1,0:T(8,128)}) custom-call(s32[432]{0:T(512)} %reshape.251.idx_ref, bf16[89,128,256]{2,1,0:T(8,128)(2,1)} %copy.90.table_ref, bf16[89,256,128]{2,1,0:T(8,128)(2,1)} %bitcast.43, bf16[27,256,256]{2,1,0:T(8,128)(2,1)} %w_ref.5, bf16[2048,256]{1,0:T(8,128)(2,1)} %grad_ref.3, ...), custom_call_target="tpu_custom_call" | custom-call | flops 6979321856 | bytes 22020096 | tf_op jit(solution)/shard_map/pallas_call | solution.py:114
  167.0 30.9 %shard_map.69 = (bf16[2048,256]{1,0:T(8,128)(2,1)}, f32[14,256,256]{2,1,0:T(8,128)}) custom-call(s32[432]{0:T(512)} %reshape.251.idx_ref, bf16[89,128,256]{2,1,0:T(8,128)(2,1)} %copy.90.table_ref, bf16[89,256,128]{2,1,0:T(8,128)(2,1)} %bitcast.44, bf16[27,256,256]{2,1,0:T(8,128)(2,1)} %w_ref.5, bf16[2048,256]{1,0:T(8,128)(2,1)} %grad_ref.3, ...), custom_call_target="tpu_custom_call" | custom-call | flops 7516192768 | bytes 22413312 | tf_op jit(solution)/shard_map/pallas_call | solution.py:114
  197.9 5.7 %pad_maximum_fusion = f32[27,256,256]{2,1,0:T(8,128)} fusion(f32[14,256,256]{2,1,0:T(8,128)} %get-tuple-element.20, f32[13,256,256]{2,1,0:T(8,128)S(1)} %copy-done.2), kind=kLoop, calls=%fused_computation | loop fusion | flops 1769472 | bytes 14155776 | tf_op jit(solution)/shard_map/concatenate | solution.py:269
  206.7 79.6 %reduce-scatter.2.cloned.1.call-done = f32[27,16,256]{2,1,0:T(8,128)} async-done(((f32[27,256,256]{2,1,0:T(8,128)}), f32[27,16,256]{2,1,0:T(8,128)}) %reduce-scatter.2.cloned.1.call-update) | async-done | bytes 442384 | tf_op jit(solution)/shard_map/reduce_scatter | solution.py:270
  288.1 3.0 collective-permute-start.2
  294.9 4.6 %fusion.3 = f32[16,128,256]{2,0,1:T(8,128)S(1)} fusion(bf16[16,4,128,256]{3,1,2,0:T(4,128)(2,1)} %all-to-all-done.1, s32[16,16]{0,1:T(8,128)S(1)} %copy.76, pred[16,16]{0,1:T(8,128)(4,1)S(1)} %copy.75), kind=kOutput, calls=%fused_computation.9 | convolution fusion | flops 67110912 | bytes 6292736 | tf_op jit(solution)/shard_map/pcj,pcvd->jvd/dot_general | solution.py:272
  299.4 5.3 %collective-permute-done.5 = f32[27,16,256]{2,1,0:T(8,128)S(1)} collective-permute-done((f32[27,16,256]{2,1,0:T(8,128)S(1)}, f32[27,16,256]{2,1,0:T(8,128)S(1)}, u32[]{:S(2)}, u32[]{:S(2)}) %collective-permute-start.5) | collective-permute-done | bytes 442400 | tf_op jit(solution)/shard_map/ppermute | solution.py:155
  304.8 2.7 collective-permute-start.6
  307.5 6.0 %fusion.2 = bf16[16,128,256]{2,1,0:T(8,128)(2,1)} fusion(f32[16,128,256]{2,0,1:T(8,128)S(1)} %fusion.11, f32[16,128,256]{2,0,1:T(8,128)S(1)} %fusion.13, f32[16,128,256]{2,0,1:T(8,128)S(1)} %fusion.3, f32[89,128,256]{2,1,0:T(8,128)} %shard_map.67), kind=kLoop, calls=%fused_computation.5 | loop fusion | flops 2097152 | bytes 9437184 | tf_op jit(solution)/shard_map/convert_element_type | solution.py:291
  313.5 4.4 %collective-permute-done.6 = f32[27,16,256]{2,1,0:T(8,128)S(1)} collective-permute-done((f32[27,16,256]{2,1,0:T(8,128)S(1)}, f32[27,16,256]{2,1,0:T(8,128)S(1)}, u32[]{:S(2)}, u32[]{:S(2)}) %collective-permute-start.6) | collective-permute-done | bytes 442400 | tf_op jit(solution)/shard_map/ppermute | solution.py:155
  (82 shorter events, 26.8 us)
Async XLA Ops:
  16.5 70.1 %all-to-all-start = ((bf16[16,4,128,256]{3,2,1,0:T(8,128)(2,1)}), bf16[16,4,128,256]{3,2,1,0:T(8,128)(2,1)}, u32[]{:S(2)}, u32[]{:S(2)}) async-start(bf16[16,4,128,256]{3,2,1,0:T(8,128)(2,1)} %copy.79), calls=%async_computation | async-start | bytes 8388608 | tf_op jit(solution)/shard_map/all_to_all | solution.py:207
  60.5 2.5 copy-start
  68.5 29.8 %copy-start.1 = (bf16[2048,256]{1,0:T(8,128)(2,1)S(1)}, bf16[2048,256]{1,0:T(8,128)(2,1)}, u32[]{:S(2)}) copy-start(bf16[2048,256]{1,0:T(8,128)(2,1)} %param.4) | copy-start | bytes 3145732
  86.6 80.3 %all-to-all-start.1 = ((bf16[16,4,128,256]{3,1,2,0:T(4,128)(2,1)}), bf16[16,4,128,256]{3,1,2,0:T(4,128)(2,1)}, u32[]{:S(2)}, u32[]{:S(2)}) async-start(bf16[16,4,128,256]{3,1,2,0:T(4,128)(2,1)} %copy.88), calls=%async_computation.1 | async-start | bytes 8388608 | tf_op jit(solution)/shard_map/all_to_all | solution.py:238
  96.3 190.0 %reduce-scatter.2.cloned.1.call-start = ((), (), s32[]{:S(2)}) async-start(), calls=%async_computation.3 | async-start | bytes 7520256 | tf_op jit(solution)/shard_map/reduce_scatter | solution.py:270
  99.4 9.6 %collective-permute-start = (bf16[4,128,256]{1,2,0:T(8,128)(2,1)S(1)}, bf16[4,128,256]{1,2,0:T(8,128)(2,1)S(1)}, u32[]{:S(2)}, u32[]{:S(2)}) collective-permute-start(bf16[4,128,256]{1,2,0:T(8,128)(2,1)S(1)} %get-tuple-element.37), channel_id=1, source_target_pairs={{0,16},{16,32},{32,48},{48,64},{64,80},{80,96},{96,112},{1,17},{17... | collective-permute-start | bytes 786440 | tf_op jit(solution)/shard_map/ppermute | solution.py:22
  105.4 8.1 %collective-permute-start.1 = (bf16[4,128,256]{1,2,0:T(8,128)(2,1)S(1)}, bf16[4,128,256]{1,2,0:T(8,128)(2,1)}, u32[]{:S(2)}, u32[]{:S(2)}) collective-permute-start(bf16[4,128,256]{1,2,0:T(8,128)(2,1)S(1)} %get-tuple-element.38), channel_id=1, source_target_pairs={{16,0},{32,16},{48,32},{64,48},{80,64},{96,80},{112,96},{17,1},{33... | collective-permute-start | bytes 786440 | tf_op jit(solution)/shard_map/ppermute | solution.py:24
  167.0 30.9 %copy-start.2 = (f32[13,256,256]{2,1,0:T(8,128)S(1)}, f32[13,256,256]{2,1,0:T(8,128)}, u32[]{:S(2)}) copy-start(f32[13,256,256]{2,1,0:T(8,128)} %get-tuple-element.19) | copy-start | bytes 10223620
  204.7 86.3 %collective-permute-start.3 = (bf16[4,128,256]{2,1,0:T(8,128)(2,1)S(1)}, bf16[4,128,256]{2,1,0:T(8,128)(2,1)S(1)}, u32[]{:S(2)}, u32[]{:S(2)}) collective-permute-start(bf16[4,128,256]{2,1,0:T(8,128)(2,1)S(1)} %get-tuple-element.36), channel_id=1, source_target_pairs={{16,0},{32,16},{48,32},{64,48},{80,64},{96,80},{112,96},{17,1},{33... | collective-permute-start | bytes 786440 | tf_op jit(solution)/shard_map/ppermute | solution.py:24
  286.3 5.3 %collective-permute-start.4 = (f32[27,16,256]{2,1,0:T(8,128)}, f32[27,16,256]{2,1,0:T(8,128)S(1)}, u32[]{:S(2)}, u32[]{:S(2)}) collective-permute-start(f32[27,16,256]{2,1,0:T(8,128)} %reduce-scatter.2.cloned.1.call-done), channel_id=1, source_target_pairs={{0,16},{16,0},{32,48},{48,32},{64,80},{80,64},{96,112},{112,96},{1... | collective-permute-start | bytes 1327112 | tf_op jit(solution)/shard_map/ppermute | solution.py:155
  288.1 6.3 %collective-permute-start.2 = (bf16[4,128,256]{2,1,0:T(8,128)(2,1)S(1)}, bf16[4,128,256]{2,1,0:T(8,128)(2,1)S(1)}, u32[]{:S(2)}, u32[]{:S(2)}) collective-permute-start(bf16[4,128,256]{2,1,0:T(8,128)(2,1)S(1)} %get-tuple-element.35), channel_id=1, source_target_pairs={{0,16},{16,32},{32,48},{48,64},{64,80},{80,96},{96,112},{1,17},{17... | collective-permute-start | bytes 786440 | tf_op jit(solution)/shard_map/ppermute | solution.py:22
  292.7 12.1 %collective-permute-start.5 = (f32[27,16,256]{2,1,0:T(8,128)S(1)}, f32[27,16,256]{2,1,0:T(8,128)S(1)}, u32[]{:S(2)}, u32[]{:S(2)}) collective-permute-start(f32[27,16,256]{2,1,0:T(8,128)S(1)} %add.175), channel_id=1, source_target_pairs={{0,32},{16,48},{32,0},{48,16},{64,96},{80,112},{96,64},{112,80},{1... | collective-permute-start | bytes 1327112 | tf_op jit(solution)/shard_map/ppermute | solution.py:155
  304.8 13.2 %collective-permute-start.6 = (f32[27,16,256]{2,1,0:T(8,128)S(1)}, f32[27,16,256]{2,1,0:T(8,128)S(1)}, u32[]{:S(2)}, u32[]{:S(2)}) collective-permute-start(f32[27,16,256]{2,1,0:T(8,128)S(1)} %add.176), channel_id=1, source_target_pairs={{0,64},{16,80},{32,96},{48,112},{64,0},{80,16},{96,32},{112,48},{1... | collective-permute-start | bytes 1327112 | tf_op jit(solution)/shard_map/ppermute | solution.py:155
Sparse Core Ops, SparseCore 0:
  203.8 82.4 reduce-scatter.1

commit v6 on v5

--- a/solution.py
+++ b/solution.py
@@ -79,73 +79,95 @@
     )(table_index.reshape(-1), grad_blocks, weights)
 
 
-def _forward_kernel(
-    idx_ref, table_ref, tablet_ref, w_ref, grad_ref, acc_in_ref, out_ref, wg_ref, g_ref, gt_ref, acc_ref,
-    *, scale, first,
-):
+def _conv_kernel(idx_ref, table_ref, w_ref, out_ref, g_ref, acc_ref):
     k = pl.program_id(0)
     voxels = table_ref.shape[1]
-    blocks = grad_ref.shape[0] // voxels
+    blocks = out_ref.shape[0] // voxels
     rows = table_ref.shape[0]
     for b in range(blocks):
-        t = jnp.clip(idx_ref[(k + first) * blocks + b], 0, rows - 1)
+        t = jnp.clip(idx_ref[k * blocks + b], 0, rows - 1)
         g_ref[pl.ds(b * voxels, voxels), :] = table_ref[t]
-        gt_ref[:, pl.ds(b * voxels, voxels)] = tablet_ref[t]
     part = jnp.dot(g_ref[...], w_ref[0], preferred_element_type=jnp.float32)
 
     @pl.when(k == 0)
     def _():
-        acc_ref[...] = acc_in_ref[...] + part
+        acc_ref[...] = part
 
     @pl.when(k > 0)
     def _():
         acc_ref[...] += part
 
-    wg_ref[0] = jnp.dot(gt_ref[...], grad_ref[...], preferred_element_type=jnp.float32) * scale
-
     @pl.when(k == pl.num_programs(0) - 1)
     def _():
         out_ref[...] = acc_ref[...].astype(out_ref.dtype)
 
 
-def forward_terms(table_index, table, tablet, weights, grad_rows, acc_in, first, last, out_dtype, scale):
+def conv_rows(table_index, table, weights, count):
     rows, voxels, channels = table.shape
+    offsets = weights.shape[0]
+    return pl.pallas_call(
+        _conv_kernel,
+        out_shape=jax.ShapeDtypeStruct((count, channels), jnp.bfloat16),
+        grid_spec=pltpu.PrefetchScalarGridSpec(
+            num_scalar_prefetch=1,
+            grid=(offsets,),
+            in_specs=[
+                pl.BlockSpec((rows, voxels, channels), lambda k, idx: (0, 0, 0)),
+                pl.BlockSpec((1, channels, channels), lambda k, idx: (k, 0, 0)),
+            ],
+            out_specs=pl.BlockSpec((count, channels), lambda k, idx: (0, 0)),
+            scratch_shapes=[
+                pltpu.VMEM((count, channels), jnp.bfloat16),
+                pltpu.VMEM((count, channels), jnp.float32),
+            ],
+        ),
+        cost_estimate=pl.CostEstimate(
+            flops=2 * offsets * count * channels * channels,
+            transcendentals=0,
+            bytes_accessed=table.size * 2 + weights.size * 2 + count * channels * 2,
+        ),
+        compiler_params=pltpu.CompilerParams(
+            dimension_semantics=("arbitrary",), vmem_limit_bytes=56 * 1024 * 1024
+        ),
+    )(table_index.reshape(-1), table, weights)
+
+
+def _weight_grad_kernel(idx_ref, tablet_ref, grad_ref, wg_ref, gt_ref, *, scale):
+    k = pl.program_id(0)
+    voxels = tablet_ref.shape[2]
+    blocks = grad_ref.shape[0] // voxels
+    rows = tablet_ref.shape[0]
+    for b in range(blocks):
+        t = jnp.clip(idx_ref[k * blocks + b], 0, rows - 1)
+        gt_ref[:, pl.ds(b * voxels, voxels)] = tablet_ref[t]
+    wg_ref[0] = jnp.dot(gt_ref[...], grad_ref[...], preferred_element_type=jnp.float32) * scale
+
+
+def weight_grad_terms(table_index, tablet, grad_rows, offsets, scale):
+    rows, channels, voxels = tablet.shape
     count = grad_rows.shape[0]
     return pl.pallas_call(
-        functools.partial(_forward_kernel, scale=scale, first=first),
-        out_shape=(
-            jax.ShapeDtypeStruct((count, channels), out_dtype),
-            jax.ShapeDtypeStruct((last - first, channels, channels), jnp.float32),
-        ),
+        functools.partial(_weight_grad_kernel, scale=scale),
+        out_shape=jax.ShapeDtypeStruct((offsets, channels, channels), jnp.float32),
         grid_spec=pltpu.PrefetchScalarGridSpec(
             num_scalar_prefetch=1,
-            grid=(last - first,),
+            grid=(offsets,),
             in_specs=[
-                pl.BlockSpec((rows, voxels, channels), lambda k, idx: (0, 0, 0)),
                 pl.BlockSpec((rows, channels, voxels), lambda k, idx: (0, 0, 0)),
-                pl.BlockSpec((1, channels, channels), lambda k, idx: (k + first, 0, 0)),
                 pl.BlockSpec((count, channels), lambda k, idx: (0, 0)),
-                pl.BlockSpec((count, channels), lambda k, idx: (0, 0)),
-            ],
-            out_specs=[
-                pl.BlockSpec((count, channels), lambda k, idx: (0, 0)),
-                pl.BlockSpec((1, channels, channels), lambda k, idx: (k, 0, 0)),
-            ],
-            scratch_shapes=[
-                pltpu.VMEM((count, channels), jnp.bfloat16),
-                pltpu.VMEM((channels, count), jnp.bfloat16),
-                pltpu.VMEM((count, channels), jnp.float32),
-            ],
+            ],
+            out_specs=pl.BlockSpec((1, channels, channels), lambda k, idx: (k, 0, 0)),
+            scratch_shapes=[pltpu.VMEM((channels, count), jnp.bfloat16)],
         ),
         cost_estimate=pl.CostEstimate(
-            flops=4 * (last - first) * count * channels * channels,
+            flops=2 * offsets * count * channels * channels,
             transcendentals=0,
-            bytes_accessed=2 * table.size * 2 + (last - first) * channels * channels * 6 + count * channels * 10,
+            bytes_accessed=tablet.size * 2 + count * channels * 2 + offsets * channels * channels * 4,
         ),
         compiler_params=pltpu.CompilerParams(
             dimension_semantics=("arbitrary",), vmem_limit_bytes=56 * 1024 * 1024
         ),
-    )(table_index.reshape(-1), table, tablet, weights, grad_rows, acc_in)
+    )(table_index.reshape(-1), tablet, grad_rows)
 
 
 def region_sum(value, count):
@@ -257,17 +279,11 @@
     tablet = jnp.swapaxes(table, 1, 2)
     scale = 1.0 / math.sqrt(total_blocks * voxels)
     grad_rows = grad_blocks.reshape(blocks_dev * voxels, channels)
-    half = offsets // 2
-    conv_part, term_a = forward_terms(
-        table_index, table, tablet, weights, grad_rows,
-        jnp.zeros((blocks_dev * voxels, channels), jnp.float32), 0, half, jnp.float32, scale,
-    )
-    returned, conv_part = lax.optimization_barrier((returned, conv_part))
-    conv_out, term_b = forward_terms(
-        table_index, table, tablet, weights, grad_rows, conv_part, half, offsets, jnp.bfloat16, scale,
-    )
-    kernel_term = jnp.concatenate([term_a, term_b], axis=0)
+    kernel_term = weight_grad_terms(table_index, tablet, grad_rows, offsets, scale)
     scattered = lax.psum_scatter(kernel_term, "shard", scatter_dimension=1, tiled=True)
+    kernel_term, table = lax.optimization_barrier((kernel_term, table))
+    conv_out = conv_rows(table_index, table, weights, blocks_dev * voxels)
+    scattered, conv_out = lax.optimization_barrier((scattered, conv_out))
     input_acc = table_grad[:blocks_dev]
     input_acc = input_acc + jnp.einsum(
         "pcj,pcvd->jvd",

time: 327 us -> 303 us (0.927)
  Pallas kernels: 87.4 us -> 72.9 us
  local copies, waits for them, and re-layouts: 41.4 us -> 32.7 us
  other arithmetic: 23.9 us -> 17.3 us
    pallas_call x2, Pallas kernels: 60.1 us -> 45.6 us  [the longest x1 25.5 us: conv_rows(): pl.pallas_call(_conv_kernel, out_shape=jax.ShapeDtypeStruct((count, chann...]
    concatenate x2 -> x1, local copies, waits for them, and re-layouts: 9.12 us -> 0.62 us  [body(): jnp.concatenate([own_blocks, incoming.reshape(n_shard * capacity, voxels,...]
    transpose x0 -> x1, local copies, waits for them, and re-layouts: none -> 8.45 us  [body(): tablet = jnp.swapaxes(table, 1, 2)]
    optimization_barrier x1 -> x0, local copies, waits for them, and re-layouts: 6.4 us -> none  [body(): lax.optimization_barrier((incoming, rims, table_grad))]
    reduce_scatter x1, waiting for transfers between devices: 79.6 us -> 85.6 us  [body(): lax.psum_scatter(kernel_term, 'shard', scatter_dimension=1, tiled=True)]
    concatenate x1 -> x0, other arithmetic: 5.72 us -> none  [body(): kernel_term = jnp.concatenate([term_a, term_b], axis=0)]
    ppermute x2, waiting for transfers between devices: 4.44 us -> 0.01 us  [padded(): lax.ppermute(head, axis, [((i + 1) % count, i) for i in range(ends)])]
  transfers between devices with their start and end apart: 10 -> 10, of which waited for: 6 -> 5; matrix products, arithmetic and copies ran while one was open for 17% -> 11% of each run, Pallas kernels for 17% -> 18%
where the time goes in v6:
time: 303 us; the launch traced here: 302 us
  waiting for transfers between devices  115 us (38%)
  Pallas kernels  72.9 us (24%)
  starting transfers between devices  38.6 us (13%)
  local copies, waits for them, and re-layouts  32.7 us (11%)
  other arithmetic  17.3 us (6%)
  between operations  14.3 us (5%)
  matrix products  10.8 us (4%)
    reduce_scatter x1, waiting for transfers between devices, body(): lax.psum_scatter(kernel_term, 'shard', scatter_dimension=1, tiled=True)  85.6 us
    pallas_call x1, Pallas kernels, table_grad_sums(): pl.pallas_call(_table_grad_kernel, out_shape=jax.ShapeDtypeStruct((rows,...  27.2 us
    pallas_call x1, Pallas kernels, conv_rows(): pl.pallas_call(_conv_kernel, out_shape=jax.ShapeDtypeStruct((count, chann...  25.5 us
    all_to_all x1, waiting for transfers between devices, body(): lax.all_to_all(outgoing, 'shard', split_axis=0, concat_axis=0, tiled=True)  21 us
    pallas_call x1, Pallas kernels, weight_grad_terms(): pl.pallas_call(functools.partial(_weight_grad_kernel, scale=scale), out_s...  20.1 us
    all_to_all x1, starting transfers between devices, body(): lax.all_to_all(remote_sums[:n_shard * capacity].reshape(n_shard, capacity...  10.5 us
    unnamed x10, local copies, waits for them, and re-layouts  9.49 us
    all_to_all x1, starting transfers between devices, body(): lax.all_to_all(outgoing, 'shard', split_axis=0, concat_axis=0, tiled=True)  8.79 us
  transfers between devices with their start and end apart: 10, of which 5 were waited for; matrix products, arithmetic and copies ran while one was open for 11% of the time, Pallas kernels for 18%

profile of v6, /device:TPU:1, one launch (start us, length us, event | category | flops | bytes accessed | tf_op | source)
XLA Modules:
  0.0 301.5 jit_solution(15702179424076869162)
XLA Ops:
  10.1 2.9 convolution_convert_fusion
  13.0 3.5 %copy.73 = bf16[16,4,128,256]{3,2,1,0:T(8,128)(2,1)} copy(bf16[16,4,128,256]{3,0,2,1:T(8,128)(2,1)S(1)} %convolution_convert_fusion) | data formatting | bytes 8388608 | tf_op jit(solution)/shard_map/convert_element_type | solution.py:222
  16.6 8.8 %all-to-all-start = ((bf16[16,4,128,256]{3,2,1,0:T(8,128)(2,1)}), bf16[16,4,128,256]{3,2,1,0:T(8,128)(2,1)}, u32[]{:S(2)}, u32[]{:S(2)}) async-start(bf16[16,4,128,256]{3,2,1,0:T(8,128)(2,1)} %copy.73), calls=%async_computation | async-start | bytes 8388608 | tf_op jit(solution)/shard_map/all_to_all | solution.py:229
  28.0 4.0 %collective-permute-start = (bf16[4,128,256]{2,1,0:T(8,128)(2,1)S(1)}, bf16[4,128,256]{2,1,0:T(8,128)(2,1)S(1)}, u32[]{:S(2)}, u32[]{:S(2)}) collective-permute-start(bf16[4,128,256]{2,1,0:T(8,128)(2,1)S(1)} %get-tuple-element.31), channel_id=1, source_target_pairs={{0,16},{16,32},{32,48},{48,64},{64,80},{80,96},{96,112},{1,17},{17... | collective-permute-start | bytes 786440 | tf_op jit(solution)/shard_map/ppermute | solution.py:22
  32.0 2.1 collective-permute-start.1
  37.0 27.2 %shard_map.67 = f32[89,128,256]{2,1,0:T(8,128)} custom-call(s32[432]{0:T(512)} %reshape.251.idx_ref, bf16[16,128,256]{2,1,0:T(8,128)(2,1)} %bitcast.45, bf16[27,256,256]{2,1,0:T(8,128)(2,1)} %w_ref.3), custom_call_target="tpu_custom_call" | custom-call | flops 7247757312 | bytes 16252928 | tf_op jit(solution)/shard_map/pallas_call | solution.py:59
  65.4 21.0 %all-to-all-done = bf16[16,4,128,256]{3,2,1,0:T(8,128)(2,1)} async-done(((bf16[16,4,128,256]{3,2,1,0:T(8,128)(2,1)}), bf16[16,4,128,256]{3,2,1,0:T(8,128)(2,1)}, u32[]{:S(2)}, u32[]{:S(2)}) %all-to-all-start) | async-done | bytes 4194336 | tf_op jit(solution)/shard_map/all_to_all | solution.py:229
  86.4 4.7 %constant_dynamic-update-slice_fusion = bf16[89,128,256]{2,1,0:T(8,128)(2,1)} fusion(bf16[89,128,256]{2,1,0:T(8,128)(2,1)} %constant_dynamic-update-slice_fusion.1, bf16[64,128,256]{2,1,0:T(8,128)(2,1)} %bitcast.10), kind=kLoop, calls=%fused_computation.42 | loop fusion | bytes 8388608
  93.2 8.4 %copy.80.tablet_ref = bf16[89,256,128]{2,1,0:T(8,128)(2,1)} copy(bf16[89,256,128]{1,2,0:T(8,128)(2,1)} %bitcast.42) | data formatting | bytes 11665408 | tf_op jit(solution)/shard_map/transpose | solution.py:279
  101.7 20.1 %shard_map.68 = f32[27,256,256]{2,1,0:T(8,128)} custom-call(s32[432]{0:T(512)} %reshape.251.idx_ref, bf16[89,256,128]{2,1,0:T(8,128)(2,1)} %copy.80.tablet_ref, bf16[2048,256]{1,0:T(8,128)(2,1)} %grad_ref.1), custom_call_target="tpu_custom_call" | custom-call | flops 7247757312 | bytes 13959168 | tf_op jit(solution)/shard_map/pallas_call | solution.py:149
  121.8 5.2 %convert.7 = bf16[89,128,256]{2,1,0:T(8,128)(2,1)S(1)} convert(f32[89,128,256]{2,1,0:T(8,128)} %shard_map.67) | non-fusion elementwise | flops 2916352 | bytes 17498112 | tf_op jit(solution)/shard_map/convert.4
  127.3 2.3 copy-done
  129.6 5.5 %copy.81 = bf16[16,4,128,256]{3,1,2,0:T(4,128)(2,1)} copy(bf16[16,4,128,256]{3,2,1,0:T(8,128)(2,1)S(1)} %bitcast.38) | data formatting | bytes 8388608 | tf_op jit(solution)/shard_map/reshape | solution.py:261
  135.1 10.5 %all-to-all-start.1 = ((bf16[16,4,128,256]{3,1,2,0:T(4,128)(2,1)}), bf16[16,4,128,256]{3,1,2,0:T(4,128)(2,1)}, u32[]{:S(2)}, u32[]{:S(2)}) async-start(bf16[16,4,128,256]{3,1,2,0:T(4,128)(2,1)} %copy.81), calls=%async_computation.2 | async-start | bytes 8388608 | tf_op jit(solution)/shard_map/all_to_all | solution.py:260
  146.7 4.4 %collective-permute-start.3 = (bf16[4,128,256]{2,1,0:T(8,128)(2,1)S(1)}, bf16[4,128,256]{2,1,0:T(8,128)(2,1)S(1)}, u32[]{:S(2)}, u32[]{:S(2)}) collective-permute-start(bf16[4,128,256]{2,1,0:T(8,128)(2,1)S(1)} %get-tuple-element.30), channel_id=1, source_target_pairs={{16,0},{32,16},{48,32},{64,48},{80,64},{96,80},{112,96},{17,1},{33... | collective-permute-start | bytes 786440 | tf_op jit(solution)/shard_map/ppermute | solution.py:24
  151.1 25.5 %shard_map.69 = bf16[2048,256]{1,0:T(8,128)(2,1)} custom-call(s32[432]{0:T(512)} %reshape.251.idx_ref, bf16[89,128,256]{2,1,0:T(8,128)(2,1)} %broadcast_dynamic-update-slice_fusion.table_ref, bf16[27,256,256]{2,1,0:T(8,128)(2,1)} %w_ref.3), custom_call_target="tpu_custom_call" | custom-call | flops 7247757312 | bytes 10420224 | tf_op jit(solution)/shard_map/pallas_call | solution.py:108
  176.6 85.6 %reduce-scatter.2.cloned.1.call-done = f32[27,16,256]{2,1,0:T(8,128)} async-done(((f32[27,256,256]{2,1,0:T(8,128)}), f32[27,16,256]{2,1,0:T(8,128)}) %reduce-scatter.2.cloned.1.call-update) | async-done | bytes 442384 | tf_op jit(solution)/shard_map/reduce_scatter | solution.py:283
  264.0 3.0 collective-permute-start.2
  270.3 1.9 fusion.13
  272.2 4.7 %fusion.3 = f32[16,128,256]{2,0,1:T(8,128)S(1)} fusion(bf16[16,4,128,256]{3,1,2,0:T(4,128)(2,1)} %all-to-all-done.1, s32[16,16]{0,1:T(8,128)S(1)} %copy.70, pred[16,16]{0,1:T(8,128)(4,1)S(1)} %copy.69), kind=kOutput, calls=%fused_computation.8 | convolution fusion | flops 67110912 | bytes 6292736 | tf_op jit(solution)/shard_map/pcj,pcvd->jvd/dot_general | solution.py:288
  276.9 3.9 %collective-permute-done.5 = f32[27,16,256]{2,1,0:T(8,128)S(1)} collective-permute-done((f32[27,16,256]{2,1,0:T(8,128)S(1)}, f32[27,16,256]{2,1,0:T(8,128)S(1)}, u32[]{:S(2)}, u32[]{:S(2)}) %collective-permute-start.5) | collective-permute-done | bytes 442400 | tf_op jit(solution)/shard_map/ppermute | solution.py:177
  280.9 2.6 collective-permute-start.6
  283.5 6.1 %fusion.2 = bf16[16,128,256]{2,1,0:T(8,128)(2,1)} fusion(f32[16,128,256]{2,0,1:T(8,128)S(1)} %fusion.11, f32[16,128,256]{2,0,1:T(8,128)S(1)} %copy-done.2, f32[16,128,256]{2,0,1:T(8,128)S(1)} %fusion.3, f32[89,128,256]{2,1,0:T(8,128)} %shard_map.67), kind=kLoop, calls=%fused_computation.4 | loop fusion | flops 2097152 | bytes 9437184 | tf_op jit(solution)/shard_map/convert_element_type | solution.py:307
  289.6 4.3 %collective-permute-done.6 = f32[27,16,256]{2,1,0:T(8,128)S(1)} collective-permute-done((f32[27,16,256]{2,1,0:T(8,128)S(1)}, f32[27,16,256]{2,1,0:T(8,128)S(1)}, u32[]{:S(2)}, u32[]{:S(2)}) %collective-permute-start.6) | collective-permute-done | bytes 442400 | tf_op jit(solution)/shard_map/ppermute | solution.py:177
  (78 shorter events, 18.9 us)
Async XLA Ops:
  16.5 10.6 %copy-start.1 = (bf16[2048,256]{1,0:T(8,128)(2,1)S(1)}, bf16[2048,256]{1,0:T(8,128)(2,1)}, u32[]{:S(2)}) copy-start(bf16[2048,256]{1,0:T(8,128)(2,1)} %param.4) | copy-start | bytes 3145732
  16.6 69.9 %all-to-all-start = ((bf16[16,4,128,256]{3,2,1,0:T(8,128)(2,1)}), bf16[16,4,128,256]{3,2,1,0:T(8,128)(2,1)}, u32[]{:S(2)}, u32[]{:S(2)}) async-start(bf16[16,4,128,256]{3,2,1,0:T(8,128)(2,1)} %copy.73), calls=%async_computation | async-start | bytes 8388608 | tf_op jit(solution)/shard_map/all_to_all | solution.py:229
  25.3 236.9 %reduce-scatter.2.cloned.1.call-start = ((), (), s32[]{:S(2)}) async-start(), calls=%async_computation.3 | async-start | bytes 7520256 | tf_op jit(solution)/shard_map/reduce_scatter | solution.py:283
  28.0 37.3 %collective-permute-start = (bf16[4,128,256]{2,1,0:T(8,128)(2,1)S(1)}, bf16[4,128,256]{2,1,0:T(8,128)(2,1)S(1)}, u32[]{:S(2)}, u32[]{:S(2)}) collective-permute-start(bf16[4,128,256]{2,1,0:T(8,128)(2,1)S(1)} %get-tuple-element.31), channel_id=1, source_target_pairs={{0,16},{16,32},{32,48},{48,64},{64,80},{80,96},{96,112},{1,17},{17... | collective-permute-start | bytes 786440 | tf_op jit(solution)/shard_map/ppermute | solution.py:22
  32.0 33.3 %collective-permute-start.1 = (bf16[4,128,256]{2,1,0:T(8,128)(2,1)S(1)}, bf16[4,128,256]{2,1,0:T(8,128)(2,1)S(1)}, u32[]{:S(2)}, u32[]{:S(2)}) collective-permute-start(bf16[4,128,256]{2,1,0:T(8,128)(2,1)S(1)} %get-tuple-element.32), channel_id=1, source_target_pairs={{16,0},{32,16},{48,32},{64,48},{80,64},{96,80},{112,96},{17,1},{33... | collective-permute-start | bytes 786440 | tf_op jit(solution)/shard_map/ppermute | solution.py:24
  127.0 2.6 copy-start
  135.1 137.1 %all-to-all-start.1 = ((bf16[16,4,128,256]{3,1,2,0:T(4,128)(2,1)}), bf16[16,4,128,256]{3,1,2,0:T(4,128)(2,1)}, u32[]{:S(2)}, u32[]{:S(2)}) async-start(bf16[16,4,128,256]{3,1,2,0:T(4,128)(2,1)} %copy.81), calls=%async_computation.2 | async-start | bytes 8388608 | tf_op jit(solution)/shard_map/all_to_all | solution.py:260
  146.7 120.3 %collective-permute-start.3 = (bf16[4,128,256]{2,1,0:T(8,128)(2,1)S(1)}, bf16[4,128,256]{2,1,0:T(8,128)(2,1)S(1)}, u32[]{:S(2)}, u32[]{:S(2)}) collective-permute-start(bf16[4,128,256]{2,1,0:T(8,128)(2,1)S(1)} %get-tuple-element.30), channel_id=1, source_target_pairs={{16,0},{32,16},{48,32},{64,48},{80,64},{96,80},{112,96},{17,1},{33... | collective-permute-start | bytes 786440 | tf_op jit(solution)/shard_map/ppermute | solution.py:24
  262.2 5.3 %collective-permute-start.4 = (f32[27,16,256]{2,1,0:T(8,128)}, f32[27,16,256]{2,1,0:T(8,128)S(1)}, u32[]{:S(2)}, u32[]{:S(2)}) collective-permute-start(f32[27,16,256]{2,1,0:T(8,128)} %reduce-scatter.2.cloned.1.call-done), channel_id=1, source_target_pairs={{0,16},{16,0},{32,48},{48,32},{64,80},{80,64},{96,112},{112,96},{1... | collective-permute-start | bytes 1327112 | tf_op jit(solution)/shard_map/ppermute | solution.py:177
  264.0 6.3 %collective-permute-start.2 = (bf16[4,128,256]{2,1,0:T(8,128)(2,1)S(1)}, bf16[4,128,256]{2,1,0:T(8,128)(2,1)S(1)}, u32[]{:S(2)}, u32[]{:S(2)}) collective-permute-start(bf16[4,128,256]{2,1,0:T(8,128)(2,1)S(1)} %get-tuple-element.29), channel_id=1, source_target_pairs={{0,16},{16,32},{32,48},{48,64},{64,80},{80,96},{96,112},{1,17},{17... | collective-permute-start | bytes 786440 | tf_op jit(solution)/shard_map/ppermute | solution.py:22
  268.6 12.2 %collective-permute-start.5 = (f32[27,16,256]{2,1,0:T(8,128)S(1)}, f32[27,16,256]{2,1,0:T(8,128)S(1)}, u32[]{:S(2)}, u32[]{:S(2)}) collective-permute-start(f32[27,16,256]{2,1,0:T(8,128)S(1)} %add.175), channel_id=1, source_target_pairs={{0,32},{16,48},{32,0},{48,16},{64,96},{80,112},{96,64},{112,80},{1... | collective-permute-start | bytes 1327112 | tf_op jit(solution)/shard_map/ppermute | solution.py:177
  272.2 11.3 %copy-start.2 = (f32[16,128,256]{2,0,1:T(8,128)S(1)}, f32[16,128,256]{2,0,1:T(8,128)}, u32[]{:S(2)}) copy-start(f32[16,128,256]{2,0,1:T(8,128)} %fusion.13) | copy-start | bytes 6291460
  280.9 12.9 %collective-permute-start.6 = (f32[27,16,256]{2,1,0:T(8,128)S(1)}, f32[27,16,256]{2,1,0:T(8,128)S(1)}, u32[]{:S(2)}, u32[]{:S(2)}) collective-permute-start(f32[27,16,256]{2,1,0:T(8,128)S(1)} %add.176), channel_id=1, source_target_pairs={{0,64},{16,80},{32,96},{48,112},{64,0},{80,16},{96,32},{112,48},{1... | collective-permute-start | bytes 1327112 | tf_op jit(solution)/shard_map/ppermute | solution.py:177
Sparse Core Ops, SparseCore 0:
  121.9 140.2 reduce-scatter.1

commit v7 on v6

--- a/solution.py
+++ b/solution.py
@@ -168,6 +168,31 @@
             dimension_semantics=("arbitrary",), vmem_limit_bytes=56 * 1024 * 1024
         ),
     )(table_index.reshape(-1), tablet, grad_rows)
+
+
+def weight_grad_sum(term, n_shard, n_region):
+    offsets, channels, width = term.shape
+    sub = channels // (n_shard * 2)
+    core = lax.axis_index("region") % 2
+    view = term.reshape(offsets, n_shard, 2, sub, width)
+    mine = lax.dynamic_index_in_dim(view, core, 2, keepdims=False)
+    theirs = lax.dynamic_index_in_dim(view, 1 - core, 2, keepdims=False)
+    swap = [(i, i ^ 1) for i in range(n_region)]
+    pair = jnp.swapaxes(mine + lax.ppermute(theirs, "region", swap), 0, 1)
+    return lax.psum_scatter(pair, "shard", scatter_dimension=0, tiled=True)[0]
+
+
+def weight_grad_finish(part, n_region):
+    core = lax.axis_index("region") % 2
+    swap = [(i, i ^ 1) for i in range(n_region)]
+    step = 2
+    while step < n_region:
+        part = part + lax.ppermute(part, "region", [(i, i ^ step) for i in range(n_region)])
+        step *= 2
+    other = lax.ppermute(part, "region", swap)
+    low = jnp.where(core == 0, part, other)
+    high = jnp.where(core == 0, other, part)
+    return jnp.concatenate([low, high], axis=1)
 
 
 def region_sum(value, count):
@@ -280,7 +305,7 @@
     scale = 1.0 / math.sqrt(total_blocks * voxels)
     grad_rows = grad_blocks.reshape(blocks_dev * voxels, channels)
     kernel_term = weight_grad_terms(table_index, tablet, grad_rows, offsets, scale)
-    scattered = lax.psum_scatter(kernel_term, "shard", scatter_dimension=1, tiled=True)
+    scattered = weight_grad_sum(kernel_term, n_shard, n_region)
     kernel_term, table = lax.optimization_barrier((kernel_term, table))
     conv_out = conv_rows(table_index, table, weights, blocks_dev * voxels)
     scattered, conv_out = lax.optimization_barrier((scattered, conv_out))
@@ -305,7 +330,7 @@
         precision=lax.Precision.HIGHEST,
     )
     in_grad = input_acc.reshape(blocks_dev * voxels, channels).astype(jnp.bfloat16)
-    weight_grad = region_sum(scattered, n_region)
+    weight_grad = weight_grad_finish(scattered, n_region)
     return (conv_out, in_grad, weight_grad)
 
 

time: 303 us -> 301 us (level)
  waiting for transfers between devices: 115 us -> 104 us
  local copies, waits for them, and re-layouts: 32.7 us -> 36.2 us
    reduce_scatter x1 -> x0, waiting for transfers between devices: 85.6 us -> none  [body(): lax.psum_scatter(kernel_term, 'shard', scatter_dimension=1, tiled=True)]
    unnamed x1 -> x2, waiting for transfers between devices: 0.02 us -> 72.9 us
    ppermute x3 -> x4, starting transfers between devices: 5.79 us -> 10.8 us  [the longest x1 4.09 us: weight_grad_finish(): other = lax.ppermute(part, 'region', swap)]
    dynamic_slice x0 -> x2, local copies, waits for them, and re-layouts: none -> 3.77 us  [the longest x1 3.54 us: weight_grad_sum(): mine = lax.dynamic_index_in_dim(view, core, 2, keepdims=False)]
    ppermute x3 -> x4, waiting for transfers between devices: 8.17 us -> 7.73 us  [the longest x1 5.85 us: weight_grad_sum(): pair = jnp.swapaxes(mine + lax.ppermute(theirs, 'region', swap), 0, 1)]
  transfers between devices with their start and end apart: 10 -> 11, of which waited for: 5 -> 5; matrix products, arithmetic and copies ran while one was open for 11% -> 11% of each run, Pallas kernels for 18% -> 18%
where the time goes in v7:
time: 301 us; the launch traced here: 299 us
  waiting for transfers between devices  104 us (35%)
  Pallas kernels  72.8 us (24%)
  starting transfers between devices  41.3 us (14%)
  local copies, waits for them, and re-layouts  36.2 us (12%)
  other arithmetic  19.6 us (7%)
  between operations  14.3 us (5%)
  matrix products  10.8 us (4%)
    unnamed x2, waiting for transfers between devices  72.9 us
    pallas_call x1, Pallas kernels, table_grad_sums(): pl.pallas_call(_table_grad_kernel, out_shape=jax.ShapeDtypeStruct((rows,...  27.3 us
    pallas_call x1, Pallas kernels, conv_rows(): pl.pallas_call(_conv_kernel, out_shape=jax.ShapeDtypeStruct((count, chann...  25.4 us
    all_to_all x1, waiting for transfers between devices, body(): lax.all_to_all(outgoing, 'shard', split_axis=0, concat_axis=0, tiled=True)  21.2 us
    pallas_call x1, Pallas kernels, weight_grad_terms(): pl.pallas_call(functools.partial(_weight_grad_kernel, scale=scale), out_s...  20.1 us
    all_to_all x1, starting transfers between devices, body(): lax.all_to_all(remote_sums[:n_shard * capacity].reshape(n_shard, capacity...  10.2 us
    unnamed x10, local copies, waits for them, and re-layouts  9.32 us
    all_to_all x1, starting transfers between devices, body(): lax.all_to_all(outgoing, 'shard', split_axis=0, concat_axis=0, tiled=True)  8.78 us
  transfers between devices with their start and end apart: 11, of which 5 were waited for; matrix products, arithmetic and copies ran while one was open for 11% of the time, Pallas kernels for 18%

profile of v7, /device:TPU:1, one launch (start us, length us, event | category | flops | bytes accessed | tf_op | source)
XLA Modules:
  0.0 299.3 jit_solution(10495274432127569415)
XLA Ops:
  10.1 2.9 convolution_convert_fusion
  13.0 3.5 %copy.79 = bf16[16,4,128,256]{3,2,1,0:T(8,128)(2,1)} copy(bf16[16,4,128,256]{3,0,2,1:T(8,128)(2,1)S(1)} %convolution_convert_fusion) | data formatting | bytes 8388608 | tf_op jit(solution)/shard_map/convert_element_type | solution.py:247
  16.5 8.8 %all-to-all-start = ((bf16[16,4,128,256]{3,2,1,0:T(8,128)(2,1)}), bf16[16,4,128,256]{3,2,1,0:T(8,128)(2,1)}, u32[]{:S(2)}, u32[]{:S(2)}) async-start(bf16[16,4,128,256]{3,2,1,0:T(8,128)(2,1)} %copy.79), calls=%async_computation | async-start | bytes 8388608 | tf_op jit(solution)/shard_map/all_to_all | solution.py:254
  28.0 4.0 %collective-permute-start = (bf16[4,128,256]{2,1,0:T(8,128)(2,1)S(1)}, bf16[4,128,256]{2,1,0:T(8,128)(2,1)S(1)}, u32[]{:S(2)}, u32[]{:S(2)}) collective-permute-start(bf16[4,128,256]{2,1,0:T(8,128)(2,1)S(1)} %get-tuple-element.33), channel_id=1, source_target_pairs={{0,16},{16,32},{32,48},{48,64},{64,80},{80,96},{96,112},{1,17},{17... | collective-permute-start | bytes 786440 | tf_op jit(solution)/shard_map/ppermute | solution.py:22
  36.8 27.3 %shard_map.67 = f32[89,128,256]{2,1,0:T(8,128)} custom-call(s32[432]{0:T(512)} %reshape.254.idx_ref, bf16[16,128,256]{2,1,0:T(8,128)(2,1)} %bitcast.61, bf16[27,256,256]{2,1,0:T(8,128)(2,1)} %w_ref.3), custom_call_target="tpu_custom_call" | custom-call | flops 7247757312 | bytes 16252928 | tf_op jit(solution)/shard_map/pallas_call | solution.py:59
  65.3 21.2 %all-to-all-done = bf16[16,4,128,256]{3,2,1,0:T(8,128)(2,1)} async-done(((bf16[16,4,128,256]{3,2,1,0:T(8,128)(2,1)}), bf16[16,4,128,256]{3,2,1,0:T(8,128)(2,1)}, u32[]{:S(2)}, u32[]{:S(2)}) %all-to-all-start) | async-done | bytes 4194336 | tf_op jit(solution)/shard_map/all_to_all | solution.py:254
  86.4 4.6 %constant_dynamic-update-slice_fusion = bf16[89,128,256]{2,1,0:T(8,128)(2,1)} fusion(bf16[89,128,256]{2,1,0:T(8,128)(2,1)} %constant_dynamic-update-slice_fusion.1, bf16[64,128,256]{2,1,0:T(8,128)(2,1)} %bitcast.10), kind=kLoop, calls=%fused_computation.48 | loop fusion | bytes 8388608
  93.1 8.4 %copy.86.tablet_ref = bf16[89,256,128]{2,1,0:T(8,128)(2,1)} copy(bf16[89,256,128]{1,2,0:T(8,128)(2,1)} %bitcast.54) | data formatting | bytes 11665408 | tf_op jit(solution)/shard_map/transpose | solution.py:304
  101.5 20.1 %shard_map.68 = f32[27,256,256]{2,1,0:T(8,128)} custom-call(s32[432]{0:T(512)} %reshape.254.idx_ref, bf16[89,256,128]{2,1,0:T(8,128)(2,1)} %copy.86.tablet_ref, bf16[2048,256]{1,0:T(8,128)(2,1)} %grad_ref.1), custom_call_target="tpu_custom_call" | custom-call | flops 7247757312 | bytes 13959168 | tf_op jit(solution)/shard_map/pallas_call | solution.py:149
  121.7 3.5 %constant_dynamic-slice_fusion.1 = (f32[27,16,1,8,256]{4,3,2,1,0:T(8,128)S(1)}, f32[27,16,1,8,256]{4,3,2,1,0:T(8,128)S(1)}) fusion(f32[27,16,2,8,256]{4,3,2,1,0:T(8,128)} %bitcast.55, s32[]{:T(128)S(6)} %select_n.71, s32[]{:T(128)S(6)} %select_n.72), kind=kLoop, calls=%fused_computation.69 | loop fusion | bytes 14155784 | tf_op jit(solution)/shard_map/jit(dynamic_index_in_dim)/dynamic_slice | solution.py:178
  125.5 2.8 collective-permute-start.2
  128.2 5.8 %collective-permute-done.2 = f32[27,16,8,256]{3,2,0,1:T(8,128)S(1)} collective-permute-done((f32[27,16,8,256]{3,2,0,1:T(8,128)S(1)}, f32[27,16,8,256]{3,2,0,1:T(8,128)S(1)}, u32[]{:S(2)}, u32[]{:S(2)}) %collective-permute-start.2) | collective-permute-done | bytes 3538976 | tf_op jit(solution)/shard_map/ppermute | solution.py:181
  136.6 5.2 %convert.7 = bf16[89,128,256]{2,1,0:T(8,128)(2,1)S(1)} convert(f32[89,128,256]{2,1,0:T(8,128)} %shard_map.67) | non-fusion elementwise | flops 2916352 | bytes 17498112 | tf_op jit(solution)/shard_map/convert.4
  144.2 5.5 %copy.89 = bf16[16,4,128,256]{3,1,2,0:T(4,128)(2,1)} copy(bf16[16,4,128,256]{3,2,1,0:T(8,128)(2,1)S(1)} %bitcast.50) | data formatting | bytes 8388608 | tf_op jit(solution)/shard_map/reshape | solution.py:286
  149.7 10.2 %all-to-all-start.1 = ((bf16[16,4,128,256]{3,1,2,0:T(4,128)(2,1)}), bf16[16,4,128,256]{3,1,2,0:T(4,128)(2,1)}, u32[]{:S(2)}, u32[]{:S(2)}) async-start(bf16[16,4,128,256]{3,1,2,0:T(4,128)(2,1)} %copy.89), calls=%async_computation.1 | async-start | bytes 8388608 | tf_op jit(solution)/shard_map/all_to_all | solution.py:285
  160.9 2.6 collective-permute-start.4
  163.5 3.1 %collective-permute-start.3 = (bf16[4,128,256]{2,1,0:T(8,128)(2,1)S(1)}, bf16[4,128,256]{2,1,0:T(8,128)(2,1)S(1)}, u32[]{:S(2)}, u32[]{:S(2)}) collective-permute-start(bf16[4,128,256]{2,1,0:T(8,128)(2,1)S(1)} %get-tuple-element.31), channel_id=1, source_target_pairs={{0,16},{16,32},{32,48},{48,64},{64,80},{80,96},{96,112},{1,17},{17... | collective-permute-start | bytes 786440 | tf_op jit(solution)/shard_map/ppermute | solution.py:22
  166.6 2.5 collective-permute-done.4
  169.7 25.4 %shard_map.69 = bf16[2048,256]{1,0:T(8,128)(2,1)} custom-call(s32[432]{0:T(512)} %reshape.254.idx_ref, bf16[89,128,256]{2,1,0:T(8,128)(2,1)} %broadcast_dynamic-update-slice_fusion.table_ref, bf16[27,256,256]{2,1,0:T(8,128)(2,1)} %w_ref.3), custom_call_target="tpu_custom_call" | custom-call | flops 7247757312 | bytes 10420224 | tf_op jit(solution)/shard_map/pallas_call | solution.py:108
  195.0 72.8 %reduce-scatter.4.cloned.1.call-done = f32[1,27,8,256]{3,2,1,0:T(8,128)} async-done(((f32[16,27,8,256]{3,2,1,0:T(8,128)}), f32[1,27,8,256]{3,2,1,0:T(8,128)}) %reduce-scatter.4.cloned.1.call-update) | async-done | bytes 221200
  273.9 2.8 collective-permute-start.6
  276.6 4.7 %fusion.4 = f32[16,128,256]{2,0,1:T(8,128)S(1)} fusion(bf16[16,4,128,256]{3,1,2,0:T(4,128)(2,1)} %all-to-all-done.1, s32[16,16]{0,1:T(8,128)S(1)} %copy.76, pred[16,16]{0,1:T(8,128)(4,1)S(1)} %copy.75), kind=kOutput, calls=%fused_computation.11 | convolution fusion | flops 67110912 | bytes 6292736 | tf_op jit(solution)/shard_map/pcj,pcvd->jvd/dot_general | solution.py:313
  281.4 4.1 %collective-permute-start.7 = (f32[27,8,256]{2,1,0:T(8,128)S(1)}, f32[27,8,256]{2,1,0:T(8,128)S(1)}, u32[]{:S(2)}, u32[]{:S(2)}) collective-permute-start(f32[27,8,256]{2,1,0:T(8,128)S(1)} %add.193), channel_id=1, source_target_pairs={{0,16},{16,0},{32,48},{48,32},{64,80},{80,64},{96,112},{112,96},{1... | collective-permute-start | bytes 663560 | tf_op jit(solution)/shard_map/ppermute | solution.py:192
  285.5 6.1 %fusion.3 = bf16[16,128,256]{2,1,0:T(8,128)(2,1)} fusion(f32[16,128,256]{2,0,1:T(8,128)S(1)} %fusion.12, f32[16,128,256]{2,0,1:T(8,128)S(1)} %copy-done.2, f32[16,128,256]{2,0,1:T(8,128)S(1)} %fusion.4, f32[89,128,256]{2,1,0:T(8,128)} %shard_map.67), kind=kLoop, calls=%fused_computation.7 | loop fusion | flops 2097152 | bytes 9437184 | tf_op jit(solution)/shard_map/convert_element_type | solution.py:332
  (84 shorter events, 27.1 us)
Async XLA Ops:
  16.5 10.6 %copy-start.1 = (bf16[2048,256]{1,0:T(8,128)(2,1)S(1)}, bf16[2048,256]{1,0:T(8,128)(2,1)}, u32[]{:S(2)}) copy-start(bf16[2048,256]{1,0:T(8,128)(2,1)} %param.4) | copy-start | bytes 3145732
  16.5 69.9 %all-to-all-start = ((bf16[16,4,128,256]{3,2,1,0:T(8,128)(2,1)}), bf16[16,4,128,256]{3,2,1,0:T(8,128)(2,1)}, u32[]{:S(2)}, u32[]{:S(2)}) async-start(bf16[16,4,128,256]{3,2,1,0:T(8,128)(2,1)} %copy.79), calls=%async_computation | async-start | bytes 8388608 | tf_op jit(solution)/shard_map/all_to_all | solution.py:254
  25.3 242.6 %reduce-scatter.4.cloned.1.call-start = ((), (), s32[]{:S(2)}) async-start(), calls=%async_computation.3 | async-start | bytes 3760128
  28.0 37.2 %collective-permute-start = (bf16[4,128,256]{2,1,0:T(8,128)(2,1)S(1)}, bf16[4,128,256]{2,1,0:T(8,128)(2,1)S(1)}, u32[]{:S(2)}, u32[]{:S(2)}) collective-permute-start(bf16[4,128,256]{2,1,0:T(8,128)(2,1)S(1)} %get-tuple-element.33), channel_id=1, source_target_pairs={{0,16},{16,32},{32,48},{48,64},{64,80},{80,96},{96,112},{1,17},{17... | collective-permute-start | bytes 786440 | tf_op jit(solution)/shard_map/ppermute | solution.py:22
  31.9 33.2 %collective-permute-start.1 = (bf16[4,128,256]{2,1,0:T(8,128)(2,1)S(1)}, bf16[4,128,256]{2,1,0:T(8,128)(2,1)S(1)}, u32[]{:S(2)}, u32[]{:S(2)}) collective-permute-start(bf16[4,128,256]{2,1,0:T(8,128)(2,1)S(1)} %get-tuple-element.34), channel_id=1, source_target_pairs={{16,0},{32,16},{48,32},{64,48},{80,64},{96,80},{112,96},{17,1},{33... | collective-permute-start | bytes 786440 | tf_op jit(solution)/shard_map/ppermute | solution.py:24
  125.5 8.6 %collective-permute-start.2 = (f32[27,16,8,256]{3,2,0,1:T(8,128)S(1)}, f32[27,16,8,256]{3,2,0,1:T(8,128)S(1)}, u32[]{:S(2)}, u32[]{:S(2)}) collective-permute-start(f32[27,16,8,256]{3,2,0,1:T(8,128)S(1)} %bitcast.56), channel_id=1, source_target_pairs={{0,16},{16,0},{32,48},{48,32},{64,80},{80,64},{96,112},{112,96},{1... | collective-permute-start | bytes 10616840 | tf_op jit(solution)/shard_map/ppermute | solution.py:181
  141.8 2.5 copy-start
  149.7 126.9 %all-to-all-start.1 = ((bf16[16,4,128,256]{3,1,2,0:T(4,128)(2,1)}), bf16[16,4,128,256]{3,1,2,0:T(4,128)(2,1)}, u32[]{:S(2)}, u32[]{:S(2)}) async-start(bf16[16,4,128,256]{3,1,2,0:T(4,128)(2,1)} %copy.89), calls=%async_computation.1 | async-start | bytes 8388608 | tf_op jit(solution)/shard_map/all_to_all | solution.py:285
  160.9 8.2 %collective-permute-start.4 = (bf16[4,128,256]{2,1,0:T(8,128)(2,1)S(1)}, bf16[4,128,256]{2,1,0:T(8,128)(2,1)S(1)}, u32[]{:S(2)}, u32[]{:S(2)}) collective-permute-start(bf16[4,128,256]{2,1,0:T(8,128)(2,1)S(1)} %get-tuple-element.32), channel_id=1, source_target_pairs={{16,0},{32,16},{48,32},{64,48},{80,64},{96,80},{112,96},{17,1},{33... | collective-permute-start | bytes 786440 | tf_op jit(solution)/shard_map/ppermute | solution.py:24
  163.5 105.6 %collective-permute-start.3 = (bf16[4,128,256]{2,1,0:T(8,128)(2,1)S(1)}, bf16[4,128,256]{2,1,0:T(8,128)(2,1)S(1)}, u32[]{:S(2)}, u32[]{:S(2)}) collective-permute-start(bf16[4,128,256]{2,1,0:T(8,128)(2,1)S(1)} %get-tuple-element.31), channel_id=1, source_target_pairs={{0,16},{16,32},{32,48},{48,64},{64,80},{80,96},{96,112},{1,17},{17... | collective-permute-start | bytes 786440 | tf_op jit(solution)/shard_map/ppermute | solution.py:22
  267.9 5.0 %collective-permute-start.5 = (f32[27,8,256]{2,1,0:T(8,128)}, f32[27,8,256]{2,1,0:T(8,128)S(1)}, u32[]{:S(2)}, u32[]{:S(2)}) collective-permute-start(f32[27,8,256]{2,1,0:T(8,128)} %bitcast.59), channel_id=1, source_target_pairs={{0,32},{16,48},{32,0},{48,16},{64,96},{80,112},{96,64},{112,80},{1... | collective-permute-start | bytes 663560 | tf_op jit(solution)/shard_map/ppermute | solution.py:190
  273.9 7.5 %collective-permute-start.6 = (f32[27,8,256]{2,1,0:T(8,128)S(1)}, f32[27,8,256]{2,1,0:T(8,128)S(1)}, u32[]{:S(2)}, u32[]{:S(2)}) collective-permute-start(f32[27,8,256]{2,1,0:T(8,128)S(1)} %add.192), channel_id=1, source_target_pairs={{0,64},{16,80},{32,96},{48,112},{64,0},{80,16},{96,32},{112,48},{1... | collective-permute-start | bytes 663560 | tf_op jit(solution)/shard_map/ppermute | solution.py:190
  276.6 8.8 %copy-start.2 = (f32[16,128,256]{2,0,1:T(8,128)S(1)}, f32[16,128,256]{2,0,1:T(8,128)}, u32[]{:S(2)}) copy-start(f32[16,128,256]{2,0,1:T(8,128)} %fusion.14) | copy-start | bytes 6291460
  281.4 10.2 %collective-permute-start.7 = (f32[27,8,256]{2,1,0:T(8,128)S(1)}, f32[27,8,256]{2,1,0:T(8,128)S(1)}, u32[]{:S(2)}, u32[]{:S(2)}) collective-permute-start(f32[27,8,256]{2,1,0:T(8,128)S(1)} %add.193), channel_id=1, source_target_pairs={{0,16},{16,0},{32,48},{48,32},{64,80},{80,64},{96,112},{112,96},{1... | collective-permute-start | bytes 663560 | tf_op jit(solution)/shard_map/ppermute | solution.py:192
Sparse Core Ops, SparseCore 0:
  136.7 131.1 reduce-scatter.3

commit v8 on v7

--- a/solution.py
+++ b/solution.py
@@ -178,8 +178,22 @@
     mine = lax.dynamic_index_in_dim(view, core, 2, keepdims=False)
     theirs = lax.dynamic_index_in_dim(view, 1 - core, 2, keepdims=False)
     swap = [(i, i ^ 1) for i in range(n_region)]
-    pair = jnp.swapaxes(mine + lax.ppermute(theirs, "region", swap), 0, 1)
-    return lax.psum_scatter(pair, "shard", scatter_dimension=0, tiled=True)[0]
+    pair = mine + lax.ppermute(theirs, "region", swap)
+    shard = lax.axis_index("shard")
+    bits = n_shard.bit_length() - 1
+    pair = pair.reshape((offsets,) + (2,) * bits + (sub, width))
+    order = [0, 2, 1, 3] if bits == 4 else list(range(bits))
+    remaining = list(range(bits - 1, -1, -1))
+    for bit in order:
+        mask = 1 << bit
+        axis = 1 + remaining.index(bit)
+        remaining.remove(bit)
+        mine_bit = (shard // mask) % 2
+        keep = lax.dynamic_index_in_dim(pair, mine_bit, axis, keepdims=False)
+        send = lax.dynamic_index_in_dim(pair, 1 - mine_bit, axis, keepdims=False)
+        got = lax.ppermute(send, "shard", [(i, i ^ mask) for i in range(n_shard)])
+        pair = keep + got
+    return pair.reshape(offsets, sub, width)
 
 
 def weight_grad_finish(part, n_region):

time: 301 us -> 307 us (1.020)
  starting transfers between devices: 41.3 us -> 56.3 us
  between operations: 14.3 us -> 1.12 us
  waiting for transfers between devices: 104 us -> 99.8 us
  other arithmetic: 19.6 us -> 23.1 us
  local copies, waits for them, and re-layouts: 36.2 us -> 39.3 us
    unnamed x2 -> x0, waiting for transfers between devices: 72.9 us -> none
    ppermute x1 -> x5, waiting for transfers between devices: 5.85 us -> 77.1 us  [the longest x4 71.1 us: weight_grad_sum(): got = lax.ppermute(send, 'shard', [(i, i ^ mask) for i in range(n_shard)])]
    add x0 -> x5, other arithmetic: none -> 6.9 us  [the longest x1 3.58 us: weight_grad_sum(): pair = mine + lax.ppermute(theirs, 'region', swap)]
    ppermute x2, starting transfers between devices: 4.49 us -> 11 us  [padded(): lax.ppermute(head, axis, [((i + 1) % count, i) for i in range(ends)])]
    ppermute x1 -> x5, starting transfers between devices: 2.76 us -> 7.93 us  [the longest x4 5.45 us: weight_grad_sum(): got = lax.ppermute(send, 'shard', [(i, i ^ mask) for i in range(n_shard)])]
    squeeze x0 -> x5, local copies, waits for them, and re-layouts: none -> 4.7 us  [the longest x4 2.41 us: weight_grad_sum(): send = lax.dynamic_index_in_dim(pair, 1 - mine_bit, axis, keepdims=False)]
    dynamic_slice x2 -> x0, local copies, waits for them, and re-layouts: 3.77 us -> none  [the longest x1 3.54 us: weight_grad_sum(): mine = lax.dynamic_index_in_dim(view, core, 2, keepdims=False)]
    unnamed x10 -> x16, local copies, waits for them, and re-layouts: 9.32 us -> 10.7 us
  transfers between devices with their start and end apart: 11 -> 14, of which waited for: 5 -> 7; matrix products, arithmetic and copies ran while one was open for 11% -> 13% of each run, Pallas kernels for 18% -> 17%
where the time goes in v8:
time: 307 us; the launch traced here: 305 us
  waiting for transfers between devices  99.8 us (33%)
  Pallas kernels  72.8 us (24%)
  starting transfers between devices  56.3 us (18%)
  local copies, waits for them, and re-layouts  39.3 us (13%)
  other arithmetic  23.1 us (8%)
  matrix products  12.7 us (4%)
    ppermute x4, waiting for transfers between devices, weight_grad_sum(): got = lax.ppermute(send, 'shard', [(i, i ^ mask) for i in range(n_shard)])  71.1 us
    pallas_call x1, Pallas kernels, table_grad_sums(): pl.pallas_call(_table_grad_kernel, out_shape=jax.ShapeDtypeStruct((rows,...  27.3 us
    pallas_call x1, Pallas kernels, conv_rows(): pl.pallas_call(_conv_kernel, out_shape=jax.ShapeDtypeStruct((count, chann...  25.4 us
    all_to_all x1, waiting for transfers between devices, body(): lax.all_to_all(outgoing, 'shard', split_axis=0, concat_axis=0, tiled=True)  21.6 us
    pallas_call x1, Pallas kernels, weight_grad_terms(): pl.pallas_call(functools.partial(_weight_grad_kernel, scale=scale), out_s...  20.2 us
    all_to_all x1, starting transfers between devices, body(): lax.all_to_all(remote_sums[:n_shard * capacity].reshape(n_shard, capacity...  11.1 us
    ppermute x2, starting transfers between devices, padded(): lax.ppermute(head, axis, [((i + 1) % count, i) for i in range(ends)])  11 us
    unnamed x16, local copies, waits for them, and re-layouts  10.7 us
  transfers between devices with their start and end apart: 14, of which 7 were waited for; matrix products, arithmetic and copies ran while one was open for 13% of the time, Pallas kernels for 17%

profile of v8, /device:TPU:1, one launch (start us, length us, event | category | flops | bytes accessed | tf_op | source)
XLA Modules:
  0.0 305.1 jit_solution(11602393927539811730)
XLA Ops:
  3.6 2.9 convolution_convert_fusion
  6.5 3.5 %copy.109 = bf16[16,4,128,256]{3,2,1,0:T(8,128)(2,1)} copy(bf16[16,4,128,256]{3,0,2,1:T(8,128)(2,1)S(1)} %convolution_convert_fusion) | data formatting | bytes 8388608 | tf_op jit(solution)/shard_map/convert_element_type | solution.py:261
  10.0 8.8 %all-to-all-start = ((bf16[16,4,128,256]{3,2,1,0:T(8,128)(2,1)}), bf16[16,4,128,256]{3,2,1,0:T(8,128)(2,1)}, u32[]{:S(2)}, u32[]{:S(2)}) async-start(bf16[16,4,128,256]{3,2,1,0:T(8,128)(2,1)} %copy.109), calls=%async_computation | async-start | bytes 8388608 | tf_op jit(solution)/shard_map/all_to_all | solution.py:268
  21.4 4.0 %collective-permute-start = (bf16[4,128,256]{2,1,0:T(8,128)(2,1)S(1)}, bf16[4,128,256]{2,1,0:T(8,128)(2,1)S(1)}, u32[]{:S(2)}, u32[]{:S(2)}) collective-permute-start(bf16[4,128,256]{2,1,0:T(8,128)(2,1)S(1)} %get-tuple-element.31), channel_id=1, source_target_pairs={{0,16},{16,32},{32,48},{48,64},{64,80},{80,96},{96,112},{1,17},{17... | collective-permute-start | bytes 786440 | tf_op jit(solution)/shard_map/ppermute | solution.py:22
  30.2 27.3 %shard_map.67 = f32[89,128,256]{2,1,0:T(8,128)} custom-call(s32[432]{0:T(512)} %reshape.257.idx_ref, bf16[16,128,256]{2,1,0:T(8,128)(2,1)} %bitcast.71, bf16[27,256,256]{2,1,0:T(8,128)(2,1)} %w_ref.3), custom_call_target="tpu_custom_call" | custom-call | flops 7247757312 | bytes 16252928 | tf_op jit(solution)/shard_map/pallas_call | solution.py:59
  58.7 21.6 %all-to-all-done = bf16[16,4,128,256]{3,2,1,0:T(8,128)(2,1)} async-done(((bf16[16,4,128,256]{3,2,1,0:T(8,128)(2,1)}), bf16[16,4,128,256]{3,2,1,0:T(8,128)(2,1)}, u32[]{:S(2)}, u32[]{:S(2)}) %all-to-all-start) | async-done | bytes 4194336 | tf_op jit(solution)/shard_map/all_to_all | solution.py:268
  80.3 4.6 %constant_dynamic-update-slice_fusion = bf16[89,128,256]{2,1,0:T(8,128)(2,1)} fusion(bf16[89,128,256]{2,1,0:T(8,128)(2,1)} %constant_dynamic-update-slice_fusion.1, bf16[64,128,256]{2,1,0:T(8,128)(2,1)} %bitcast.10), kind=kLoop, calls=%fused_computation.55 | loop fusion | bytes 8388608
  87.0 8.5 %copy.116.tablet_ref = bf16[89,256,128]{2,1,0:T(8,128)(2,1)} copy(bf16[89,256,128]{1,2,0:T(8,128)(2,1)} %bitcast.66) | data formatting | bytes 11665408 | tf_op jit(solution)/shard_map/transpose | solution.py:318
  95.5 20.2 %shard_map.68 = f32[27,256,256]{2,1,0:T(8,128)} custom-call(s32[432]{0:T(512)} %reshape.257.idx_ref, bf16[89,256,128]{2,1,0:T(8,128)(2,1)} %copy.116.tablet_ref, bf16[2048,256]{1,0:T(8,128)(2,1)} %grad_ref.1), custom_call_target="tpu_custom_call" | custom-call | flops 7247757312 | bytes 13959168 | tf_op jit(solution)/shard_map/pallas_call | solution.py:149
  120.4 6.0 %collective-permute-done.2 = f32[27,16,8,256]{3,2,1,0:T(8,128)} collective-permute-done((f32[27,16,8,256]{3,2,1,0:T(8,128)S(1)}, f32[27,16,8,256]{3,2,1,0:T(8,128)}, u32[]{:S(2)}, u32[]{:S(2)}) %collective-permute-start.2) | collective-permute-done | bytes 3538976 | tf_op jit(solution)/shard_map/ppermute | solution.py:181
  126.4 3.6 %bitcast_add_fusion = f32[27,16,8,256]{3,2,1,0:T(8,128)S(1)} fusion(f32[27,16,8,256]{3,2,1,0:T(8,128)} %collective-permute-done.2, f32[27,16,2,8,256]{4,3,2,1,0:T(8,128)} %bitcast.68, s32[]{:T(128)S(6)} %select_n.126), kind=kLoop, calls=%fused_computation.2 | loop fusion | flops 884736 | bytes 10616836 | tf_op jit(solution)/shard_map/add | solution.py:181
  131.5 5.2 %convert.7 = bf16[89,128,256]{2,1,0:T(8,128)(2,1)S(1)} convert(f32[89,128,256]{2,1,0:T(8,128)} %shard_map.67) | non-fusion elementwise | flops 2916352 | bytes 17498112 | tf_op jit(solution)/shard_map/convert.4
  139.3 5.5 %copy.117 = bf16[16,4,128,256]{3,1,2,0:T(4,128)(2,1)} copy(bf16[16,4,128,256]{3,2,1,0:T(8,128)(2,1)S(1)} %bitcast.60) | data formatting | bytes 8388608 | tf_op jit(solution)/shard_map/reshape | solution.py:300
  144.8 11.1 %all-to-all-start.1 = ((bf16[16,4,128,256]{3,1,2,0:T(4,128)(2,1)}), bf16[16,4,128,256]{3,1,2,0:T(4,128)(2,1)}, u32[]{:S(2)}, u32[]{:S(2)}) async-start(bf16[16,4,128,256]{3,1,2,0:T(4,128)(2,1)} %copy.117), calls=%async_computation.1 | async-start | bytes 8388608 | tf_op jit(solution)/shard_map/all_to_all | solution.py:299
  155.9 39.6 %collective-permute-done.3 = f32[27,2,2,2,8,256]{5,4,3,2,1,0:T(8,128)} collective-permute-done((f32[27,2,2,2,8,256]{5,4,3,2,1,0:T(8,128)}, f32[27,2,2,2,8,256]{5,4,3,2,1,0:T(8,128)}, u32[]{:S(2)}, u32[]{:S(2)}) %collective-permute-start.3) | collective-permute-done | bytes 1769504 | tf_op jit(solution)/shard_map/ppermute | solution.py:194
  200.6 9.1 %collective-permute-start.8 = (bf16[4,128,256]{2,1,0:T(8,128)(2,1)S(1)}, bf16[4,128,256]{2,1,0:T(8,128)(2,1)}, u32[]{:S(2)}, u32[]{:S(2)}) collective-permute-start(bf16[4,128,256]{2,1,0:T(8,128)(2,1)S(1)} %get-tuple-element.30), channel_id=1, source_target_pairs={{16,0},{32,16},{48,32},{64,48},{80,64},{96,80},{112,96},{17,1},{33... | collective-permute-start | bytes 786440 | tf_op jit(solution)/shard_map/ppermute | solution.py:24
  209.7 25.8 %collective-permute-done.4 = f32[27,2,2,8,256]{4,3,2,1,0:T(8,128)S(1)} collective-permute-done((f32[27,2,2,8,256]{4,3,2,1,0:T(8,128)S(1)}, f32[27,2,2,8,256]{4,3,2,1,0:T(8,128)S(1)}, u32[]{:S(2)}, u32[]{:S(2)}) %collective-permute-start.4) | collective-permute-done | bytes 884768 | tf_op jit(solution)/shard_map/ppermute | solution.py:194
  237.6 4.6 %collective-permute-start.7 = (bf16[4,128,256]{2,1,0:T(8,128)(2,1)}, bf16[4,128,256]{2,1,0:T(8,128)(2,1)}, u32[]{:S(2)}, u32[]{:S(2)}) collective-permute-start(bf16[4,128,256]{2,1,0:T(8,128)(2,1)} %get-tuple-element.29), channel_id=1, source_target_pairs={{0,16},{16,32},{32,48},{48,64},{64,80},{80,96},{96,112},{1,17},{17... | collective-permute-start | bytes 786440 | tf_op jit(solution)/shard_map/ppermute | solution.py:22
  243.8 5.7 %collective-permute-done.5 = f32[27,2,8,256]{3,2,1,0:T(8,128)S(1)} collective-permute-done((f32[27,2,8,256]{3,2,1,0:T(8,128)}, f32[27,2,8,256]{3,2,1,0:T(8,128)S(1)}, u32[]{:S(2)}, u32[]{:S(2)}) %collective-permute-start.5) | collective-permute-done | bytes 442400 | tf_op jit(solution)/shard_map/ppermute | solution.py:194
  249.6 5.4 %collective-permute-start.6 = (f32[27,8,256]{2,1,0:T(8,128)S(1)}, f32[27,8,256]{2,1,0:T(8,128)S(1)}, u32[]{:S(2)}, u32[]{:S(2)}) collective-permute-start(f32[27,8,256]{2,1,0:T(8,128)S(1)} %dynamic-slice_bitcast_fusion.4), channel_id=1, source_target_pairs={{0,8},{1,9},{2,10},{3,11},{4,12},{5,13},{6,14},{7,15},{8,0},{9,1},... | collective-permute-start | bytes 663560 | tf_op jit(solution)/shard_map/ppermute | solution.py:194
  255.0 25.4 %shard_map.69 = bf16[2048,256]{1,0:T(8,128)(2,1)} custom-call(s32[432]{0:T(512)} %reshape.257.idx_ref, bf16[89,128,256]{2,1,0:T(8,128)(2,1)} %broadcast_dynamic-update-slice_fusion.table_ref, bf16[27,256,256]{2,1,0:T(8,128)(2,1)} %w_ref.3), custom_call_target="tpu_custom_call" | custom-call | flops 7247757312 | bytes 10420224 | tf_op jit(solution)/shard_map/pallas_call | solution.py:108
  288.2 4.7 %fusion.3 = f32[16,128,256]{2,0,1:T(8,128)S(1)} fusion(bf16[16,4,128,256]{3,1,2,0:T(4,128)(2,1)} %all-to-all-done.1, s32[16,16]{0,1:T(8,128)S(1)} %copy.106, pred[16,16]{0,1:T(8,128)(4,1)S(1)} %copy.105), kind=kOutput, calls=%fused_computation.12 | convolution fusion | flops 67110912 | bytes 6292736 | tf_op jit(solution)/shard_map/pcj,pcvd->jvd/dot_general | solution.py:327
  293.4 4.7 %collective-permute-start.11 = (f32[27,8,256]{2,1,0:T(8,128)S(1)}, f32[27,8,256]{2,1,0:T(8,128)S(1)}, u32[]{:S(2)}, u32[]{:S(2)}) collective-permute-start(f32[27,8,256]{2,1,0:T(8,128)S(1)} %add.267), channel_id=1, source_target_pairs={{0,16},{16,0},{32,48},{48,32},{64,80},{80,64},{96,112},{112,96},{1... | collective-permute-start | bytes 663560 | tf_op jit(solution)/shard_map/ppermute | solution.py:206
  298.1 6.1 %fusion.2 = bf16[16,128,256]{2,1,0:T(8,128)(2,1)} fusion(f32[16,128,256]{2,0,1:T(8,128)S(1)} %fusion.11, f32[16,128,256]{2,0,1:T(8,128)S(1)} %copy-done.2, f32[16,128,256]{2,0,1:T(8,128)S(1)} %fusion.3, f32[89,128,256]{2,1,0:T(8,128)} %shard_map.67), kind=kLoop, calls=%fused_computation.6 | loop fusion | flops 2097152 | bytes 9437184 | tf_op jit(solution)/shard_map/convert_element_type | solution.py:346
  (102 shorter events, 40.2 us)
Async XLA Ops:
  10.0 10.6 %copy-start.1 = (bf16[2048,256]{1,0:T(8,128)(2,1)S(1)}, bf16[2048,256]{1,0:T(8,128)(2,1)}, u32[]{:S(2)}) copy-start(bf16[2048,256]{1,0:T(8,128)(2,1)} %param.4) | copy-start | bytes 3145732
  10.0 70.3 %all-to-all-start = ((bf16[16,4,128,256]{3,2,1,0:T(8,128)(2,1)}), bf16[16,4,128,256]{3,2,1,0:T(8,128)(2,1)}, u32[]{:S(2)}, u32[]{:S(2)}) async-start(bf16[16,4,128,256]{3,2,1,0:T(8,128)(2,1)} %copy.109), calls=%async_computation | async-start | bytes 8388608 | tf_op jit(solution)/shard_map/all_to_all | solution.py:268
  20.5 4.8 %copy-start.4 = (pred[4,16]{1,0:T(4,128)(4,1)}, pred[4,16]{1,0:T(4,128)(4,1)S(1)}, u32[]{:S(2)}) copy-start(pred[4,16]{1,0:T(4,128)(4,1)S(1)} %fusion.29) | copy-start | bytes 196
  21.4 37.2 %collective-permute-start = (bf16[4,128,256]{2,1,0:T(8,128)(2,1)S(1)}, bf16[4,128,256]{2,1,0:T(8,128)(2,1)S(1)}, u32[]{:S(2)}, u32[]{:S(2)}) collective-permute-start(bf16[4,128,256]{2,1,0:T(8,128)(2,1)S(1)} %get-tuple-element.31), channel_id=1, source_target_pairs={{0,16},{16,32},{32,48},{48,64},{64,80},{80,96},{96,112},{1,17},{17... | collective-permute-start | bytes 786440 | tf_op jit(solution)/shard_map/ppermute | solution.py:22
  25.4 33.2 %collective-permute-start.1 = (bf16[4,128,256]{2,1,0:T(8,128)(2,1)S(1)}, bf16[4,128,256]{2,1,0:T(8,128)(2,1)S(1)}, u32[]{:S(2)}, u32[]{:S(2)}) collective-permute-start(bf16[4,128,256]{2,1,0:T(8,128)(2,1)S(1)} %get-tuple-element.32), channel_id=1, source_target_pairs={{16,0},{32,16},{48,32},{64,48},{80,64},{96,80},{112,96},{17,1},{33... | collective-permute-start | bytes 786440 | tf_op jit(solution)/shard_map/ppermute | solution.py:24
  118.0 8.5 %collective-permute-start.2 = (f32[27,16,8,256]{3,2,1,0:T(8,128)S(1)}, f32[27,16,8,256]{3,2,1,0:T(8,128)}, u32[]{:S(2)}, u32[]{:S(2)}) collective-permute-start(f32[27,16,8,256]{3,2,1,0:T(8,128)S(1)} %dynamic-slice_bitcast_fusion), channel_id=1, source_target_pairs={{0,16},{16,0},{32,48},{48,32},{64,80},{80,64},{96,112},{112,96},{1... | collective-permute-start | bytes 10616840 | tf_op jit(solution)/shard_map/ppermute | solution.py:181
  131.5 64.0 %collective-permute-start.3 = (f32[27,2,2,2,8,256]{5,4,3,2,1,0:T(8,128)}, f32[27,2,2,2,8,256]{5,4,3,2,1,0:T(8,128)}, u32[]{:S(2)}, u32[]{:S(2)}) collective-permute-start(f32[27,2,2,2,8,256]{5,4,3,2,1,0:T(8,128)} %dynamic-slice_bitcast_fusion.1), channel_id=1, source_target_pairs={{0,1},{1,0},{2,3},{3,2},{4,5},{5,4},{6,7},{7,6},{8,9},{9,8},{10,11... | collective-permute-start | bytes 5308424 | tf_op jit(solution)/shard_map/ppermute | solution.py:194
  136.7 2.6 copy-start
  144.8 143.4 %all-to-all-start.1 = ((bf16[16,4,128,256]{3,1,2,0:T(4,128)(2,1)}), bf16[16,4,128,256]{3,1,2,0:T(4,128)(2,1)}, u32[]{:S(2)}, u32[]{:S(2)}) async-start(bf16[16,4,128,256]{3,1,2,0:T(4,128)(2,1)} %copy.117), calls=%async_computation.1 | async-start | bytes 8388608 | tf_op jit(solution)/shard_map/all_to_all | solution.py:299
  197.4 1.2 copy-start.3
  198.6 43.7 %copy-start.5 = (pred[4,16]{1,0:T(4,128)(4,1)S(1)}, pred[4,16]{1,0:T(4,128)(4,1)}, u32[]{:S(2)}) copy-start(pred[4,16]{1,0:T(4,128)(4,1)} %copy-done.4) | copy-start | bytes 196
  198.7 36.8 %collective-permute-start.4 = (f32[27,2,2,8,256]{4,3,2,1,0:T(8,128)S(1)}, f32[27,2,2,8,256]{4,3,2,1,0:T(8,128)S(1)}, u32[]{:S(2)}, u32[]{:S(2)}) collective-permute-start(f32[27,2,2,8,256]{4,3,2,1,0:T(8,128)S(1)} %dynamic-slice_bitcast_fusion.2), channel_id=1, source_target_pairs={{0,4},{1,5},{2,6},{3,7},{4,0},{5,1},{6,2},{7,3},{8,12},{9,13},{10,... | collective-permute-start | bytes 2654216 | tf_op jit(solution)/shard_map/ppermute | solution.py:194
  200.6 41.7 %collective-permute-start.8 = (bf16[4,128,256]{2,1,0:T(8,128)(2,1)S(1)}, bf16[4,128,256]{2,1,0:T(8,128)(2,1)}, u32[]{:S(2)}, u32[]{:S(2)}) collective-permute-start(bf16[4,128,256]{2,1,0:T(8,128)(2,1)S(1)} %get-tuple-element.30), channel_id=1, source_target_pairs={{16,0},{32,16},{48,32},{64,48},{80,64},{96,80},{112,96},{17,1},{33... | collective-permute-start | bytes 786440 | tf_op jit(solution)/shard_map/ppermute | solution.py:24
  237.6 11.9 %collective-permute-start.5 = (f32[27,2,8,256]{3,2,1,0:T(8,128)}, f32[27,2,8,256]{3,2,1,0:T(8,128)S(1)}, u32[]{:S(2)}, u32[]{:S(2)}) collective-permute-start(f32[27,2,8,256]{3,2,1,0:T(8,128)} %dynamic-slice_bitcast_fusion.3), channel_id=1, source_target_pairs={{0,2},{1,3},{2,0},{3,1},{4,6},{5,7},{6,4},{7,5},{8,10},{9,11},{10,... | collective-permute-start | bytes 1327112 | tf_op jit(solution)/shard_map/ppermute | solution.py:194
  237.6 44.1 %collective-permute-start.7 = (bf16[4,128,256]{2,1,0:T(8,128)(2,1)}, bf16[4,128,256]{2,1,0:T(8,128)(2,1)}, u32[]{:S(2)}, u32[]{:S(2)}) collective-permute-start(bf16[4,128,256]{2,1,0:T(8,128)(2,1)} %get-tuple-element.29), channel_id=1, source_target_pairs={{0,16},{16,32},{32,48},{48,64},{64,80},{80,96},{96,112},{1,17},{17... | collective-permute-start | bytes 786440 | tf_op jit(solution)/shard_map/ppermute | solution.py:22
  249.6 30.7 %collective-permute-start.6 = (f32[27,8,256]{2,1,0:T(8,128)S(1)}, f32[27,8,256]{2,1,0:T(8,128)S(1)}, u32[]{:S(2)}, u32[]{:S(2)}) collective-permute-start(f32[27,8,256]{2,1,0:T(8,128)S(1)} %dynamic-slice_bitcast_fusion.4), channel_id=1, source_target_pairs={{0,8},{1,9},{2,10},{3,11},{4,12},{5,13},{6,14},{7,15},{8,0},{9,1},... | collective-permute-start | bytes 663560 | tf_op jit(solution)/shard_map/ppermute | solution.py:194
  280.4 4.9 %collective-permute-start.9 = (f32[27,8,256]{2,1,0:T(8,128)S(1)}, f32[27,8,256]{2,1,0:T(8,128)S(1)}, u32[]{:S(2)}, u32[]{:S(2)}) collective-permute-start(f32[27,8,256]{2,1,0:T(8,128)S(1)} %bitcast_add_fusion.4), channel_id=1, source_target_pairs={{0,32},{16,48},{32,0},{48,16},{64,96},{80,112},{96,64},{112,80},{1... | collective-permute-start | bytes 663560 | tf_op jit(solution)/shard_map/ppermute | solution.py:204
  285.3 8.1 %collective-permute-start.10 = (f32[27,8,256]{2,1,0:T(8,128)S(1)}, f32[27,8,256]{2,1,0:T(8,128)S(1)}, u32[]{:S(2)}, u32[]{:S(2)}) collective-permute-start(f32[27,8,256]{2,1,0:T(8,128)S(1)} %add.266), channel_id=1, source_target_pairs={{0,64},{16,80},{32,96},{48,112},{64,0},{80,16},{96,32},{112,48},{1... | collective-permute-start | bytes 663560 | tf_op jit(solution)/shard_map/ppermute | solution.py:204
  288.2 9.9 %copy-start.2 = (f32[16,128,256]{2,0,1:T(8,128)S(1)}, f32[16,128,256]{2,0,1:T(8,128)}, u32[]{:S(2)}) copy-start(f32[16,128,256]{2,0,1:T(8,128)} %fusion.13) | copy-start | bytes 6291460
  293.4 10.9 %collective-permute-start.11 = (f32[27,8,256]{2,1,0:T(8,128)S(1)}, f32[27,8,256]{2,1,0:T(8,128)S(1)}, u32[]{:S(2)}, u32[]{:S(2)}) collective-permute-start(f32[27,8,256]{2,1,0:T(8,128)S(1)} %add.267), channel_id=1, source_target_pairs={{0,16},{16,0},{32,48},{48,32},{64,80},{80,64},{96,112},{112,96},{1... | collective-permute-start | bytes 663560 | tf_op jit(solution)/shard_map/ppermute | solution.py:206

commit v9 on v7

--- a/solution.py
+++ b/solution.py
@@ -305,6 +305,7 @@
     scale = 1.0 / math.sqrt(total_blocks * voxels)
     grad_rows = grad_blocks.reshape(blocks_dev * voxels, channels)
     kernel_term = weight_grad_terms(table_index, tablet, grad_rows, offsets, scale)
+    kernel_term, returned = lax.optimization_barrier((kernel_term, returned))
     scattered = weight_grad_sum(kernel_term, n_shard, n_region)
     kernel_term, table = lax.optimization_barrier((kernel_term, table))
     conv_out = conv_rows(table_index, table, weights, blocks_dev * voxels)

time: 301 us -> 271 us (0.900)
  waiting for transfers between devices: 104 us -> 72.4 us
    unnamed x2, waiting for transfers between devices: 72.9 us -> 38 us
    ppermute x2, waiting for transfers between devices: 2.51 us -> 6.9 us  [padded(): lax.ppermute(head, axis, [((i + 1) % count, i) for i in range(ends)])]
    unnamed x10 -> x8, local copies, waits for them, and re-layouts: 9.32 us -> 9.48 us
  transfers between devices with their start and end apart: 11 -> 11, of which waited for: 5 -> 7; matrix products, arithmetic and copies ran while one was open for 11% -> 17% of each run, Pallas kernels for 18% -> 27%
where the time goes in v9:
time: 271 us; the launch traced here: 269 us
  Pallas kernels  72.8 us (27%)
  waiting for transfers between devices  72.4 us (27%)
  starting transfers between devices  44.1 us (16%)
  local copies, waits for them, and re-layouts  36.4 us (13%)
  other arithmetic  19.6 us (7%)
  between operations  14.3 us (5%)
  matrix products  9.19 us (3%)
    unnamed x2, waiting for transfers between devices  38 us
    pallas_call x1, Pallas kernels, table_grad_sums(): pl.pallas_call(_table_grad_kernel, out_shape=jax.ShapeDtypeStruct((rows,...  27.3 us
    pallas_call x1, Pallas kernels, conv_rows(): pl.pallas_call(_conv_kernel, out_shape=jax.ShapeDtypeStruct((count, chann...  25.5 us
    pallas_call x1, Pallas kernels, weight_grad_terms(): pl.pallas_call(functools.partial(_weight_grad_kernel, scale=scale), out_s...  20.1 us
    all_to_all x1, waiting for transfers between devices, body(): lax.all_to_all(outgoing, 'shard', split_axis=0, concat_axis=0, tiled=True)  18.2 us
    ppermute x2, starting transfers between devices, padded(): lax.ppermute(tail, axis, [(i, (i + 1) % count) for i in range(ends)])  9.83 us
    all_to_all x1, starting transfers between devices, body(): lax.all_to_all(remote_sums[:n_shard * capacity].reshape(n_shard, capacity...  9.63 us
    unnamed x8, local copies, waits for them, and re-layouts  9.48 us
  transfers between devices with their start and end apart: 11, of which 7 were waited for; matrix products, arithmetic and copies ran while one was open for 17% of the time, Pallas kernels for 27%

profile of v9, /device:TPU:1, one launch (start us, length us, event | category | flops | bytes accessed | tf_op | source)
XLA Modules:
  0.0 268.9 jit_solution(1173678152184430745)
XLA Ops:
  10.1 2.9 %convolution_convert_fusion = bf16[16,4,128,256]{3,0,2,1:T(8,128)(2,1)S(1)} fusion(bf16[16,128,256]{2,1,0:T(8,128)(2,1)} %bitcast.51, s32[16,16]{0,1:T(8,128)S(1)} %copy.76, pred[16,16]{0,1:T(8,128)(4,1)S(1)} %copy.75), kind=kOutput, calls=%fused_computation.5 | convolution fusion | flops 69208064 | bytes 5244160 | tf_op jit(solution)/shard_map/pcj,jvd->pcvd/dot_general | solution.py:245
  13.0 3.5 %copy.79 = bf16[16,4,128,256]{3,2,1,0:T(8,128)(2,1)} copy(bf16[16,4,128,256]{3,0,2,1:T(8,128)(2,1)S(1)} %convolution_convert_fusion) | data formatting | bytes 8388608 | tf_op jit(solution)/shard_map/convert_element_type | solution.py:247
  16.5 8.6 %all-to-all-start = ((bf16[16,4,128,256]{3,2,1,0:T(8,128)(2,1)}), bf16[16,4,128,256]{3,2,1,0:T(8,128)(2,1)}, u32[]{:S(2)}, u32[]{:S(2)}) async-start(bf16[16,4,128,256]{3,2,1,0:T(8,128)(2,1)} %copy.79), calls=%async_computation | async-start | bytes 8388608 | tf_op jit(solution)/shard_map/all_to_all | solution.py:254
  28.1 27.3 %shard_map.67 = f32[89,128,256]{2,1,0:T(8,128)} custom-call(s32[432]{0:T(512)} %reshape.254.idx_ref, bf16[16,128,256]{2,1,0:T(8,128)(2,1)} %bitcast.60, bf16[27,256,256]{2,1,0:T(8,128)(2,1)} %w_ref.3), custom_call_target="tpu_custom_call" | custom-call | flops 7247757312 | bytes 16252928 | tf_op jit(solution)/shard_map/pallas_call | solution.py:59
  55.4 5.2 %convert.7 = bf16[89,128,256]{2,1,0:T(8,128)(2,1)S(1)} convert(f32[89,128,256]{2,1,0:T(8,128)} %shard_map.67) | non-fusion elementwise | flops 2916352 | bytes 17498112 | tf_op jit(solution)/shard_map/convert.4
  63.1 5.5 %copy.87 = bf16[16,4,128,256]{3,1,2,0:T(4,128)(2,1)} copy(bf16[16,4,128,256]{3,2,1,0:T(8,128)(2,1)S(1)} %bitcast.50) | data formatting | bytes 8388608 | tf_op jit(solution)/shard_map/reshape | solution.py:286
  68.5 18.2 %all-to-all-done = bf16[16,4,128,256]{3,2,1,0:T(8,128)(2,1)} async-done(((bf16[16,4,128,256]{3,2,1,0:T(8,128)(2,1)}), bf16[16,4,128,256]{3,2,1,0:T(8,128)(2,1)}, u32[]{:S(2)}, u32[]{:S(2)}) %all-to-all-start) | async-done | bytes 4194336 | tf_op jit(solution)/shard_map/all_to_all | solution.py:254
  86.7 9.6 %all-to-all-start.1 = ((bf16[16,4,128,256]{3,1,2,0:T(4,128)(2,1)}), bf16[16,4,128,256]{3,1,2,0:T(4,128)(2,1)}, u32[]{:S(2)}, u32[]{:S(2)}) async-start(bf16[16,4,128,256]{3,1,2,0:T(4,128)(2,1)} %copy.87), calls=%async_computation.1 | async-start | bytes 8388608 | tf_op jit(solution)/shard_map/all_to_all | solution.py:285
  99.0 6.1 %collective-permute-start = (bf16[4,128,256]{2,1,0:T(8,128)(2,1)S(1)}, bf16[4,128,256]{2,1,0:T(8,128)(2,1)S(1)}, u32[]{:S(2)}, u32[]{:S(2)}) collective-permute-start(bf16[4,128,256]{2,1,0:T(8,128)(2,1)S(1)} %get-tuple-element.37), channel_id=1, source_target_pairs={{0,16},{16,32},{32,48},{48,64},{64,80},{80,96},{96,112},{1,17},{17... | collective-permute-start | bytes 786440 | tf_op jit(solution)/shard_map/ppermute | solution.py:22
  108.4 4.8 %collective-permute-done.1 = bf16[4,128,256]{2,1,0:T(8,128)(2,1)S(1)} collective-permute-done((bf16[4,128,256]{2,1,0:T(8,128)(2,1)S(1)}, bf16[4,128,256]{2,1,0:T(8,128)(2,1)S(1)}, u32[]{:S(2)}, u32[]{:S(2)}) %collective-permute-start.1) | collective-permute-done | bytes 262176 | tf_op jit(solution)/shard_map/ppermute | solution.py:24
  113.3 4.7 %constant_dynamic-update-slice_fusion = bf16[89,128,256]{2,1,0:T(8,128)(2,1)} fusion(bf16[89,128,256]{2,1,0:T(8,128)(2,1)} %constant_dynamic-update-slice_fusion.1, bf16[64,128,256]{2,1,0:T(8,128)(2,1)} %bitcast.10), kind=kLoop, calls=%fused_computation.48 | loop fusion | bytes 8388608
  120.1 8.5 %copy.86.tablet_ref = bf16[89,256,128]{2,1,0:T(8,128)(2,1)} copy(bf16[89,256,128]{1,2,0:T(8,128)(2,1)} %bitcast.11) | data formatting | bytes 11665408 | tf_op jit(solution)/shard_map/transpose | solution.py:304
  128.5 20.1 %shard_map.68 = f32[27,256,256]{2,1,0:T(8,128)} custom-call(s32[432]{0:T(512)} %reshape.254.idx_ref, bf16[89,256,128]{2,1,0:T(8,128)(2,1)} %copy.86.tablet_ref, bf16[2048,256]{1,0:T(8,128)(2,1)} %grad_ref.1), custom_call_target="tpu_custom_call" | custom-call | flops 7247757312 | bytes 13959168 | tf_op jit(solution)/shard_map/pallas_call | solution.py:149
  148.6 3.5 %constant_dynamic-slice_fusion.1 = (f32[27,16,1,8,256]{4,3,2,1,0:T(8,128)S(1)}, f32[27,16,1,8,256]{4,3,2,1,0:T(8,128)S(1)}) fusion(f32[27,16,2,8,256]{4,3,2,1,0:T(8,128)} %bitcast.54, s32[]{:T(128)S(6)} %select_n.71, s32[]{:T(128)S(6)} %select_n.72), kind=kLoop, calls=%fused_computation.69 | loop fusion | bytes 14155784 | tf_op jit(solution)/shard_map/jit(dynamic_index_in_dim)/dynamic_slice | solution.py:178
  152.4 4.0 %collective-permute-start.2 = (f32[27,16,8,256]{3,2,0,1:T(8,128)S(1)}, f32[27,16,8,256]{3,2,0,1:T(8,128)S(1)}, u32[]{:S(2)}, u32[]{:S(2)}) collective-permute-start(f32[27,16,8,256]{3,2,0,1:T(8,128)S(1)} %bitcast.55), channel_id=1, source_target_pairs={{0,16},{16,0},{32,48},{48,32},{64,80},{80,64},{96,112},{112,96},{1... | collective-permute-start | bytes 10616840 | tf_op jit(solution)/shard_map/ppermute | solution.py:181
  156.4 5.8 %collective-permute-done.2 = f32[27,16,8,256]{3,2,0,1:T(8,128)S(1)} collective-permute-done((f32[27,16,8,256]{3,2,0,1:T(8,128)S(1)}, f32[27,16,8,256]{3,2,0,1:T(8,128)S(1)}, u32[]{:S(2)}, u32[]{:S(2)}) %collective-permute-start.2) | collective-permute-done | bytes 3538976 | tf_op jit(solution)/shard_map/ppermute | solution.py:181
  168.0 3.7 %collective-permute-start.3 = (bf16[4,128,256]{2,1,0:T(8,128)(2,1)S(1)}, bf16[4,128,256]{2,1,0:T(8,128)(2,1)S(1)}, u32[]{:S(2)}, u32[]{:S(2)}) collective-permute-start(bf16[4,128,256]{2,1,0:T(8,128)(2,1)S(1)} %get-tuple-element.35), channel_id=1, source_target_pairs={{0,16},{16,32},{32,48},{48,64},{64,80},{80,96},{96,112},{1,17},{17... | collective-permute-start | bytes 786440 | tf_op jit(solution)/shard_map/ppermute | solution.py:22
  174.4 25.5 %shard_map.69 = bf16[2048,256]{1,0:T(8,128)(2,1)} custom-call(s32[432]{0:T(512)} %reshape.254.idx_ref, bf16[89,128,256]{2,1,0:T(8,128)(2,1)} %broadcast_dynamic-update-slice_fusion.table_ref, bf16[27,256,256]{2,1,0:T(8,128)(2,1)} %w_ref.3), custom_call_target="tpu_custom_call" | custom-call | flops 7247757312 | bytes 10420224 | tf_op jit(solution)/shard_map/pallas_call | solution.py:108
  199.9 38.0 %reduce-scatter.4.cloned.1.call-done = f32[1,27,8,256]{3,2,1,0:T(8,128)} async-done(((f32[16,27,8,256]{3,2,1,0:T(8,128)}), f32[1,27,8,256]{3,2,1,0:T(8,128)}) %reduce-scatter.4.cloned.1.call-update) | async-done | bytes 221200
  239.6 3.3 %collective-permute-done.5 = f32[27,8,256]{2,1,0:T(8,128)S(1)} collective-permute-done((f32[27,8,256]{2,1,0:T(8,128)}, f32[27,8,256]{2,1,0:T(8,128)S(1)}, u32[]{:S(2)}, u32[]{:S(2)}) %collective-permute-start.5) | collective-permute-done | bytes 221216 | tf_op jit(solution)/shard_map/ppermute | solution.py:190
  243.8 2.8 %collective-permute-start.6 = (f32[27,8,256]{2,1,0:T(8,128)S(1)}, f32[27,8,256]{2,1,0:T(8,128)S(1)}, u32[]{:S(2)}, u32[]{:S(2)}) collective-permute-start(f32[27,8,256]{2,1,0:T(8,128)S(1)} %add.192), channel_id=1, source_target_pairs={{0,64},{16,80},{32,96},{48,112},{64,0},{80,16},{96,32},{112,48},{1... | collective-permute-start | bytes 663560 | tf_op jit(solution)/shard_map/ppermute | solution.py:190
  246.6 4.6 %fusion.4 = f32[16,128,256]{2,0,1:T(8,128)S(1)} fusion(bf16[16,4,128,256]{3,1,2,0:T(4,128)(2,1)} %all-to-all-done.1, s32[16,16]{0,1:T(8,128)S(1)} %copy.76, pred[16,16]{0,1:T(8,128)(4,1)S(1)} %copy.75), kind=kOutput, calls=%fused_computation.11 | convolution fusion | flops 67110912 | bytes 6292736 | tf_op jit(solution)/shard_map/pcj,pcvd->jvd/dot_general | solution.py:314
  251.2 3.9 %collective-permute-start.7 = (f32[27,8,256]{2,1,0:T(8,128)S(1)}, f32[27,8,256]{2,1,0:T(8,128)S(1)}, u32[]{:S(2)}, u32[]{:S(2)}) collective-permute-start(f32[27,8,256]{2,1,0:T(8,128)S(1)} %add.193), channel_id=1, source_target_pairs={{0,16},{16,0},{32,48},{48,32},{64,80},{80,64},{96,112},{112,96},{1... | collective-permute-start | bytes 663560 | tf_op jit(solution)/shard_map/ppermute | solution.py:192
  255.1 6.1 %fusion.3 = bf16[16,128,256]{2,1,0:T(8,128)(2,1)} fusion(f32[16,128,256]{2,0,1:T(8,128)S(1)} %fusion.12, f32[16,128,256]{2,0,1:T(8,128)S(1)} %fusion.14, f32[16,128,256]{2,0,1:T(8,128)S(1)} %fusion.4, f32[89,128,256]{2,1,0:T(8,128)} %shard_map.67), kind=kLoop, calls=%fused_computation.7 | loop fusion | flops 2097152 | bytes 9437184 | tf_op jit(solution)/shard_map/convert_element_type | solution.py:333
  (82 shorter events, 28.5 us)
Async XLA Ops:
  16.5 70.1 %all-to-all-start = ((bf16[16,4,128,256]{3,2,1,0:T(8,128)(2,1)}), bf16[16,4,128,256]{3,2,1,0:T(8,128)(2,1)}, u32[]{:S(2)}, u32[]{:S(2)}) async-start(bf16[16,4,128,256]{3,2,1,0:T(8,128)(2,1)} %copy.79), calls=%async_computation | async-start | bytes 8388608 | tf_op jit(solution)/shard_map/all_to_all | solution.py:254
  60.6 2.5 copy-start
  68.5 29.6 %copy-start.1 = (bf16[2048,256]{1,0:T(8,128)(2,1)S(1)}, bf16[2048,256]{1,0:T(8,128)(2,1)}, u32[]{:S(2)}) copy-start(bf16[2048,256]{1,0:T(8,128)(2,1)} %param.4) | copy-start | bytes 3145732
  86.7 61.9 %all-to-all-start.1 = ((bf16[16,4,128,256]{3,1,2,0:T(4,128)(2,1)}), bf16[16,4,128,256]{3,1,2,0:T(4,128)(2,1)}, u32[]{:S(2)}, u32[]{:S(2)}) async-start(bf16[16,4,128,256]{3,1,2,0:T(4,128)(2,1)} %copy.87), calls=%async_computation.1 | async-start | bytes 8388608 | tf_op jit(solution)/shard_map/all_to_all | solution.py:285
  96.3 141.5 %reduce-scatter.4.cloned.1.call-start = ((), (), s32[]{:S(2)}) async-start(), calls=%async_computation.3 | async-start | bytes 3760128
  99.0 9.4 %collective-permute-start = (bf16[4,128,256]{2,1,0:T(8,128)(2,1)S(1)}, bf16[4,128,256]{2,1,0:T(8,128)(2,1)S(1)}, u32[]{:S(2)}, u32[]{:S(2)}) collective-permute-start(bf16[4,128,256]{2,1,0:T(8,128)(2,1)S(1)} %get-tuple-element.37), channel_id=1, source_target_pairs={{0,16},{16,32},{32,48},{48,64},{64,80},{80,96},{96,112},{1,17},{17... | collective-permute-start | bytes 786440 | tf_op jit(solution)/shard_map/ppermute | solution.py:22
  105.1 8.1 %collective-permute-start.1 = (bf16[4,128,256]{2,1,0:T(8,128)(2,1)S(1)}, bf16[4,128,256]{2,1,0:T(8,128)(2,1)S(1)}, u32[]{:S(2)}, u32[]{:S(2)}) collective-permute-start(bf16[4,128,256]{2,1,0:T(8,128)(2,1)S(1)} %get-tuple-element.38), channel_id=1, source_target_pairs={{16,0},{32,16},{48,32},{64,48},{80,64},{96,80},{112,96},{17,1},{33... | collective-permute-start | bytes 786440 | tf_op jit(solution)/shard_map/ppermute | solution.py:24
  152.4 9.8 %collective-permute-start.2 = (f32[27,16,8,256]{3,2,0,1:T(8,128)S(1)}, f32[27,16,8,256]{3,2,0,1:T(8,128)S(1)}, u32[]{:S(2)}, u32[]{:S(2)}) collective-permute-start(f32[27,16,8,256]{3,2,0,1:T(8,128)S(1)} %bitcast.55), channel_id=1, source_target_pairs={{0,16},{16,0},{32,48},{48,32},{64,80},{80,64},{96,112},{112,96},{1... | collective-permute-start | bytes 10616840 | tf_op jit(solution)/shard_map/ppermute | solution.py:181
  165.7 8.2 %collective-permute-start.4 = (bf16[4,128,256]{2,1,0:T(8,128)(2,1)S(1)}, bf16[4,128,256]{2,1,0:T(8,128)(2,1)S(1)}, u32[]{:S(2)}, u32[]{:S(2)}) collective-permute-start(bf16[4,128,256]{2,1,0:T(8,128)(2,1)S(1)} %get-tuple-element.36), channel_id=1, source_target_pairs={{16,0},{32,16},{48,32},{64,48},{80,64},{96,80},{112,96},{17,1},{33... | collective-permute-start | bytes 786440 | tf_op jit(solution)/shard_map/ppermute | solution.py:24
  168.0 71.0 %collective-permute-start.3 = (bf16[4,128,256]{2,1,0:T(8,128)(2,1)S(1)}, bf16[4,128,256]{2,1,0:T(8,128)(2,1)S(1)}, u32[]{:S(2)}, u32[]{:S(2)}) collective-permute-start(bf16[4,128,256]{2,1,0:T(8,128)(2,1)S(1)} %get-tuple-element.35), channel_id=1, source_target_pairs={{0,16},{16,32},{32,48},{48,64},{64,80},{80,96},{96,112},{1,17},{17... | collective-permute-start | bytes 786440 | tf_op jit(solution)/shard_map/ppermute | solution.py:22
  237.8 5.0 %collective-permute-start.5 = (f32[27,8,256]{2,1,0:T(8,128)}, f32[27,8,256]{2,1,0:T(8,128)S(1)}, u32[]{:S(2)}, u32[]{:S(2)}) collective-permute-start(f32[27,8,256]{2,1,0:T(8,128)} %bitcast.58), channel_id=1, source_target_pairs={{0,32},{16,48},{32,0},{48,16},{64,96},{80,112},{96,64},{112,80},{1... | collective-permute-start | bytes 663560 | tf_op jit(solution)/shard_map/ppermute | solution.py:190
  243.8 7.3 %collective-permute-start.6 = (f32[27,8,256]{2,1,0:T(8,128)S(1)}, f32[27,8,256]{2,1,0:T(8,128)S(1)}, u32[]{:S(2)}, u32[]{:S(2)}) collective-permute-start(f32[27,8,256]{2,1,0:T(8,128)S(1)} %add.192), channel_id=1, source_target_pairs={{0,64},{16,80},{32,96},{48,112},{64,0},{80,16},{96,32},{112,48},{1... | collective-permute-start | bytes 663560 | tf_op jit(solution)/shard_map/ppermute | solution.py:190
  251.2 10.0 %collective-permute-start.7 = (f32[27,8,256]{2,1,0:T(8,128)S(1)}, f32[27,8,256]{2,1,0:T(8,128)S(1)}, u32[]{:S(2)}, u32[]{:S(2)}) collective-permute-start(f32[27,8,256]{2,1,0:T(8,128)S(1)} %add.193), channel_id=1, source_target_pairs={{0,16},{16,0},{32,48},{48,32},{64,80},{80,64},{96,112},{112,96},{1... | collective-permute-start | bytes 663560 | tf_op jit(solution)/shard_map/ppermute | solution.py:192
Sparse Core Ops, SparseCore 0:
  164.8 73.0 reduce-scatter.3

commit v10 on v9

--- a/solution.py
+++ b/solution.py
@@ -309,7 +309,6 @@
     scattered = weight_grad_sum(kernel_term, n_shard, n_region)
     kernel_term, table = lax.optimization_barrier((kernel_term, table))
     conv_out = conv_rows(table_index, table, weights, blocks_dev * voxels)
-    scattered, conv_out = lax.optimization_barrier((scattered, conv_out))
     input_acc = table_grad[:blocks_dev]
     input_acc = input_acc + jnp.einsum(
         "pcj,pcvd->jvd",
@@ -331,6 +330,7 @@
         precision=lax.Precision.HIGHEST,
     )
     in_grad = input_acc.reshape(blocks_dev * voxels, channels).astype(jnp.bfloat16)
+    scattered, conv_out, in_grad = lax.optimization_barrier((scattered, conv_out, in_grad))
     weight_grad = weight_grad_finish(scattered, n_region)
     return (conv_out, in_grad, weight_grad)
 

time: 271 us -> 266 us (0.982)
  waiting for transfers between devices: 72.4 us -> 66.5 us
    unnamed x2, waiting for transfers between devices: 38 us -> 26.2 us
    ppermute x2, waiting for transfers between devices: 3.28 us -> 7.39 us  [weight_grad_finish(): lax.ppermute(part, 'region', [(i, i ^ step) for i in range(n_region)])]
  transfers between devices with their start and end apart: 11 -> 11, of which waited for: 7 -> 10; matrix products, arithmetic and copies ran while one was open for 17% -> 17% of each run, Pallas kernels for 27% -> 28%
where the time goes in v10:
time: 266 us; the launch traced here: 264 us
  Pallas kernels  72.9 us (27%)
  waiting for transfers between devices  66.5 us (25%)
  starting transfers between devices  45 us (17%)
  local copies, waits for them, and re-layouts  36.4 us (14%)
  other arithmetic  19.5 us (7%)
  between operations  14.3 us (5%)
  matrix products  9.23 us (3%)
    pallas_call x1, Pallas kernels, table_grad_sums(): pl.pallas_call(_table_grad_kernel, out_shape=jax.ShapeDtypeStruct((rows,...  27.3 us
    unnamed x2, waiting for transfers between devices  26.2 us
    pallas_call x1, Pallas kernels, conv_rows(): pl.pallas_call(_conv_kernel, out_shape=jax.ShapeDtypeStruct((count, chann...  25.5 us
    pallas_call x1, Pallas kernels, weight_grad_terms(): pl.pallas_call(functools.partial(_weight_grad_kernel, scale=scale), out_s...  20.1 us
    all_to_all x1, waiting for transfers between devices, body(): lax.all_to_all(outgoing, 'shard', split_axis=0, concat_axis=0, tiled=True)  18.2 us
    ppermute x2, starting transfers between devices, padded(): lax.ppermute(tail, axis, [(i, (i + 1) % count) for i in range(ends)])  9.83 us
    all_to_all x1, starting transfers between devices, body(): lax.all_to_all(remote_sums[:n_shard * capacity].reshape(n_shard, capacity...  9.63 us
    unnamed x8, local copies, waits for them, and re-layouts  9.48 us
  transfers between devices with their start and end apart: 11, of which 10 were waited for; matrix products, arithmetic and copies ran while one was open for 17% of the time, Pallas kernels for 28%

profile of v10, /device:TPU:1, one launch (start us, length us, event | category | flops | bytes accessed | tf_op | source)
XLA Modules:
  0.0 263.8 jit_solution(12081959671407030883)
XLA Ops:
  10.1 2.9 %convolution_convert_fusion = bf16[16,4,128,256]{3,0,2,1:T(8,128)(2,1)S(1)} fusion(bf16[16,128,256]{2,1,0:T(8,128)(2,1)} %bitcast.51, s32[16,16]{0,1:T(8,128)S(1)} %copy.76, pred[16,16]{0,1:T(8,128)(4,1)S(1)} %copy.75), kind=kOutput, calls=%fused_computation.5 | convolution fusion | flops 69208064 | bytes 5244160 | tf_op jit(solution)/shard_map/pcj,jvd->pcvd/dot_general | solution.py:245
  13.0 3.5 %copy.79 = bf16[16,4,128,256]{3,2,1,0:T(8,128)(2,1)} copy(bf16[16,4,128,256]{3,0,2,1:T(8,128)(2,1)S(1)} %convolution_convert_fusion) | data formatting | bytes 8388608 | tf_op jit(solution)/shard_map/convert_element_type | solution.py:247
  16.5 8.6 %all-to-all-start = ((bf16[16,4,128,256]{3,2,1,0:T(8,128)(2,1)}), bf16[16,4,128,256]{3,2,1,0:T(8,128)(2,1)}, u32[]{:S(2)}, u32[]{:S(2)}) async-start(bf16[16,4,128,256]{3,2,1,0:T(8,128)(2,1)} %copy.79), calls=%async_computation | async-start | bytes 8388608 | tf_op jit(solution)/shard_map/all_to_all | solution.py:254
  28.1 27.3 %shard_map.67 = f32[89,128,256]{2,1,0:T(8,128)} custom-call(s32[432]{0:T(512)} %reshape.254.idx_ref, bf16[16,128,256]{2,1,0:T(8,128)(2,1)} %bitcast.60, bf16[27,256,256]{2,1,0:T(8,128)(2,1)} %w_ref.3), custom_call_target="tpu_custom_call" | custom-call | flops 7247757312 | bytes 16252928 | tf_op jit(solution)/shard_map/pallas_call | solution.py:59
  55.4 5.2 %convert.7 = bf16[89,128,256]{2,1,0:T(8,128)(2,1)S(1)} convert(f32[89,128,256]{2,1,0:T(8,128)} %shard_map.67) | non-fusion elementwise | flops 2916352 | bytes 17498112 | tf_op jit(solution)/shard_map/convert.4
  63.1 5.5 %copy.87 = bf16[16,4,128,256]{3,1,2,0:T(4,128)(2,1)} copy(bf16[16,4,128,256]{3,2,1,0:T(8,128)(2,1)S(1)} %bitcast.50) | data formatting | bytes 8388608 | tf_op jit(solution)/shard_map/reshape | solution.py:286
  68.5 18.2 %all-to-all-done = bf16[16,4,128,256]{3,2,1,0:T(8,128)(2,1)} async-done(((bf16[16,4,128,256]{3,2,1,0:T(8,128)(2,1)}), bf16[16,4,128,256]{3,2,1,0:T(8,128)(2,1)}, u32[]{:S(2)}, u32[]{:S(2)}) %all-to-all-start) | async-done | bytes 4194336 | tf_op jit(solution)/shard_map/all_to_all | solution.py:254
  86.7 9.6 %all-to-all-start.1 = ((bf16[16,4,128,256]{3,1,2,0:T(4,128)(2,1)}), bf16[16,4,128,256]{3,1,2,0:T(4,128)(2,1)}, u32[]{:S(2)}, u32[]{:S(2)}) async-start(bf16[16,4,128,256]{3,1,2,0:T(4,128)(2,1)} %copy.87), calls=%async_computation.1 | async-start | bytes 8388608 | tf_op jit(solution)/shard_map/all_to_all | solution.py:285
  99.0 6.1 %collective-permute-start = (bf16[4,128,256]{2,1,0:T(8,128)(2,1)S(1)}, bf16[4,128,256]{2,1,0:T(8,128)(2,1)S(1)}, u32[]{:S(2)}, u32[]{:S(2)}) collective-permute-start(bf16[4,128,256]{2,1,0:T(8,128)(2,1)S(1)} %get-tuple-element.39), channel_id=1, source_target_pairs={{0,16},{16,32},{32,48},{48,64},{64,80},{80,96},{96,112},{1,17},{17... | collective-permute-start | bytes 786440 | tf_op jit(solution)/shard_map/ppermute | solution.py:22
  108.4 4.8 %collective-permute-done.1 = bf16[4,128,256]{2,1,0:T(8,128)(2,1)S(1)} collective-permute-done((bf16[4,128,256]{2,1,0:T(8,128)(2,1)S(1)}, bf16[4,128,256]{2,1,0:T(8,128)(2,1)S(1)}, u32[]{:S(2)}, u32[]{:S(2)}) %collective-permute-start.1) | collective-permute-done | bytes 262176 | tf_op jit(solution)/shard_map/ppermute | solution.py:24
  113.3 4.7 %constant_dynamic-update-slice_fusion = bf16[89,128,256]{2,1,0:T(8,128)(2,1)} fusion(bf16[89,128,256]{2,1,0:T(8,128)(2,1)} %constant_dynamic-update-slice_fusion.1, bf16[64,128,256]{2,1,0:T(8,128)(2,1)} %bitcast.10), kind=kLoop, calls=%fused_computation.48 | loop fusion | bytes 8388608
  120.1 8.5 %copy.86.tablet_ref = bf16[89,256,128]{2,1,0:T(8,128)(2,1)} copy(bf16[89,256,128]{1,2,0:T(8,128)(2,1)} %bitcast.11) | data formatting | bytes 11665408 | tf_op jit(solution)/shard_map/transpose | solution.py:304
  128.5 20.1 %shard_map.68 = f32[27,256,256]{2,1,0:T(8,128)} custom-call(s32[432]{0:T(512)} %reshape.254.idx_ref, bf16[89,256,128]{2,1,0:T(8,128)(2,1)} %copy.86.tablet_ref, bf16[2048,256]{1,0:T(8,128)(2,1)} %grad_ref.1), custom_call_target="tpu_custom_call" | custom-call | flops 7247757312 | bytes 13959168 | tf_op jit(solution)/shard_map/pallas_call | solution.py:149
  148.6 3.5 %constant_dynamic-slice_fusion.1 = (f32[27,16,1,8,256]{4,3,2,1,0:T(8,128)S(1)}, f32[27,16,1,8,256]{4,3,2,1,0:T(8,128)S(1)}) fusion(f32[27,16,2,8,256]{4,3,2,1,0:T(8,128)} %bitcast.54, s32[]{:T(128)S(6)} %select_n.71, s32[]{:T(128)S(6)} %select_n.72), kind=kLoop, calls=%fused_computation.69 | loop fusion | bytes 14155784 | tf_op jit(solution)/shard_map/jit(dynamic_index_in_dim)/dynamic_slice | solution.py:178
  152.4 4.0 %collective-permute-start.2 = (f32[27,16,8,256]{3,2,0,1:T(8,128)S(1)}, f32[27,16,8,256]{3,2,0,1:T(8,128)S(1)}, u32[]{:S(2)}, u32[]{:S(2)}) collective-permute-start(f32[27,16,8,256]{3,2,0,1:T(8,128)S(1)} %bitcast.55), channel_id=1, source_target_pairs={{0,16},{16,0},{32,48},{48,32},{64,80},{80,64},{96,112},{112,96},{1... | collective-permute-start | bytes 10616840 | tf_op jit(solution)/shard_map/ppermute | solution.py:181
  156.4 5.8 %collective-permute-done.2 = f32[27,16,8,256]{3,2,0,1:T(8,128)S(1)} collective-permute-done((f32[27,16,8,256]{3,2,0,1:T(8,128)S(1)}, f32[27,16,8,256]{3,2,0,1:T(8,128)S(1)}, u32[]{:S(2)}, u32[]{:S(2)}) %collective-permute-start.2) | collective-permute-done | bytes 3538976 | tf_op jit(solution)/shard_map/ppermute | solution.py:181
  168.0 3.7 %collective-permute-start.3 = (bf16[4,128,256]{2,1,0:T(8,128)(2,1)S(1)}, bf16[4,128,256]{2,1,0:T(8,128)(2,1)S(1)}, u32[]{:S(2)}, u32[]{:S(2)}) collective-permute-start(bf16[4,128,256]{2,1,0:T(8,128)(2,1)S(1)} %get-tuple-element.37), channel_id=1, source_target_pairs={{0,16},{16,32},{32,48},{48,64},{64,80},{80,96},{96,112},{1,17},{17... | collective-permute-start | bytes 786440 | tf_op jit(solution)/shard_map/ppermute | solution.py:22
  175.6 4.6 %fusion.4 = f32[16,128,256]{2,0,1:T(8,128)S(1)} fusion(bf16[16,4,128,256]{3,1,2,0:T(4,128)(2,1)} %all-to-all-done.1, s32[16,16]{0,1:T(8,128)S(1)} %copy.76, pred[16,16]{0,1:T(8,128)(4,1)S(1)} %copy.75), kind=kOutput, calls=%fused_computation.11 | convolution fusion | flops 67110912 | bytes 6292736 | tf_op jit(solution)/shard_map/pcj,pcvd->jvd/dot_general | solution.py:313
  180.2 6.0 %fusion.3 = bf16[16,128,256]{2,1,0:T(8,128)(2,1)} fusion(f32[16,128,256]{2,0,1:T(8,128)S(1)} %fusion.12, f32[16,128,256]{2,0,1:T(8,128)S(1)} %fusion.14, f32[16,128,256]{2,0,1:T(8,128)S(1)} %fusion.4, f32[89,128,256]{2,1,0:T(8,128)} %shard_map.67), kind=kLoop, calls=%fused_computation.7 | loop fusion | flops 2097152 | bytes 9437184 | tf_op jit(solution)/shard_map/convert_element_type | solution.py:332
  186.2 25.5 %shard_map.69 = bf16[2048,256]{1,0:T(8,128)(2,1)} custom-call(s32[432]{0:T(512)} %reshape.254.idx_ref, bf16[89,128,256]{2,1,0:T(8,128)(2,1)} %broadcast_dynamic-update-slice_fusion.table_ref, bf16[27,256,256]{2,1,0:T(8,128)(2,1)} %w_ref.3), custom_call_target="tpu_custom_call" | custom-call | flops 7247757312 | bytes 10420224 | tf_op jit(solution)/shard_map/pallas_call | solution.py:108
  211.7 26.2 %reduce-scatter.4.cloned.1.call-done = f32[1,27,8,256]{3,2,1,0:T(8,128)} async-done(((f32[16,27,8,256]{3,2,1,0:T(8,128)}), f32[1,27,8,256]{3,2,1,0:T(8,128)}) %reduce-scatter.4.cloned.1.call-update) | async-done | bytes 221200
  239.1 3.8 %collective-permute-done.5 = f32[27,8,256]{2,1,0:T(8,128)S(1)} collective-permute-done((f32[27,8,256]{2,1,0:T(8,128)}, f32[27,8,256]{2,1,0:T(8,128)S(1)}, u32[]{:S(2)}, u32[]{:S(2)}) %collective-permute-start.5) | collective-permute-done | bytes 221216 | tf_op jit(solution)/shard_map/ppermute | solution.py:190
  246.7 3.6 %collective-permute-done.6 = f32[27,8,256]{2,1,0:T(8,128)S(1)} collective-permute-done((f32[27,8,256]{2,1,0:T(8,128)S(1)}, f32[27,8,256]{2,1,0:T(8,128)S(1)}, u32[]{:S(2)}, u32[]{:S(2)}) %collective-permute-start.6) | collective-permute-done | bytes 221216 | tf_op jit(solution)/shard_map/ppermute | solution.py:190
  250.3 4.7 %collective-permute-start.7 = (f32[27,8,256]{2,1,0:T(8,128)S(1)}, f32[27,8,256]{2,1,0:T(8,128)S(1)}, u32[]{:S(2)}, u32[]{:S(2)}) collective-permute-start(f32[27,8,256]{2,1,0:T(8,128)S(1)} %add.193), channel_id=1, source_target_pairs={{0,16},{16,0},{32,48},{48,32},{64,80},{80,64},{96,112},{112,96},{1... | collective-permute-start | bytes 663560 | tf_op jit(solution)/shard_map/ppermute | solution.py:192
  (82 shorter events, 33.1 us)
Async XLA Ops:
  16.5 70.1 %all-to-all-start = ((bf16[16,4,128,256]{3,2,1,0:T(8,128)(2,1)}), bf16[16,4,128,256]{3,2,1,0:T(8,128)(2,1)}, u32[]{:S(2)}, u32[]{:S(2)}) async-start(bf16[16,4,128,256]{3,2,1,0:T(8,128)(2,1)} %copy.79), calls=%async_computation | async-start | bytes 8388608 | tf_op jit(solution)/shard_map/all_to_all | solution.py:254
  60.6 2.5 copy-start
  68.5 29.6 %copy-start.1 = (bf16[2048,256]{1,0:T(8,128)(2,1)S(1)}, bf16[2048,256]{1,0:T(8,128)(2,1)}, u32[]{:S(2)}) copy-start(bf16[2048,256]{1,0:T(8,128)(2,1)} %param.4) | copy-start | bytes 3145732
  86.7 61.9 %all-to-all-start.1 = ((bf16[16,4,128,256]{3,1,2,0:T(4,128)(2,1)}), bf16[16,4,128,256]{3,1,2,0:T(4,128)(2,1)}, u32[]{:S(2)}, u32[]{:S(2)}) async-start(bf16[16,4,128,256]{3,1,2,0:T(4,128)(2,1)} %copy.87), calls=%async_computation.1 | async-start | bytes 8388608 | tf_op jit(solution)/shard_map/all_to_all | solution.py:285
  96.3 141.6 %reduce-scatter.4.cloned.1.call-start = ((), (), s32[]{:S(2)}) async-start(), calls=%async_computation.3 | async-start | bytes 3760128
  99.0 9.4 %collective-permute-start = (bf16[4,128,256]{2,1,0:T(8,128)(2,1)S(1)}, bf16[4,128,256]{2,1,0:T(8,128)(2,1)S(1)}, u32[]{:S(2)}, u32[]{:S(2)}) collective-permute-start(bf16[4,128,256]{2,1,0:T(8,128)(2,1)S(1)} %get-tuple-element.39), channel_id=1, source_target_pairs={{0,16},{16,32},{32,48},{48,64},{64,80},{80,96},{96,112},{1,17},{17... | collective-permute-start | bytes 786440 | tf_op jit(solution)/shard_map/ppermute | solution.py:22
  105.1 8.1 %collective-permute-start.1 = (bf16[4,128,256]{2,1,0:T(8,128)(2,1)S(1)}, bf16[4,128,256]{2,1,0:T(8,128)(2,1)S(1)}, u32[]{:S(2)}, u32[]{:S(2)}) collective-permute-start(bf16[4,128,256]{2,1,0:T(8,128)(2,1)S(1)} %get-tuple-element.40), channel_id=1, source_target_pairs={{16,0},{32,16},{48,32},{64,48},{80,64},{96,80},{112,96},{17,1},{33... | collective-permute-start | bytes 786440 | tf_op jit(solution)/shard_map/ppermute | solution.py:24
  152.4 9.8 %collective-permute-start.2 = (f32[27,16,8,256]{3,2,0,1:T(8,128)S(1)}, f32[27,16,8,256]{3,2,0,1:T(8,128)S(1)}, u32[]{:S(2)}, u32[]{:S(2)}) collective-permute-start(f32[27,16,8,256]{3,2,0,1:T(8,128)S(1)} %bitcast.55), channel_id=1, source_target_pairs={{0,16},{16,0},{32,48},{48,32},{64,80},{80,64},{96,112},{112,96},{1... | collective-permute-start | bytes 10616840 | tf_op jit(solution)/shard_map/ppermute | solution.py:181
  165.7 8.2 %collective-permute-start.4 = (bf16[4,128,256]{2,1,0:T(8,128)(2,1)S(1)}, bf16[4,128,256]{2,1,0:T(8,128)(2,1)S(1)}, u32[]{:S(2)}, u32[]{:S(2)}) collective-permute-start(bf16[4,128,256]{2,1,0:T(8,128)(2,1)S(1)} %get-tuple-element.38), channel_id=1, source_target_pairs={{16,0},{32,16},{48,32},{64,48},{80,64},{96,80},{112,96},{17,1},{33... | collective-permute-start | bytes 786440 | tf_op jit(solution)/shard_map/ppermute | solution.py:24
  168.0 7.0 %collective-permute-start.3 = (bf16[4,128,256]{2,1,0:T(8,128)(2,1)S(1)}, bf16[4,128,256]{2,1,0:T(8,128)(2,1)S(1)}, u32[]{:S(2)}, u32[]{:S(2)}) collective-permute-start(bf16[4,128,256]{2,1,0:T(8,128)(2,1)S(1)} %get-tuple-element.37), channel_id=1, source_target_pairs={{0,16},{16,32},{32,48},{48,64},{64,80},{80,96},{96,112},{1,17},{17... | collective-permute-start | bytes 786440 | tf_op jit(solution)/shard_map/ppermute | solution.py:22
  237.9 5.0 %collective-permute-start.5 = (f32[27,8,256]{2,1,0:T(8,128)}, f32[27,8,256]{2,1,0:T(8,128)S(1)}, u32[]{:S(2)}, u32[]{:S(2)}) collective-permute-start(f32[27,8,256]{2,1,0:T(8,128)} %bitcast.58), channel_id=1, source_target_pairs={{0,32},{16,48},{32,0},{48,16},{64,96},{80,112},{96,64},{112,80},{1... | collective-permute-start | bytes 663560 | tf_op jit(solution)/shard_map/ppermute | solution.py:190
  243.9 6.4 %collective-permute-start.6 = (f32[27,8,256]{2,1,0:T(8,128)S(1)}, f32[27,8,256]{2,1,0:T(8,128)S(1)}, u32[]{:S(2)}, u32[]{:S(2)}) collective-permute-start(f32[27,8,256]{2,1,0:T(8,128)S(1)} %add.192), channel_id=1, source_target_pairs={{0,64},{16,80},{32,96},{48,112},{64,0},{80,16},{96,32},{112,48},{1... | collective-permute-start | bytes 663560 | tf_op jit(solution)/shard_map/ppermute | solution.py:190
  250.3 5.8 %collective-permute-start.7 = (f32[27,8,256]{2,1,0:T(8,128)S(1)}, f32[27,8,256]{2,1,0:T(8,128)S(1)}, u32[]{:S(2)}, u32[]{:S(2)}) collective-permute-start(f32[27,8,256]{2,1,0:T(8,128)S(1)} %add.193), channel_id=1, source_target_pairs={{0,16},{16,0},{32,48},{48,32},{64,80},{80,64},{96,112},{112,96},{1... | collective-permute-start | bytes 663560 | tf_op jit(solution)/shard_map/ppermute | solution.py:192
Sparse Core Ops, SparseCore 0:
  164.8 73.0 reduce-scatter.3

commit v11 on v10

--- a/solution.py
+++ b/solution.py
@@ -132,20 +132,21 @@
     )(table_index.reshape(-1), table, weights)
 
 
-def _weight_grad_kernel(idx_ref, tablet_ref, grad_ref, wg_ref, gt_ref, *, scale):
+def _weight_grad_kernel(idx_ref, table_ref, gradt_ref, wg_ref, g_ref, *, scale):
     k = pl.program_id(0)
-    voxels = tablet_ref.shape[2]
-    blocks = grad_ref.shape[0] // voxels
-    rows = tablet_ref.shape[0]
+    voxels = table_ref.shape[1]
+    blocks = gradt_ref.shape[1] // voxels
+    rows = table_ref.shape[0]
     for b in range(blocks):
         t = jnp.clip(idx_ref[k * blocks + b], 0, rows - 1)
-        gt_ref[:, pl.ds(b * voxels, voxels)] = tablet_ref[t]
-    wg_ref[0] = jnp.dot(gt_ref[...], grad_ref[...], preferred_element_type=jnp.float32) * scale
-
-
-def weight_grad_terms(table_index, tablet, grad_rows, offsets, scale):
-    rows, channels, voxels = tablet.shape
-    count = grad_rows.shape[0]
+        g_ref[pl.ds(b * voxels, voxels), :] = table_ref[t]
+    flipped = jnp.dot(gradt_ref[...], g_ref[...], preferred_element_type=jnp.float32)
+    wg_ref[0] = flipped.T * scale
+
+
+def weight_grad_terms(table_index, table, gradt, offsets, scale):
+    rows, voxels, channels = table.shape
+    count = gradt.shape[1]
     return pl.pallas_call(
         functools.partial(_weight_grad_kernel, scale=scale),
         out_shape=jax.ShapeDtypeStruct((offsets, channels, channels), jnp.float32),
@@ -153,21 +154,21 @@
             num_scalar_prefetch=1,
             grid=(offsets,),
             in_specs=[
-                pl.BlockSpec((rows, channels, voxels), lambda k, idx: (0, 0, 0)),
-                pl.BlockSpec((count, channels), lambda k, idx: (0, 0)),
+                pl.BlockSpec((rows, voxels, channels), lambda k, idx: (0, 0, 0)),
+                pl.BlockSpec((channels, count), lambda k, idx: (0, 0)),
             ],
             out_specs=pl.BlockSpec((1, channels, channels), lambda k, idx: (k, 0, 0)),
-            scratch_shapes=[pltpu.VMEM((channels, count), jnp.bfloat16)],
+            scratch_shapes=[pltpu.VMEM((count, channels), jnp.bfloat16)],
         ),
         cost_estimate=pl.CostEstimate(
             flops=2 * offsets * count * channels * channels,
             transcendentals=0,
-            bytes_accessed=tablet.size * 2 + count * channels * 2 + offsets * channels * channels * 4,
+            bytes_accessed=table.size * 2 + count * channels * 2 + offsets * channels * channels * 4,
         ),
         compiler_params=pltpu.CompilerParams(
             dimension_semantics=("arbitrary",), vmem_limit_bytes=56 * 1024 * 1024
         ),
-    )(table_index.reshape(-1), tablet, grad_rows)
+    )(table_index.reshape(-1), table, gradt)
 
 
 def weight_grad_sum(term, n_shard, n_region):
@@ -301,10 +302,9 @@
         ],
         axis=0,
     )
-    tablet = jnp.swapaxes(table, 1, 2)
     scale = 1.0 / math.sqrt(total_blocks * voxels)
     grad_rows = grad_blocks.reshape(blocks_dev * voxels, channels)
-    kernel_term = weight_grad_terms(table_index, tablet, grad_rows, offsets, scale)
+    kernel_term = weight_grad_terms(table_index, table, grad_rows.T, offsets, scale)
     kernel_term, returned = lax.optimization_barrier((kernel_term, returned))
     scattered = weight_grad_sum(kernel_term, n_shard, n_region)
     kernel_term, table = lax.optimization_barrier((kernel_term, table))

time: 266 us -> 266 us (level)
  local copies, waits for them, and re-layouts: 36.4 us -> 29.4 us
  starting transfers between devices: 45 us -> 48.5 us
    transpose x1 -> x0, local copies, waits for them, and re-layouts: 8.45 us -> none  [body(): tablet = jnp.swapaxes(table, 1, 2)]
    ppermute x1, starting transfers between devices: 3.95 us -> 8.04 us  [weight_grad_sum(): pair = jnp.swapaxes(mine + lax.ppermute(theirs, 'region', swap), 0, 1)]
    all_to_all x1, waiting for transfers between devices: 0.01 us -> 2.93 us  [body(): lax.all_to_all(remote_sums[:n_shard * capacity].reshape(n_shard, capacity...]
    unnamed x8 -> x11, local copies, waits for them, and re-layouts: 9.48 us -> 10.9 us
  transfers between devices with their start and end apart: 11 -> 11, of which waited for: 10 -> 10; matrix products, arithmetic and copies ran while one was open for 17% -> 15% of each run, Pallas kernels for 28% -> 28%
where the time goes in v11:
time: 266 us; the launch traced here: 264 us
  Pallas kernels  73.3 us (28%)
  waiting for transfers between devices  68.8 us (26%)
  starting transfers between devices  48.5 us (18%)
  local copies, waits for them, and re-layouts  29.4 us (11%)
  other arithmetic  20.6 us (8%)
  between operations  14.3 us (5%)
  matrix products  9.21 us (3%)
    pallas_call x1, Pallas kernels, table_grad_sums(): pl.pallas_call(_table_grad_kernel, out_shape=jax.ShapeDtypeStruct((rows,...  27.3 us
    unnamed x2, waiting for transfers between devices  26.9 us
    pallas_call x1, Pallas kernels, conv_rows(): pl.pallas_call(_conv_kernel, out_shape=jax.ShapeDtypeStruct((count, chann...  25.5 us
    pallas_call x1, Pallas kernels, weight_grad_terms(): pl.pallas_call(functools.partial(_weight_grad_kernel, scale=scale), out_s...  20.6 us
    all_to_all x1, waiting for transfers between devices, body(): lax.all_to_all(outgoing, 'shard', split_axis=0, concat_axis=0, tiled=True)  18.3 us
    unnamed x11, local copies, waits for them, and re-layouts  10.9 us
    all_to_all x1, starting transfers between devices, body(): lax.all_to_all(remote_sums[:n_shard * capacity].reshape(n_shard, capacity...  9.51 us
    ppermute x2, starting transfers between devices, padded(): lax.ppermute(tail, axis, [(i, (i + 1) % count) for i in range(ends)])  9.31 us
  transfers between devices with their start and end apart: 11, of which 10 were waited for; matrix products, arithmetic and copies ran while one was open for 15% of the time, Pallas kernels for 28%

profile of v11, /device:TPU:1, one launch (start us, length us, event | category | flops | bytes accessed | tf_op | source)
XLA Modules:
  0.0 264.1 jit_solution(8580664175351339615)
XLA Ops:
  10.1 2.9 %convolution_convert_fusion = bf16[16,4,128,256]{3,0,2,1:T(8,128)(2,1)S(1)} fusion(bf16[16,128,256]{2,1,0:T(8,128)(2,1)} %bitcast.51, s32[16,16]{0,1:T(8,128)S(1)} %copy.76, pred[16,16]{0,1:T(8,128)(4,1)S(1)} %copy.75), kind=kOutput, calls=%fused_computation.5 | convolution fusion | flops 69208064 | bytes 5244160 | tf_op jit(solution)/shard_map/pcj,jvd->pcvd/dot_general | solution.py:246
  13.0 3.5 %copy.79 = bf16[16,4,128,256]{3,2,1,0:T(8,128)(2,1)} copy(bf16[16,4,128,256]{3,0,2,1:T(8,128)(2,1)S(1)} %convolution_convert_fusion) | data formatting | bytes 8388608 | tf_op jit(solution)/shard_map/convert_element_type | solution.py:248
  16.5 8.7 %all-to-all-start = ((bf16[16,4,128,256]{3,2,1,0:T(8,128)(2,1)}), bf16[16,4,128,256]{3,2,1,0:T(8,128)(2,1)}, u32[]{:S(2)}, u32[]{:S(2)}) async-start(bf16[16,4,128,256]{3,2,1,0:T(8,128)(2,1)} %copy.79), calls=%async_computation | async-start | bytes 8388608 | tf_op jit(solution)/shard_map/all_to_all | solution.py:255
  28.1 27.3 %shard_map.67 = f32[89,128,256]{2,1,0:T(8,128)} custom-call(s32[432]{0:T(512)} %reshape.254.idx_ref, bf16[16,128,256]{2,1,0:T(8,128)(2,1)} %bitcast.57, bf16[27,256,256]{2,1,0:T(8,128)(2,1)} %w_ref.3), custom_call_target="tpu_custom_call" | custom-call | flops 7247757312 | bytes 16252928 | tf_op jit(solution)/shard_map/pallas_call | solution.py:59
  55.4 5.2 %convert.7 = bf16[89,128,256]{2,1,0:T(8,128)(2,1)S(1)} convert(f32[89,128,256]{2,1,0:T(8,128)} %shard_map.67) | non-fusion elementwise | flops 2916352 | bytes 17498112 | tf_op jit(solution)/shard_map/convert.4
  63.1 5.5 %copy.87 = bf16[16,4,128,256]{3,1,2,0:T(4,128)(2,1)} copy(bf16[16,4,128,256]{3,2,1,0:T(8,128)(2,1)S(1)} %bitcast.50) | data formatting | bytes 8388608 | tf_op jit(solution)/shard_map/reshape | solution.py:287
  68.6 18.3 %all-to-all-done = bf16[16,4,128,256]{3,2,1,0:T(8,128)(2,1)} async-done(((bf16[16,4,128,256]{3,2,1,0:T(8,128)(2,1)}), bf16[16,4,128,256]{3,2,1,0:T(8,128)(2,1)}, u32[]{:S(2)}, u32[]{:S(2)}) %all-to-all-start) | async-done | bytes 4194336 | tf_op jit(solution)/shard_map/all_to_all | solution.py:255
  86.9 9.5 %all-to-all-start.1 = ((bf16[16,4,128,256]{3,1,2,0:T(4,128)(2,1)}), bf16[16,4,128,256]{3,1,2,0:T(4,128)(2,1)}, u32[]{:S(2)}, u32[]{:S(2)}) async-start(bf16[16,4,128,256]{3,1,2,0:T(4,128)(2,1)} %copy.87), calls=%async_computation.1 | async-start | bytes 8388608 | tf_op jit(solution)/shard_map/all_to_all | solution.py:286
  99.1 6.0 %collective-permute-start = (bf16[4,128,256]{2,1,0:T(8,128)(2,1)S(1)}, bf16[4,128,256]{2,1,0:T(8,128)(2,1)S(1)}, u32[]{:S(2)}, u32[]{:S(2)}) collective-permute-start(bf16[4,128,256]{2,1,0:T(8,128)(2,1)S(1)} %get-tuple-element.39), channel_id=1, source_target_pairs={{0,16},{16,32},{32,48},{48,64},{64,80},{80,96},{96,112},{1,17},{17... | collective-permute-start | bytes 786440 | tf_op jit(solution)/shard_map/ppermute | solution.py:22
  109.6 3.6 %collective-permute-done.1 = bf16[4,128,256]{2,1,0:T(8,128)(2,1)} collective-permute-done((bf16[4,128,256]{2,1,0:T(8,128)(2,1)S(1)}, bf16[4,128,256]{2,1,0:T(8,128)(2,1)}, u32[]{:S(2)}, u32[]{:S(2)}) %collective-permute-start.1) | collective-permute-done | bytes 262176 | tf_op jit(solution)/shard_map/ppermute | solution.py:24
  114.3 4.7 %constant_dynamic-update-slice_fusion = bf16[89,128,256]{2,1,0:T(8,128)(2,1)} fusion(bf16[89,128,256]{2,1,0:T(8,128)(2,1)} %constant_dynamic-update-slice_fusion.1, bf16[64,128,256]{2,1,0:T(8,128)(2,1)} %bitcast.10), kind=kLoop, calls=%fused_computation.48 | loop fusion | bytes 8388608
  121.0 20.6 %shard_map.68 = f32[27,256,256]{2,1,0:T(8,128)} custom-call(s32[432]{0:T(512)} %reshape.254.idx_ref, bf16[89,128,256]{2,1,0:T(8,128)(2,1)} %broadcast_dynamic-update-slice_fusion.table_ref, bf16[256,2048]{1,0:T(8,128)(2,1)} %bitcast.58), custom_call_target="tpu_custom_call" | custom-call | flops 7247757312 | bytes 13959168 | tf_op jit(solution)/shard_map/pallas_call | solution.py:150
  141.7 2.9 %all-to-all-done.1 = bf16[16,4,128,256]{3,1,2,0:T(4,128)(2,1)} async-done(((bf16[16,4,128,256]{3,1,2,0:T(4,128)(2,1)}), bf16[16,4,128,256]{3,1,2,0:T(4,128)(2,1)}, u32[]{:S(2)}, u32[]{:S(2)}) %all-to-all-start.1) | async-done | bytes 4194336 | tf_op jit(solution)/shard_map/all_to_all | solution.py:286
  144.6 3.5 %constant_dynamic-slice_fusion.1 = (f32[27,16,1,8,256]{4,3,2,1,0:T(8,128)S(1)}, f32[27,16,1,8,256]{4,3,2,1,0:T(8,128)S(1)}) fusion(f32[27,16,2,8,256]{4,3,2,1,0:T(8,128)} %bitcast.54, s32[]{:T(128)S(6)} %select_n.71, s32[]{:T(128)S(6)} %select_n.72), kind=kLoop, calls=%fused_computation.69 | loop fusion | bytes 14155784 | tf_op jit(solution)/shard_map/jit(dynamic_index_in_dim)/dynamic_slice | solution.py:179
  148.4 8.0 %collective-permute-start.2 = (f32[27,16,8,256]{3,2,0,1:T(8,128)S(1)}, f32[27,16,8,256]{3,2,0,1:T(8,128)S(1)}, u32[]{:S(2)}, u32[]{:S(2)}) collective-permute-start(f32[27,16,8,256]{3,2,0,1:T(8,128)S(1)} %bitcast.55), channel_id=1, source_target_pairs={{0,16},{16,0},{32,48},{48,32},{64,80},{80,64},{96,112},{112,96},{1... | collective-permute-start | bytes 10616840 | tf_op jit(solution)/shard_map/ppermute | solution.py:182
  156.4 5.8 %collective-permute-done.2 = f32[27,16,8,256]{3,2,0,1:T(8,128)S(1)} collective-permute-done((f32[27,16,8,256]{3,2,0,1:T(8,128)S(1)}, f32[27,16,8,256]{3,2,0,1:T(8,128)S(1)}, u32[]{:S(2)}, u32[]{:S(2)}) %collective-permute-start.2) | collective-permute-done | bytes 3538976 | tf_op jit(solution)/shard_map/ppermute | solution.py:182
  168.2 3.3 %collective-permute-start.3 = (bf16[4,128,256]{2,1,0:T(8,128)(2,1)S(1)}, bf16[4,128,256]{2,1,0:T(8,128)(2,1)S(1)}, u32[]{:S(2)}, u32[]{:S(2)}) collective-permute-start(bf16[4,128,256]{2,1,0:T(8,128)(2,1)S(1)} %get-tuple-element.37), channel_id=1, source_target_pairs={{0,16},{16,32},{32,48},{48,64},{64,80},{80,96},{96,112},{1,17},{17... | collective-permute-start | bytes 786440 | tf_op jit(solution)/shard_map/ppermute | solution.py:22
  175.3 4.6 %fusion.4 = f32[16,128,256]{2,0,1:T(8,128)S(1)} fusion(bf16[16,4,128,256]{3,1,2,0:T(4,128)(2,1)} %all-to-all-done.1, s32[16,16]{0,1:T(8,128)S(1)} %copy.76, pred[16,16]{0,1:T(8,128)(4,1)S(1)} %copy.75), kind=kOutput, calls=%fused_computation.11 | convolution fusion | flops 67110912 | bytes 6292736 | tf_op jit(solution)/shard_map/pcj,pcvd->jvd/dot_general | solution.py:313
  179.8 6.0 %fusion.3 = bf16[16,128,256]{2,1,0:T(8,128)(2,1)} fusion(f32[16,128,256]{2,0,1:T(8,128)S(1)} %fusion.12, f32[16,128,256]{2,0,1:T(8,128)S(1)} %fusion.14, f32[16,128,256]{2,0,1:T(8,128)S(1)} %fusion.4, f32[89,128,256]{2,1,0:T(8,128)} %shard_map.67), kind=kLoop, calls=%fused_computation.7 | loop fusion | flops 2097152 | bytes 9437184 | tf_op jit(solution)/shard_map/convert_element_type | solution.py:332
  185.9 25.5 %shard_map.69 = bf16[2048,256]{1,0:T(8,128)(2,1)} custom-call(s32[432]{0:T(512)} %reshape.254.idx_ref, bf16[89,128,256]{2,1,0:T(8,128)(2,1)} %broadcast_dynamic-update-slice_fusion.table_ref, bf16[27,256,256]{2,1,0:T(8,128)(2,1)} %w_ref.3), custom_call_target="tpu_custom_call" | custom-call | flops 7247757312 | bytes 10420224 | tf_op jit(solution)/shard_map/pallas_call | solution.py:108
  211.3 26.9 %reduce-scatter.4.cloned.1.call-done = f32[1,27,8,256]{3,2,1,0:T(8,128)} async-done(((f32[16,27,8,256]{3,2,1,0:T(8,128)}), f32[1,27,8,256]{3,2,1,0:T(8,128)}) %reduce-scatter.4.cloned.1.call-update) | async-done | bytes 221200
  239.4 3.8 %collective-permute-done.5 = f32[27,8,256]{2,1,0:T(8,128)S(1)} collective-permute-done((f32[27,8,256]{2,1,0:T(8,128)}, f32[27,8,256]{2,1,0:T(8,128)S(1)}, u32[]{:S(2)}, u32[]{:S(2)}) %collective-permute-start.5) | collective-permute-done | bytes 221216 | tf_op jit(solution)/shard_map/ppermute | solution.py:191
  247.0 3.6 %collective-permute-done.6 = f32[27,8,256]{2,1,0:T(8,128)S(1)} collective-permute-done((f32[27,8,256]{2,1,0:T(8,128)S(1)}, f32[27,8,256]{2,1,0:T(8,128)S(1)}, u32[]{:S(2)}, u32[]{:S(2)}) %collective-permute-start.6) | collective-permute-done | bytes 221216 | tf_op jit(solution)/shard_map/ppermute | solution.py:191
  250.6 4.7 %collective-permute-start.7 = (f32[27,8,256]{2,1,0:T(8,128)S(1)}, f32[27,8,256]{2,1,0:T(8,128)S(1)}, u32[]{:S(2)}, u32[]{:S(2)}) collective-permute-start(f32[27,8,256]{2,1,0:T(8,128)S(1)} %add.193), channel_id=1, source_target_pairs={{0,16},{16,0},{32,48},{48,32},{64,80},{80,64},{96,112},{112,96},{1... | collective-permute-start | bytes 663560 | tf_op jit(solution)/shard_map/ppermute | solution.py:193
  (84 shorter events, 35.3 us)
Async XLA Ops:
  16.5 70.4 %all-to-all-start = ((bf16[16,4,128,256]{3,2,1,0:T(8,128)(2,1)}), bf16[16,4,128,256]{3,2,1,0:T(8,128)(2,1)}, u32[]{:S(2)}, u32[]{:S(2)}) async-start(bf16[16,4,128,256]{3,2,1,0:T(8,128)(2,1)} %copy.79), calls=%async_computation | async-start | bytes 8388608 | tf_op jit(solution)/shard_map/all_to_all | solution.py:255
  60.6 2.5 copy-start
  68.6 29.6 %copy-start.1 = (bf16[2048,256]{1,0:T(8,128)(2,1)S(1)}, bf16[2048,256]{1,0:T(8,128)(2,1)}, u32[]{:S(2)}) copy-start(bf16[2048,256]{1,0:T(8,128)(2,1)} %param.4) | copy-start | bytes 3145732
  68.6 38.4 %copy-start.2 = (bf16[2048,256]{1,0:T(8,128)(2,1)S(1)}, bf16[2048,256]{1,0:T(8,128)(2,1)}, u32[]{:S(2)}) copy-start(bf16[2048,256]{1,0:T(8,128)(2,1)} %param.7) | copy-start | bytes 3145732
  86.9 57.7 %all-to-all-start.1 = ((bf16[16,4,128,256]{3,1,2,0:T(4,128)(2,1)}), bf16[16,4,128,256]{3,1,2,0:T(4,128)(2,1)}, u32[]{:S(2)}, u32[]{:S(2)}) async-start(bf16[16,4,128,256]{3,1,2,0:T(4,128)(2,1)} %copy.87), calls=%async_computation.1 | async-start | bytes 8388608 | tf_op jit(solution)/shard_map/all_to_all | solution.py:286
  96.4 141.8 %reduce-scatter.4.cloned.1.call-start = ((), (), s32[]{:S(2)}) async-start(), calls=%async_computation.3 | async-start | bytes 3760128
  99.1 10.6 %collective-permute-start = (bf16[4,128,256]{2,1,0:T(8,128)(2,1)S(1)}, bf16[4,128,256]{2,1,0:T(8,128)(2,1)S(1)}, u32[]{:S(2)}, u32[]{:S(2)}) collective-permute-start(bf16[4,128,256]{2,1,0:T(8,128)(2,1)S(1)} %get-tuple-element.39), channel_id=1, source_target_pairs={{0,16},{16,32},{32,48},{48,64},{64,80},{80,96},{96,112},{1,17},{17... | collective-permute-start | bytes 786440 | tf_op jit(solution)/shard_map/ppermute | solution.py:22
  105.1 8.1 %collective-permute-start.1 = (bf16[4,128,256]{2,1,0:T(8,128)(2,1)S(1)}, bf16[4,128,256]{2,1,0:T(8,128)(2,1)}, u32[]{:S(2)}, u32[]{:S(2)}) collective-permute-start(bf16[4,128,256]{2,1,0:T(8,128)(2,1)S(1)} %get-tuple-element.40), channel_id=1, source_target_pairs={{16,0},{32,16},{48,32},{64,48},{80,64},{96,80},{112,96},{17,1},{33... | collective-permute-start | bytes 786440 | tf_op jit(solution)/shard_map/ppermute | solution.py:24
  148.4 13.9 %collective-permute-start.2 = (f32[27,16,8,256]{3,2,0,1:T(8,128)S(1)}, f32[27,16,8,256]{3,2,0,1:T(8,128)S(1)}, u32[]{:S(2)}, u32[]{:S(2)}) collective-permute-start(f32[27,16,8,256]{3,2,0,1:T(8,128)S(1)} %bitcast.55), channel_id=1, source_target_pairs={{0,16},{16,0},{32,48},{48,32},{64,80},{80,64},{96,112},{112,96},{1... | collective-permute-start | bytes 10616840 | tf_op jit(solution)/shard_map/ppermute | solution.py:182
  165.9 7.7 %collective-permute-start.4 = (bf16[4,128,256]{2,1,0:T(8,128)(2,1)S(1)}, bf16[4,128,256]{2,1,0:T(8,128)(2,1)S(1)}, u32[]{:S(2)}, u32[]{:S(2)}) collective-permute-start(bf16[4,128,256]{2,1,0:T(8,128)(2,1)S(1)} %get-tuple-element.38), channel_id=1, source_target_pairs={{16,0},{32,16},{48,32},{64,48},{80,64},{96,80},{112,96},{17,1},{33... | collective-permute-start | bytes 786440 | tf_op jit(solution)/shard_map/ppermute | solution.py:24
  168.2 6.6 %collective-permute-start.3 = (bf16[4,128,256]{2,1,0:T(8,128)(2,1)S(1)}, bf16[4,128,256]{2,1,0:T(8,128)(2,1)S(1)}, u32[]{:S(2)}, u32[]{:S(2)}) collective-permute-start(bf16[4,128,256]{2,1,0:T(8,128)(2,1)S(1)} %get-tuple-element.37), channel_id=1, source_target_pairs={{0,16},{16,32},{32,48},{48,64},{64,80},{80,96},{96,112},{1,17},{17... | collective-permute-start | bytes 786440 | tf_op jit(solution)/shard_map/ppermute | solution.py:22
  238.2 5.0 %collective-permute-start.5 = (f32[27,8,256]{2,1,0:T(8,128)}, f32[27,8,256]{2,1,0:T(8,128)S(1)}, u32[]{:S(2)}, u32[]{:S(2)}) collective-permute-start(f32[27,8,256]{2,1,0:T(8,128)} %bitcast.60), channel_id=1, source_target_pairs={{0,32},{16,48},{32,0},{48,16},{64,96},{80,112},{96,64},{112,80},{1... | collective-permute-start | bytes 663560 | tf_op jit(solution)/shard_map/ppermute | solution.py:191
  244.2 6.4 %collective-permute-start.6 = (f32[27,8,256]{2,1,0:T(8,128)S(1)}, f32[27,8,256]{2,1,0:T(8,128)S(1)}, u32[]{:S(2)}, u32[]{:S(2)}) collective-permute-start(f32[27,8,256]{2,1,0:T(8,128)S(1)} %add.192), channel_id=1, source_target_pairs={{0,64},{16,80},{32,96},{48,112},{64,0},{80,16},{96,32},{112,48},{1... | collective-permute-start | bytes 663560 | tf_op jit(solution)/shard_map/ppermute | solution.py:191
  250.6 5.8 %collective-permute-start.7 = (f32[27,8,256]{2,1,0:T(8,128)S(1)}, f32[27,8,256]{2,1,0:T(8,128)S(1)}, u32[]{:S(2)}, u32[]{:S(2)}) collective-permute-start(f32[27,8,256]{2,1,0:T(8,128)S(1)} %add.193), channel_id=1, source_target_pairs={{0,16},{16,0},{32,48},{48,32},{64,80},{80,64},{96,112},{112,96},{1... | collective-permute-start | bytes 663560 | tf_op jit(solution)/shard_map/ppermute | solution.py:193
Sparse Core Ops, SparseCore 0:
  164.9 73.2 reduce-scatter.3

commit v12 on v11

--- a/solution.py
+++ b/solution.py
@@ -180,7 +180,35 @@
     theirs = lax.dynamic_index_in_dim(view, 1 - core, 2, keepdims=False)
     swap = [(i, i ^ 1) for i in range(n_region)]
     pair = jnp.swapaxes(mine + lax.ppermute(theirs, "region", swap), 0, 1)
-    return lax.psum_scatter(pair, "shard", scatter_dimension=0, tiled=True)[0]
+    inner = 4 if n_shard % 4 == 0 else n_shard
+    outer = n_shard // inner
+    pair = pair.reshape((outer, inner) + pair.shape[1:])
+    half = width // 2
+    parts = []
+    for lo, step in ((0, 1), (half, -1)):
+        value = pair[..., lo : lo + half]
+        value = ring_scatter(value, 1, inner, 1, n_shard, step)
+        value = ring_scatter(value, 0, outer, inner, n_shard, step)
+        parts.append(value)
+    return jnp.concatenate(parts, axis=-1)
+
+
+def ring_scatter(value, axis, ring, stride, n_shard, step):
+    if ring == 1:
+        return lax.index_in_dim(value, 0, axis, keepdims=False)
+    shard = lax.axis_index("shard")
+    place = (shard // stride) % ring
+    pairs = []
+    for i in range(n_shard):
+        p = (i // stride) % ring
+        pairs.append((i, i + stride * ((p + step) % ring - p)))
+    for t in range(ring - 1):
+        send = lax.dynamic_index_in_dim(value, (place - step * (t + 1)) % ring, axis, keepdims=False)
+        got = lax.ppermute(send, "shard", pairs)
+        where = (place - step * (t + 2)) % ring
+        current = lax.dynamic_index_in_dim(value, where, axis, keepdims=False)
+        value = lax.dynamic_update_index_in_dim(value, current + got, where, axis)
+    return lax.dynamic_index_in_dim(value, place, axis, keepdims=False)
 
 
 def weight_grad_finish(part, n_region):

time: 266 us -> 268 us (level)
  starting transfers between devices: 48.5 us -> 63.1 us
  between operations: 14.3 us -> 1.52 us
  waiting for transfers between devices: 68.8 us -> 61.5 us
  matrix products: 9.21 us -> 13.8 us
  local copies, waits for them, and re-layouts: 29.4 us -> 33.8 us
    unnamed x2 -> x0, waiting for transfers between devices: 26.9 us -> none
    ppermute x0 -> x12, waiting for transfers between devices: none -> 21.4 us  [ring_scatter(): got = lax.ppermute(send, 'shard', pairs)]
    ppermute x0 -> x12, starting transfers between devices: none -> 15.7 us  [ring_scatter(): got = lax.ppermute(send, 'shard', pairs)]
    ppermute x1, waiting for transfers between devices: 5.85 us -> 0.01 us  [weight_grad_sum(): pair = jnp.swapaxes(mine + lax.ppermute(theirs, 'region', swap), 0, 1)]
    all_to_all x1, waiting for transfers between devices: 2.93 us -> 5.78 us  [body(): lax.all_to_all(remote_sums[:n_shard * capacity].reshape(n_shard, capacity...]
    unnamed x11 -> x17, local copies, waits for them, and re-layouts: 10.9 us -> 11.4 us
  transfers between devices with their start and end apart: 11 -> 22, of which waited for: 10 -> 15; matrix products, arithmetic and copies ran while one was open for 15% -> 17% of each run, Pallas kernels for 28% -> 27%
where the time goes in v12:
time: 268 us; the launch traced here: 267 us
  Pallas kernels  73.2 us (27%)
  starting transfers between devices  63.1 us (24%)
  waiting for transfers between devices  61.5 us (23%)
  local copies, waits for them, and re-layouts  33.8 us (13%)
  other arithmetic  19.8 us (7%)
  matrix products  13.8 us (5%)
    pallas_call x1, Pallas kernels, table_grad_sums(): pl.pallas_call(_table_grad_kernel, out_shape=jax.ShapeDtypeStruct((rows,...  27.3 us
    pallas_call x1, Pallas kernels, conv_rows(): pl.pallas_call(_conv_kernel, out_shape=jax.ShapeDtypeStruct((count, chann...  25.4 us
    ppermute x12, waiting for transfers between devices, ring_scatter(): got = lax.ppermute(send, 'shard', pairs)  21.4 us
    pallas_call x1, Pallas kernels, weight_grad_terms(): pl.pallas_call(functools.partial(_weight_grad_kernel, scale=scale), out_s...  20.6 us
    all_to_all x1, waiting for transfers between devices, body(): lax.all_to_all(outgoing, 'shard', split_axis=0, concat_axis=0, tiled=True)  17.8 us
    ppermute x12, starting transfers between devices, ring_scatter(): got = lax.ppermute(send, 'shard', pairs)  15.7 us
    unnamed x17, local copies, waits for them, and re-layouts  11.4 us
    all_to_all x1, starting transfers between devices, body(): lax.all_to_all(remote_sums[:n_shard * capacity].reshape(n_shard, capacity...  10.5 us
  transfers between devices with their start and end apart: 22, of which 15 were waited for; matrix products, arithmetic and copies ran while one was open for 17% of the time, Pallas kernels for 27%

profile of v12, /device:TPU:1, one launch (start us, length us, event | category | flops | bytes accessed | tf_op | source)
XLA Modules:
  0.0 266.7 jit_solution(1624464513697210419)
XLA Ops:
  6.5 3.5 %copy.77 = bf16[16,4,128,256]{3,2,1,0:T(8,128)(2,1)} copy(bf16[16,4,128,256]{3,0,2,1:T(8,128)(2,1)S(1)} %convolution_convert_fusion) | data formatting | bytes 8388608 | tf_op jit(solution)/shard_map/convert_element_type | solution.py:276
  10.0 8.7 %all-to-all-start = ((bf16[16,4,128,256]{3,2,1,0:T(8,128)(2,1)}), bf16[16,4,128,256]{3,2,1,0:T(8,128)(2,1)}, u32[]{:S(2)}, u32[]{:S(2)}) async-start(bf16[16,4,128,256]{3,2,1,0:T(8,128)(2,1)} %copy.77), calls=%async_computation | async-start | bytes 8388608 | tf_op jit(solution)/shard_map/all_to_all | solution.py:283
  21.5 27.3 %shard_map.67 = f32[89,128,256]{2,1,0:T(8,128)} custom-call(s32[432]{0:T(512)} %reshape.265.idx_ref, bf16[16,128,256]{2,1,0:T(8,128)(2,1)} %bitcast.158, bf16[27,256,256]{2,1,0:T(8,128)(2,1)} %w_ref.3), custom_call_target="tpu_custom_call" | custom-call | flops 7247757312 | bytes 16252928 | tf_op jit(solution)/shard_map/pallas_call | solution.py:59
  48.8 5.2 %convert.7 = bf16[89,128,256]{2,1,0:T(8,128)(2,1)S(1)} convert(f32[89,128,256]{2,1,0:T(8,128)} %shard_map.67) | non-fusion elementwise | flops 2916352 | bytes 17498112 | tf_op jit(solution)/shard_map/convert.4
  56.4 5.5 %copy.85 = bf16[16,4,128,256]{3,1,2,0:T(4,128)(2,1)} copy(bf16[16,4,128,256]{3,2,1,0:T(8,128)(2,1)S(1)} %bitcast.151) | data formatting | bytes 8388608 | tf_op jit(solution)/shard_map/reshape | solution.py:315
  62.0 17.8 %all-to-all-done = bf16[16,4,128,256]{3,2,1,0:T(8,128)(2,1)} async-done(((bf16[16,4,128,256]{3,2,1,0:T(8,128)(2,1)}), bf16[16,4,128,256]{3,2,1,0:T(8,128)(2,1)}, u32[]{:S(2)}, u32[]{:S(2)}) %all-to-all-start) | async-done | bytes 4194336 | tf_op jit(solution)/shard_map/all_to_all | solution.py:283
  79.8 10.5 %all-to-all-start.1 = ((bf16[16,4,128,256]{3,1,2,0:T(4,128)(2,1)}), bf16[16,4,128,256]{3,1,2,0:T(4,128)(2,1)}, u32[]{:S(2)}, u32[]{:S(2)}) async-start(bf16[16,4,128,256]{3,1,2,0:T(4,128)(2,1)} %copy.85), calls=%async_computation.1 | async-start | bytes 8388608 | tf_op jit(solution)/shard_map/all_to_all | solution.py:314
  93.5 5.5 %collective-permute-start = (bf16[4,128,256]{2,1,0:T(8,128)(2,1)S(1)}, bf16[4,128,256]{2,1,0:T(8,128)(2,1)S(1)}, u32[]{:S(2)}, u32[]{:S(2)}) collective-permute-start(bf16[4,128,256]{2,1,0:T(8,128)(2,1)S(1)} %get-tuple-element.53), channel_id=1, source_target_pairs={{0,16},{16,32},{32,48},{48,64},{64,80},{80,96},{96,112},{1,17},{17... | collective-permute-start | bytes 786440 | tf_op jit(solution)/shard_map/ppermute | solution.py:22
  103.7 3.4 %collective-permute-done.1 = bf16[4,128,256]{2,1,0:T(8,128)(2,1)} collective-permute-done((bf16[4,128,256]{2,1,0:T(8,128)(2,1)S(1)}, bf16[4,128,256]{2,1,0:T(8,128)(2,1)}, u32[]{:S(2)}, u32[]{:S(2)}) %collective-permute-start.1) | collective-permute-done | bytes 262176 | tf_op jit(solution)/shard_map/ppermute | solution.py:24
  108.1 4.7 %constant_dynamic-update-slice_fusion = bf16[89,128,256]{2,1,0:T(8,128)(2,1)} fusion(bf16[89,128,256]{2,1,0:T(8,128)(2,1)} %constant_dynamic-update-slice_fusion.1, bf16[64,128,256]{2,1,0:T(8,128)(2,1)} %bitcast.10), kind=kLoop, calls=%fused_computation.88 | loop fusion | bytes 8388608
  114.9 20.6 %shard_map.68 = f32[27,256,256]{2,1,0:T(8,128)} custom-call(s32[432]{0:T(512)} %reshape.265.idx_ref, bf16[89,128,256]{2,1,0:T(8,128)(2,1)} %broadcast_dynamic-update-slice_fusion.table_ref, bf16[256,2048]{1,0:T(8,128)(2,1)} %bitcast.159), custom_call_target="tpu_custom_call" | custom-call | flops 7247757312 | bytes 13959168 | tf_op jit(solution)/shard_map/pallas_call | solution.py:150
  135.5 5.8 %all-to-all-done.1 = bf16[16,4,128,256]{3,1,2,0:T(4,128)(2,1)} async-done(((bf16[16,4,128,256]{3,1,2,0:T(4,128)(2,1)}), bf16[16,4,128,256]{3,1,2,0:T(4,128)(2,1)}, u32[]{:S(2)}, u32[]{:S(2)}) %all-to-all-start.1) | async-done | bytes 4194336 | tf_op jit(solution)/shard_map/all_to_all | solution.py:314
  141.3 3.6 %constant_dynamic-slice_fusion.11 = (f32[27,16,1,8,256]{4,3,2,1,0:T(8,128)S(1)}, f32[27,16,1,8,256]{4,3,2,1,0:T(8,128)S(1)}) fusion(f32[27,16,2,8,256]{4,3,2,1,0:T(8,128)} %bitcast.156, s32[]{:T(128)S(6)} %select_n.260, s32[]{:T(128)S(6)} %select_n.261), kind=kLoop, calls=%fused_computation.101 | loop fusion | bytes 14155784 | tf_op jit(solution)/shard_map/jit(dynamic_index_in_dim)/dynamic_slice | solution.py:179
  146.9 5.6 %collective-permute-start.2 = (f32[27,16,8,256]{3,2,0,1:T(8,128)}, f32[27,16,8,256]{3,2,0,1:T(8,128)}, u32[]{:S(2)}, u32[]{:S(2)}) collective-permute-start(f32[27,16,8,256]{3,2,0,1:T(8,128)} %bitcast.150), channel_id=1, source_target_pairs={{0,16},{16,0},{32,48},{48,32},{64,80},{80,64},{96,112},{112,96},{1... | collective-permute-start | bytes 10616840 | tf_op jit(solution)/shard_map/ppermute | solution.py:182
  156.3 3.6 %collective-permute-start.15 = (bf16[4,128,256]{2,1,0:T(8,128)(2,1)}, bf16[4,128,256]{2,1,0:T(8,128)(2,1)}, u32[]{:S(2)}, u32[]{:S(2)}) collective-permute-start(bf16[4,128,256]{2,1,0:T(8,128)(2,1)} %get-tuple-element.37), channel_id=1, source_target_pairs={{0,16},{16,32},{32,48},{48,64},{64,80},{80,96},{96,112},{1,17},{17... | collective-permute-start | bytes 786440 | tf_op jit(solution)/shard_map/ppermute | solution.py:22
  171.2 25.4 %shard_map.69 = bf16[2048,256]{1,0:T(8,128)(2,1)} custom-call(s32[432]{0:T(512)} %reshape.265.idx_ref, bf16[89,128,256]{2,1,0:T(8,128)(2,1)} %broadcast_dynamic-update-slice_fusion.table_ref, bf16[27,256,256]{2,1,0:T(8,128)(2,1)} %w_ref.3), custom_call_target="tpu_custom_call" | custom-call | flops 7247757312 | bytes 10420224 | tf_op jit(solution)/shard_map/pallas_call | solution.py:108
  199.3 4.6 %fusion.3 = f32[16,128,256]{2,0,1:T(8,128)S(1)} fusion(bf16[16,4,128,256]{3,1,2,0:T(4,128)(2,1)} %all-to-all-done.1, s32[16,16]{0,1:T(8,128)S(1)} %copy.74, pred[16,16]{0,1:T(8,128)(4,1)S(1)} %copy.73), kind=kOutput, calls=%fused_computation.10 | convolution fusion | flops 67110912 | bytes 6292736 | tf_op jit(solution)/shard_map/pcj,pcvd->jvd/dot_general | solution.py:341
  207.1 3.2 %collective-permute-start.10 = (f32[4,27,8,128]{3,2,1,0:T(8,128)S(1)}, f32[4,27,8,128]{3,2,1,0:T(8,128)S(1)}, u32[]{:S(2)}, u32[]{:S(2)}) collective-permute-start(f32[4,27,8,128]{3,2,1,0:T(8,128)S(1)} %get-tuple-element.50), channel_id=1, source_target_pairs={{0,3},{1,0},{2,1},{3,2},{4,7},{5,4},{6,5},{7,6},{8,11},{9,8},{10,9... | collective-permute-start | bytes 1327112 | tf_op jit(solution)/shard_map/ppermute | solution.py:207
  211.0 6.0 %fusion.2 = bf16[16,128,256]{2,1,0:T(8,128)(2,1)} fusion(f32[16,128,256]{2,0,1:T(8,128)S(1)} %copy-done.2, f32[16,128,256]{2,0,1:T(8,128)S(1)} %copy-done.3, f32[16,128,256]{2,0,1:T(8,128)S(1)} %fusion.3, f32[89,128,256]{2,1,0:T(8,128)} %shard_map.67), kind=kLoop, calls=%fused_computation.6 | loop fusion | flops 2097152 | bytes 9437184 | tf_op jit(solution)/shard_map/convert_element_type | solution.py:360
  223.4 9.0 %collective-permute-done.11 = f32[4,27,8,128]{3,2,1,0:T(8,128)S(1)} collective-permute-done((f32[4,27,8,128]{3,2,1,0:T(8,128)S(1)}, f32[4,27,8,128]{3,2,1,0:T(8,128)S(1)}, u32[]{:S(2)}, u32[]{:S(2)}) %collective-permute-start.11) | collective-permute-done | bytes 442400 | tf_op jit(solution)/shard_map/ppermute | solution.py:207
  245.2 4.8 %collective-permute-done.17 = f32[27,8,256]{2,1,0:T(8,128)S(1)} collective-permute-done((f32[27,8,256]{2,1,0:T(8,128)S(1)}, f32[27,8,256]{2,1,0:T(8,128)S(1)}, u32[]{:S(2)}, u32[]{:S(2)}) %collective-permute-start.17) | collective-permute-done | bytes 221216 | tf_op jit(solution)/shard_map/ppermute | solution.py:219
  250.0 3.7 %collective-permute-start.18 = (f32[27,8,256]{2,1,0:T(8,128)S(1)}, f32[27,8,256]{2,1,0:T(8,128)S(1)}, u32[]{:S(2)}, u32[]{:S(2)}) collective-permute-start(f32[27,8,256]{2,1,0:T(8,128)S(1)} %add.456), channel_id=1, source_target_pairs={{0,64},{16,80},{32,96},{48,112},{64,0},{80,16},{96,32},{112,48},{1... | collective-permute-start | bytes 663560 | tf_op jit(solution)/shard_map/ppermute | solution.py:219
  253.7 5.2 %collective-permute-done.18 = f32[27,8,256]{2,1,0:T(8,128)S(1)} collective-permute-done((f32[27,8,256]{2,1,0:T(8,128)S(1)}, f32[27,8,256]{2,1,0:T(8,128)S(1)}, u32[]{:S(2)}, u32[]{:S(2)}) %collective-permute-start.18) | collective-permute-done | bytes 221216 | tf_op jit(solution)/shard_map/ppermute | solution.py:219
  259.0 5.8 %collective-permute-start.19 = (f32[27,8,256]{2,1,0:T(8,128)S(1)}, f32[27,8,256]{2,1,0:T(8,128)S(1)}, u32[]{:S(2)}, u32[]{:S(2)}) collective-permute-start(f32[27,8,256]{2,1,0:T(8,128)S(1)} %add.457), channel_id=1, source_target_pairs={{0,16},{16,0},{32,48},{48,32},{64,80},{80,64},{96,112},{112,96},{1... | collective-permute-start | bytes 663560 | tf_op jit(solution)/shard_map/ppermute | solution.py:221
  (141 shorter events, 66.5 us)
Async XLA Ops:
  10.0 69.8 %all-to-all-start = ((bf16[16,4,128,256]{3,2,1,0:T(8,128)(2,1)}), bf16[16,4,128,256]{3,2,1,0:T(8,128)(2,1)}, u32[]{:S(2)}, u32[]{:S(2)}) async-start(bf16[16,4,128,256]{3,2,1,0:T(8,128)(2,1)} %copy.77), calls=%async_computation | async-start | bytes 8388608 | tf_op jit(solution)/shard_map/all_to_all | solution.py:283
  62.0 30.6 %copy-start.1 = (bf16[2048,256]{1,0:T(8,128)(2,1)S(1)}, bf16[2048,256]{1,0:T(8,128)(2,1)}, u32[]{:S(2)}) copy-start(bf16[2048,256]{1,0:T(8,128)(2,1)} %param.4) | copy-start | bytes 3145732
  79.8 61.5 %all-to-all-start.1 = ((bf16[16,4,128,256]{3,1,2,0:T(4,128)(2,1)}), bf16[16,4,128,256]{3,1,2,0:T(4,128)(2,1)}, u32[]{:S(2)}, u32[]{:S(2)}) async-start(bf16[16,4,128,256]{3,1,2,0:T(4,128)(2,1)} %copy.85), calls=%async_computation.1 | async-start | bytes 8388608 | tf_op jit(solution)/shard_map/all_to_all | solution.py:314
  90.3 10.8 %copy-start.4 = (bf16[2048,256]{1,0:T(8,128)(2,1)S(1)}, bf16[2048,256]{1,0:T(8,128)(2,1)}, u32[]{:S(2)}) copy-start(bf16[2048,256]{1,0:T(8,128)(2,1)} %param.7) | copy-start | bytes 3145732
  93.5 10.2 %collective-permute-start = (bf16[4,128,256]{2,1,0:T(8,128)(2,1)S(1)}, bf16[4,128,256]{2,1,0:T(8,128)(2,1)S(1)}, u32[]{:S(2)}, u32[]{:S(2)}) collective-permute-start(bf16[4,128,256]{2,1,0:T(8,128)(2,1)S(1)} %get-tuple-element.53), channel_id=1, source_target_pairs={{0,16},{16,32},{32,48},{48,64},{64,80},{80,96},{96,112},{1,17},{17... | collective-permute-start | bytes 786440 | tf_op jit(solution)/shard_map/ppermute | solution.py:22
  99.0 8.1 %collective-permute-start.1 = (bf16[4,128,256]{2,1,0:T(8,128)(2,1)S(1)}, bf16[4,128,256]{2,1,0:T(8,128)(2,1)}, u32[]{:S(2)}, u32[]{:S(2)}) collective-permute-start(bf16[4,128,256]{2,1,0:T(8,128)(2,1)S(1)} %get-tuple-element.54), channel_id=1, source_target_pairs={{16,0},{32,16},{48,32},{64,48},{80,64},{96,80},{112,96},{17,1},{33... | collective-permute-start | bytes 786440 | tf_op jit(solution)/shard_map/ppermute | solution.py:24
  146.9 21.0 %collective-permute-start.2 = (f32[27,16,8,256]{3,2,0,1:T(8,128)}, f32[27,16,8,256]{3,2,0,1:T(8,128)}, u32[]{:S(2)}, u32[]{:S(2)}) collective-permute-start(f32[27,16,8,256]{3,2,0,1:T(8,128)} %bitcast.150), channel_id=1, source_target_pairs={{0,16},{16,0},{32,48},{48,32},{64,80},{80,64},{96,112},{112,96},{1... | collective-permute-start | bytes 10616840 | tf_op jit(solution)/shard_map/ppermute | solution.py:182
  154.3 8.0 %collective-permute-start.16 = (bf16[4,128,256]{2,1,0:T(8,128)(2,1)}, bf16[4,128,256]{2,1,0:T(8,128)(2,1)}, u32[]{:S(2)}, u32[]{:S(2)}) collective-permute-start(bf16[4,128,256]{2,1,0:T(8,128)(2,1)} %get-tuple-element.38), channel_id=1, source_target_pairs={{16,0},{32,16},{48,32},{64,48},{80,64},{96,80},{112,96},{17,1},{33... | collective-permute-start | bytes 786440 | tf_op jit(solution)/shard_map/ppermute | solution.py:24
  156.3 8.9 %collective-permute-start.15 = (bf16[4,128,256]{2,1,0:T(8,128)(2,1)}, bf16[4,128,256]{2,1,0:T(8,128)(2,1)}, u32[]{:S(2)}, u32[]{:S(2)}) collective-permute-start(bf16[4,128,256]{2,1,0:T(8,128)(2,1)} %get-tuple-element.37), channel_id=1, source_target_pairs={{0,16},{16,32},{32,48},{48,64},{64,80},{80,96},{96,112},{1,17},{17... | collective-permute-start | bytes 786440 | tf_op jit(solution)/shard_map/ppermute | solution.py:22
  170.8 28.3 %collective-permute-start.3 = (f32[4,27,8,128]{3,2,1,0:T(8,128)S(1)}, f32[4,27,8,128]{3,2,1,0:T(8,128)S(1)}, u32[]{:S(2)}, u32[]{:S(2)}) collective-permute-start(f32[4,27,8,128]{3,2,1,0:T(8,128)S(1)} %get-tuple-element.46), channel_id=1, source_target_pairs={{0,1},{1,2},{2,3},{3,0},{4,5},{5,6},{6,7},{7,4},{8,9},{9,10},{10,1... | collective-permute-start | bytes 1327112 | tf_op jit(solution)/shard_map/ppermute | solution.py:207
  196.6 10.3 %collective-permute-start.9 = (f32[4,27,8,128]{3,2,1,0:T(8,128)S(1)}, f32[4,27,8,128]{3,2,1,0:T(8,128)S(1)}, u32[]{:S(2)}, u32[]{:S(2)}) collective-permute-start(f32[4,27,8,128]{3,2,1,0:T(8,128)S(1)} %get-tuple-element.52), channel_id=1, source_target_pairs={{0,3},{1,0},{2,1},{3,2},{4,7},{5,4},{6,5},{7,6},{8,11},{9,8},{10,9... | collective-permute-start | bytes 1327112 | tf_op jit(solution)/shard_map/ppermute | solution.py:207
  199.2 11.3 %collective-permute-start.4 = (f32[4,27,8,128]{3,2,1,0:T(8,128)S(1)}, f32[4,27,8,128]{3,2,1,0:T(8,128)S(1)}, u32[]{:S(2)}, u32[]{:S(2)}) collective-permute-start(f32[4,27,8,128]{3,2,1,0:T(8,128)S(1)} %get-tuple-element.44), channel_id=1, source_target_pairs={{0,1},{1,2},{2,3},{3,0},{4,5},{5,6},{6,7},{7,4},{8,9},{9,10},{10,1... | collective-permute-start | bytes 1327112 | tf_op jit(solution)/shard_map/ppermute | solution.py:207
  207.1 12.1 %collective-permute-start.10 = (f32[4,27,8,128]{3,2,1,0:T(8,128)S(1)}, f32[4,27,8,128]{3,2,1,0:T(8,128)S(1)}, u32[]{:S(2)}, u32[]{:S(2)}) collective-permute-start(f32[4,27,8,128]{3,2,1,0:T(8,128)S(1)} %get-tuple-element.50), channel_id=1, source_target_pairs={{0,3},{1,0},{2,1},{3,2},{4,7},{5,4},{6,5},{7,6},{8,11},{9,8},{10,9... | collective-permute-start | bytes 1327112 | tf_op jit(solution)/shard_map/ppermute | solution.py:207
  210.7 12.6 %collective-permute-start.5 = (f32[4,27,8,128]{3,2,1,0:T(8,128)S(1)}, f32[4,27,8,128]{3,2,1,0:T(8,128)S(1)}, u32[]{:S(2)}, u32[]{:S(2)}) collective-permute-start(f32[4,27,8,128]{3,2,1,0:T(8,128)S(1)} %get-tuple-element.42), channel_id=1, source_target_pairs={{0,1},{1,2},{2,3},{3,0},{4,5},{5,6},{6,7},{7,4},{8,9},{9,10},{10,1... | collective-permute-start | bytes 1327112 | tf_op jit(solution)/shard_map/ppermute | solution.py:207
  219.3 13.1 %collective-permute-start.11 = (f32[4,27,8,128]{3,2,1,0:T(8,128)S(1)}, f32[4,27,8,128]{3,2,1,0:T(8,128)S(1)}, u32[]{:S(2)}, u32[]{:S(2)}) collective-permute-start(f32[4,27,8,128]{3,2,1,0:T(8,128)S(1)} %get-tuple-element.48), channel_id=1, source_target_pairs={{0,3},{1,0},{2,1},{3,2},{4,7},{5,4},{6,5},{7,6},{8,11},{9,8},{10,9... | collective-permute-start | bytes 1327112 | tf_op jit(solution)/shard_map/ppermute | solution.py:207
  223.3 9.3 %collective-permute-start.6 = (f32[27,8,128]{2,1,0:T(8,128)S(1)}, f32[27,8,128]{2,1,0:T(8,128)S(1)}, u32[]{:S(2)}, u32[]{:S(2)}) collective-permute-start(f32[27,8,128]{2,1,0:T(8,128)S(1)} %dynamic-slice_bitcast_fusion.15), channel_id=1, source_target_pairs={{0,4},{1,5},{2,6},{3,7},{4,8},{5,9},{6,10},{7,11},{8,12},{9,13},{1... | collective-permute-start | bytes 331784 | tf_op jit(solution)/shard_map/ppermute | solution.py:207
  232.5 4.2 %collective-permute-start.12 = (f32[27,8,128]{2,1,0:T(8,128)S(1)}, f32[27,8,128]{2,1,0:T(8,128)S(1)}, u32[]{:S(2)}, u32[]{:S(2)}) collective-permute-start(f32[27,8,128]{2,1,0:T(8,128)S(1)} %dynamic-slice_bitcast_fusion.11), channel_id=1, source_target_pairs={{0,12},{1,13},{2,14},{3,15},{4,0},{5,1},{6,2},{7,3},{8,4},{9,5},{1... | collective-permute-start | bytes 331784 | tf_op jit(solution)/shard_map/ppermute | solution.py:207
  232.7 5.7 %collective-permute-start.7 = (f32[27,8,128]{2,1,0:T(8,128)S(1)}, f32[27,8,128]{2,1,0:T(8,128)S(1)}, u32[]{:S(2)}, u32[]{:S(2)}) collective-permute-start(f32[27,8,128]{2,1,0:T(8,128)S(1)} %get-tuple-element.60), channel_id=1, source_target_pairs={{0,4},{1,5},{2,6},{3,7},{4,8},{5,9},{6,10},{7,11},{8,12},{9,13},{1... | collective-permute-start | bytes 331784 | tf_op jit(solution)/shard_map/ppermute | solution.py:207
  236.8 3.7 %collective-permute-start.13 = (f32[27,8,128]{2,1,0:T(8,128)S(1)}, f32[27,8,128]{2,1,0:T(8,128)S(1)}, u32[]{:S(2)}, u32[]{:S(2)}) collective-permute-start(f32[27,8,128]{2,1,0:T(8,128)S(1)} %get-tuple-element.64), channel_id=1, source_target_pairs={{0,12},{1,13},{2,14},{3,15},{4,0},{5,1},{6,2},{7,3},{8,4},{9,5},{1... | collective-permute-start | bytes 331784 | tf_op jit(solution)/shard_map/ppermute | solution.py:207
  238.5 4.9 %collective-permute-start.8 = (f32[27,8,128]{2,1,0:T(8,128)S(1)}, f32[27,8,128]{2,1,0:T(8,128)S(1)}, u32[]{:S(2)}, u32[]{:S(2)}) collective-permute-start(f32[27,8,128]{2,1,0:T(8,128)S(1)} %get-tuple-element.58), channel_id=1, source_target_pairs={{0,4},{1,5},{2,6},{3,7},{4,8},{5,9},{6,10},{7,11},{8,12},{9,13},{1... | collective-permute-start | bytes 331784 | tf_op jit(solution)/shard_map/ppermute | solution.py:207
  240.5 4.6 %collective-permute-start.14 = (f32[27,8,128]{2,1,0:T(8,128)S(1)}, f32[27,8,128]{2,1,0:T(8,128)S(1)}, u32[]{:S(2)}, u32[]{:S(2)}) collective-permute-start(f32[27,8,128]{2,1,0:T(8,128)S(1)} %get-tuple-element.62), channel_id=1, source_target_pairs={{0,12},{1,13},{2,14},{3,15},{4,0},{5,1},{6,2},{7,3},{8,4},{9,5},{1... | collective-permute-start | bytes 331784 | tf_op jit(solution)/shard_map/ppermute | solution.py:207
  245.2 4.9 %collective-permute-start.17 = (f32[27,8,256]{2,1,0:T(8,128)S(1)}, f32[27,8,256]{2,1,0:T(8,128)S(1)}, u32[]{:S(2)}, u32[]{:S(2)}) collective-permute-start(f32[27,8,256]{2,1,0:T(8,128)S(1)} %pad_maximum_fusion.2), channel_id=1, source_target_pairs={{0,32},{16,48},{32,0},{48,16},{64,96},{80,112},{96,64},{112,80},{1... | collective-permute-start | bytes 663560 | tf_op jit(solution)/shard_map/ppermute | solution.py:219
  250.0 8.9 %collective-permute-start.18 = (f32[27,8,256]{2,1,0:T(8,128)S(1)}, f32[27,8,256]{2,1,0:T(8,128)S(1)}, u32[]{:S(2)}, u32[]{:S(2)}) collective-permute-start(f32[27,8,256]{2,1,0:T(8,128)S(1)} %add.456), channel_id=1, source_target_pairs={{0,64},{16,80},{32,96},{48,112},{64,0},{80,16},{96,32},{112,48},{1... | collective-permute-start | bytes 663560 | tf_op jit(solution)/shard_map/ppermute | solution.py:219
  259.0 6.9 %collective-permute-start.19 = (f32[27,8,256]{2,1,0:T(8,128)S(1)}, f32[27,8,256]{2,1,0:T(8,128)S(1)}, u32[]{:S(2)}, u32[]{:S(2)}) collective-permute-start(f32[27,8,256]{2,1,0:T(8,128)S(1)} %add.457), channel_id=1, source_target_pairs={{0,16},{16,0},{32,48},{48,32},{64,80},{80,64},{96,112},{112,96},{1... | collective-permute-start | bytes 663560 | tf_op jit(solution)/shard_map/ppermute | solution.py:221
  (4 other events, 11.0 us)

commit v13 on v11

--- a/solution.py
+++ b/solution.py
@@ -79,19 +79,19 @@
     )(table_index.reshape(-1), grad_blocks, weights)
 
 
-def _conv_kernel(idx_ref, table_ref, w_ref, out_ref, g_ref, acc_ref):
+def _conv_kernel(idx_ref, table_ref, w_ref, acc_in_ref, out_ref, g_ref, acc_ref, *, first):
     k = pl.program_id(0)
     voxels = table_ref.shape[1]
     blocks = out_ref.shape[0] // voxels
     rows = table_ref.shape[0]
     for b in range(blocks):
-        t = jnp.clip(idx_ref[k * blocks + b], 0, rows - 1)
+        t = jnp.clip(idx_ref[(k + first) * blocks + b], 0, rows - 1)
         g_ref[pl.ds(b * voxels, voxels), :] = table_ref[t]
     part = jnp.dot(g_ref[...], w_ref[0], preferred_element_type=jnp.float32)
 
     @pl.when(k == 0)
     def _():
-        acc_ref[...] = part
+        acc_ref[...] = acc_in_ref[...] + part
 
     @pl.when(k > 0)
     def _():
@@ -102,18 +102,19 @@
         out_ref[...] = acc_ref[...].astype(out_ref.dtype)
 
 
-def conv_rows(table_index, table, weights, count):
+def conv_rows(table_index, table, weights, acc_in, first, last, out_dtype):
     rows, voxels, channels = table.shape
-    offsets = weights.shape[0]
+    count = acc_in.shape[0]
     return pl.pallas_call(
-        _conv_kernel,
-        out_shape=jax.ShapeDtypeStruct((count, channels), jnp.bfloat16),
+        functools.partial(_conv_kernel, first=first),
+        out_shape=jax.ShapeDtypeStruct((count, channels), out_dtype),
         grid_spec=pltpu.PrefetchScalarGridSpec(
             num_scalar_prefetch=1,
-            grid=(offsets,),
+            grid=(last - first,),
             in_specs=[
                 pl.BlockSpec((rows, voxels, channels), lambda k, idx: (0, 0, 0)),
-                pl.BlockSpec((1, channels, channels), lambda k, idx: (k, 0, 0)),
+                pl.BlockSpec((1, channels, channels), lambda k, idx: (k + first, 0, 0)),
+                pl.BlockSpec((count, channels), lambda k, idx: (0, 0)),
             ],
             out_specs=pl.BlockSpec((count, channels), lambda k, idx: (0, 0)),
             scratch_shapes=[
@@ -122,14 +123,14 @@
             ],
         ),
         cost_estimate=pl.CostEstimate(
-            flops=2 * offsets * count * channels * channels,
+            flops=2 * (last - first) * count * channels * channels,
             transcendentals=0,
-            bytes_accessed=table.size * 2 + weights.size * 2 + count * channels * 2,
+            bytes_accessed=table.size * 2 + (last - first) * channels * channels * 2 + count * channels * 8,
         ),
         compiler_params=pltpu.CompilerParams(
             dimension_semantics=("arbitrary",), vmem_limit_bytes=56 * 1024 * 1024
         ),
-    )(table_index.reshape(-1), table, weights)
+    )(table_index.reshape(-1), table, weights, acc_in)
 
 
 def _weight_grad_kernel(idx_ref, table_ref, gradt_ref, wg_ref, g_ref, *, scale):
@@ -171,7 +172,7 @@
     )(table_index.reshape(-1), table, gradt)
 
 
-def weight_grad_sum(term, n_shard, n_region):
+def weight_grad_sum(term, n_shard, n_region, between):
     offsets, channels, width = term.shape
     sub = channels // (n_shard * 2)
     core = lax.axis_index("region") % 2
@@ -180,7 +181,38 @@
     theirs = lax.dynamic_index_in_dim(view, 1 - core, 2, keepdims=False)
     swap = [(i, i ^ 1) for i in range(n_region)]
     pair = jnp.swapaxes(mine + lax.ppermute(theirs, "region", swap), 0, 1)
-    return lax.psum_scatter(pair, "shard", scatter_dimension=0, tiled=True)[0]
+    inner = 4 if n_shard % 4 == 0 else n_shard
+    outer = n_shard // inner
+    pair = pair.reshape((outer, inner) + pair.shape[1:])
+    half = width // 2
+    values = [(pair[..., :half], 1), (pair[..., half:], -1)]
+    values = ring_scatter(values, 1, inner, 1, n_shard, between)
+    values = ring_scatter(values, 0, outer, inner, n_shard, None)
+    return jnp.concatenate([v for v, _ in values], axis=-1)
+
+
+def ring_scatter(values, axis, ring, stride, n_shard, between):
+    if ring == 1:
+        return [(lax.index_in_dim(v, 0, axis, keepdims=False), st) for v, st in values]
+    shard = lax.axis_index("shard")
+    place = (shard // stride) % ring
+    for t in range(ring - 1):
+        stepped = []
+        for value, step in values:
+            pairs = []
+            for i in range(n_shard):
+                p = (i // stride) % ring
+                pairs.append((i, i + stride * ((p + step) % ring - p)))
+            send = lax.dynamic_index_in_dim(value, (place - step * (t + 1)) % ring, axis, keepdims=False)
+            got = lax.ppermute(send, "shard", pairs)
+            where = (place - step * (t + 2)) % ring
+            current = lax.dynamic_index_in_dim(value, where, axis, keepdims=False)
+            stepped.append((lax.dynamic_update_index_in_dim(value, current + got, where, axis), step))
+        values = stepped
+        if between is not None:
+            tied = between(t, ring - 1, [v for v, _ in values])
+            values = [(v, st) for v, (_, st) in zip(tied, values)]
+    return [(lax.dynamic_index_in_dim(v, place, axis, keepdims=False), st) for v, st in values]
 
 
 def weight_grad_finish(part, n_region):
@@ -306,9 +338,19 @@
     grad_rows = grad_blocks.reshape(blocks_dev * voxels, channels)
     kernel_term = weight_grad_terms(table_index, table, grad_rows.T, offsets, scale)
     kernel_term, returned = lax.optimization_barrier((kernel_term, returned))
-    scattered = weight_grad_sum(kernel_term, n_shard, n_region)
     kernel_term, table = lax.optimization_barrier((kernel_term, table))
-    conv_out = conv_rows(table_index, table, weights, blocks_dev * voxels)
+    state = {"acc": jnp.zeros((blocks_dev * voxels, channels), jnp.float32)}
+
+    def between(t, pieces, vals):
+        first = offsets * t // pieces
+        last = offsets * (t + 1) // pieces
+        dtype = jnp.bfloat16 if last == offsets else jnp.float32
+        out = conv_rows(table_index, table, weights, state["acc"], first, last, dtype)
+        vals, state["acc"] = lax.optimization_barrier((vals, out))
+        return vals
+
+    scattered = weight_grad_sum(kernel_term, n_shard, n_region, between)
+    conv_out = state["acc"]
     input_acc = table_grad[:blocks_dev]
     input_acc = input_acc + jnp.einsum(
         "pcj,pcvd->jvd",

time: 266 us -> 269 us (1.011)
  waiting for transfers between devices: 68.8 us -> 50.3 us
  between operations: 14.3 us -> 1.59 us
  Pallas kernels: 73.3 us -> 84.8 us
  starting transfers between devices: 48.5 us -> 58.5 us
  local copies, waits for them, and re-layouts: 29.4 us -> 34.6 us
  matrix products: 9.21 us -> 12.5 us
    unnamed x2 -> x0, waiting for transfers between devices: 26.9 us -> none
    ppermute x0 -> x12, starting transfers between devices: none -> 14.2 us  [ring_scatter(): got = lax.ppermute(send, 'shard', pairs)]
    pallas_call x1 -> x3, Pallas kernels: 25.5 us -> 36.9 us  [conv_rows(): pl.pallas_call(functools.partial(_conv_kernel, first=first), out_shape=ja...]
    ppermute x0 -> x12, waiting for transfers between devices: none -> 7.94 us  [ring_scatter(): got = lax.ppermute(send, 'shard', pairs)]
    ppermute x1, waiting for transfers between devices: 5.85 us -> 0.01 us  [weight_grad_sum(): pair = jnp.swapaxes(mine + lax.ppermute(theirs, 'region', swap), 0, 1)]
    ppermute x2, waiting for transfers between devices: 7.41 us -> 11.2 us  [weight_grad_finish(): lax.ppermute(part, 'region', [(i, i ^ step) for i in range(n_region)])]
    dynamic_update_slice x0 -> x12, other arithmetic: none -> 3.71 us  [ring_scatter(): lax.dynamic_update_index_in_dim(value, current + got, where, axis)]
    dynamic_slice x0 -> x10, local copies, waits for them, and re-layouts: none -> 3.11 us  [ring_scatter(): current = lax.dynamic_index_in_dim(value, where, axis, keepdims=False)]
  transfers between devices with their start and end apart: 11 -> 22, of which waited for: 10 -> 10; matrix products, arithmetic and copies ran while one was open for 15% -> 18% of each run, Pallas kernels for 28% -> 32%
where the time goes in v13:
time: 269 us; the launch traced here: 265 us
  Pallas kernels  84.8 us (32%)
  starting transfers between devices  58.5 us (22%)
  waiting for transfers between devices  50.3 us (19%)
  local copies, waits for them, and re-layouts  34.6 us (13%)
  other arithmetic  23.1 us (9%)
  matrix products  12.5 us (5%)
    pallas_call x3, Pallas kernels, conv_rows(): pl.pallas_call(functools.partial(_conv_kernel, first=first), out_shape=ja...  36.9 us
    pallas_call x1, Pallas kernels, table_grad_sums(): pl.pallas_call(_table_grad_kernel, out_shape=jax.ShapeDtypeStruct((rows,...  27.2 us
    pallas_call x1, Pallas kernels, weight_grad_terms(): pl.pallas_call(functools.partial(_weight_grad_kernel, scale=scale), out_s...  20.6 us
    all_to_all x1, waiting for transfers between devices, body(): lax.all_to_all(outgoing, 'shard', split_axis=0, concat_axis=0, tiled=True)  18.1 us
    ppermute x12, starting transfers between devices, ring_scatter(): got = lax.ppermute(send, 'shard', pairs)  14.2 us
    ppermute x2, waiting for transfers between devices, weight_grad_finish(): lax.ppermute(part, 'region', [(i, i ^ step) for i in range(n_region)])  11.2 us
    all_to_all x1, starting transfers between devices, body(): lax.all_to_all(remote_sums[:n_shard * capacity].reshape(n_shard, capacity...  9.75 us
    ppermute x2, starting transfers between devices, padded(): lax.ppermute(tail, axis, [(i, (i + 1) % count) for i in range(ends)])  9.5 us
  transfers between devices with their start and end apart: 22, of which 10 were waited for; matrix products, arithmetic and copies ran while one was open for 18% of the time, Pallas kernels for 32%

profile of v13, /device:TPU:1, one launch (start us, length us, event | category | flops | bytes accessed | tf_op | source)
XLA Modules:
  0.0 265.4 jit_solution(6665733225165972802)
XLA Ops:
  6.5 3.4 %copy.77 = bf16[16,4,128,256]{3,2,1,0:T(8,128)(2,1)} copy(bf16[16,4,128,256]{3,0,2,1:T(8,128)(2,1)S(1)} %convolution_convert_fusion) | data formatting | bytes 8388608 | tf_op jit(solution)/shard_map/convert_element_type | solution.py:280
  9.9 8.7 %all-to-all-start = ((bf16[16,4,128,256]{3,2,1,0:T(8,128)(2,1)}), bf16[16,4,128,256]{3,2,1,0:T(8,128)(2,1)}, u32[]{:S(2)}, u32[]{:S(2)}) async-start(bf16[16,4,128,256]{3,2,1,0:T(8,128)(2,1)} %copy.77), calls=%async_computation | async-start | bytes 8388608 | tf_op jit(solution)/shard_map/all_to_all | solution.py:287
  21.4 27.2 %shard_map.67 = f32[89,128,256]{2,1,0:T(8,128)} custom-call(s32[432]{0:T(512)} %reshape.267.idx_ref, bf16[16,128,256]{2,1,0:T(8,128)(2,1)} %bitcast.158, bf16[27,256,256]{2,1,0:T(8,128)(2,1)} %w_ref.7), custom_call_target="tpu_custom_call" | custom-call | flops 7247757312 | bytes 16252928 | tf_op jit(solution)/shard_map/pallas_call | solution.py:59
  48.7 5.2 %convert.7 = bf16[89,128,256]{2,1,0:T(8,128)(2,1)S(1)} convert(f32[89,128,256]{2,1,0:T(8,128)} %shard_map.67) | non-fusion elementwise | flops 2916352 | bytes 17498112 | tf_op jit(solution)/shard_map/convert.4
  56.4 5.5 %copy.85 = bf16[16,4,128,256]{3,1,2,0:T(4,128)(2,1)} copy(bf16[16,4,128,256]{3,2,1,0:T(8,128)(2,1)S(1)} %bitcast.151) | data formatting | bytes 8388608 | tf_op jit(solution)/shard_map/reshape | solution.py:319
  62.0 18.1 %all-to-all-done = bf16[16,4,128,256]{3,2,1,0:T(8,128)(2,1)} async-done(((bf16[16,4,128,256]{3,2,1,0:T(8,128)(2,1)}), bf16[16,4,128,256]{3,2,1,0:T(8,128)(2,1)}, u32[]{:S(2)}, u32[]{:S(2)}) %all-to-all-start) | async-done | bytes 4194336 | tf_op jit(solution)/shard_map/all_to_all | solution.py:287
  80.1 9.7 %all-to-all-start.1 = ((bf16[16,4,128,256]{3,1,2,0:T(4,128)(2,1)}), bf16[16,4,128,256]{3,1,2,0:T(4,128)(2,1)}, u32[]{:S(2)}, u32[]{:S(2)}) async-start(bf16[16,4,128,256]{3,1,2,0:T(4,128)(2,1)} %copy.85), calls=%async_computation.1 | async-start | bytes 8388608 | tf_op jit(solution)/shard_map/all_to_all | solution.py:318
  92.5 5.9 %collective-permute-start = (bf16[4,128,256]{2,1,0:T(8,128)(2,1)S(1)}, bf16[4,128,256]{2,1,0:T(8,128)(2,1)S(1)}, u32[]{:S(2)}, u32[]{:S(2)}) collective-permute-start(bf16[4,128,256]{2,1,0:T(8,128)(2,1)S(1)} %get-tuple-element.73), channel_id=1, source_target_pairs={{0,16},{16,32},{32,48},{48,64},{64,80},{80,96},{96,112},{1,17},{17... | collective-permute-start | bytes 786440 | tf_op jit(solution)/shard_map/ppermute | solution.py:22
  102.1 4.4 %collective-permute-done.1 = bf16[4,128,256]{2,1,0:T(8,128)(2,1)} collective-permute-done((bf16[4,128,256]{2,1,0:T(8,128)(2,1)S(1)}, bf16[4,128,256]{2,1,0:T(8,128)(2,1)}, u32[]{:S(2)}, u32[]{:S(2)}) %collective-permute-start.1) | collective-permute-done | bytes 262176 | tf_op jit(solution)/shard_map/ppermute | solution.py:24
  112.8 20.6 %shard_map.68 = f32[27,256,256]{2,1,0:T(8,128)} custom-call(s32[432]{0:T(512)} %reshape.267.idx_ref, bf16[89,128,256]{2,1,0:T(8,128)(2,1)} %copy-done, bf16[256,2048]{1,0:T(8,128)(2,1)} %bitcast.159), custom_call_target="tpu_custom_call" | custom-call | flops 7247757312 | bytes 13959168 | tf_op jit(solution)/shard_map/pallas_call | solution.py:151
  133.4 5.4 %all-to-all-done.1 = bf16[16,4,128,256]{3,1,2,0:T(4,128)(2,1)} async-done(((bf16[16,4,128,256]{3,1,2,0:T(4,128)(2,1)}), bf16[16,4,128,256]{3,1,2,0:T(4,128)(2,1)}, u32[]{:S(2)}, u32[]{:S(2)}) %all-to-all-start.1) | async-done | bytes 4194336 | tf_op jit(solution)/shard_map/all_to_all | solution.py:318
  138.9 3.6 %constant_dynamic-slice_fusion.11 = (f32[27,16,1,8,256]{4,3,2,1,0:T(8,128)S(1)}, f32[27,16,1,8,256]{4,3,2,1,0:T(8,128)S(1)}) fusion(f32[27,16,2,8,256]{4,3,2,1,0:T(8,128)} %bitcast.156, s32[]{:T(128)S(6)} %select_n.254, s32[]{:T(128)S(6)} %select_n.255), kind=kLoop, calls=%fused_computation.101 | loop fusion | bytes 14155784 | tf_op jit(solution)/shard_map/jit(dynamic_index_in_dim)/dynamic_slice | solution.py:180
  144.5 7.2 %collective-permute-start.2 = (f32[27,16,8,256]{3,2,0,1:T(8,128)}, f32[27,16,8,256]{3,2,0,1:T(8,128)}, u32[]{:S(2)}, u32[]{:S(2)}) collective-permute-start(f32[27,16,8,256]{3,2,0,1:T(8,128)} %bitcast.150), channel_id=1, source_target_pairs={{0,16},{16,0},{32,48},{48,32},{64,80},{80,64},{96,112},{112,96},{1... | collective-permute-start | bytes 10616840 | tf_op jit(solution)/shard_map/ppermute | solution.py:183
  155.5 3.6 %collective-permute-start.15 = (bf16[4,128,256]{2,1,0:T(8,128)(2,1)}, bf16[4,128,256]{2,1,0:T(8,128)(2,1)}, u32[]{:S(2)}, u32[]{:S(2)}) collective-permute-start(bf16[4,128,256]{2,1,0:T(8,128)(2,1)} %get-tuple-element.57), channel_id=1, source_target_pairs={{0,16},{16,32},{32,48},{48,64},{64,80},{80,96},{96,112},{1,17},{17... | collective-permute-start | bytes 786440 | tf_op jit(solution)/shard_map/ppermute | solution.py:22
  172.1 12.4 %shard_map.69.acc_in_ref = f32[2048,256]{1,0:T(8,128)} custom-call(s32[432]{0:T(512)} %reshape.267.idx_ref, bf16[89,128,256]{2,1,0:T(8,128)(2,1)} %copy-done, bf16[27,256,256]{2,1,0:T(8,128)(2,1)} %w_ref.7, f32[2048,256]{1,0:T(8,128)} %broadcast_in_dim.116.acc_in_ref), custom_call_target="tpu_custom_call" | custom-call | flops 2415919104 | bytes 11206656 | tf_op jit(solution)/shard_map/pallas_call | solution.py:108
  186.7 4.6 %fusion.3 = f32[16,128,256]{2,0,1:T(8,128)S(1)} fusion(bf16[16,4,128,256]{3,1,2,0:T(4,128)(2,1)} %all-to-all-done.1, s32[16,16]{0,1:T(8,128)S(1)} %copy.74, pred[16,16]{0,1:T(8,128)(4,1)S(1)} %copy.73), kind=kOutput, calls=%fused_computation.10 | convolution fusion | flops 67110912 | bytes 6292736 | tf_op jit(solution)/shard_map/pcj,pcvd->jvd/dot_general | solution.py:355
  192.5 12.5 %shard_map.70.acc_in_ref = f32[2048,256]{1,0:T(8,128)} custom-call(s32[432]{0:T(512)} %reshape.267.idx_ref, bf16[89,128,256]{2,1,0:T(8,128)(2,1)} %copy-done, bf16[27,256,256]{2,1,0:T(8,128)(2,1)} %w_ref.7, f32[2048,256]{1,0:T(8,128)} %shard_map.69.acc_in_ref), custom_call_target="tpu_custom_call" | custom-call | flops 2415919104 | bytes 11206656 | tf_op jit(solution)/shard_map/pallas_call | solution.py:108
  210.7 5.9 %fusion.2 = bf16[16,128,256]{2,1,0:T(8,128)(2,1)} fusion(f32[16,128,256]{2,0,1:T(8,128)S(1)} %copy-done.3, f32[16,128,256]{2,0,1:T(8,128)S(1)} %fusion.13, f32[16,128,256]{2,0,1:T(8,128)S(1)} %fusion.3, f32[89,128,256]{2,1,0:T(8,128)} %shard_map.67), kind=kLoop, calls=%fused_computation.6 | loop fusion | flops 2097152 | bytes 9437184 | tf_op jit(solution)/shard_map/convert_element_type | solution.py:374
  216.7 12.0 %shard_map.71 = bf16[2048,256]{1,0:T(8,128)(2,1)} custom-call(s32[432]{0:T(512)} %reshape.267.idx_ref, bf16[89,128,256]{2,1,0:T(8,128)(2,1)} %copy-done, bf16[27,256,256]{2,1,0:T(8,128)(2,1)} %w_ref.7, f32[2048,256]{1,0:T(8,128)} %shard_map.70.acc_in_ref), custom_call_target="tpu_custom_call" | custom-call | flops 2415919104 | bytes 11206656 | tf_op jit(solution)/shard_map/pallas_call | solution.py:108
  235.1 2.9 %collective-permute-start.13 = (f32[27,8,128]{2,1,0:T(8,128)S(1)}, f32[27,8,128]{2,1,0:T(8,128)S(1)}, u32[]{:S(2)}, u32[]{:S(2)}) collective-permute-start(f32[27,8,128]{2,1,0:T(8,128)S(1)} %get-tuple-element.84), channel_id=1, source_target_pairs={{0,12},{1,13},{2,14},{3,15},{4,0},{5,1},{6,2},{7,3},{8,4},{9,5},{1... | collective-permute-start | bytes 331784 | tf_op jit(solution)/shard_map/ppermute | solution.py:207
  238.0 3.2 %collective-permute-done.10 = f32[27,8,128]{2,1,0:T(8,128)S(1)} collective-permute-done((f32[27,8,128]{2,1,0:T(8,128)S(1)}, f32[27,8,128]{2,1,0:T(8,128)S(1)}, u32[]{:S(2)}, u32[]{:S(2)}) %collective-permute-start.10) | collective-permute-done | bytes 110624 | tf_op jit(solution)/shard_map/ppermute | solution.py:207
  247.1 4.8 %collective-permute-done.17 = f32[27,8,256]{2,1,0:T(8,128)S(1)} collective-permute-done((f32[27,8,256]{2,1,0:T(8,128)S(1)}, f32[27,8,256]{2,1,0:T(8,128)S(1)}, u32[]{:S(2)}, u32[]{:S(2)}) %collective-permute-start.17) | collective-permute-done | bytes 221216 | tf_op jit(solution)/shard_map/ppermute | solution.py:223
  253.3 6.4 %collective-permute-done.18 = f32[27,8,256]{2,1,0:T(8,128)S(1)} collective-permute-done((f32[27,8,256]{2,1,0:T(8,128)S(1)}, f32[27,8,256]{2,1,0:T(8,128)S(1)}, u32[]{:S(2)}, u32[]{:S(2)}) %collective-permute-start.18) | collective-permute-done | bytes 221216 | tf_op jit(solution)/shard_map/ppermute | solution.py:223
  259.8 3.7 %collective-permute-start.19 = (f32[27,8,256]{2,1,0:T(8,128)S(1)}, f32[27,8,256]{2,1,0:T(8,128)S(1)}, u32[]{:S(2)}, u32[]{:S(2)}) collective-permute-start(f32[27,8,256]{2,1,0:T(8,128)S(1)} %add.452), channel_id=1, source_target_pairs={{0,16},{16,0},{32,48},{48,32},{64,80},{80,64},{96,112},{112,96},{1... | collective-permute-start | bytes 663560 | tf_op jit(solution)/shard_map/ppermute | solution.py:225
  (144 shorter events, 66.7 us)
Async XLA Ops:
  9.9 70.2 %all-to-all-start = ((bf16[16,4,128,256]{3,2,1,0:T(8,128)(2,1)}), bf16[16,4,128,256]{3,2,1,0:T(8,128)(2,1)}, u32[]{:S(2)}, u32[]{:S(2)}) async-start(bf16[16,4,128,256]{3,2,1,0:T(8,128)(2,1)} %copy.77), calls=%async_computation | async-start | bytes 8388608 | tf_op jit(solution)/shard_map/all_to_all | solution.py:287
  62.0 29.7 %copy-start.2 = (bf16[2048,256]{1,0:T(8,128)(2,1)S(1)}, bf16[2048,256]{1,0:T(8,128)(2,1)}, u32[]{:S(2)}) copy-start(bf16[2048,256]{1,0:T(8,128)(2,1)} %param.4) | copy-start | bytes 3145732
  80.1 58.8 %all-to-all-start.1 = ((bf16[16,4,128,256]{3,1,2,0:T(4,128)(2,1)}), bf16[16,4,128,256]{3,1,2,0:T(4,128)(2,1)}, u32[]{:S(2)}, u32[]{:S(2)}) async-start(bf16[16,4,128,256]{3,1,2,0:T(4,128)(2,1)} %copy.85), calls=%async_computation.1 | async-start | bytes 8388608 | tf_op jit(solution)/shard_map/all_to_all | solution.py:318
  89.8 10.7 %copy-start.4 = (bf16[2048,256]{1,0:T(8,128)(2,1)S(1)}, bf16[2048,256]{1,0:T(8,128)(2,1)}, u32[]{:S(2)}) copy-start(bf16[2048,256]{1,0:T(8,128)(2,1)} %param.7) | copy-start | bytes 3145732
  92.5 9.5 %collective-permute-start = (bf16[4,128,256]{2,1,0:T(8,128)(2,1)S(1)}, bf16[4,128,256]{2,1,0:T(8,128)(2,1)S(1)}, u32[]{:S(2)}, u32[]{:S(2)}) collective-permute-start(bf16[4,128,256]{2,1,0:T(8,128)(2,1)S(1)} %get-tuple-element.73), channel_id=1, source_target_pairs={{0,16},{16,32},{32,48},{48,64},{64,80},{80,96},{96,112},{1,17},{17... | collective-permute-start | bytes 786440 | tf_op jit(solution)/shard_map/ppermute | solution.py:22
  98.4 8.1 %collective-permute-start.1 = (bf16[4,128,256]{2,1,0:T(8,128)(2,1)S(1)}, bf16[4,128,256]{2,1,0:T(8,128)(2,1)}, u32[]{:S(2)}, u32[]{:S(2)}) collective-permute-start(bf16[4,128,256]{2,1,0:T(8,128)(2,1)S(1)} %get-tuple-element.74), channel_id=1, source_target_pairs={{16,0},{32,16},{48,32},{64,48},{80,64},{96,80},{112,96},{17,1},{33... | collective-permute-start | bytes 786440 | tf_op jit(solution)/shard_map/ppermute | solution.py:24
  144.5 20.0 %collective-permute-start.2 = (f32[27,16,8,256]{3,2,0,1:T(8,128)}, f32[27,16,8,256]{3,2,0,1:T(8,128)}, u32[]{:S(2)}, u32[]{:S(2)}) collective-permute-start(f32[27,16,8,256]{3,2,0,1:T(8,128)} %bitcast.150), channel_id=1, source_target_pairs={{0,16},{16,0},{32,48},{48,32},{64,80},{80,64},{96,112},{112,96},{1... | collective-permute-start | bytes 10616840 | tf_op jit(solution)/shard_map/ppermute | solution.py:183
  153.6 8.0 %collective-permute-start.16 = (bf16[4,128,256]{2,1,0:T(8,128)(2,1)}, bf16[4,128,256]{2,1,0:T(8,128)(2,1)}, u32[]{:S(2)}, u32[]{:S(2)}) collective-permute-start(bf16[4,128,256]{2,1,0:T(8,128)(2,1)} %get-tuple-element.58), channel_id=1, source_target_pairs={{16,0},{32,16},{48,32},{64,48},{80,64},{96,80},{112,96},{17,1},{33... | collective-permute-start | bytes 786440 | tf_op jit(solution)/shard_map/ppermute | solution.py:24
  155.5 11.9 %collective-permute-start.15 = (bf16[4,128,256]{2,1,0:T(8,128)(2,1)}, bf16[4,128,256]{2,1,0:T(8,128)(2,1)}, u32[]{:S(2)}, u32[]{:S(2)}) collective-permute-start(bf16[4,128,256]{2,1,0:T(8,128)(2,1)} %get-tuple-element.57), channel_id=1, source_target_pairs={{0,16},{16,32},{32,48},{48,64},{64,80},{80,96},{96,112},{1,17},{17... | collective-permute-start | bytes 786440 | tf_op jit(solution)/shard_map/ppermute | solution.py:22
  167.3 17.1 %collective-permute-start.4 = (f32[4,27,8,128]{3,2,1,0:T(8,128)S(1)}, f32[4,27,8,128]{3,2,1,0:T(8,128)S(1)}, u32[]{:S(2)}, u32[]{:S(2)}) collective-permute-start(f32[4,27,8,128]{3,2,1,0:T(8,128)S(1)} %get-tuple-element.70), channel_id=1, source_target_pairs={{0,3},{1,0},{2,1},{3,2},{4,7},{5,4},{6,5},{7,6},{8,11},{9,8},{10,9... | collective-permute-start | bytes 1327112 | tf_op jit(solution)/shard_map/ppermute | solution.py:207
  169.0 15.5 %collective-permute-start.3 = (f32[4,27,8,128]{3,2,1,0:T(8,128)S(1)}, f32[4,27,8,128]{3,2,1,0:T(8,128)S(1)}, u32[]{:S(2)}, u32[]{:S(2)}) collective-permute-start(f32[4,27,8,128]{3,2,1,0:T(8,128)S(1)} %get-tuple-element.72), channel_id=1, source_target_pairs={{0,1},{1,2},{2,3},{3,0},{4,5},{5,6},{6,7},{7,4},{8,9},{9,10},{10,1... | collective-permute-start | bytes 1327112 | tf_op jit(solution)/shard_map/ppermute | solution.py:207
  185.4 19.5 %collective-permute-start.6 = (f32[4,27,8,128]{3,2,1,0:T(8,128)}, f32[4,27,8,128]{3,2,1,0:T(8,128)}, u32[]{:S(2)}, u32[]{:S(2)}) collective-permute-start(f32[4,27,8,128]{3,2,1,0:T(8,128)} %get-tuple-element.66), channel_id=1, source_target_pairs={{0,3},{1,0},{2,1},{3,2},{4,7},{5,4},{6,5},{7,6},{8,11},{9,8},{10,9... | collective-permute-start | bytes 1327112 | tf_op jit(solution)/shard_map/ppermute | solution.py:207
  192.2 14.0 %collective-permute-start.5 = (f32[4,27,8,128]{3,2,1,0:T(8,128)}, f32[4,27,8,128]{3,2,1,0:T(8,128)}, u32[]{:S(2)}, u32[]{:S(2)}) collective-permute-start(f32[4,27,8,128]{3,2,1,0:T(8,128)} %get-tuple-element.68), channel_id=1, source_target_pairs={{0,1},{1,2},{2,3},{3,0},{4,5},{5,6},{6,7},{7,4},{8,9},{9,10},{10,1... | collective-permute-start | bytes 1327112 | tf_op jit(solution)/shard_map/ppermute | solution.py:207
  208.2 20.5 %collective-permute-start.8 = (f32[4,27,8,128]{3,2,1,0:T(8,128)}, f32[4,27,8,128]{3,2,1,0:T(8,128)}, u32[]{:S(2)}, u32[]{:S(2)}) collective-permute-start(f32[4,27,8,128]{3,2,1,0:T(8,128)} %get-tuple-element.62), channel_id=1, source_target_pairs={{0,3},{1,0},{2,1},{3,2},{4,7},{5,4},{6,5},{7,6},{8,11},{9,8},{10,9... | collective-permute-start | bytes 1327112 | tf_op jit(solution)/shard_map/ppermute | solution.py:207
  216.7 13.2 %collective-permute-start.7 = (f32[4,27,8,128]{3,2,1,0:T(8,128)S(1)}, f32[4,27,8,128]{3,2,1,0:T(8,128)S(1)}, u32[]{:S(2)}, u32[]{:S(2)}) collective-permute-start(f32[4,27,8,128]{3,2,1,0:T(8,128)S(1)} %get-tuple-element.64), channel_id=1, source_target_pairs={{0,1},{1,2},{2,3},{3,0},{4,5},{5,6},{6,7},{7,4},{8,9},{9,10},{10,1... | collective-permute-start | bytes 1327112 | tf_op jit(solution)/shard_map/ppermute | solution.py:207
  230.0 4.9 %collective-permute-start.9 = (f32[27,8,128]{2,1,0:T(8,128)S(1)}, f32[27,8,128]{2,1,0:T(8,128)S(1)}, u32[]{:S(2)}, u32[]{:S(2)}) collective-permute-start(f32[27,8,128]{2,1,0:T(8,128)S(1)} %dynamic-slice_bitcast_fusion.15), channel_id=1, source_target_pairs={{0,4},{1,5},{2,6},{3,7},{4,8},{5,9},{6,10},{7,11},{8,12},{9,13},{1... | collective-permute-start | bytes 331784 | tf_op jit(solution)/shard_map/ppermute | solution.py:207
  230.1 4.9 %collective-permute-start.12 = (f32[27,8,128]{2,1,0:T(8,128)S(1)}, f32[27,8,128]{2,1,0:T(8,128)S(1)}, u32[]{:S(2)}, u32[]{:S(2)}) collective-permute-start(f32[27,8,128]{2,1,0:T(8,128)S(1)} %dynamic-slice_bitcast_fusion.11), channel_id=1, source_target_pairs={{0,12},{1,13},{2,14},{3,15},{4,0},{5,1},{6,2},{7,3},{8,4},{9,5},{1... | collective-permute-start | bytes 331784 | tf_op jit(solution)/shard_map/ppermute | solution.py:207
  234.9 6.3 %collective-permute-start.10 = (f32[27,8,128]{2,1,0:T(8,128)S(1)}, f32[27,8,128]{2,1,0:T(8,128)S(1)}, u32[]{:S(2)}, u32[]{:S(2)}) collective-permute-start(f32[27,8,128]{2,1,0:T(8,128)S(1)} %get-tuple-element.80), channel_id=1, source_target_pairs={{0,4},{1,5},{2,6},{3,7},{4,8},{5,9},{6,10},{7,11},{8,12},{9,13},{1... | collective-permute-start | bytes 331784 | tf_op jit(solution)/shard_map/ppermute | solution.py:207
  235.1 6.3 %collective-permute-start.13 = (f32[27,8,128]{2,1,0:T(8,128)S(1)}, f32[27,8,128]{2,1,0:T(8,128)S(1)}, u32[]{:S(2)}, u32[]{:S(2)}) collective-permute-start(f32[27,8,128]{2,1,0:T(8,128)S(1)} %get-tuple-element.84), channel_id=1, source_target_pairs={{0,12},{1,13},{2,14},{3,15},{4,0},{5,1},{6,2},{7,3},{8,4},{9,5},{1... | collective-permute-start | bytes 331784 | tf_op jit(solution)/shard_map/ppermute | solution.py:207
  241.3 5.5 %collective-permute-start.11 = (f32[27,8,128]{2,1,0:T(8,128)S(1)}, f32[27,8,128]{2,1,0:T(8,128)S(1)}, u32[]{:S(2)}, u32[]{:S(2)}) collective-permute-start(f32[27,8,128]{2,1,0:T(8,128)S(1)} %get-tuple-element.78), channel_id=1, source_target_pairs={{0,4},{1,5},{2,6},{3,7},{4,8},{5,9},{6,10},{7,11},{8,12},{9,13},{1... | collective-permute-start | bytes 331784 | tf_op jit(solution)/shard_map/ppermute | solution.py:207
  241.5 5.4 %collective-permute-start.14 = (f32[27,8,128]{2,1,0:T(8,128)S(1)}, f32[27,8,128]{2,1,0:T(8,128)S(1)}, u32[]{:S(2)}, u32[]{:S(2)}) collective-permute-start(f32[27,8,128]{2,1,0:T(8,128)S(1)} %get-tuple-element.82), channel_id=1, source_target_pairs={{0,12},{1,13},{2,14},{3,15},{4,0},{5,1},{6,2},{7,3},{8,4},{9,5},{1... | collective-permute-start | bytes 331784 | tf_op jit(solution)/shard_map/ppermute | solution.py:207
  247.0 4.9 %collective-permute-start.17 = (f32[27,8,256]{2,1,0:T(8,128)S(1)}, f32[27,8,256]{2,1,0:T(8,128)S(1)}, u32[]{:S(2)}, u32[]{:S(2)}) collective-permute-start(f32[27,8,256]{2,1,0:T(8,128)S(1)} %pad_maximum_fusion.2), channel_id=1, source_target_pairs={{0,32},{16,48},{32,0},{48,16},{64,96},{80,112},{96,64},{112,80},{1... | collective-permute-start | bytes 663560 | tf_op jit(solution)/shard_map/ppermute | solution.py:223
  251.9 7.9 %collective-permute-start.18 = (f32[27,8,256]{2,1,0:T(8,128)S(1)}, f32[27,8,256]{2,1,0:T(8,128)S(1)}, u32[]{:S(2)}, u32[]{:S(2)}) collective-permute-start(f32[27,8,256]{2,1,0:T(8,128)S(1)} %add.451), channel_id=1, source_target_pairs={{0,64},{16,80},{32,96},{48,112},{64,0},{80,16},{96,32},{112,48},{1... | collective-permute-start | bytes 663560 | tf_op jit(solution)/shard_map/ppermute | solution.py:223
  259.8 4.8 %collective-permute-start.19 = (f32[27,8,256]{2,1,0:T(8,128)S(1)}, f32[27,8,256]{2,1,0:T(8,128)S(1)}, u32[]{:S(2)}, u32[]{:S(2)}) collective-permute-start(f32[27,8,256]{2,1,0:T(8,128)S(1)} %add.452), channel_id=1, source_target_pairs={{0,16},{16,0},{32,48},{48,32},{64,80},{80,64},{96,112},{112,96},{1... | collective-permute-start | bytes 663560 | tf_op jit(solution)/shard_map/ppermute | solution.py:225
  (4 other events, 21.0 us)

commit v14 on v11

--- a/solution.py
+++ b/solution.py
@@ -306,7 +306,7 @@
     grad_rows = grad_blocks.reshape(blocks_dev * voxels, channels)
     kernel_term = weight_grad_terms(table_index, table, grad_rows.T, offsets, scale)
     kernel_term, returned = lax.optimization_barrier((kernel_term, returned))
-    scattered = weight_grad_sum(kernel_term, n_shard, n_region)
+    scattered = lax.psum_scatter(kernel_term, "shard", scatter_dimension=1, tiled=True)
     kernel_term, table = lax.optimization_barrier((kernel_term, table))
     conv_out = conv_rows(table_index, table, weights, blocks_dev * voxels)
     input_acc = table_grad[:blocks_dev]
@@ -331,7 +331,7 @@
     )
     in_grad = input_acc.reshape(blocks_dev * voxels, channels).astype(jnp.bfloat16)
     scattered, conv_out, in_grad = lax.optimization_barrier((scattered, conv_out, in_grad))
-    weight_grad = weight_grad_finish(scattered, n_region)
+    weight_grad = region_sum(scattered, n_region)
     return (conv_out, in_grad, weight_grad)
 
 

time: 266 us -> 271 us (1.019)
  waiting for transfers between devices: 68.8 us -> 82.9 us
  starting transfers between devices: 48.5 us -> 44.7 us
  local copies, waits for them, and re-layouts: 29.4 us -> 25.7 us
    reduce_scatter x0 -> x1, waiting for transfers between devices: none -> 34.1 us  [body(): lax.psum_scatter(kernel_term, 'shard', scatter_dimension=1, tiled=True)]
    unnamed x2 -> x1, waiting for transfers between devices: 26.9 us -> 0.02 us
    ppermute x4 -> x3, starting transfers between devices: 16.7 us -> 5.73 us  [region_sum(): value = value + lax.ppermute(value, 'region', pairs)]
    ppermute x2, starting transfers between devices: 4.2 us -> 11.8 us  [padded(): lax.ppermute(head, axis, [((i + 1) % count, i) for i in range(ends)])]
    ppermute x4 -> x3, waiting for transfers between devices: 14.4 us -> 21.2 us  [region_sum(): value = value + lax.ppermute(value, 'region', pairs)]
    dynamic_slice x2 -> x0, local copies, waits for them, and re-layouts: 3.78 us -> none  [the longest x1 3.54 us: weight_grad_sum(): mine = lax.dynamic_index_in_dim(view, core, 2, keepdims=False)]
  transfers between devices with their start and end apart: 11 -> 10, of which waited for: 10 -> 9; matrix products, arithmetic and copies ran while one was open for 15% -> 15% of each run, Pallas kernels for 28% -> 27%
where the time goes in v14:
time: 271 us; the launch traced here: 268 us
  waiting for transfers between devices  82.9 us (31%)
  Pallas kernels  73.4 us (27%)
  starting transfers between devices  44.7 us (16%)
  local copies, waits for them, and re-layouts  25.7 us (9%)
  other arithmetic  18.2 us (7%)
  between operations  14.3 us (5%)
  matrix products  9.19 us (3%)
    reduce_scatter x1, waiting for transfers between devices, body(): lax.psum_scatter(kernel_term, 'shard', scatter_dimension=1, tiled=True)  34.1 us
    pallas_call x1, Pallas kernels, table_grad_sums(): pl.pallas_call(_table_grad_kernel, out_shape=jax.ShapeDtypeStruct((rows,...  27.3 us
    pallas_call x1, Pallas kernels, conv_rows(): pl.pallas_call(_conv_kernel, out_shape=jax.ShapeDtypeStruct((count, chann...  25.5 us
    ppermute x3, waiting for transfers between devices, region_sum(): value = value + lax.ppermute(value, 'region', pairs)  21.2 us
    pallas_call x1, Pallas kernels, weight_grad_terms(): pl.pallas_call(functools.partial(_weight_grad_kernel, scale=scale), out_s...  20.6 us
    all_to_all x1, waiting for transfers between devices, body(): lax.all_to_all(outgoing, 'shard', split_axis=0, concat_axis=0, tiled=True)  18.3 us
    ppermute x2, starting transfers between devices, padded(): lax.ppermute(head, axis, [((i + 1) % count, i) for i in range(ends)])  11.8 us
    unnamed x11, local copies, waits for them, and re-layouts  10.9 us
  transfers between devices with their start and end apart: 10, of which 9 were waited for; matrix products, arithmetic and copies ran while one was open for 15% of the time, Pallas kernels for 27%

profile of v14, /device:TPU:1, one launch (start us, length us, event | category | flops | bytes accessed | tf_op | source)
XLA Modules:
  0.0 268.3 jit_solution(17748336264305895997)
XLA Ops:
  10.1 2.9 %convolution_convert_fusion = bf16[16,4,128,256]{3,0,2,1:T(8,128)(2,1)S(1)} fusion(bf16[16,128,256]{2,1,0:T(8,128)(2,1)} %bitcast.39, s32[16,16]{0,1:T(8,128)S(1)} %copy.70, pred[16,16]{0,1:T(8,128)(4,1)S(1)} %copy.69), kind=kOutput, calls=%fused_computation.2 | convolution fusion | flops 69208064 | bytes 5244160 | tf_op jit(solution)/shard_map/pcj,jvd->pcvd/dot_general | solution.py:246
  13.0 3.5 %copy.73 = bf16[16,4,128,256]{3,2,1,0:T(8,128)(2,1)} copy(bf16[16,4,128,256]{3,0,2,1:T(8,128)(2,1)S(1)} %convolution_convert_fusion) | data formatting | bytes 8388608 | tf_op jit(solution)/shard_map/convert_element_type | solution.py:248
  16.5 8.7 %all-to-all-start = ((bf16[16,4,128,256]{3,2,1,0:T(8,128)(2,1)}), bf16[16,4,128,256]{3,2,1,0:T(8,128)(2,1)}, u32[]{:S(2)}, u32[]{:S(2)}) async-start(bf16[16,4,128,256]{3,2,1,0:T(8,128)(2,1)} %copy.73), calls=%async_computation | async-start | bytes 8388608 | tf_op jit(solution)/shard_map/all_to_all | solution.py:255
  28.1 27.3 %shard_map.67 = f32[89,128,256]{2,1,0:T(8,128)} custom-call(s32[432]{0:T(512)} %reshape.251.idx_ref, bf16[16,128,256]{2,1,0:T(8,128)(2,1)} %bitcast.43, bf16[27,256,256]{2,1,0:T(8,128)(2,1)} %w_ref.3), custom_call_target="tpu_custom_call" | custom-call | flops 7247757312 | bytes 16252928 | tf_op jit(solution)/shard_map/pallas_call | solution.py:59
  55.4 5.2 %convert.7 = bf16[89,128,256]{2,1,0:T(8,128)(2,1)S(1)} convert(f32[89,128,256]{2,1,0:T(8,128)} %shard_map.67) | non-fusion elementwise | flops 2916352 | bytes 17498112 | tf_op jit(solution)/shard_map/convert.4
  60.9 2.2 copy-done
  63.1 5.5 %copy.81 = bf16[16,4,128,256]{3,1,2,0:T(4,128)(2,1)} copy(bf16[16,4,128,256]{3,2,1,0:T(8,128)(2,1)S(1)} %bitcast.38) | data formatting | bytes 8388608 | tf_op jit(solution)/shard_map/reshape | solution.py:287
  68.6 18.3 %all-to-all-done = bf16[16,4,128,256]{3,2,1,0:T(8,128)(2,1)} async-done(((bf16[16,4,128,256]{3,2,1,0:T(8,128)(2,1)}), bf16[16,4,128,256]{3,2,1,0:T(8,128)(2,1)}, u32[]{:S(2)}, u32[]{:S(2)}) %all-to-all-start) | async-done | bytes 4194336 | tf_op jit(solution)/shard_map/all_to_all | solution.py:255
  86.9 9.5 %all-to-all-start.1 = ((bf16[16,4,128,256]{3,1,2,0:T(4,128)(2,1)}), bf16[16,4,128,256]{3,1,2,0:T(4,128)(2,1)}, u32[]{:S(2)}, u32[]{:S(2)}) async-start(bf16[16,4,128,256]{3,1,2,0:T(4,128)(2,1)} %copy.81), calls=%async_computation.1 | async-start | bytes 8388608 | tf_op jit(solution)/shard_map/all_to_all | solution.py:286
  99.1 6.0 %collective-permute-start = (bf16[4,128,256]{2,1,0:T(8,128)(2,1)S(1)}, bf16[4,128,256]{2,1,0:T(8,128)(2,1)S(1)}, u32[]{:S(2)}, u32[]{:S(2)}) collective-permute-start(bf16[4,128,256]{2,1,0:T(8,128)(2,1)S(1)} %get-tuple-element.37), channel_id=1, source_target_pairs={{0,16},{16,32},{32,48},{48,64},{64,80},{80,96},{96,112},{1,17},{17... | collective-permute-start | bytes 786440 | tf_op jit(solution)/shard_map/ppermute | solution.py:22
  109.6 3.6 %collective-permute-done.1 = bf16[4,128,256]{2,1,0:T(8,128)(2,1)} collective-permute-done((bf16[4,128,256]{2,1,0:T(8,128)(2,1)S(1)}, bf16[4,128,256]{2,1,0:T(8,128)(2,1)}, u32[]{:S(2)}, u32[]{:S(2)}) %collective-permute-start.1) | collective-permute-done | bytes 262176 | tf_op jit(solution)/shard_map/ppermute | solution.py:24
  114.3 4.7 %constant_dynamic-update-slice_fusion = bf16[89,128,256]{2,1,0:T(8,128)(2,1)} fusion(bf16[89,128,256]{2,1,0:T(8,128)(2,1)} %constant_dynamic-update-slice_fusion.1, bf16[64,128,256]{2,1,0:T(8,128)(2,1)} %bitcast.10), kind=kLoop, calls=%fused_computation.42 | loop fusion | bytes 8388608
  121.0 20.6 %shard_map.68 = f32[27,256,256]{2,1,0:T(8,128)} custom-call(s32[432]{0:T(512)} %reshape.251.idx_ref, bf16[89,128,256]{2,1,0:T(8,128)(2,1)} %broadcast_dynamic-update-slice_fusion.table_ref, bf16[256,2048]{1,0:T(8,128)(2,1)} %bitcast.44), custom_call_target="tpu_custom_call" | custom-call | flops 7247757312 | bytes 13959168 | tf_op jit(solution)/shard_map/pallas_call | solution.py:150
  141.7 2.9 %all-to-all-done.1 = bf16[16,4,128,256]{3,1,2,0:T(4,128)(2,1)} async-done(((bf16[16,4,128,256]{3,1,2,0:T(4,128)(2,1)}), bf16[16,4,128,256]{3,1,2,0:T(4,128)(2,1)}, u32[]{:S(2)}, u32[]{:S(2)}) %all-to-all-start.1) | async-done | bytes 4194336 | tf_op jit(solution)/shard_map/all_to_all | solution.py:286
  145.7 9.9 %collective-permute-start.3 = (bf16[4,128,256]{2,1,0:T(8,128)(2,1)S(1)}, bf16[4,128,256]{2,1,0:T(8,128)(2,1)S(1)}, u32[]{:S(2)}, u32[]{:S(2)}) collective-permute-start(bf16[4,128,256]{2,1,0:T(8,128)(2,1)S(1)} %get-tuple-element.36), channel_id=1, source_target_pairs={{16,0},{32,16},{48,32},{64,48},{80,64},{96,80},{112,96},{17,1},{33... | collective-permute-start | bytes 786440 | tf_op jit(solution)/shard_map/ppermute | solution.py:24
  155.6 3.0 %collective-permute-start.2 = (bf16[4,128,256]{2,1,0:T(8,128)(2,1)S(1)}, bf16[4,128,256]{2,1,0:T(8,128)(2,1)S(1)}, u32[]{:S(2)}, u32[]{:S(2)}) collective-permute-start(bf16[4,128,256]{2,1,0:T(8,128)(2,1)S(1)} %get-tuple-element.35), channel_id=1, source_target_pairs={{0,16},{16,32},{32,48},{48,64},{64,80},{80,96},{96,112},{1,17},{17... | collective-permute-start | bytes 786440 | tf_op jit(solution)/shard_map/ppermute | solution.py:22
  158.5 2.1 collective-permute-done.3
  162.4 4.6 %fusion.3 = f32[16,128,256]{2,0,1:T(8,128)S(1)} fusion(bf16[16,4,128,256]{3,1,2,0:T(4,128)(2,1)} %all-to-all-done.1, s32[16,16]{0,1:T(8,128)S(1)} %copy.70, pred[16,16]{0,1:T(8,128)(4,1)S(1)} %copy.69), kind=kOutput, calls=%fused_computation.8 | convolution fusion | flops 67110912 | bytes 6292736 | tf_op jit(solution)/shard_map/pcj,pcvd->jvd/dot_general | solution.py:313
  166.9 6.0 %fusion.2 = bf16[16,128,256]{2,1,0:T(8,128)(2,1)} fusion(f32[16,128,256]{2,0,1:T(8,128)S(1)} %fusion.11, f32[16,128,256]{2,0,1:T(8,128)S(1)} %fusion.13, f32[16,128,256]{2,0,1:T(8,128)S(1)} %fusion.3, f32[89,128,256]{2,1,0:T(8,128)} %shard_map.67), kind=kLoop, calls=%fused_computation.4 | loop fusion | flops 2097152 | bytes 9437184 | tf_op jit(solution)/shard_map/convert_element_type | solution.py:332
  172.9 25.5 %shard_map.69 = bf16[2048,256]{1,0:T(8,128)(2,1)} custom-call(s32[432]{0:T(512)} %reshape.251.idx_ref, bf16[89,128,256]{2,1,0:T(8,128)(2,1)} %broadcast_dynamic-update-slice_fusion.table_ref, bf16[27,256,256]{2,1,0:T(8,128)(2,1)} %w_ref.3), custom_call_target="tpu_custom_call" | custom-call | flops 7247757312 | bytes 10420224 | tf_op jit(solution)/shard_map/pallas_call | solution.py:108
  198.5 34.1 %reduce-scatter.2.cloned.1.call-done = f32[27,16,256]{2,1,0:T(8,128)} async-done(((f32[27,256,256]{2,1,0:T(8,128)}), f32[27,16,256]{2,1,0:T(8,128)}) %reduce-scatter.2.cloned.1.call-update) | async-done | bytes 442384 | tf_op jit(solution)/shard_map/reduce_scatter | solution.py:309
  238.3 10.3 %collective-permute-done.5 = f32[27,16,256]{2,1,0:T(8,128)S(1)} collective-permute-done((f32[27,16,256]{2,1,0:T(8,128)S(1)}, f32[27,16,256]{2,1,0:T(8,128)S(1)}, u32[]{:S(2)}, u32[]{:S(2)}) %collective-permute-start.5) | collective-permute-done | bytes 442400 | tf_op jit(solution)/shard_map/ppermute | solution.py:203
  248.6 2.7 %collective-permute-start.6 = (f32[27,16,256]{2,1,0:T(8,128)S(1)}, f32[27,16,256]{2,1,0:T(8,128)S(1)}, u32[]{:S(2)}, u32[]{:S(2)}) collective-permute-start(f32[27,16,256]{2,1,0:T(8,128)S(1)} %add.176), channel_id=1, source_target_pairs={{0,64},{16,80},{32,96},{48,112},{64,0},{80,16},{96,32},{112,48},{1... | collective-permute-start | bytes 1327112 | tf_op jit(solution)/shard_map/ppermute | solution.py:203
  251.4 9.3 %collective-permute-done.6 = f32[27,16,256]{2,1,0:T(8,128)S(1)} collective-permute-done((f32[27,16,256]{2,1,0:T(8,128)S(1)}, f32[27,16,256]{2,1,0:T(8,128)S(1)}, u32[]{:S(2)}, u32[]{:S(2)}) %collective-permute-start.6) | collective-permute-done | bytes 442400 | tf_op jit(solution)/shard_map/ppermute | solution.py:203
  (78 shorter events, 25.7 us)
Async XLA Ops:
  16.5 70.4 %all-to-all-start = ((bf16[16,4,128,256]{3,2,1,0:T(8,128)(2,1)}), bf16[16,4,128,256]{3,2,1,0:T(8,128)(2,1)}, u32[]{:S(2)}, u32[]{:S(2)}) async-start(bf16[16,4,128,256]{3,2,1,0:T(8,128)(2,1)} %copy.73), calls=%async_computation | async-start | bytes 8388608 | tf_op jit(solution)/shard_map/all_to_all | solution.py:255
  60.6 2.5 copy-start
  68.6 29.6 %copy-start.1 = (bf16[2048,256]{1,0:T(8,128)(2,1)S(1)}, bf16[2048,256]{1,0:T(8,128)(2,1)}, u32[]{:S(2)}) copy-start(bf16[2048,256]{1,0:T(8,128)(2,1)} %param.4) | copy-start | bytes 3145732
  68.6 38.4 %copy-start.2 = (bf16[2048,256]{1,0:T(8,128)(2,1)S(1)}, bf16[2048,256]{1,0:T(8,128)(2,1)}, u32[]{:S(2)}) copy-start(bf16[2048,256]{1,0:T(8,128)(2,1)} %param.7) | copy-start | bytes 3145732
  86.9 57.7 %all-to-all-start.1 = ((bf16[16,4,128,256]{3,1,2,0:T(4,128)(2,1)}), bf16[16,4,128,256]{3,1,2,0:T(4,128)(2,1)}, u32[]{:S(2)}, u32[]{:S(2)}) async-start(bf16[16,4,128,256]{3,1,2,0:T(4,128)(2,1)} %copy.81), calls=%async_computation.1 | async-start | bytes 8388608 | tf_op jit(solution)/shard_map/all_to_all | solution.py:286
  96.4 136.2 %reduce-scatter.2.cloned.1.call-start = ((), (), s32[]{:S(2)}) async-start(), calls=%async_computation.3 | async-start | bytes 7520256 | tf_op jit(solution)/shard_map/reduce_scatter | solution.py:309
  99.1 10.5 %collective-permute-start = (bf16[4,128,256]{2,1,0:T(8,128)(2,1)S(1)}, bf16[4,128,256]{2,1,0:T(8,128)(2,1)S(1)}, u32[]{:S(2)}, u32[]{:S(2)}) collective-permute-start(bf16[4,128,256]{2,1,0:T(8,128)(2,1)S(1)} %get-tuple-element.37), channel_id=1, source_target_pairs={{0,16},{16,32},{32,48},{48,64},{64,80},{80,96},{96,112},{1,17},{17... | collective-permute-start | bytes 786440 | tf_op jit(solution)/shard_map/ppermute | solution.py:22
  105.1 8.1 %collective-permute-start.1 = (bf16[4,128,256]{2,1,0:T(8,128)(2,1)S(1)}, bf16[4,128,256]{2,1,0:T(8,128)(2,1)}, u32[]{:S(2)}, u32[]{:S(2)}) collective-permute-start(bf16[4,128,256]{2,1,0:T(8,128)(2,1)S(1)} %get-tuple-element.38), channel_id=1, source_target_pairs={{16,0},{32,16},{48,32},{64,48},{80,64},{96,80},{112,96},{17,1},{33... | collective-permute-start | bytes 786440 | tf_op jit(solution)/shard_map/ppermute | solution.py:24
  145.7 15.0 %collective-permute-start.3 = (bf16[4,128,256]{2,1,0:T(8,128)(2,1)S(1)}, bf16[4,128,256]{2,1,0:T(8,128)(2,1)S(1)}, u32[]{:S(2)}, u32[]{:S(2)}) collective-permute-start(bf16[4,128,256]{2,1,0:T(8,128)(2,1)S(1)} %get-tuple-element.36), channel_id=1, source_target_pairs={{16,0},{32,16},{48,32},{64,48},{80,64},{96,80},{112,96},{17,1},{33... | collective-permute-start | bytes 786440 | tf_op jit(solution)/shard_map/ppermute | solution.py:24
  155.6 6.3 %collective-permute-start.2 = (bf16[4,128,256]{2,1,0:T(8,128)(2,1)S(1)}, bf16[4,128,256]{2,1,0:T(8,128)(2,1)S(1)}, u32[]{:S(2)}, u32[]{:S(2)}) collective-permute-start(bf16[4,128,256]{2,1,0:T(8,128)(2,1)S(1)} %get-tuple-element.35), channel_id=1, source_target_pairs={{0,16},{16,32},{32,48},{48,64},{64,80},{80,96},{96,112},{1,17},{17... | collective-permute-start | bytes 786440 | tf_op jit(solution)/shard_map/ppermute | solution.py:22
  232.6 3.4 %collective-permute-start.4 = (f32[27,16,256]{2,1,0:T(8,128)}, f32[27,16,256]{2,1,0:T(8,128)S(1)}, u32[]{:S(2)}, u32[]{:S(2)}) collective-permute-start(f32[27,16,256]{2,1,0:T(8,128)} %reduce-scatter.2.cloned.1.call-done), channel_id=1, source_target_pairs={{0,16},{16,0},{32,48},{48,32},{64,80},{80,64},{96,112},{112,96},{1... | collective-permute-start | bytes 1327112 | tf_op jit(solution)/shard_map/ppermute | solution.py:203
  237.1 11.5 %collective-permute-start.5 = (f32[27,16,256]{2,1,0:T(8,128)S(1)}, f32[27,16,256]{2,1,0:T(8,128)S(1)}, u32[]{:S(2)}, u32[]{:S(2)}) collective-permute-start(f32[27,16,256]{2,1,0:T(8,128)S(1)} %add.175), channel_id=1, source_target_pairs={{0,32},{16,48},{32,0},{48,16},{64,96},{80,112},{96,64},{112,80},{1... | collective-permute-start | bytes 1327112 | tf_op jit(solution)/shard_map/ppermute | solution.py:203
  248.6 12.0 %collective-permute-start.6 = (f32[27,16,256]{2,1,0:T(8,128)S(1)}, f32[27,16,256]{2,1,0:T(8,128)S(1)}, u32[]{:S(2)}, u32[]{:S(2)}) collective-permute-start(f32[27,16,256]{2,1,0:T(8,128)S(1)} %add.176), channel_id=1, source_target_pairs={{0,64},{16,80},{32,96},{48,112},{64,0},{80,16},{96,32},{112,48},{1... | collective-permute-start | bytes 1327112 | tf_op jit(solution)/shard_map/ppermute | solution.py:203
Sparse Core Ops, SparseCore 0:
  144.7 87.8 reduce-scatter.1

commit v15 on v11

--- a/solution.py
+++ b/solution.py
@@ -132,7 +132,7 @@
     )(table_index.reshape(-1), table, weights)
 
 
-def _weight_grad_kernel(idx_ref, table_ref, gradt_ref, wg_ref, g_ref, *, scale):
+def _weight_grad_kernel(idx_ref, core_ref, table_ref, gradt_ref, mine_ref, theirs_ref, g_ref, *, scale):
     k = pl.program_id(0)
     voxels = table_ref.shape[1]
     blocks = gradt_ref.shape[1] // voxels
@@ -141,23 +141,35 @@
         t = jnp.clip(idx_ref[k * blocks + b], 0, rows - 1)
         g_ref[pl.ds(b * voxels, voxels), :] = table_ref[t]
     flipped = jnp.dot(gradt_ref[...], g_ref[...], preferred_element_type=jnp.float32)
-    wg_ref[0] = flipped.T * scale
-
-
-def weight_grad_terms(table_index, table, gradt, offsets, scale):
+    term = flipped.T * scale
+    groups, _, sub, width = mine_ref.shape
+    split = term.reshape(groups, 2, sub, width)
+    low = split[:, 0]
+    high = split[:, 1]
+    first = core_ref[0] == 0
+    mine_ref[:, 0] = jnp.where(first, low, high)
+    theirs_ref[:, 0] = jnp.where(first, high, low)
+
+
+def weight_grad_terms(table_index, core, table, gradt, offsets, groups, scale):
     rows, voxels, channels = table.shape
     count = gradt.shape[1]
+    sub = channels // (groups * 2)
+    half = jax.ShapeDtypeStruct((groups, offsets, sub, channels), jnp.float32)
     return pl.pallas_call(
         functools.partial(_weight_grad_kernel, scale=scale),
-        out_shape=jax.ShapeDtypeStruct((offsets, channels, channels), jnp.float32),
+        out_shape=(half, half),
         grid_spec=pltpu.PrefetchScalarGridSpec(
-            num_scalar_prefetch=1,
+            num_scalar_prefetch=2,
             grid=(offsets,),
             in_specs=[
-                pl.BlockSpec((rows, voxels, channels), lambda k, idx: (0, 0, 0)),
-                pl.BlockSpec((channels, count), lambda k, idx: (0, 0)),
-            ],
-            out_specs=pl.BlockSpec((1, channels, channels), lambda k, idx: (k, 0, 0)),
+                pl.BlockSpec((rows, voxels, channels), lambda k, idx, c: (0, 0, 0)),
+                pl.BlockSpec((channels, count), lambda k, idx, c: (0, 0)),
+            ],
+            out_specs=[
+                pl.BlockSpec((groups, 1, sub, channels), lambda k, idx, c: (0, k, 0, 0)),
+                pl.BlockSpec((groups, 1, sub, channels), lambda k, idx, c: (0, k, 0, 0)),
+            ],
             scratch_shapes=[pltpu.VMEM((count, channels), jnp.bfloat16)],
         ),
         cost_estimate=pl.CostEstimate(
@@ -168,18 +180,13 @@
         compiler_params=pltpu.CompilerParams(
             dimension_semantics=("arbitrary",), vmem_limit_bytes=56 * 1024 * 1024
         ),
-    )(table_index.reshape(-1), table, gradt)
-
-
-def weight_grad_sum(term, n_shard, n_region):
-    offsets, channels, width = term.shape
-    sub = channels // (n_shard * 2)
-    core = lax.axis_index("region") % 2
-    view = term.reshape(offsets, n_shard, 2, sub, width)
-    mine = lax.dynamic_index_in_dim(view, core, 2, keepdims=False)
-    theirs = lax.dynamic_index_in_dim(view, 1 - core, 2, keepdims=False)
+    )(table_index.reshape(-1), core.reshape(1), table, gradt)
+
+
+def weight_grad_sum(terms, n_shard, n_region):
+    mine, theirs = terms
     swap = [(i, i ^ 1) for i in range(n_region)]
-    pair = jnp.swapaxes(mine + lax.ppermute(theirs, "region", swap), 0, 1)
+    pair = mine + lax.ppermute(theirs, "region", swap)
     return lax.psum_scatter(pair, "shard", scatter_dimension=0, tiled=True)[0]
 
 
@@ -304,7 +311,8 @@
     )
     scale = 1.0 / math.sqrt(total_blocks * voxels)
     grad_rows = grad_blocks.reshape(blocks_dev * voxels, channels)
-    kernel_term = weight_grad_terms(table_index, table, grad_rows.T, offsets, scale)
+    core = (lax.axis_index("region") % 2).astype(jnp.int32)
+    kernel_term = weight_grad_terms(table_index, core, table, grad_rows.T, offsets, n_shard, scale)
     kernel_term, returned = lax.optimization_barrier((kernel_term, returned))
     scattered = weight_grad_sum(kernel_term, n_shard, n_region)
     kernel_term, table = lax.optimization_barrier((kernel_term, table))

time: 266 us -> 264 us (level)
  local copies, waits for them, and re-layouts: 29.4 us -> 25.4 us
    add x0 -> x1, other arithmetic: none -> 4.33 us  [weight_grad_sum(): pair = mine + lax.ppermute(theirs, 'region', swap)]
    dynamic_slice x2 -> x0, local copies, waits for them, and re-layouts: 3.78 us -> none  [the longest x1 3.54 us: weight_grad_sum(): mine = lax.dynamic_index_in_dim(view, core, 2, keepdims=False)]
where the time goes in v15:
time: 264 us; the launch traced here: 262 us
  Pallas kernels  73.8 us (28%)
  waiting for transfers between devices  68.7 us (26%)
  starting transfers between devices  48.4 us (18%)
  local copies, waits for them, and re-layouts  25.4 us (10%)
  other arithmetic  22.4 us (8%)
  between operations  14.3 us (5%)
  matrix products  9.21 us (3%)
    pallas_call x1, Pallas kernels, table_grad_sums(): pl.pallas_call(_table_grad_kernel, out_shape=jax.ShapeDtypeStruct((rows,...  27.3 us
    unnamed x2, waiting for transfers between devices  26.9 us
    pallas_call x1, Pallas kernels, conv_rows(): pl.pallas_call(_conv_kernel, out_shape=jax.ShapeDtypeStruct((count, chann...  25.5 us
    pallas_call x1, Pallas kernels, weight_grad_terms(): pl.pallas_call(functools.partial(_weight_grad_kernel, scale=scale), out_s...  21.1 us
    all_to_all x1, waiting for transfers between devices, body(): lax.all_to_all(outgoing, 'shard', split_axis=0, concat_axis=0, tiled=True)  18.3 us
    unnamed x11, local copies, waits for them, and re-layouts  10.8 us
    all_to_all x1, starting transfers between devices, body(): lax.all_to_all(remote_sums[:n_shard * capacity].reshape(n_shard, capacity...  9.51 us
    ppermute x2, starting transfers between devices, padded(): lax.ppermute(tail, axis, [(i, (i + 1) % count) for i in range(ends)])  9.31 us
  transfers between devices with their start and end apart: 11, of which 10 were waited for; matrix products, arithmetic and copies ran while one was open for 15% of the time, Pallas kernels for 28%

profile of v15, /device:TPU:1, one launch (start us, length us, event | category | flops | bytes accessed | tf_op | source)
XLA Modules:
  0.0 262.2 jit_solution(7774404813005954945)
XLA Ops:
  10.1 2.9 %convolution_convert_fusion = bf16[16,4,128,256]{3,0,2,1:T(8,128)(2,1)S(1)} fusion(bf16[16,128,256]{2,1,0:T(8,128)(2,1)} %bitcast.42, s32[16,16]{0,1:T(8,128)S(1)} %copy.70, pred[16,16]{0,1:T(8,128)(4,1)S(1)} %copy.69), kind=kOutput, calls=%fused_computation.2 | convolution fusion | flops 69208064 | bytes 5244160 | tf_op jit(solution)/shard_map/pcj,jvd->pcvd/dot_general | solution.py:253
  13.0 3.5 %copy.73 = bf16[16,4,128,256]{3,2,1,0:T(8,128)(2,1)} copy(bf16[16,4,128,256]{3,0,2,1:T(8,128)(2,1)S(1)} %convolution_convert_fusion) | data formatting | bytes 8388608 | tf_op jit(solution)/shard_map/convert_element_type | solution.py:255
  16.5 8.7 %all-to-all-start = ((bf16[16,4,128,256]{3,2,1,0:T(8,128)(2,1)}), bf16[16,4,128,256]{3,2,1,0:T(8,128)(2,1)}, u32[]{:S(2)}, u32[]{:S(2)}) async-start(bf16[16,4,128,256]{3,2,1,0:T(8,128)(2,1)} %copy.73), calls=%async_computation | async-start | bytes 8388608 | tf_op jit(solution)/shard_map/all_to_all | solution.py:262
  28.1 27.3 %shard_map.67 = f32[89,128,256]{2,1,0:T(8,128)} custom-call(s32[432]{0:T(512)} %reshape.254.idx_ref, bf16[16,128,256]{2,1,0:T(8,128)(2,1)} %bitcast.46, bf16[27,256,256]{2,1,0:T(8,128)(2,1)} %w_ref.3), custom_call_target="tpu_custom_call" | custom-call | flops 7247757312 | bytes 16252928 | tf_op jit(solution)/shard_map/pallas_call | solution.py:59
  55.3 5.2 %convert.7 = bf16[89,128,256]{2,1,0:T(8,128)(2,1)S(1)} convert(f32[89,128,256]{2,1,0:T(8,128)} %shard_map.67) | non-fusion elementwise | flops 2916352 | bytes 17498112 | tf_op jit(solution)/shard_map/convert.4
  63.0 5.5 %copy.81 = bf16[16,4,128,256]{3,1,2,0:T(4,128)(2,1)} copy(bf16[16,4,128,256]{3,2,1,0:T(8,128)(2,1)S(1)} %bitcast.41) | data formatting | bytes 8388608 | tf_op jit(solution)/shard_map/reshape | solution.py:294
  68.5 18.3 %all-to-all-done = bf16[16,4,128,256]{3,2,1,0:T(8,128)(2,1)} async-done(((bf16[16,4,128,256]{3,2,1,0:T(8,128)(2,1)}), bf16[16,4,128,256]{3,2,1,0:T(8,128)(2,1)}, u32[]{:S(2)}, u32[]{:S(2)}) %all-to-all-start) | async-done | bytes 4194336 | tf_op jit(solution)/shard_map/all_to_all | solution.py:262
  86.8 9.5 %all-to-all-start.1 = ((bf16[16,4,128,256]{3,1,2,0:T(4,128)(2,1)}), bf16[16,4,128,256]{3,1,2,0:T(4,128)(2,1)}, u32[]{:S(2)}, u32[]{:S(2)}) async-start(bf16[16,4,128,256]{3,1,2,0:T(4,128)(2,1)} %copy.81), calls=%async_computation.1 | async-start | bytes 8388608 | tf_op jit(solution)/shard_map/all_to_all | solution.py:293
  99.0 6.0 %collective-permute-start = (bf16[4,128,256]{2,1,0:T(8,128)(2,1)S(1)}, bf16[4,128,256]{2,1,0:T(8,128)(2,1)S(1)}, u32[]{:S(2)}, u32[]{:S(2)}) collective-permute-start(bf16[4,128,256]{2,1,0:T(8,128)(2,1)S(1)} %get-tuple-element.43), channel_id=1, source_target_pairs={{0,16},{16,32},{32,48},{48,64},{64,80},{80,96},{96,112},{1,17},{17... | collective-permute-start | bytes 786440 | tf_op jit(solution)/shard_map/ppermute | solution.py:22
  109.5 3.7 %collective-permute-done.1 = bf16[4,128,256]{2,1,0:T(8,128)(2,1)} collective-permute-done((bf16[4,128,256]{2,1,0:T(8,128)(2,1)S(1)}, bf16[4,128,256]{2,1,0:T(8,128)(2,1)}, u32[]{:S(2)}, u32[]{:S(2)}) %collective-permute-start.1) | collective-permute-done | bytes 262176 | tf_op jit(solution)/shard_map/ppermute | solution.py:24
  114.2 4.7 %constant_dynamic-update-slice_fusion = bf16[89,128,256]{2,1,0:T(8,128)(2,1)} fusion(bf16[89,128,256]{2,1,0:T(8,128)(2,1)} %constant_dynamic-update-slice_fusion.1, bf16[64,128,256]{2,1,0:T(8,128)(2,1)} %bitcast.11), kind=kLoop, calls=%fused_computation.45 | loop fusion | bytes 8388608
  121.0 21.1 %shard_map.68 = (f32[16,27,8,256]{3,2,1,0:T(8,128)}, f32[16,27,8,256]{3,2,1,0:T(8,128)}) custom-call(s32[432]{0:T(512)} %reshape.254.idx_ref, s32[1]{0:T(128)} %bitcast.2.core_ref, bf16[89,128,256]{2,1,0:T(8,128)(2,1)} %broadcast_dynamic-update-slice_fusion.table_ref, bf16[256,2048]{1,0:T(8,128)(2,1)} %bitcast.47), custom_call_target="tpu_custom_call" | custom-call | flops 7247757312 | bytes 13959168 | tf_op jit(solution)/shard_map/pallas_call | solution.py:159
  144.5 8.0 %collective-permute-start.2 = (f32[16,27,8,256]{3,2,1,0:T(8,128)}, f32[16,27,8,256]{3,2,1,0:T(8,128)S(1)}, u32[]{:S(2)}, u32[]{:S(2)}) collective-permute-start(f32[16,27,8,256]{3,2,1,0:T(8,128)} %get-tuple-element.20), channel_id=1, source_target_pairs={{0,16},{16,0},{32,48},{48,32},{64,80},{80,64},{96,112},{112,96},{1... | collective-permute-start | bytes 10616840 | tf_op jit(solution)/shard_map/ppermute | solution.py:189
  152.5 6.1 %collective-permute-done.2 = f32[16,27,8,256]{3,2,1,0:T(8,128)S(1)} collective-permute-done((f32[16,27,8,256]{3,2,1,0:T(8,128)}, f32[16,27,8,256]{3,2,1,0:T(8,128)S(1)}, u32[]{:S(2)}, u32[]{:S(2)}) %collective-permute-start.2) | collective-permute-done | bytes 3538976 | tf_op jit(solution)/shard_map/ppermute | solution.py:189
  158.5 4.3 %add.178 = f32[16,27,8,256]{3,2,1,0:T(8,128)} add(f32[16,27,8,256]{3,2,1,0:T(8,128)} %get-tuple-element.19, f32[16,27,8,256]{3,2,1,0:T(8,128)S(1)} %collective-permute-done.2) | non-fusion elementwise | flops 884736 | bytes 10616832 | tf_op jit(solution)/shard_map/add | solution.py:189
  166.3 3.3 %collective-permute-start.3 = (bf16[4,128,256]{2,1,0:T(8,128)(2,1)S(1)}, bf16[4,128,256]{2,1,0:T(8,128)(2,1)S(1)}, u32[]{:S(2)}, u32[]{:S(2)}) collective-permute-start(bf16[4,128,256]{2,1,0:T(8,128)(2,1)S(1)} %get-tuple-element.41), channel_id=1, source_target_pairs={{0,16},{16,32},{32,48},{48,64},{64,80},{80,96},{96,112},{1,17},{17... | collective-permute-start | bytes 786440 | tf_op jit(solution)/shard_map/ppermute | solution.py:22
  173.4 4.6 %fusion.3 = f32[16,128,256]{2,0,1:T(8,128)S(1)} fusion(bf16[16,4,128,256]{3,1,2,0:T(4,128)(2,1)} %all-to-all-done.1, s32[16,16]{0,1:T(8,128)S(1)} %copy.70, pred[16,16]{0,1:T(8,128)(4,1)S(1)} %copy.69), kind=kOutput, calls=%fused_computation.8 | convolution fusion | flops 67110912 | bytes 6292736 | tf_op jit(solution)/shard_map/pcj,pcvd->jvd/dot_general | solution.py:321
  177.9 6.0 %fusion.2 = bf16[16,128,256]{2,1,0:T(8,128)(2,1)} fusion(f32[16,128,256]{2,0,1:T(8,128)S(1)} %fusion.11, f32[16,128,256]{2,0,1:T(8,128)S(1)} %fusion.13, f32[16,128,256]{2,0,1:T(8,128)S(1)} %fusion.3, f32[89,128,256]{2,1,0:T(8,128)} %shard_map.67), kind=kLoop, calls=%fused_computation.4 | loop fusion | flops 2097152 | bytes 9437184 | tf_op jit(solution)/shard_map/convert_element_type | solution.py:340
  184.0 25.5 %shard_map.69 = bf16[2048,256]{1,0:T(8,128)(2,1)} custom-call(s32[432]{0:T(512)} %reshape.254.idx_ref, bf16[89,128,256]{2,1,0:T(8,128)(2,1)} %broadcast_dynamic-update-slice_fusion.table_ref, bf16[27,256,256]{2,1,0:T(8,128)(2,1)} %w_ref.3), custom_call_target="tpu_custom_call" | custom-call | flops 7247757312 | bytes 10420224 | tf_op jit(solution)/shard_map/pallas_call | solution.py:108
  209.4 26.9 %reduce-scatter.4.cloned.1.call-done = f32[1,27,8,256]{3,2,1,0:T(8,128)} async-done(((f32[16,27,8,256]{3,2,1,0:T(8,128)}), f32[1,27,8,256]{3,2,1,0:T(8,128)}) %reduce-scatter.4.cloned.1.call-update) | async-done | bytes 221200
  237.5 3.8 %collective-permute-done.5 = f32[27,8,256]{2,1,0:T(8,128)S(1)} collective-permute-done((f32[27,8,256]{2,1,0:T(8,128)}, f32[27,8,256]{2,1,0:T(8,128)S(1)}, u32[]{:S(2)}, u32[]{:S(2)}) %collective-permute-start.5) | collective-permute-done | bytes 221216 | tf_op jit(solution)/shard_map/ppermute | solution.py:198
  242.3 2.8 %collective-permute-start.6 = (f32[27,8,256]{2,1,0:T(8,128)S(1)}, f32[27,8,256]{2,1,0:T(8,128)S(1)}, u32[]{:S(2)}, u32[]{:S(2)}) collective-permute-start(f32[27,8,256]{2,1,0:T(8,128)S(1)} %add.182), channel_id=1, source_target_pairs={{0,64},{16,80},{32,96},{48,112},{64,0},{80,16},{96,32},{112,48},{1... | collective-permute-start | bytes 663560 | tf_op jit(solution)/shard_map/ppermute | solution.py:198
  245.1 3.6 %collective-permute-done.6 = f32[27,8,256]{2,1,0:T(8,128)S(1)} collective-permute-done((f32[27,8,256]{2,1,0:T(8,128)S(1)}, f32[27,8,256]{2,1,0:T(8,128)S(1)}, u32[]{:S(2)}, u32[]{:S(2)}) %collective-permute-start.6) | collective-permute-done | bytes 221216 | tf_op jit(solution)/shard_map/ppermute | solution.py:198
  248.7 4.7 %collective-permute-start.7 = (f32[27,8,256]{2,1,0:T(8,128)S(1)}, f32[27,8,256]{2,1,0:T(8,128)S(1)}, u32[]{:S(2)}, u32[]{:S(2)}) collective-permute-start(f32[27,8,256]{2,1,0:T(8,128)S(1)} %add.183), channel_id=1, source_target_pairs={{0,16},{16,0},{32,48},{48,32},{64,80},{80,64},{96,112},{112,96},{1... | collective-permute-start | bytes 663560 | tf_op jit(solution)/shard_map/ppermute | solution.py:200
  (82 shorter events, 32.1 us)
Async XLA Ops:
  16.5 70.4 %all-to-all-start = ((bf16[16,4,128,256]{3,2,1,0:T(8,128)(2,1)}), bf16[16,4,128,256]{3,2,1,0:T(8,128)(2,1)}, u32[]{:S(2)}, u32[]{:S(2)}) async-start(bf16[16,4,128,256]{3,2,1,0:T(8,128)(2,1)} %copy.73), calls=%async_computation | async-start | bytes 8388608 | tf_op jit(solution)/shard_map/all_to_all | solution.py:262
  60.5 2.5 copy-start
  68.5 29.7 %copy-start.1 = (bf16[2048,256]{1,0:T(8,128)(2,1)S(1)}, bf16[2048,256]{1,0:T(8,128)(2,1)}, u32[]{:S(2)}) copy-start(bf16[2048,256]{1,0:T(8,128)(2,1)} %param.4) | copy-start | bytes 3145732
  68.5 38.5 %copy-start.2 = (bf16[2048,256]{1,0:T(8,128)(2,1)S(1)}, bf16[2048,256]{1,0:T(8,128)(2,1)}, u32[]{:S(2)}) copy-start(bf16[2048,256]{1,0:T(8,128)(2,1)} %param.7) | copy-start | bytes 3145732
  86.8 57.7 %all-to-all-start.1 = ((bf16[16,4,128,256]{3,1,2,0:T(4,128)(2,1)}), bf16[16,4,128,256]{3,1,2,0:T(4,128)(2,1)}, u32[]{:S(2)}, u32[]{:S(2)}) async-start(bf16[16,4,128,256]{3,1,2,0:T(4,128)(2,1)} %copy.81), calls=%async_computation.1 | async-start | bytes 8388608 | tf_op jit(solution)/shard_map/all_to_all | solution.py:293
  96.4 139.9 %reduce-scatter.4.cloned.1.call-start = ((), (), s32[]{:S(2)}) async-start(), calls=%async_computation.3 | async-start | bytes 3760128
  99.0 10.5 %collective-permute-start = (bf16[4,128,256]{2,1,0:T(8,128)(2,1)S(1)}, bf16[4,128,256]{2,1,0:T(8,128)(2,1)S(1)}, u32[]{:S(2)}, u32[]{:S(2)}) collective-permute-start(bf16[4,128,256]{2,1,0:T(8,128)(2,1)S(1)} %get-tuple-element.43), channel_id=1, source_target_pairs={{0,16},{16,32},{32,48},{48,64},{64,80},{80,96},{96,112},{1,17},{17... | collective-permute-start | bytes 786440 | tf_op jit(solution)/shard_map/ppermute | solution.py:22
  105.0 8.1 %collective-permute-start.1 = (bf16[4,128,256]{2,1,0:T(8,128)(2,1)S(1)}, bf16[4,128,256]{2,1,0:T(8,128)(2,1)}, u32[]{:S(2)}, u32[]{:S(2)}) collective-permute-start(bf16[4,128,256]{2,1,0:T(8,128)(2,1)S(1)} %get-tuple-element.44), channel_id=1, source_target_pairs={{16,0},{32,16},{48,32},{64,48},{80,64},{96,80},{112,96},{17,1},{33... | collective-permute-start | bytes 786440 | tf_op jit(solution)/shard_map/ppermute | solution.py:24
  144.5 14.0 %collective-permute-start.2 = (f32[16,27,8,256]{3,2,1,0:T(8,128)}, f32[16,27,8,256]{3,2,1,0:T(8,128)S(1)}, u32[]{:S(2)}, u32[]{:S(2)}) collective-permute-start(f32[16,27,8,256]{3,2,1,0:T(8,128)} %get-tuple-element.20), channel_id=1, source_target_pairs={{0,16},{16,0},{32,48},{48,32},{64,80},{80,64},{96,112},{112,96},{1... | collective-permute-start | bytes 10616840 | tf_op jit(solution)/shard_map/ppermute | solution.py:189
  164.0 7.7 %collective-permute-start.4 = (bf16[4,128,256]{2,1,0:T(8,128)(2,1)S(1)}, bf16[4,128,256]{2,1,0:T(8,128)(2,1)S(1)}, u32[]{:S(2)}, u32[]{:S(2)}) collective-permute-start(bf16[4,128,256]{2,1,0:T(8,128)(2,1)S(1)} %get-tuple-element.42), channel_id=1, source_target_pairs={{16,0},{32,16},{48,32},{64,48},{80,64},{96,80},{112,96},{17,1},{33... | collective-permute-start | bytes 786440 | tf_op jit(solution)/shard_map/ppermute | solution.py:24
  166.3 6.6 %collective-permute-start.3 = (bf16[4,128,256]{2,1,0:T(8,128)(2,1)S(1)}, bf16[4,128,256]{2,1,0:T(8,128)(2,1)S(1)}, u32[]{:S(2)}, u32[]{:S(2)}) collective-permute-start(bf16[4,128,256]{2,1,0:T(8,128)(2,1)S(1)} %get-tuple-element.41), channel_id=1, source_target_pairs={{0,16},{16,32},{32,48},{48,64},{64,80},{80,96},{96,112},{1,17},{17... | collective-permute-start | bytes 786440 | tf_op jit(solution)/shard_map/ppermute | solution.py:22
  236.3 5.0 %collective-permute-start.5 = (f32[27,8,256]{2,1,0:T(8,128)}, f32[27,8,256]{2,1,0:T(8,128)S(1)}, u32[]{:S(2)}, u32[]{:S(2)}) collective-permute-start(f32[27,8,256]{2,1,0:T(8,128)} %bitcast.49), channel_id=1, source_target_pairs={{0,32},{16,48},{32,0},{48,16},{64,96},{80,112},{96,64},{112,80},{1... | collective-permute-start | bytes 663560 | tf_op jit(solution)/shard_map/ppermute | solution.py:198
  242.3 6.4 %collective-permute-start.6 = (f32[27,8,256]{2,1,0:T(8,128)S(1)}, f32[27,8,256]{2,1,0:T(8,128)S(1)}, u32[]{:S(2)}, u32[]{:S(2)}) collective-permute-start(f32[27,8,256]{2,1,0:T(8,128)S(1)} %add.182), channel_id=1, source_target_pairs={{0,64},{16,80},{32,96},{48,112},{64,0},{80,16},{96,32},{112,48},{1... | collective-permute-start | bytes 663560 | tf_op jit(solution)/shard_map/ppermute | solution.py:198
  248.7 5.8 %collective-permute-start.7 = (f32[27,8,256]{2,1,0:T(8,128)S(1)}, f32[27,8,256]{2,1,0:T(8,128)S(1)}, u32[]{:S(2)}, u32[]{:S(2)}) collective-permute-start(f32[27,8,256]{2,1,0:T(8,128)S(1)} %add.183), channel_id=1, source_target_pairs={{0,16},{16,0},{32,48},{48,32},{64,80},{80,64},{96,112},{112,96},{1... | collective-permute-start | bytes 663560 | tf_op jit(solution)/shard_map/ppermute | solution.py:200
Sparse Core Ops, SparseCore 0:
  163.0 73.2 reduce-scatter.3

commit v16 on v15

--- a/solution.py
+++ b/solution.py
@@ -250,9 +250,10 @@
     chosen_lower, _ = choose_slots(asked_lower, capacity)
     chosen_upper, _ = choose_slots(asked_upper, capacity)
     chosen_rims = jnp.concatenate([chosen_lower, chosen_upper], axis=0)
-    outgoing = jnp.einsum(
-        "pcj,jvd->pcvd", chosen.astype(jnp.bfloat16), own_blocks, preferred_element_type=jnp.float32
-    ).astype(jnp.bfloat16)
+    slot_source = jnp.where(
+        jnp.any(chosen, axis=-1), jnp.sum(jnp.where(chosen, block_range, 0), axis=-1), blocks_dev
+    )
+    outgoing = jnp.take(own_blocks, slot_source, axis=0, mode="fill", fill_value=0)
     rim_blocks = jnp.einsum(
         "cj,jvd->cvd",
         chosen_rims.astype(jnp.bfloat16),

time: 264 us -> 266 us (level)
  other arithmetic: 22.4 us -> 27 us
  matrix products: 9.21 us -> 6.32 us
    select_n x0 -> x2, other arithmetic: none -> 4.52 us  [body(): jnp.take(own_blocks, slot_source, axis=0, mode='fill', fill_value=0)]
    gather x0 -> x1, local copies, waits for them, and re-layouts: none -> 3.97 us  [body(): jnp.take(own_blocks, slot_source, axis=0, mode='fill', fill_value=0)]
    all_to_all x1, waiting for transfers between devices: 2.46 us -> 5.93 us  [body(): lax.all_to_all(remote_sums[:n_shard * capacity].reshape(n_shard, capacity...]
    convert_element_type x1 -> x0, local copies, waits for them, and re-layouts: 3.47 us -> none  [body(): outgoing = jnp.einsum('pcj,jvd->pcvd', chosen.astype(jnp.bfloat16), own_b...]
    dot_general x1 -> x0, matrix products: 2.92 us -> none  [body(): jnp.einsum('pcj,jvd->pcvd', chosen.astype(jnp.bfloat16), own_blocks, pref...]
where the time goes in v16:
time: 266 us; the launch traced here: 265 us
  Pallas kernels  73.8 us (28%)
  waiting for transfers between devices  70.5 us (27%)
  starting transfers between devices  46.4 us (17%)
  other arithmetic  27 us (10%)
  local copies, waits for them, and re-layouts  26.2 us (10%)
  between operations  14.3 us (5%)
  matrix products  6.32 us (2%)
    pallas_call x1, Pallas kernels, table_grad_sums(): pl.pallas_call(_table_grad_kernel, out_shape=jax.ShapeDtypeStruct((rows,...  27.3 us
    unnamed x2, waiting for transfers between devices  25.9 us
    pallas_call x1, Pallas kernels, conv_rows(): pl.pallas_call(_conv_kernel, out_shape=jax.ShapeDtypeStruct((count, chann...  25.5 us
    pallas_call x1, Pallas kernels, weight_grad_terms(): pl.pallas_call(functools.partial(_weight_grad_kernel, scale=scale), out_s...  21.1 us
    all_to_all x1, waiting for transfers between devices, body(): lax.all_to_all(outgoing, 'shard', split_axis=0, concat_axis=0, tiled=True)  17.7 us
    unnamed x11, local copies, waits for them, and re-layouts  10.8 us
    all_to_all x1, starting transfers between devices, body(): lax.all_to_all(remote_sums[:n_shard * capacity].reshape(n_shard, capacity...  10.5 us
    ppermute x2, starting transfers between devices, padded(): lax.ppermute(tail, axis, [(i, (i + 1) % count) for i in range(ends)])  8.72 us
  transfers between devices with their start and end apart: 11, of which 10 were waited for; matrix products, arithmetic and copies ran while one was open for 15% of the time, Pallas kernels for 28%

profile of v16, /device:TPU:1, one launch (start us, length us, event | category | flops | bytes accessed | tf_op | source)
XLA Modules:
  0.0 264.6 jit_solution(2202830848112196916)
XLA Ops:
  10.5 4.0 %gather_fusion = bf16[64,128,256]{2,1,0:T(8,128)(2,1)} fusion(bf16[16,128,256]{2,1,0:T(8,128)(2,1)} %bitcast.38, s32[1024]{0:T(1024)S(1)} %pad_clamp_fusion), kind=kCustom, calls=%fused_computation | custom fusion | bytes 8388864 | tf_op jit(solution)/shard_map/jit(_take)/gather | solution.py:256
  14.4 4.5 %broadcast_select_fusion = bf16[16,4,128,256]{3,2,1,0:T(8,128)(2,1)} fusion(bf16[16,4,128,256]{3,2,1,0:T(8,128)(2,1)} %bitcast.41, pred[16,4]{1,0:T(8,128)(4,1)S(1)} %copy.68), kind=kLoop, calls=%fused_computation.3 | loop fusion | flops 2097152 | bytes 8388672 | tf_op jit(solution)/shard_map/jit(_take)/select_n | solution.py:256
  18.9 8.7 %all-to-all-start = ((bf16[16,4,128,256]{3,2,1,0:T(8,128)(2,1)}), bf16[16,4,128,256]{3,2,1,0:T(8,128)(2,1)}, u32[]{:S(2)}, u32[]{:S(2)}) async-start(bf16[16,4,128,256]{3,2,1,0:T(8,128)(2,1)} %broadcast_select_fusion), calls=%async_computation | async-start | bytes 8388608 | tf_op jit(solution)/shard_map/all_to_all | solution.py:263
  30.5 27.3 %shard_map.67 = f32[89,128,256]{2,1,0:T(8,128)} custom-call(s32[432]{0:T(512)} %reshape.282.idx_ref, bf16[16,128,256]{2,1,0:T(8,128)(2,1)} %bitcast.44, bf16[27,256,256]{2,1,0:T(8,128)(2,1)} %w_ref.3), custom_call_target="tpu_custom_call" | custom-call | flops 7247757312 | bytes 16252928 | tf_op jit(solution)/shard_map/pallas_call | solution.py:59
  57.8 5.2 %convert.7 = bf16[89,128,256]{2,1,0:T(8,128)(2,1)S(1)} convert(f32[89,128,256]{2,1,0:T(8,128)} %shard_map.67) | non-fusion elementwise | flops 2916352 | bytes 17498112 | tf_op jit(solution)/shard_map/convert.4
  65.4 5.5 %copy.77 = bf16[16,4,128,256]{3,1,2,0:T(4,128)(2,1)} copy(bf16[16,4,128,256]{3,2,1,0:T(8,128)(2,1)S(1)} %bitcast.42) | data formatting | bytes 8388608 | tf_op jit(solution)/shard_map/reshape | solution.py:295
  71.0 17.7 %all-to-all-done = bf16[16,4,128,256]{3,2,1,0:T(8,128)(2,1)} async-done(((bf16[16,4,128,256]{3,2,1,0:T(8,128)(2,1)}), bf16[16,4,128,256]{3,2,1,0:T(8,128)(2,1)}, u32[]{:S(2)}, u32[]{:S(2)}) %all-to-all-start) | async-done | bytes 4194336 | tf_op jit(solution)/shard_map/all_to_all | solution.py:263
  88.7 10.5 %all-to-all-start.1 = ((bf16[16,4,128,256]{3,1,2,0:T(4,128)(2,1)}), bf16[16,4,128,256]{3,1,2,0:T(4,128)(2,1)}, u32[]{:S(2)}, u32[]{:S(2)}) async-start(bf16[16,4,128,256]{3,1,2,0:T(4,128)(2,1)} %copy.77), calls=%async_computation.1 | async-start | bytes 8388608 | tf_op jit(solution)/shard_map/all_to_all | solution.py:294
  101.8 5.4 %collective-permute-start = (bf16[4,128,256]{2,1,0:T(8,128)(2,1)S(1)}, bf16[4,128,256]{2,1,0:T(8,128)(2,1)S(1)}, u32[]{:S(2)}, u32[]{:S(2)}) collective-permute-start(bf16[4,128,256]{2,1,0:T(8,128)(2,1)S(1)} %get-tuple-element.43), channel_id=1, source_target_pairs={{0,16},{16,32},{32,48},{48,64},{64,80},{80,96},{96,112},{1,17},{17... | collective-permute-start | bytes 786440 | tf_op jit(solution)/shard_map/ppermute | solution.py:22
  111.7 3.7 %collective-permute-done.1 = bf16[4,128,256]{2,1,0:T(8,128)(2,1)} collective-permute-done((bf16[4,128,256]{2,1,0:T(8,128)(2,1)S(1)}, bf16[4,128,256]{2,1,0:T(8,128)(2,1)}, u32[]{:S(2)}, u32[]{:S(2)}) %collective-permute-start.1) | collective-permute-done | bytes 262176 | tf_op jit(solution)/shard_map/ppermute | solution.py:24
  116.5 4.7 %constant_dynamic-update-slice_fusion = bf16[89,128,256]{2,1,0:T(8,128)(2,1)} fusion(bf16[89,128,256]{2,1,0:T(8,128)(2,1)} %constant_dynamic-update-slice_fusion.1, bf16[64,128,256]{2,1,0:T(8,128)(2,1)} %bitcast.11), kind=kLoop, calls=%fused_computation.43 | loop fusion | bytes 8388608
  123.2 21.1 %shard_map.68 = (f32[16,27,8,256]{3,2,1,0:T(8,128)}, f32[16,27,8,256]{3,2,1,0:T(8,128)}) custom-call(s32[432]{0:T(512)} %reshape.282.idx_ref, s32[1]{0:T(128)} %bitcast.2.core_ref, bf16[89,128,256]{2,1,0:T(8,128)(2,1)} %broadcast_dynamic-update-slice_fusion.table_ref, bf16[256,2048]{1,0:T(8,128)(2,1)} %bitcast.45), custom_call_target="tpu_custom_call" | custom-call | flops 7247757312 | bytes 13959168 | tf_op jit(solution)/shard_map/pallas_call | solution.py:159
  144.3 5.9 %all-to-all-done.1 = bf16[16,4,128,256]{3,1,2,0:T(4,128)(2,1)} async-done(((bf16[16,4,128,256]{3,1,2,0:T(4,128)(2,1)}), bf16[16,4,128,256]{3,1,2,0:T(4,128)(2,1)}, u32[]{:S(2)}, u32[]{:S(2)}) %all-to-all-start.1) | async-done | bytes 4194336 | tf_op jit(solution)/shard_map/all_to_all | solution.py:294
  150.2 5.6 %collective-permute-start.2 = (f32[16,27,8,256]{3,2,1,0:T(8,128)}, f32[16,27,8,256]{3,2,1,0:T(8,128)S(1)}, u32[]{:S(2)}, u32[]{:S(2)}) collective-permute-start(f32[16,27,8,256]{3,2,1,0:T(8,128)} %get-tuple-element.20), channel_id=1, source_target_pairs={{0,16},{16,0},{32,48},{48,32},{64,80},{80,64},{96,112},{112,96},{1... | collective-permute-start | bytes 10616840 | tf_op jit(solution)/shard_map/ppermute | solution.py:189
  155.8 6.1 %collective-permute-done.2 = f32[16,27,8,256]{3,2,1,0:T(8,128)S(1)} collective-permute-done((f32[16,27,8,256]{3,2,1,0:T(8,128)}, f32[16,27,8,256]{3,2,1,0:T(8,128)S(1)}, u32[]{:S(2)}, u32[]{:S(2)}) %collective-permute-start.2) | collective-permute-done | bytes 3538976 | tf_op jit(solution)/shard_map/ppermute | solution.py:189
  161.8 4.3 %add.197 = f32[16,27,8,256]{3,2,1,0:T(8,128)} add(f32[16,27,8,256]{3,2,1,0:T(8,128)} %get-tuple-element.19, f32[16,27,8,256]{3,2,1,0:T(8,128)S(1)} %collective-permute-done.2) | non-fusion elementwise | flops 884736 | bytes 10616832 | tf_op jit(solution)/shard_map/add | solution.py:189
  169.6 3.3 %collective-permute-start.3 = (bf16[4,128,256]{2,1,0:T(8,128)(2,1)S(1)}, bf16[4,128,256]{2,1,0:T(8,128)(2,1)S(1)}, u32[]{:S(2)}, u32[]{:S(2)}) collective-permute-start(bf16[4,128,256]{2,1,0:T(8,128)(2,1)S(1)} %get-tuple-element.41), channel_id=1, source_target_pairs={{0,16},{16,32},{32,48},{48,64},{64,80},{80,96},{96,112},{1,17},{17... | collective-permute-start | bytes 786440 | tf_op jit(solution)/shard_map/ppermute | solution.py:22
  176.7 4.6 %fusion.3 = f32[16,128,256]{2,0,1:T(8,128)S(1)} fusion(bf16[16,4,128,256]{3,1,2,0:T(4,128)(2,1)} %all-to-all-done.1, s32[16,16]{0,1:T(8,128)S(1)} %copy.67, pred[16,16]{0,1:T(8,128)(4,1)S(1)} %copy.66), kind=kOutput, calls=%fused_computation.9 | convolution fusion | flops 67110912 | bytes 6292736 | tf_op jit(solution)/shard_map/pcj,pcvd->jvd/dot_general | solution.py:322
  181.3 6.0 %fusion.2 = bf16[16,128,256]{2,1,0:T(8,128)(2,1)} fusion(f32[16,128,256]{2,0,1:T(8,128)S(1)} %fusion.9, f32[16,128,256]{2,0,1:T(8,128)S(1)} %fusion.11, f32[16,128,256]{2,0,1:T(8,128)S(1)} %fusion.3, f32[89,128,256]{2,1,0:T(8,128)} %shard_map.67), kind=kLoop, calls=%fused_computation.5 | loop fusion | flops 2097152 | bytes 9437184 | tf_op jit(solution)/shard_map/convert_element_type | solution.py:341
  187.3 25.5 %shard_map.69 = bf16[2048,256]{1,0:T(8,128)(2,1)} custom-call(s32[432]{0:T(512)} %reshape.282.idx_ref, bf16[89,128,256]{2,1,0:T(8,128)(2,1)} %broadcast_dynamic-update-slice_fusion.table_ref, bf16[27,256,256]{2,1,0:T(8,128)(2,1)} %w_ref.3), custom_call_target="tpu_custom_call" | custom-call | flops 7247757312 | bytes 10420224 | tf_op jit(solution)/shard_map/pallas_call | solution.py:108
  212.8 25.9 %reduce-scatter.4.cloned.1.call-done = f32[1,27,8,256]{3,2,1,0:T(8,128)} async-done(((f32[16,27,8,256]{3,2,1,0:T(8,128)}), f32[1,27,8,256]{3,2,1,0:T(8,128)}) %reduce-scatter.4.cloned.1.call-update) | async-done | bytes 221200
  239.8 3.8 %collective-permute-done.5 = f32[27,8,256]{2,1,0:T(8,128)S(1)} collective-permute-done((f32[27,8,256]{2,1,0:T(8,128)}, f32[27,8,256]{2,1,0:T(8,128)S(1)}, u32[]{:S(2)}, u32[]{:S(2)}) %collective-permute-start.5) | collective-permute-done | bytes 221216 | tf_op jit(solution)/shard_map/ppermute | solution.py:198
  247.4 3.6 %collective-permute-done.6 = f32[27,8,256]{2,1,0:T(8,128)S(1)} collective-permute-done((f32[27,8,256]{2,1,0:T(8,128)S(1)}, f32[27,8,256]{2,1,0:T(8,128)S(1)}, u32[]{:S(2)}, u32[]{:S(2)}) %collective-permute-start.6) | collective-permute-done | bytes 221216 | tf_op jit(solution)/shard_map/ppermute | solution.py:198
  251.0 4.8 %collective-permute-start.7 = (f32[27,8,256]{2,1,0:T(8,128)S(1)}, f32[27,8,256]{2,1,0:T(8,128)S(1)}, u32[]{:S(2)}, u32[]{:S(2)}) collective-permute-start(f32[27,8,256]{2,1,0:T(8,128)S(1)} %add.202), channel_id=1, source_target_pairs={{0,16},{16,0},{32,48},{48,32},{64,80},{80,64},{96,112},{112,96},{1... | collective-permute-start | bytes 663560 | tf_op jit(solution)/shard_map/ppermute | solution.py:200
  (90 shorter events, 32.8 us)
Async XLA Ops:
  18.9 69.8 %all-to-all-start = ((bf16[16,4,128,256]{3,2,1,0:T(8,128)(2,1)}), bf16[16,4,128,256]{3,2,1,0:T(8,128)(2,1)}, u32[]{:S(2)}, u32[]{:S(2)}) async-start(bf16[16,4,128,256]{3,2,1,0:T(8,128)(2,1)} %broadcast_select_fusion), calls=%async_computation | async-start | bytes 8388608 | tf_op jit(solution)/shard_map/all_to_all | solution.py:263
  63.0 2.5 copy-start.1
  71.0 30.0 %copy-start = (bf16[2048,256]{1,0:T(8,128)(2,1)S(1)}, bf16[2048,256]{1,0:T(8,128)(2,1)}, u32[]{:S(2)}) copy-start(bf16[2048,256]{1,0:T(8,128)(2,1)} %param.4) | copy-start | bytes 3145732
  71.0 38.3 %copy-start.2 = (bf16[2048,256]{1,0:T(8,128)(2,1)S(1)}, bf16[2048,256]{1,0:T(8,128)(2,1)}, u32[]{:S(2)}) copy-start(bf16[2048,256]{1,0:T(8,128)(2,1)} %param.7) | copy-start | bytes 3145732
  88.7 61.5 %all-to-all-start.1 = ((bf16[16,4,128,256]{3,1,2,0:T(4,128)(2,1)}), bf16[16,4,128,256]{3,1,2,0:T(4,128)(2,1)}, u32[]{:S(2)}, u32[]{:S(2)}) async-start(bf16[16,4,128,256]{3,1,2,0:T(4,128)(2,1)} %copy.77), calls=%async_computation.1 | async-start | bytes 8388608 | tf_op jit(solution)/shard_map/all_to_all | solution.py:294
  99.2 139.4 %reduce-scatter.4.cloned.1.call-start = ((), (), s32[]{:S(2)}) async-start(), calls=%async_computation.3 | async-start | bytes 3760128
  101.8 9.9 %collective-permute-start = (bf16[4,128,256]{2,1,0:T(8,128)(2,1)S(1)}, bf16[4,128,256]{2,1,0:T(8,128)(2,1)S(1)}, u32[]{:S(2)}, u32[]{:S(2)}) collective-permute-start(bf16[4,128,256]{2,1,0:T(8,128)(2,1)S(1)} %get-tuple-element.43), channel_id=1, source_target_pairs={{0,16},{16,32},{32,48},{48,64},{64,80},{80,96},{96,112},{1,17},{17... | collective-permute-start | bytes 786440 | tf_op jit(solution)/shard_map/ppermute | solution.py:22
  107.3 8.1 %collective-permute-start.1 = (bf16[4,128,256]{2,1,0:T(8,128)(2,1)S(1)}, bf16[4,128,256]{2,1,0:T(8,128)(2,1)}, u32[]{:S(2)}, u32[]{:S(2)}) collective-permute-start(bf16[4,128,256]{2,1,0:T(8,128)(2,1)S(1)} %get-tuple-element.44), channel_id=1, source_target_pairs={{16,0},{32,16},{48,32},{64,48},{80,64},{96,80},{112,96},{17,1},{33... | collective-permute-start | bytes 786440 | tf_op jit(solution)/shard_map/ppermute | solution.py:24
  150.2 11.6 %collective-permute-start.2 = (f32[16,27,8,256]{3,2,1,0:T(8,128)}, f32[16,27,8,256]{3,2,1,0:T(8,128)S(1)}, u32[]{:S(2)}, u32[]{:S(2)}) collective-permute-start(f32[16,27,8,256]{3,2,1,0:T(8,128)} %get-tuple-element.20), channel_id=1, source_target_pairs={{0,16},{16,0},{32,48},{48,32},{64,80},{80,64},{96,112},{112,96},{1... | collective-permute-start | bytes 10616840 | tf_op jit(solution)/shard_map/ppermute | solution.py:189
  167.3 7.7 %collective-permute-start.4 = (bf16[4,128,256]{2,1,0:T(8,128)(2,1)S(1)}, bf16[4,128,256]{2,1,0:T(8,128)(2,1)S(1)}, u32[]{:S(2)}, u32[]{:S(2)}) collective-permute-start(bf16[4,128,256]{2,1,0:T(8,128)(2,1)S(1)} %get-tuple-element.42), channel_id=1, source_target_pairs={{16,0},{32,16},{48,32},{64,48},{80,64},{96,80},{112,96},{17,1},{33... | collective-permute-start | bytes 786440 | tf_op jit(solution)/shard_map/ppermute | solution.py:24
  169.6 6.6 %collective-permute-start.3 = (bf16[4,128,256]{2,1,0:T(8,128)(2,1)S(1)}, bf16[4,128,256]{2,1,0:T(8,128)(2,1)S(1)}, u32[]{:S(2)}, u32[]{:S(2)}) collective-permute-start(bf16[4,128,256]{2,1,0:T(8,128)(2,1)S(1)} %get-tuple-element.41), channel_id=1, source_target_pairs={{0,16},{16,32},{32,48},{48,64},{64,80},{80,96},{96,112},{1,17},{17... | collective-permute-start | bytes 786440 | tf_op jit(solution)/shard_map/ppermute | solution.py:22
  238.6 5.0 %collective-permute-start.5 = (f32[27,8,256]{2,1,0:T(8,128)}, f32[27,8,256]{2,1,0:T(8,128)S(1)}, u32[]{:S(2)}, u32[]{:S(2)}) collective-permute-start(f32[27,8,256]{2,1,0:T(8,128)} %bitcast.47), channel_id=1, source_target_pairs={{0,32},{16,48},{32,0},{48,16},{64,96},{80,112},{96,64},{112,80},{1... | collective-permute-start | bytes 663560 | tf_op jit(solution)/shard_map/ppermute | solution.py:198
  244.6 6.4 %collective-permute-start.6 = (f32[27,8,256]{2,1,0:T(8,128)S(1)}, f32[27,8,256]{2,1,0:T(8,128)S(1)}, u32[]{:S(2)}, u32[]{:S(2)}) collective-permute-start(f32[27,8,256]{2,1,0:T(8,128)S(1)} %add.201), channel_id=1, source_target_pairs={{0,64},{16,80},{32,96},{48,112},{64,0},{80,16},{96,32},{112,48},{1... | collective-permute-start | bytes 663560 | tf_op jit(solution)/shard_map/ppermute | solution.py:198
  251.0 5.9 %collective-permute-start.7 = (f32[27,8,256]{2,1,0:T(8,128)S(1)}, f32[27,8,256]{2,1,0:T(8,128)S(1)}, u32[]{:S(2)}, u32[]{:S(2)}) collective-permute-start(f32[27,8,256]{2,1,0:T(8,128)S(1)} %add.202), channel_id=1, source_target_pairs={{0,16},{16,0},{32,48},{48,32},{64,80},{80,64},{96,112},{112,96},{1... | collective-permute-start | bytes 663560 | tf_op jit(solution)/shard_map/ppermute | solution.py:200
Sparse Core Ops, SparseCore 0:
  166.3 72.2 reduce-scatter.3
